TPU v7x, 32 devices: a whole 2x2x4 slice. The times are simulated.
32 devices in a mesh: lang: 4 (over x, core), dp: 8 (over z, y).
Axes of the slice: x: 2, y: 2, z: 4, core: 2. Of those that a mesh axis runs over, the one named last changes fastest.
Arguments:
- src_emb: bfloat16 [4096, 768], P(('lang', 'dp')), may hold values from -6 to 6
- tgt_emb: bfloat16 [4, 1024, 768], P(None, ('lang', 'dp')), may hold values from -6 to 6
- slot_group: int32 [4], replicated, may hold values from 0 to 3, each once
- counts: int32 [4], replicated, may hold values from 256 to 1024, as said below
- align: int32 [4, 1024], P('lang'), may hold values from 0 to 1023, each once within a row
- pair_weight: float32 [4], replicated, may hold values from 4 to 40
Outputs:
- grad_src: bfloat16 [4096, 768], P(('lang', 'dp'))
- grad_tgt: bfloat16 [4, 1024, 768], P(None, ('lang', 'dp'))
- pair_loss: float32 [4], P('lang')
Inputs may be any that keep to these rules, and one draw needn't show every extreme that they name: `counts`: at least one pair has all 1024 sentences live. `align`: each row is a permutation.
All inputs are finite; a program needn't handle non-finite values.
Results may differ from a plain program's by a relative error of at most 0.0057.
Values may be sent and summed in bfloat16 or wider, within the bound.
No kernel may reach another device: no remote copies, remote signals or barrier semaphores. Data moves between devices by JAX's collectives and lax.ppermute only.
A program may use at most 64 MiB of HBM per device.

v0:
```python
import math

import jax
import jax.numpy as jnp
from jax import lax
from jax.sharding import PartitionSpec as P

MARGIN = 0.3
LOW_FILL = -1e30


def combined_all(value, axis, combine):
    everything = jax.tree.map(lambda part: lax.all_gather(part, axis), value)
    initial = jax.tree.map(lambda part: part[0], everything)

    def lap(k, so_far):
        return combine(so_far, jax.tree.map(lambda part: part[k], everything))

    return lax.fori_loop(1, lax.axis_size(axis), lap, initial)


def target_index(offset, col_count, row_count, per_slot, data_size):
    position = offset + jnp.arange(col_count, dtype=jnp.int32)
    source = position // row_count
    within = position % row_count
    return (within // per_slot * data_size + source) * per_slot + within % per_slot


def tile_scores(
    src_rows, tile_rows, offset, my_align, col_live_global, per_slot, data_size, inv_root
):
    row_count = src_rows.shape[0]
    tgt_index = target_index(offset, tile_rows.shape[0], row_count, per_slot, data_size)
    raw_dot = lax.dot_general(
        src_rows, tile_rows, (((1,), (1,)), ((), ())), preferred_element_type=jnp.float32
    )
    is_pos = tgt_index[None, :] == my_align[:, None]
    scores_f = raw_dot * inv_root - MARGIN * is_pos.astype(jnp.float32)
    col_ok = col_live_global[tgt_index] > 0.5
    return (scores_f, is_pos, col_ok)


def row_update(old_max, scores_f, col_ok):
    masked = jnp.where(col_ok[None, :], scores_f, LOW_FILL)
    new_max = jnp.maximum(old_max, jnp.max(masked, axis=1))
    fresh = jnp.sum(jnp.where(col_ok[None, :], jnp.exp(scores_f - new_max[:, None]), 0.0), axis=1)
    return (new_max, fresh)


def column_stats(scores_f, row_live):
    col_max = jnp.max(jnp.where(row_live[:, None], scores_f, LOW_FILL), axis=0)
    col_sum = jnp.sum(
        jnp.where(row_live[:, None], jnp.exp(scores_f - col_max[None, :]), 0.0), axis=0
    )
    return (col_max, col_sum)


def grad_block(scores_f, is_pos, col_ok, row_lse, col_lse_all, row_live, weight):
    both_live = row_live[:, None] & col_ok[None, :]
    by_row = jnp.where(both_live, jnp.exp(scores_f - row_lse[:, None]), 0.0)
    by_col = jnp.where(both_live, jnp.exp(scores_f - col_lse_all[None, :]), 0.0)
    pos_hit = (is_pos & row_live[:, None]).astype(jnp.float32)
    return (weight * (by_row + by_col - 2.0 * pos_hit)).astype(jnp.bfloat16)


def merge_columns(first_part, second_part):
    top_val = jnp.maximum(first_part[0], second_part[0])
    summed = first_part[1] * jnp.exp(first_part[0] - top_val) + second_part[1] * jnp.exp(
        second_part[0] - top_val
    )
    return (top_val, summed)


def per_device(src_emb, tgt_emb, slot_group, counts, align, pair_weight):
    lang_size = lax.axis_size("lang")
    data_size = lax.axis_size("dp")
    row_count, emb_width = src_emb.shape
    per_slot = tgt_emb.shape[1]
    pair_rows = row_count * data_size
    inv_root = 1.0 / math.sqrt(emb_width)
    group_index = lax.axis_index("lang")
    shard_index = lax.axis_index("dp")
    slot_ids = jnp.arange(lang_size, dtype=jnp.int32)
    slot_of_group = jnp.zeros((lang_size,), jnp.int32).at[slot_group].set(slot_ids)
    ordered = tgt_emb[slot_of_group]
    arrived = lax.all_to_all(ordered, "lang", split_axis=0, concat_axis=1, tiled=True)
    partner = arrived[0]
    live_count = counts[group_index]
    weight = pair_weight[group_index]
    pair_align = align[0]
    all_rows = jnp.arange(pair_rows, dtype=jnp.int32)
    col_live_global = (
        jnp.zeros((pair_rows,), jnp.float32)
        .at[pair_align]
        .set((all_rows < live_count).astype(jnp.float32))
    )
    my_rows = shard_index * row_count + jnp.arange(row_count, dtype=jnp.int32)
    row_live = my_rows < live_count
    my_align = lax.dynamic_slice_in_dim(pair_align, shard_index * row_count, row_count)
    gathered_index = target_index(0, pair_rows, row_count, per_slot, data_size)
    col_live_gathered = col_live_global[gathered_index]
    start_max = jnp.full((row_count,), LOW_FILL, jnp.float32)
    all_targets = lax.all_gather(partner, "dp", axis=0, tiled=True)
    scores_f, is_pos, col_ok = tile_scores(
        src_emb, all_targets, 0, my_align, col_live_global, per_slot, data_size, inv_root
    )
    row_max, row_sum = row_update(start_max, scores_f, col_ok)
    col_max, col_sum = column_stats(scores_f, row_live)
    pos_score = jnp.sum(jnp.where(is_pos, scores_f, 0.0), axis=1)
    merged_max, merged_sum = combined_all((col_max, col_sum), "dp", merge_columns)
    col_lse_all = merged_max + jnp.log(merged_sum + (1.0 - col_live_gathered))
    col_lse_global = jnp.zeros((pair_rows,), jnp.float32).at[gathered_index].set(col_lse_all)
    row_lse = row_max + jnp.log(row_sum + (1.0 - row_live.astype(jnp.float32)))
    terms = jnp.where(row_live, row_lse + col_lse_global[my_align] - 2.0 * pos_score, 0.0)
    loss_total = lax.psum(jnp.sum(terms), "dp")
    pair_loss = (loss_total / live_count.astype(jnp.float32)).reshape(1)
    grad_tile = grad_block(scores_f, is_pos, col_ok, row_lse, col_lse_all, row_live, weight)
    grad_rows = jnp.dot(grad_tile, all_targets, preferred_element_type=jnp.float32)
    own_terms = lax.psum_scatter(
        lax.dot_general(
            grad_tile, src_emb, (((0,), (0,)), ((), ())), preferred_element_type=jnp.float32
        ),
        "dp",
        scatter_dimension=0,
        tiled=True,
    )
    grad_src = (grad_rows * inv_root).astype(jnp.bfloat16)
    grad_local = (own_terms * inv_root).astype(jnp.bfloat16)
    returned = lax.all_to_all(
        grad_local.reshape(1, row_count, emb_width), "lang", split_axis=1, concat_axis=0, tiled=True
    )
    grad_tgt = returned[slot_group]
    return (grad_src, grad_tgt, pair_loss)


def solution(mesh):
    in_specs = (
        P(("lang", "dp"), None),
        P(None, ("lang", "dp"), None),
        P(),
        P(),
        P("lang", None),
        P(),
    )
    out_specs = (P(("lang", "dp"), None), P(None, ("lang", "dp"), None), P("lang"))
    return jax.shard_map(
        per_device, mesh=mesh, in_specs=in_specs, out_specs=out_specs, check_vma=False
    )
```

profile of v0, /device:TPU:0, one launch (start us, length us, event | category | flops | bytes accessed | tf_op | source)
XLA Modules:
  0.0 235.0 jit_solution(11630180335252715976)
XLA Ops:
  7.2 0.0 copy-start
  7.2 0.0 all-gather.4.cloned.1.call-start
  7.2 0.7 compare_select_fusion.9
  7.9 0.6 scatter_custom_fusion.1
  8.5 1.5 gather_fusion.1
  10.0 9.4 %all_to_all.21 = bf16[4,32,768]{2,1,0:T(8,128)(2,1)} all-to-all(bf16[4,32,768]{2,1,0:T(8,128)(2,1)S(1)} %gather_fusion.1), channel_id=1, replica_groups=mesh['lang'=4,'dp'=8] {'lang'}, dimensions={0} | all-to-all | bytes 393216 | tf_op jit(solution)/shard_map/all_to_all | solution.py:86
  19.5 0.0 all-gather.4.cloned.1.call-update
  19.5 0.0 reduce-scatter.2.cloned.1.call-start
  19.6 1.2 dynamic_slice.32
  20.8 1.3 dynamic_slice.31
  22.1 0.6 fusion.29
  22.7 0.7 compare_select_fusion.3
  23.4 4.3 %scatter_custom_fusion = f32[1024]{0:T(1024)S(1)} fusion(s32[1024]{0:T(1024)S(1)} %bitcast.43, f32[1024]{0:T(1024)S(1)} %fusion.29, f32[]{:T(128)} %constant.133.clone.1), kind=kCustom, calls=%fused_computation.86 | custom fusion | bytes 4100 | tf_op jit(solution)/shard_map/scatter | solution.py:95
  27.8 4.5 %gather_fusion = f32[1024]{0:T(1024)S(1)} fusion(f32[1024]{0:T(1024)S(1)} %scatter_custom_fusion, s32[1024]{0:T(1024)S(1)} %broadcast_clamp_fusion), kind=kCustom, calls=%fused_computation | custom fusion | bytes 12288 | tf_op jit(solution)/shard_map/gather | solution.py:39
  32.3 0.7 add_compare_fusion
  33.0 0.7 fusion.38
  33.6 0.7 fusion.35
  34.3 30.3 %all-gather.4.cloned.1.call-done = bf16[1024,768]{1,0:T(8,128)(2,1)} async-done(((bf16[128,768]{1,0:T(8,128)(2,1)}), bf16[1024,768]{1,0:T(8,128)(2,1)}) %all-gather.4.cloned.1.call-update) | async-done | bytes 1572880 | tf_op jit(solution)/shard_map/all_gather | solution.py:103
  64.6 0.0 copy-done
  64.6 2.4 %select_reduce_fusion.3 = (f32[128]{0:T(128)S(1)}, f32[1024]{0:T(1024)S(1)}, f32[128,1024]{0,1:T(8,128)S(1)}) fusion(pred[1024]{0:T(1024)(128)(4,1)S(1)} %broadcast_compare_fusion, pred[128]{0:T(512)(128)(4,1)S(1)} %add_compare_fusion, s32[128]{0:T(128)S(1)} %fusion.38, s32[1024]{0:T(1024)S(1)} %fusion.19, ...), kind=kOutput, calls=%fused_computation.28 | convolution fusion | flops 202374016 | bytes 2304128 | tf_op jit(solution)/shard_map/dot_general | solution.py:34
  67.0 30.6 %all-gather = f32[8192]{0:T(1024)S(1)} all-gather(f32[1024]{0:T(1024)S(1)} %get-tuple-element.142), channel_id=2, replica_groups=mesh['lang'=4,'dp'=8] {'dp'}, dimensions={0}, use_global_device_ids=true | all-gather | bytes 36864 | tf_op jit(solution)/shard_map/all_gather | solution.py:13
  97.7 1.0 fusion.7
  98.7 30.6 %all-gather.1 = f32[8192]{0:T(1024)S(1)} all-gather(f32[1024]{0:T(1024)S(1)} %get-tuple-element.139), channel_id=3, replica_groups=mesh['lang'=4,'dp'=8] {'dp'}, dimensions={0}, use_global_device_ids=true | all-gather | bytes 36864 | tf_op jit(solution)/shard_map/all_gather | solution.py:13
  129.3 0.4 while.17
  129.7 4.3 %scatter_custom_fusion.2 = f32[1024]{0:T(1024)S(1)} fusion(s32[1024]{0:T(1024)S(1)} %bitcast.42, f32[1024]{0:T(1024)S(1)} %log_add_fusion, f32[]{:T(128)} %constant.133.clone.1), kind=kCustom, calls=%fused_computation.84 | custom fusion | bytes 4100 | tf_op jit(solution)/shard_map/scatter | solution.py:112
  134.1 1.0 gather_fusion.3
  135.0 1.3 select_reduce_fusion.4
  136.3 3.3 %fusion.39 = f32[1024,768]{1,0:T(8,128)} fusion(bf16[128,768]{1,0:T(8,128)(2,1)S(1)} %copy-done, f32[128,1024]{0,1:T(8,128)S(1)} %get-tuple-element.159, f32[1024]{0:T(1024)S(1)} %log_add_fusion, f32[128]{0:T(128)S(1)} %get-tuple-element.156, s32[128]{0:T(128)S(1)} %fusion.38, f32[]{:T(128)} %bitcast.2, s32[1024]{0:T(1024)S(1)} %fusion.19, ...), kind=kOutput, calls=%fused_computation.97 | convolution fusion | flops 202899456 | bytes 3876996 | tf_op jit(solution)/shard_map/dot_general | solution.py:120
  139.6 0.0 reduce-scatter.2.cloned.1.call-update
  139.7 0.0 copy-start.1
  140.4 19.9 %psum.7 = f32[]{:T(128)} all-reduce(f32[]{:T(128)} %get-tuple-element.155), channel_id=1, replica_groups=mesh['lang'=4,'dp'=8] {'dp'}, use_global_device_ids=true, to_apply=%region_12.13 | all-reduce | flops 1 | bytes 8 | tf_op jit(solution)/shard_map/psum | solution.py:115
  161.0 51.6 %reduce-scatter.2.cloned.1.call-done = f32[128,768]{1,0:T(8,128)} async-done(((f32[1024,768]{1,0:T(8,128)}), f32[128,768]{1,0:T(8,128)}) %reduce-scatter.2.cloned.1.call-update) | async-done | bytes 393232 | tf_op jit(solution)/shard_map/reduce_scatter | solution.py:119
  212.5 1.0 fusion.8
  213.5 0.3 copy.13
  213.8 0.5 broadcast.420
  214.4 1.8 reduce
  216.2 0.7 reshape.359
  216.9 3.4 %all-to-all-start.1 = ((bf16[4,2,12288]{2,1,0:T(2,128)(2,1)}), bf16[4,2,12288]{2,1,0:T(2,128)(2,1)S(1)}, u32[]{:S(2)}, u32[]{:S(2)}) async-start(bf16[4,2,12288]{2,1,0:T(2,128)(2,1)} %reshape.359), calls=%async_computation.2 | async-start | bytes 393216 | tf_op jit(solution)/shard_map/all_to_all | solution.py:129
  220.3 0.0 copy-done.1
  220.3 2.3 fusion.2
  222.6 2.9 %all-to-all-done.1 = bf16[4,2,12288]{2,1,0:T(2,128)(2,1)S(1)} async-done(((bf16[4,2,12288]{2,1,0:T(2,128)(2,1)}), bf16[4,2,12288]{2,1,0:T(2,128)(2,1)S(1)}, u32[]{:S(2)}, u32[]{:S(2)}) %all-to-all-start.1) | async-done | bytes 196640 | tf_op jit(solution)/shard_map/all_to_all | solution.py:129
  225.6 0.2 reshape.360
  225.8 1.2 gather_fusion.2
  (30 shorter events, 0.3 us)
Async XLA Ops:
  7.2 57.4 %copy-start = (bf16[128,768]{1,0:T(8,128)(2,1)S(1)}, bf16[128,768]{1,0:T(8,128)(2,1)}, u32[]{:S(2)}) copy-start(bf16[128,768]{1,0:T(8,128)(2,1)} %param.8) | copy-start | bytes 589828
  7.2 57.4 %all-gather.4.cloned.1.call-start = ((), (), s32[]{:S(2)}) async-start(), calls=%async_computation.3 | async-start | bytes 1769472 | tf_op jit(solution)/shard_map/all_gather | solution.py:103
  19.5 193.0 %reduce-scatter.2.cloned.1.call-start = ((), (), s32[]{:S(2)}) async-start(), calls=%async_computation.4 | async-start | bytes 3538944 | tf_op jit(solution)/shard_map/reduce_scatter | solution.py:119
  139.7 80.7 %copy-start.1 = (bf16[1024,768]{1,0:T(8,128)(2,1)S(1)}, bf16[1024,768]{1,0:T(8,128)(2,1)}, u32[]{:S(2)}) copy-start(bf16[1024,768]{1,0:T(8,128)(2,1)} %all-gather.4.cloned.1.call-done) | copy-start | bytes 4718596
  216.9 8.6 %all-to-all-start.1 = ((bf16[4,2,12288]{2,1,0:T(2,128)(2,1)}), bf16[4,2,12288]{2,1,0:T(2,128)(2,1)S(1)}, u32[]{:S(2)}, u32[]{:S(2)}) async-start(bf16[4,2,12288]{2,1,0:T(2,128)(2,1)} %reshape.359), calls=%async_computation.2 | async-start | bytes 393216 | tf_op jit(solution)/shard_map/all_to_all | solution.py:129
Sparse Core Ops, SparseCore 0:
  19.6 44.9 all-gather.3
  139.8 72.6 reduce-scatter.1
where the time goes:
time: 236 us; the launch traced here: 235 us
  blocking collectives  90.5 us (38%)
  waiting for transfers between devices  84.8 us (36%)
  local copies, waits for them, and re-layouts  22.5 us (10%)
  between operations  16.8 us (7%)
  other arithmetic  8.68 us (4%)
  matrix products  8.05 us (3%)
  starting transfers between devices  3.45 us (1%)
    all_gather x2, blocking collectives, combined_all(): everything = jax.tree.map(lambda part: lax.all_gather(part, axis), value)  61.2 us
    reduce_scatter x1, waiting for transfers between devices, per_device(): lax.psum_scatter(lax.dot_general(grad_tile, src_emb, (((0,), (0,)), ((),...  51.6 us
    all_gather x1, waiting for transfers between devices, per_device(): all_targets = lax.all_gather(partner, 'dp', axis=0, tiled=True)  30.3 us
    psum x1, blocking collectives, per_device(): loss_total = lax.psum(jnp.sum(terms), 'dp')  19.9 us
    all_to_all x1, blocking collectives, per_device(): lax.all_to_all(ordered, 'lang', split_axis=0, concat_axis=1, tiled=True)  9.44 us
  transfers between devices with their start and end apart: 3, of which 3 were waited for; matrix products, arithmetic and copies ran while one was open for 7% of the time, Pallas kernels for 0%

commit v1 on v0

v1 whole, which is shorter than its diff:
```python
import math

import jax
import jax.numpy as jnp
from jax import lax
from jax.sharding import PartitionSpec as P

MARGIN = 0.3
LOW_FILL = -1e30
BLOCK_BYTES = 8 * 1024 * 1024


def target_index(col_count, row_count, per_slot, data_size):
    position = jnp.arange(col_count, dtype=jnp.int32)
    source = position // row_count
    within = position % row_count
    return (within // per_slot * data_size + source) * per_slot + within % per_slot


def scores_of(x_rows, y_rows, pos_mask, inv_root):
    raw_dot = lax.dot_general(
        x_rows, y_rows, (((1,), (1,)), ((), ())), preferred_element_type=jnp.float32
    )
    return raw_dot * inv_root - MARGIN * pos_mask.astype(jnp.float32)


def block_stats(scores_f, is_pos, row_live, col_ok):
    row_max = jnp.max(jnp.where(col_ok[None, :], scores_f, LOW_FILL), axis=1)
    row_sum = jnp.sum(
        jnp.where(col_ok[None, :], jnp.exp(scores_f - row_max[:, None]), 0.0), axis=1
    )
    row_lse = row_max + jnp.log(row_sum + (1.0 - row_live.astype(jnp.float32)))
    pos_score = jnp.sum(jnp.where(is_pos, scores_f, 0.0), axis=1)
    col_max = jnp.max(jnp.where(row_live[:, None], scores_f, LOW_FILL), axis=0)
    col_sum = jnp.sum(
        jnp.where(row_live[:, None], jnp.exp(scores_f - col_max[None, :]), 0.0), axis=0
    )
    return row_lse, pos_score, col_max, col_sum


def grad_of(scores_f, is_pos, row_ok, col_ok, row_lse, col_lse, weight):
    both_live = row_ok[:, None] & col_ok[None, :]
    by_row = jnp.where(both_live, jnp.exp(scores_f - row_lse[:, None]), 0.0)
    by_col = jnp.where(both_live, jnp.exp(scores_f - col_lse[None, :]), 0.0)
    pos_hit = (is_pos & row_ok[:, None]).astype(jnp.float32)
    return (weight * (by_row + by_col - 2.0 * pos_hit)).astype(jnp.bfloat16)


def per_device(src_emb, tgt_emb, slot_group, counts, align, pair_weight):
    lang_size = lax.axis_size("lang")
    data_size = lax.axis_size("dp")
    row_count, emb_width = src_emb.shape
    per_slot = tgt_emb.shape[1]
    pair_rows = row_count * data_size
    inv_root = 1.0 / math.sqrt(emb_width)
    group_index = lax.axis_index("lang")
    shard_index = lax.axis_index("dp")
    slot_ids = jnp.arange(lang_size, dtype=jnp.int32)
    slot_of_group = jnp.zeros((lang_size,), jnp.int32).at[slot_group].set(slot_ids)
    ordered = tgt_emb[slot_of_group]
    arrived = lax.all_to_all(ordered, "lang", split_axis=0, concat_axis=1, tiled=True)
    partner = arrived[0]
    live_count = counts[group_index]
    weight = pair_weight[group_index]
    pair_align = align[0]
    all_rows = jnp.arange(pair_rows, dtype=jnp.int32)
    row_live = all_rows < live_count
    col_live_global = (
        jnp.zeros((pair_rows,), jnp.int32).at[pair_align].set(row_live.astype(jnp.int32))
    )
    perm = target_index(pair_rows, row_count, per_slot, data_size)
    col_live = col_live_global[perm] > 0
    x_all = lax.all_gather(src_emb, "dp", axis=0, tiled=True)
    y_all = lax.all_gather(partner, "dp", axis=0, tiled=True)

    block = max(1, min(pair_rows, BLOCK_BYTES // (4 * pair_rows)))
    steps = pair_rows // block
    if steps == 1:
        is_pos = perm[None, :] == pair_align[:, None]
        scores_f = scores_of(x_all, y_all, is_pos, inv_root)
        row_lse, pos_score, col_max, col_sum = block_stats(scores_f, is_pos, row_live, col_live)
    else:
        def one_block(k, carry):
            row_lse, pos_score, col_max, col_sum = carry
            start = k * block
            x_blk = lax.dynamic_slice_in_dim(x_all, start, block)
            a_blk = lax.dynamic_slice_in_dim(pair_align, start, block)
            r_blk = lax.dynamic_slice_in_dim(row_live, start, block)
            is_pos = perm[None, :] == a_blk[:, None]
            s_blk = scores_of(x_blk, y_all, is_pos, inv_root)
            b_lse, b_pos, b_max, b_sum = block_stats(s_blk, is_pos, r_blk, col_live)
            top = jnp.maximum(col_max, b_max)
            col_sum = col_sum * jnp.exp(col_max - top) + b_sum * jnp.exp(b_max - top)
            row_lse = lax.dynamic_update_slice_in_dim(row_lse, b_lse, start, 0)
            pos_score = lax.dynamic_update_slice_in_dim(pos_score, b_pos, start, 0)
            return row_lse, pos_score, top, col_sum

        zeros = jnp.zeros((pair_rows,), jnp.float32)
        init = (zeros, zeros, jnp.full((pair_rows,), LOW_FILL, jnp.float32), zeros)
        row_lse, pos_score, col_max, col_sum = lax.fori_loop(0, steps, one_block, init)
    col_lse = col_max + jnp.log(col_sum + (1.0 - col_live.astype(jnp.float32)))

    row_f = row_live.astype(jnp.float32)
    col_f = col_live.astype(jnp.float32)
    total = jnp.sum(row_f * (row_lse - 2.0 * pos_score)) + jnp.sum(col_f * col_lse)
    pair_loss = (total / live_count.astype(jnp.float32)).reshape(1)

    mine = shard_index * row_count
    x_my = lax.dynamic_slice_in_dim(x_all, mine, row_count)
    a_my = lax.dynamic_slice_in_dim(pair_align, mine, row_count)
    r_my = lax.dynamic_slice_in_dim(row_live, mine, row_count)
    lse_my = lax.dynamic_slice_in_dim(row_lse, mine, row_count)
    pos_rows = perm[None, :] == a_my[:, None]
    s_rows = scores_of(x_my, y_all, pos_rows, inv_root)
    g_rows = grad_of(s_rows, pos_rows, r_my, col_live, lse_my, col_lse, weight)
    grad_src = (
        jnp.dot(g_rows, y_all, preferred_element_type=jnp.float32) * inv_root
    ).astype(jnp.bfloat16)

    p_my = lax.dynamic_slice_in_dim(perm, mine, row_count)
    c_my = lax.dynamic_slice_in_dim(col_live, mine, row_count)
    clse_my = lax.dynamic_slice_in_dim(col_lse, mine, row_count)
    pos_cols = p_my[None, :] == pair_align[:, None]
    s_cols = scores_of(x_all, partner, pos_cols, inv_root)
    g_cols = grad_of(s_cols, pos_cols, row_live, c_my, row_lse, clse_my, weight)
    own_terms = lax.dot_general(
        g_cols, x_all, (((0,), (0,)), ((), ())), preferred_element_type=jnp.float32
    )
    grad_local = (own_terms * inv_root).astype(jnp.bfloat16)
    returned = lax.all_to_all(
        grad_local.reshape(1, row_count, emb_width), "lang", split_axis=1, concat_axis=0, tiled=True
    )
    grad_tgt = returned[slot_group]
    return (grad_src, grad_tgt, pair_loss)


def solution(mesh):
    in_specs = (
        P(("lang", "dp"), None),
        P(None, ("lang", "dp"), None),
        P(),
        P(),
        P("lang", None),
        P(),
    )
    out_specs = (P(("lang", "dp"), None), P(None, ("lang", "dp"), None), P("lang"))
    return jax.shard_map(
        per_device, mesh=mesh, in_specs=in_specs, out_specs=out_specs, check_vma=False
    )
```

time: 236 us -> 134 us (0.57)
  blocking collectives: 90.5 us -> 9.44 us
  waiting for transfers between devices: 84.8 us -> 69.6 us
  local copies, waits for them, and re-layouts: 22.5 us -> 15.2 us
    all_gather x2 -> x0, blocking collectives: 61.2 us -> none  [combined_all(): everything = jax.tree.map(lambda part: lax.all_gather(part, axis), value)]
    reduce_scatter x1 -> x0, waiting for transfers between devices: 51.6 us -> none  [per_device(): lax.psum_scatter(lax.dot_general(grad_tile, src_emb, (((0,), (0,)), ((),...]
    all_gather x1 -> x2, waiting for transfers between devices: 30.3 us -> 68.9 us  [the longest x1 44.8 us: per_device(): y_all = lax.all_gather(partner, 'dp', axis=0, tiled=True)]
    psum x1 -> x0, blocking collectives: 19.9 us -> none  [per_device(): loss_total = lax.psum(jnp.sum(terms), 'dp')]
    scatter x2 -> x1, local copies, waits for them, and re-layouts: 8.62 us -> 4.31 us  [per_device(): jnp.zeros((pair_rows,), jnp.int32).at[pair_align]]
    all_to_all x1, waiting for transfers between devices: 2.94 us -> 0.01 us  [per_device(): lax.all_to_all(grad_local.reshape(1, row_count, emb_width), 'lang', split...]
    dot_general x3, matrix products: 8.05 us -> 10.4 us  [the longest x1 4.5 us: scores_of(): lax.dot_general(x_rows, y_rows, (((1,), (1,)), ((), ())), preferred_eleme...]
    gather x2 -> x1, local copies, waits for them, and re-layouts: 5.5 us -> 4.53 us  [per_device(): col_live = col_live_global[perm] > 0]
  transfers between devices with their start and end apart: 3 -> 3, of which waited for: 3 -> 2; matrix products, arithmetic and copies ran while one was open for 7% -> 14% of each run, Pallas kernels for 0% -> 0%
where the time goes in v1:
time: 134 us
  waiting for transfers between devices  69.6 us (52%)
  between operations  17.3 us (13%)
  local copies, waits for them, and re-layouts  15.2 us (11%)
  matrix products  10.4 us (8%)
  blocking collectives  9.44 us (7%)
  other arithmetic  8.34 us (6%)
  starting transfers between devices  3.44 us (3%)
    all_gather x1, waiting for transfers between devices, per_device(): y_all = lax.all_gather(partner, 'dp', axis=0, tiled=True)  44.8 us
    all_gather x1, waiting for transfers between devices, per_device(): x_all = lax.all_gather(src_emb, 'dp', axis=0, tiled=True)  24.2 us
    all_to_all x1, blocking collectives, per_device(): lax.all_to_all(ordered, 'lang', split_axis=0, concat_axis=1, tiled=True)  9.44 us
    gather x1, local copies, waits for them, and re-layouts, per_device(): col_live = col_live_global[perm] > 0  4.53 us
    dot_general x1, matrix products, scores_of(): lax.dot_general(x_rows, y_rows, (((1,), (1,)), ((), ())), preferred_eleme...  4.5 us
    scatter x1, local copies, waits for them, and re-layouts, per_device(): jnp.zeros((pair_rows,), jnp.int32).at[pair_align]  4.31 us
    dot_general x1, matrix products, per_device(): jnp.dot(g_rows, y_all, preferred_element_type=jnp.float32) * inv_root  4.24 us
    all_to_all x1, starting transfers between devices, per_device(): lax.all_to_all(grad_local.reshape(1, row_count, emb_width), 'lang', split...  3.37 us
  transfers between devices with their start and end apart: 3, of which 2 were waited for; matrix products, arithmetic and copies ran while one was open for 14% of the time, Pallas kernels for 0%

profile of v1, /device:TPU:0, one launch (start us, length us, event | category | flops | bytes accessed | tf_op | source)
XLA Modules:
  0.0 133.8 jit_solution(15715575883117667560)
XLA Ops:
  7.2 0.0 copy-start
  7.2 0.0 copy-start.2
  7.2 0.0 copy-start.4
  7.2 0.0 all-gather.3.cloned.1.call-start
  7.2 0.7 all-gather.3.cloned.1.call-update
  7.9 0.0 all-gather.5.cloned.1.call-start
  8.0 0.7 compare_select_fusion.10
  8.6 0.6 scatter_custom_fusion.1
  9.3 0.0 copy-done
  9.3 0.6 gather_fusion.1
  9.8 9.4 %all_to_all.21 = bf16[4,32,768]{2,1,0:T(8,128)(2,1)} all-to-all(bf16[4,32,768]{2,1,0:T(8,128)(2,1)S(1)} %gather_fusion.1), channel_id=1, replica_groups=mesh['lang'=4,'dp'=8] {'lang'}, dimensions={0} | all-to-all | bytes 393216 | tf_op jit(solution)/shard_map/all_to_all | solution.py:61
  19.3 0.0 all-gather.5.cloned.1.call-update
  19.3 1.2 dynamic_slice.28
  21.2 0.7 fusion.61
  21.9 0.7 compare_select_fusion.5
  22.6 4.3 %scatter_custom_fusion = s32[1024]{0:T(1024)S(1)} fusion(s32[1024]{0:T(1024)S(1)} %bitcast.44, s32[1024]{0:T(1024)S(1)} %fusion.61, s32[]{:T(128)} %constant.94.clone.1), kind=kCustom, calls=%fused_computation.116 | custom fusion | bytes 4100 | tf_op jit(solution)/shard_map/scatter | solution.py:69
  26.9 4.5 %gather_fusion = s32[1024]{0:T(1024)S(1)} fusion(s32[1024]{0:T(1024)S(1)} %scatter_custom_fusion, s32[1024]{0:T(1024)S(1)} %broadcast_clamp_fusion), kind=kCustom, calls=%fused_computation | custom fusion | bytes 12288 | tf_op jit(solution)/shard_map/gather | solution.py:72
  31.5 0.1 dynamic_slice.33
  31.6 0.1 dynamic_slice.34
  31.7 0.0 copy-done.4
  31.7 0.6 dynamic_slice.27
  32.3 0.6 iota_compare_fusion
  32.9 0.1 dynamic_slice.29
  33.0 0.0 copy-done.2
  33.0 24.2 %all-gather.3.cloned.1.call-done = bf16[1024,768]{1,0:T(8,128)(2,1)} async-done(((bf16[128,768]{1,0:T(8,128)(2,1)}), bf16[1024,768]{1,0:T(8,128)(2,1)}) %all-gather.3.cloned.1.call-update) | async-done | bytes 1572880 | tf_op jit(solution)/shard_map/all_gather | solution.py:73
  57.2 44.8 %all-gather.5.cloned.1.call-done = bf16[1024,768]{1,0:T(8,128)(2,1)} async-done(((bf16[128,768]{1,0:T(8,128)(2,1)}), bf16[1024,768]{1,0:T(8,128)(2,1)}) %all-gather.5.cloned.1.call-update) | async-done | bytes 1572880 | tf_op jit(solution)/shard_map/all_gather | solution.py:74
  101.9 4.5 %select_reduce_fusion.3 = (f32[1024]{0:T(1024)S(1)}, f32[1024]{0:T(1024)S(1)}, f32[1024,1024]{0,1:T(8,128)S(1)}) fusion(pred[1024]{0:T(1024)(128)(4,1)S(1)} %broadcast_compare_fusion, pred[1024]{0:T(1024)(128)(4,1)S(1)} %iota_compare_fusion, s32[1024]{0:T(1024)S(1)} %bitcast.40, s32[1024]{0:T(1024)S(1)} %fusion.50, ...), kind=kOutput, calls=%fused_computation.12 | convolution fusion | flops 1618999296 | bytes 7358464 | tf_op jit(solution)/shard_map/dot_general | solution.py:21
  106.4 0.0 copy-start.1
  106.4 0.0 copy-start.3
  106.5 2.5 %fusion.1 = (f32[1024]{0:T(1024)S(1)}, f32[1024]{0:T(1024)S(1)}, f32[1024]{0:T(1024)S(1)}) fusion(f32[1024,1024]{0,1:T(8,128)S(1)} %get-tuple-element.12, s32[1024]{0:T(1024)S(1)} %bitcast.41, s32[1024]{0:T(1024)S(1)} %fusion.50, f32[1024]{0:T(1024)S(1)} %get-tuple-element.7, pred[1024]{0:T(1024)(128)(4,1)S(1)} %iota_compare_fusion, ...), kind=kLoop, calls=%fused_computation.8 | loop fusion | flops 9434112 | bytes 4225024 | tf_op jit(solution)/shard_map/reduce_sum | solution.py:33
  108.9 1.3 select_reduce_fusion.4
  110.2 0.1 dynamic_slice.35
  110.3 0.1 dynamic_slice.32
  110.4 0.0 copy-done.1
  110.4 0.0 copy-done.3
  110.4 1.7 %fusion.7 = bf16[1,128,768]{2,1,0:T(8,128)(2,1)S(1)} fusion(bf16[1024,768]{1,0:T(8,128)(2,1)S(1)} %copy-done.3, bf16[128,768]{1,0:T(8,128)(2,1)S(1)} %bitcast.38, f32[128]{0:T(128)S(1)} %dynamic_slice.35, f32[1024]{0:T(1024)S(1)} %get-tuple-element.14, s32[1024]{0:T(1024)S(1)} %bitcast.42, f32[]{:T(128)} %bitcast, s32[128]{0:T(128)S(1)} %dynamic_slice.34, ...), kind=kOutput, calls=%fused_computation.22 | convolution fusion | flops 404815872 | bytes 1976452 | tf_op jit(solution)/shard_map/dot_general | solution.py:126
  112.1 0.3 copy.13
  112.4 0.5 broadcast.415
  112.9 1.8 %reduce = bf16[128,768]{1,0:T(8,128)(2,1)S(1)} reduce(bf16[128,1,768]{2,1,0:T(2,128)(2,1)S(1)} %bitcast.36, bf16[]{:T(256)} %broadcast.415), dimensions={1}, to_apply=%bitcast.34.reduce_sub_computation | reduce | bytes 393218
  114.7 0.7 reshape.320
  115.5 3.4 %all-to-all-start.1 = ((bf16[4,2,12288]{2,1,0:T(2,128)(2,1)}), bf16[4,2,12288]{2,1,0:T(2,128)(2,1)S(1)}, u32[]{:S(2)}, u32[]{:S(2)}) async-start(bf16[4,2,12288]{2,1,0:T(2,128)(2,1)} %reshape.320), calls=%async_computation.1 | async-start | bytes 393216 | tf_op jit(solution)/shard_map/all_to_all | solution.py:130
  118.8 4.2 %fusion.5 = bf16[128,768]{1,0:T(8,128)(2,1)} fusion(bf16[1024,768]{1,0:T(8,128)(2,1)} %all-gather.5.cloned.1.call-done, f32[1024]{0:T(1024)S(1)} %get-tuple-element.9, f32[128]{0:T(128)S(1)} %dynamic_slice.32, s32[1024]{0:T(1024)S(1)} %fusion.50, f32[]{:T(128)} %bitcast, s32[128]{0:T(128)S(1)} %dynamic-slice_bitcast_fusion, ...), kind=kOutput, calls=%fused_computation.20 | convolution fusion | flops 404815872 | bytes 3550212 | tf_op jit(solution)/shard_map/dot_general | solution.py:117
  124.4 0.0 all-to-all-done.1
  124.4 0.2 reshape.321
  124.6 1.2 gather_fusion.2
  (10 shorter events, 0.1 us)
Async XLA Ops:
  7.2 2.1 %copy-start = (bf16[4,32,768]{2,1,0:T(8,128)(2,1)S(1)}, bf16[4,32,768]{2,1,0:T(8,128)(2,1)}, u32[]{:S(2)}) copy-start(bf16[4,32,768]{2,1,0:T(8,128)(2,1)} %param.7) | copy-start | bytes 589828
  7.2 25.8 %copy-start.2 = (s32[1,1024]{1,0:T(1,128)S(1)}, s32[1,1024]{1,0:T(1,128)}, u32[]{:S(2)}) copy-start(s32[1,1024]{1,0:T(1,128)} %param.10) | copy-start | bytes 12292
  7.2 24.5 %copy-start.4 = (f32[4]{0:T(128)S(1)}, f32[4]{0:T(128)}, u32[]{:S(2)}) copy-start(f32[4]{0:T(128)} %param.11) | copy-start | bytes 52
  7.2 50.0 %all-gather.3.cloned.1.call-start = ((), (), s32[]{:S(2)}) async-start(), calls=%async_computation.2 | async-start | bytes 1769472 | tf_op jit(solution)/shard_map/all_gather | solution.py:73
  7.9 94.0 %all-gather.5.cloned.1.call-start = ((), (), s32[]{:S(2)}) async-start(), calls=%async_computation.3 | async-start | bytes 1769472 | tf_op jit(solution)/shard_map/all_gather | solution.py:74
  106.4 4.0 %copy-start.1 = (bf16[4,32,768]{2,1,0:T(8,128)(2,1)S(1)}, bf16[4,32,768]{2,1,0:T(8,128)(2,1)}, u32[]{:S(2)}) copy-start(bf16[4,32,768]{2,1,0:T(8,128)(2,1)} %all_to_all.21) | copy-start | bytes 589828
  106.4 3.9 %copy-start.3 = (bf16[1024,768]{1,0:T(8,128)(2,1)S(1)}, bf16[1024,768]{1,0:T(8,128)(2,1)}, u32[]{:S(2)}) copy-start(bf16[1024,768]{1,0:T(8,128)(2,1)} %all-gather.3.cloned.1.call-done) | copy-start | bytes 4718596
  115.5 8.9 %all-to-all-start.1 = ((bf16[4,2,12288]{2,1,0:T(2,128)(2,1)}), bf16[4,2,12288]{2,1,0:T(2,128)(2,1)S(1)}, u32[]{:S(2)}, u32[]{:S(2)}) async-start(bf16[4,2,12288]{2,1,0:T(2,128)(2,1)} %reshape.320), calls=%async_computation.1 | async-start | bytes 393216 | tf_op jit(solution)/shard_map/all_to_all | solution.py:130
Sparse Core Ops, SparseCore 0:
  10.2 46.9 all-gather.2
  59.4 42.5 all-gather.4

commit v2 on v1

--- a/solution.py
+++ b/solution.py
@@ -1,3 +1,4 @@
+import functools
 import math
 
 import jax
@@ -15,6 +16,51 @@
     source = position // row_count
     within = position % row_count
     return (within // per_slot * data_size + source) * per_slot + within % per_slot
+
+
+def snake_ring(mesh):
+    count = mesh.shape["dp"]
+    try:
+        spots = [tuple(dev.coords) for dev in mesh.devices.reshape(-1, count)[0]]
+    except (AttributeError, TypeError):
+        return list(range(count))
+    ys = sorted({s[1] for s in spots})
+    zs = sorted({s[2] for s in spots})
+    where = {(s[1], s[2]): d for d, s in enumerate(spots)}
+    if len(where) != count or len(ys) * len(zs) != count:
+        return list(range(count))
+    rows, cols = (ys, zs) if len(ys) % 2 == 0 else (zs, ys)
+    at = lambda r, c: where[(r, c) if rows is ys else (c, r)]
+    if len(rows) == 1 or len(cols) == 1:
+        return [at(r, c) for r in rows for c in cols]
+    order = [at(rows[0], cols[0])]
+    for k, r in enumerate(rows):
+        seq = cols[1:] if k % 2 == 0 else cols[:0:-1]
+        order += [at(r, c) for c in seq]
+    order += [at(r, cols[0]) for r in rows[:0:-1]]
+    return order
+
+
+def ring_gather(block, ring):
+    count = len(ring)
+    place = [0] * count
+    for p, d in enumerate(ring):
+        place[d] = p
+    ring_arr = jnp.array(ring, jnp.int32)
+    my_dp = lax.axis_index("dp")
+    my_pos = jnp.array(place, jnp.int32)[my_dp]
+    ahead = [(ring[p], ring[(p + 1) % count]) for p in range(count)]
+    behind = [(ring[p], ring[(p - 1) % count]) for p in range(count)]
+    rows = block.shape[0]
+    out = jnp.zeros((count * rows,) + block.shape[1:], block.dtype)
+    out = lax.dynamic_update_slice_in_dim(out, block, my_dp * rows, 0)
+    for pairs, steps, sign in ((ahead, count // 2, -1), (behind, count - 1 - count // 2, 1)):
+        cur = block
+        for t in range(1, steps + 1):
+            cur = lax.ppermute(cur, "dp", pairs)
+            origin = ring_arr[(my_pos + sign * t) % count]
+            out = lax.dynamic_update_slice_in_dim(out, cur, origin * rows, 0)
+    return out
 
 
 def scores_of(x_rows, y_rows, pos_mask, inv_root):
@@ -46,7 +92,7 @@
     return (weight * (by_row + by_col - 2.0 * pos_hit)).astype(jnp.bfloat16)
 
 
-def per_device(src_emb, tgt_emb, slot_group, counts, align, pair_weight):
+def per_device(ring, src_emb, tgt_emb, slot_group, counts, align, pair_weight):
     lang_size = lax.axis_size("lang")
     data_size = lax.axis_size("dp")
     row_count, emb_width = src_emb.shape
@@ -65,13 +111,11 @@
     pair_align = align[0]
     all_rows = jnp.arange(pair_rows, dtype=jnp.int32)
     row_live = all_rows < live_count
-    col_live_global = (
-        jnp.zeros((pair_rows,), jnp.int32).at[pair_align].set(row_live.astype(jnp.int32))
-    )
     perm = target_index(pair_rows, row_count, per_slot, data_size)
-    col_live = col_live_global[perm] > 0
-    x_all = lax.all_gather(src_emb, "dp", axis=0, tiled=True)
-    y_all = lax.all_gather(partner, "dp", axis=0, tiled=True)
+    live_pos = (perm[None, :] == pair_align[:, None]) & row_live[:, None]
+    col_live = jnp.max(live_pos.astype(jnp.int32), axis=0) > 0
+    x_all = ring_gather(src_emb, ring)
+    y_all = ring_gather(partner, ring)
 
     block = max(1, min(pair_rows, BLOCK_BYTES // (4 * pair_rows)))
     steps = pair_rows // block
@@ -106,12 +150,11 @@
     pair_loss = (total / live_count.astype(jnp.float32)).reshape(1)
 
     mine = shard_index * row_count
-    x_my = lax.dynamic_slice_in_dim(x_all, mine, row_count)
     a_my = lax.dynamic_slice_in_dim(pair_align, mine, row_count)
     r_my = lax.dynamic_slice_in_dim(row_live, mine, row_count)
     lse_my = lax.dynamic_slice_in_dim(row_lse, mine, row_count)
     pos_rows = perm[None, :] == a_my[:, None]
-    s_rows = scores_of(x_my, y_all, pos_rows, inv_root)
+    s_rows = scores_of(src_emb, y_all, pos_rows, inv_root)
     g_rows = grad_of(s_rows, pos_rows, r_my, col_live, lse_my, col_lse, weight)
     grad_src = (
         jnp.dot(g_rows, y_all, preferred_element_type=jnp.float32) * inv_root
@@ -145,5 +188,5 @@
     )
     out_specs = (P(("lang", "dp"), None), P(None, ("lang", "dp"), None), P("lang"))
     return jax.shard_map(
-        per_device, mesh=mesh, in_specs=in_specs, out_specs=out_specs, check_vma=False
+        functools.partial(per_device, snake_ring(mesh)), mesh=mesh, in_specs=in_specs, out_specs=out_specs, check_vma=False
     )

time: 134 us -> 87.2 us (0.65)
  waiting for transfers between devices: 69.6 us -> 17.7 us
  starting transfers between devices: 3.44 us -> 24.1 us
  blocking collectives: 9.44 us -> 0 us
  between operations: 17.3 us -> 13.3 us
  matrix products: 10.4 us -> 7.97 us
    all_gather x2 -> x0, waiting for transfers between devices: 68.9 us -> none  [the longest x1 44.8 us: per_device(): y_all = lax.all_gather(partner, 'dp', axis=0, tiled=True)]
    ppermute x0 -> x14, starting transfers between devices: none -> 17.3 us  [ring_gather(): cur = lax.ppermute(cur, 'dp', pairs)]
    ppermute x0 -> x14, waiting for transfers between devices: none -> 16.3 us  [ring_gather(): cur = lax.ppermute(cur, 'dp', pairs)]
    all_to_all x1 -> x0, blocking collectives: 9.44 us -> none  [per_device(): lax.all_to_all(ordered, 'lang', split_axis=0, concat_axis=1, tiled=True)]
    gather x1 -> x0, local copies, waits for them, and re-layouts: 4.53 us -> none  [per_device(): col_live = col_live_global[perm] > 0]
    scatter x1 -> x0, local copies, waits for them, and re-layouts: 4.31 us -> none  [per_device(): jnp.zeros((pair_rows,), jnp.int32).at[pair_align]]
    all_to_all x0 -> x1, starting transfers between devices: none -> 3.37 us  [per_device(): lax.all_to_all(ordered, 'lang', split_axis=0, concat_axis=1, tiled=True)]
    dynamic_update_slice x0 -> x16, local copies, waits for them, and re-layouts: none -> 2.17 us  [the longest x14 2.13 us: ring_gather(): out = lax.dynamic_update_slice_in_dim(out, cur, origin * rows, 0)]
  transfers between devices with their start and end apart: 3 -> 16, of which waited for: 2 -> 8; matrix products, arithmetic and copies ran while one was open for 14% -> 17% of each run, Pallas kernels for 0% -> 0%
where the time goes in v2:
time: 87.2 us; the launch traced here: 86.5 us
  starting transfers between devices  24.1 us (28%)
  waiting for transfers between devices  17.7 us (20%)
  local copies, waits for them, and re-layouts  15.1 us (17%)
  between operations  13.3 us (15%)
  other arithmetic  8.42 us (10%)
  matrix products  7.97 us (9%)
    ppermute x14, starting transfers between devices, ring_gather(): cur = lax.ppermute(cur, 'dp', pairs)  17.3 us
    ppermute x14, waiting for transfers between devices, ring_gather(): cur = lax.ppermute(cur, 'dp', pairs)  16.3 us
    all_to_all x1, starting transfers between devices, per_device(): lax.all_to_all(ordered, 'lang', split_axis=0, concat_axis=1, tiled=True)  3.37 us
    all_to_all x1, starting transfers between devices, per_device(): lax.all_to_all(grad_local.reshape(1, row_count, emb_width), 'lang', split...  3.37 us
    dot_general x1, matrix products, per_device(): lax.dot_general(g_cols, x_all, (((0,), (0,)), ((), ())), preferred_elemen...  3.13 us
    dot_general x1, matrix products, per_device(): jnp.dot(g_rows, y_all, preferred_element_type=jnp.float32) * inv_root  2.44 us
    reduce_sum x1, other arithmetic, block_stats(): pos_score = jnp.sum(jnp.where(is_pos, scores_f, 0.0), axis=1)  2.43 us
    dot_general x1, matrix products, scores_of(): lax.dot_general(x_rows, y_rows, (((1,), (1,)), ((), ())), preferred_eleme...  2.4 us
  transfers between devices with their start and end apart: 16, of which 8 were waited for; matrix products, arithmetic and copies ran while one was open for 17% of the time, Pallas kernels for 0%

profile of v2, /device:TPU:0, one launch (start us, length us, event | category | flops | bytes accessed | tf_op | source)
XLA Modules:
  0.0 86.5 jit_solution(14308576832871278637)
XLA Ops:
  0.7 3.1 %collective-permute-start.7 = (bf16[128,768]{1,0:T(8,128)(2,1)}, bf16[128,768]{1,0:T(8,128)(2,1)}, u32[]{:S(2)}, u32[]{:S(2)}) collective-permute-start(bf16[128,768]{1,0:T(8,128)(2,1)} %param.10), channel_id=1, source_target_pairs={{0,2},{2,4},{4,6},{6,7},{7,5},{5,3},{3,1},{1,0},{8,10},{10,12},{12... | collective-permute-start | bytes 589832 | tf_op jit(solution)/shard_map/ppermute | solution.py:60
  3.8 0.7 compare_select_fusion.5
  4.5 0.6 scatter_custom_fusion
  5.1 1.2 %gather_fusion = bf16[4,32,768]{2,1,0:T(8,128)(2,1)} fusion(bf16[4,32,768]{2,1,0:T(8,128)(2,1)S(1)} %copy-done, s32[1024]{0:T(1024)S(1)} %pad_clamp_fusion.1), kind=kCustom, calls=%fused_computation | custom fusion | bytes 393232 | tf_op jit(solution)/shard_map/gather | solution.py:106
  6.3 3.4 %all-to-all-start = ((bf16[4,32,768]{2,1,0:T(8,128)(2,1)}), bf16[4,32,768]{2,1,0:T(8,128)(2,1)S(1)}, u32[]{:S(2)}, u32[]{:S(2)}) async-start(bf16[4,32,768]{2,1,0:T(8,128)(2,1)} %gather_fusion), calls=%async_computation | async-start | bytes 393216 | tf_op jit(solution)/shard_map/all_to_all | solution.py:107
  9.7 1.3 %dynamic_slice.73 = s32[1]{0:T(128)} dynamic-slice(s32[4]{0:T(128)} %param.13, s32[]{:T(128)S(6)} %select_n.250), dynamic_slice_sizes={1} | dynamic-slice | bytes 12 | tf_op jit(solution)/shard_map/dynamic_slice | solution.py:109
  11.1 0.7 iota_compare_fusion
  11.8 1.5 %convert_reduce_fusion = s32[1024]{0:T(1024)S(1)} fusion(s32[1024]{0:T(1024)} %bitcast.51, s32[1024]{0:T(1024)S(1)} %fusion.47, pred[1024]{0:T(1024)(128)(4,1)S(1)} %iota_compare_fusion), kind=kLoop, calls=%fused_computation.12 | loop fusion | flops 4193280 | bytes 13312 | tf_op jit(solution)/shard_map/reduce_max | solution.py:116
  13.3 0.1 broadcast.195.clone.1
  13.5 0.6 dynamic_slice.75
  18.7 0.7 fusion.67
  24.5 0.6 dynamic_slice.94
  25.1 0.6 dynamic_slice.74
  25.7 0.6 dynamic_slice.93
  26.3 0.6 dynamic_slice.72
  26.9 0.5 fusion.56
  27.4 2.0 %collective-permute-start = (bf16[128,768]{1,0:T(8,128)(2,1)S(1)}, bf16[128,768]{1,0:T(8,128)(2,1)S(1)}, u32[]{:S(2)}, u32[]{:S(2)}) collective-permute-start(bf16[128,768]{1,0:T(8,128)(2,1)S(1)} %bitcast.46), channel_id=1, source_target_pairs={{0,2},{2,4},{4,6},{6,7},{7,5},{5,3},{3,1},{1,0},{8,10},{10,12},{12... | collective-permute-start | bytes 589832 | tf_op jit(solution)/shard_map/ppermute | solution.py:60
  29.5 0.1 broadcast.195.clone
  29.6 2.1 %collective-permute-start.8 = (bf16[128,768]{1,0:T(8,128)(2,1)}, bf16[128,768]{1,0:T(8,128)(2,1)S(1)}, u32[]{:S(2)}, u32[]{:S(2)}) collective-permute-start(bf16[128,768]{1,0:T(8,128)(2,1)} %collective-permute-done.7), channel_id=1, source_target_pairs={{0,2},{2,4},{4,6},{6,7},{7,5},{5,3},{3,1},{1,0},{8,10},{10,12},{12... | collective-permute-start | bytes 589832 | tf_op jit(solution)/shard_map/ppermute | solution.py:60
  31.7 1.0 %constant_dynamic-update-slice_fusion.1 = bf16[1024,768]{1,0:T(8,128)(2,1)S(1)} fusion(bf16[1024,768]{1,0:T(8,128)(2,1)S(1)} %constant_dynamic-update-slice_fusion.7, bf16[128,768]{1,0:T(8,128)(2,1)} %collective-permute-done.7, s32[]{:T(128)S(6)} %select_n.261), kind=kLoop, calls=%fused_computation.75 | loop fusion | bytes 393220 | tf_op jit(solution)/shard_map/dynamic_update_slice | solution.py:62
  32.6 2.5 %collective-permute-done = bf16[128,768]{1,0:T(8,128)(2,1)S(1)} collective-permute-done((bf16[128,768]{1,0:T(8,128)(2,1)S(1)}, bf16[128,768]{1,0:T(8,128)(2,1)S(1)}, u32[]{:S(2)}, u32[]{:S(2)}) %collective-permute-start) | collective-permute-done | bytes 196640 | tf_op jit(solution)/shard_map/ppermute | solution.py:60
  35.2 2.0 %collective-permute-start.1 = (bf16[128,768]{1,0:T(8,128)(2,1)S(1)}, bf16[128,768]{1,0:T(8,128)(2,1)S(1)}, u32[]{:S(2)}, u32[]{:S(2)}) collective-permute-start(bf16[128,768]{1,0:T(8,128)(2,1)S(1)} %collective-permute-done), channel_id=1, source_target_pairs={{0,2},{2,4},{4,6},{6,7},{7,5},{5,3},{3,1},{1,0},{8,10},{10,12},{12... | collective-permute-start | bytes 589832 | tf_op jit(solution)/shard_map/ppermute | solution.py:60
  37.2 2.2 %collective-permute-done.8 = bf16[128,768]{1,0:T(8,128)(2,1)S(1)} collective-permute-done((bf16[128,768]{1,0:T(8,128)(2,1)}, bf16[128,768]{1,0:T(8,128)(2,1)S(1)}, u32[]{:S(2)}, u32[]{:S(2)}) %collective-permute-start.8) | collective-permute-done | bytes 196640 | tf_op jit(solution)/shard_map/ppermute | solution.py:60
  39.4 2.0 %collective-permute-start.9 = (bf16[128,768]{1,0:T(8,128)(2,1)S(1)}, bf16[128,768]{1,0:T(8,128)(2,1)S(1)}, u32[]{:S(2)}, u32[]{:S(2)}) collective-permute-start(bf16[128,768]{1,0:T(8,128)(2,1)S(1)} %collective-permute-done.8), channel_id=1, source_target_pairs={{0,2},{2,4},{4,6},{6,7},{7,5},{5,3},{3,1},{1,0},{8,10},{10,12},{12... | collective-permute-start | bytes 589832 | tf_op jit(solution)/shard_map/ppermute | solution.py:60
  41.5 2.2 %collective-permute-done.1 = bf16[128,768]{1,0:T(8,128)(2,1)S(1)} collective-permute-done((bf16[128,768]{1,0:T(8,128)(2,1)S(1)}, bf16[128,768]{1,0:T(8,128)(2,1)S(1)}, u32[]{:S(2)}, u32[]{:S(2)}) %collective-permute-start.1) | collective-permute-done | bytes 196640 | tf_op jit(solution)/shard_map/ppermute | solution.py:60
  43.6 2.0 %collective-permute-start.2 = (bf16[128,768]{1,0:T(8,128)(2,1)S(1)}, bf16[128,768]{1,0:T(8,128)(2,1)S(1)}, u32[]{:S(2)}, u32[]{:S(2)}) collective-permute-start(bf16[128,768]{1,0:T(8,128)(2,1)S(1)} %collective-permute-done.1), channel_id=1, source_target_pairs={{0,2},{2,4},{4,6},{6,7},{7,5},{5,3},{3,1},{1,0},{8,10},{10,12},{12... | collective-permute-start | bytes 589832 | tf_op jit(solution)/shard_map/ppermute | solution.py:60
  45.7 2.2 %collective-permute-done.9 = bf16[128,768]{1,0:T(8,128)(2,1)S(1)} collective-permute-done((bf16[128,768]{1,0:T(8,128)(2,1)S(1)}, bf16[128,768]{1,0:T(8,128)(2,1)S(1)}, u32[]{:S(2)}, u32[]{:S(2)}) %collective-permute-start.9) | collective-permute-done | bytes 196640 | tf_op jit(solution)/shard_map/ppermute | solution.py:60
  47.8 2.0 %collective-permute-start.10 = (bf16[128,768]{1,0:T(8,128)(2,1)S(1)}, bf16[128,768]{1,0:T(8,128)(2,1)S(1)}, u32[]{:S(2)}, u32[]{:S(2)}) collective-permute-start(bf16[128,768]{1,0:T(8,128)(2,1)S(1)} %collective-permute-done.9), channel_id=1, source_target_pairs={{0,2},{2,4},{4,6},{6,7},{7,5},{5,3},{3,1},{1,0},{8,10},{10,12},{12... | collective-permute-start | bytes 589832 | tf_op jit(solution)/shard_map/ppermute | solution.py:60
  49.9 2.2 %collective-permute-done.2 = bf16[128,768]{1,0:T(8,128)(2,1)S(1)} collective-permute-done((bf16[128,768]{1,0:T(8,128)(2,1)S(1)}, bf16[128,768]{1,0:T(8,128)(2,1)S(1)}, u32[]{:S(2)}, u32[]{:S(2)}) %collective-permute-start.2) | collective-permute-done | bytes 196640 | tf_op jit(solution)/shard_map/ppermute | solution.py:60
  52.0 2.0 %collective-permute-start.3 = (bf16[128,768]{1,0:T(8,128)(2,1)S(1)}, bf16[128,768]{1,0:T(8,128)(2,1)S(1)}, u32[]{:S(2)}, u32[]{:S(2)}) collective-permute-start(bf16[128,768]{1,0:T(8,128)(2,1)S(1)} %collective-permute-done.2), channel_id=1, source_target_pairs={{0,2},{2,4},{4,6},{6,7},{7,5},{5,3},{3,1},{1,0},{8,10},{10,12},{12... | collective-permute-start | bytes 589832 | tf_op jit(solution)/shard_map/ppermute | solution.py:60
  54.1 2.2 %collective-permute-done.10 = bf16[128,768]{1,0:T(8,128)(2,1)S(1)} collective-permute-done((bf16[128,768]{1,0:T(8,128)(2,1)S(1)}, bf16[128,768]{1,0:T(8,128)(2,1)S(1)}, u32[]{:S(2)}, u32[]{:S(2)}) %collective-permute-start.10) | collective-permute-done | bytes 196640 | tf_op jit(solution)/shard_map/ppermute | solution.py:60
  56.3 0.9 %constant_dynamic-update-slice_fusion.2 = bf16[1024,768]{1,0:T(8,128)(2,1)S(1)} fusion(bf16[1024,768]{1,0:T(8,128)(2,1)S(1)} %constant_dynamic-update-slice_fusion.3, bf16[128,768]{1,0:T(8,128)(2,1)} %collective-permute-done.11, s32[]{:T(128)S(6)} %select_n.273), kind=kLoop, calls=%fused_computation.76 | loop fusion | bytes 393220 | tf_op jit(solution)/shard_map/dynamic_update_slice | solution.py:62
  57.3 2.9 %collective-permute-done.3 = bf16[128,768]{1,0:T(8,128)(2,1)S(1)} collective-permute-done((bf16[128,768]{1,0:T(8,128)(2,1)S(1)}, bf16[128,768]{1,0:T(8,128)(2,1)S(1)}, u32[]{:S(2)}, u32[]{:S(2)}) %collective-permute-start.3) | collective-permute-done | bytes 196640 | tf_op jit(solution)/shard_map/ppermute | solution.py:60
  60.3 2.4 %select_reduce_fusion.3 = (f32[1024]{0:T(1024)S(1)}, f32[1024]{0:T(1024)S(1)}, f32[1024,1024]{0,1:T(8,128)S(1)}) fusion(pred[1024]{0:T(1024)(128)(4,1)S(1)} %copy-done.6, pred[1024]{0:T(1024)(128)(4,1)S(1)} %copy-done.12, s32[1024]{0:T(1024)S(1)} %bitcast.52, s32[1024]{0:T(1024)S(1)} %fusion.47, ...), kind=kOutput, calls=%fused_computation.11 | convolution fusion | flops 1618999296 | bytes 7358464 | tf_op jit(solution)/shard_map/dot_general | solution.py:67
  62.7 2.4 %fusion.1 = (f32[1024]{0:T(1024)S(1)}, f32[1024]{0:T(1024)S(1)}, f32[1024]{0:T(1024)S(1)}) fusion(f32[1024,1024]{0,1:T(8,128)S(1)} %get-tuple-element.19, s32[1024]{0:T(1024)S(1)} %bitcast.53, s32[1024]{0:T(1024)S(1)} %fusion.47, f32[1024]{0:T(1024)S(1)} %get-tuple-element.7, pred[1024]{0:T(1024)(128)(4,1)S(1)} %copy-done.12, f32[1024]{0:T(1024)S(1)} %get-tuple-element.6, ...), kind=kLoop, calls=%fused_computation.7 | loop fusion | flops 9434112 | bytes 4225024 | tf_op jit(solution)/shard_map/reduce_sum | solution.py:79
  65.2 1.3 %select_reduce_fusion.4 = (f32[]{:T(128)}, f32[1024]{0:T(1024)S(1)}, f32[]{:T(128)}, f32[1024]{0:T(1024)S(1)}) fusion(f32[1024]{0:T(1024)S(1)} %get-tuple-element.7, f32[1024]{0:T(1024)S(1)} %get-tuple-element.4, f32[1024]{0:T(1024)S(1)} %get-tuple-element.3, f32[1024]{0:T(1024)S(1)} %get-tuple-element.6, f32[1024]{0:T(1024)S(1)} %get-tuple-element.5, ...), kind=kLoop, calls=%fused_computation.103 | loop fusion | flops 16382 | bytes 32780 | tf_op jit(solution)/shard_map/reduce_sum | solution.py:149
  66.5 0.6 copy-done.8
  67.1 0.6 dynamic_slice.92
  67.8 3.1 %fusion.7 = bf16[1,128,768]{2,1,0:T(8,128)(2,1)} fusion(bf16[1024,768]{1,0:T(8,128)(2,1)S(1)} %constant_dynamic-update-slice_fusion.6, bf16[128,768]{1,0:T(8,128)(2,1)S(1)} %bitcast.49, f32[128]{0:T(128)S(1)} %dynamic_slice.95, f32[1024]{0:T(1024)} %copy-done.10, s32[128]{0:T(128)} %dynamic_slice.94, f32[]{:T(128)} %bitcast, s32[1024]{0:T(1024)S(1)} %bitcast.54, ...), kind=kOutput, calls=%fused_computation.22 | convolution fusion | flops 404815872 | bytes 1976452 | tf_op jit(solution)/shard_map/dot_general | solution.py:169
  71.0 1.3 %copy.17 = bf16[1,128,768]{2,0,1:T(2,128)(2,1)S(1)} copy(bf16[1,128,768]{2,1,0:T(8,128)(2,1)} %fusion.7) | data formatting | bytes 393216 | tf_op jit(solution)/shard_map/reshape | solution.py:174
  72.2 0.5 broadcast.239
  72.8 1.8 %reduce = bf16[128,768]{1,0:T(8,128)(2,1)S(1)} reduce(bf16[128,1,768]{2,1,0:T(2,128)(2,1)S(1)} %bitcast.45, bf16[]{:T(256)} %broadcast.239), dimensions={1}, to_apply=%bitcast.43.reduce_sub_computation | reduce | bytes 393218
  74.6 0.7 reshape.196
  75.3 3.4 %all-to-all-start.1 = ((bf16[4,2,12288]{2,1,0:T(2,128)(2,1)}), bf16[4,2,12288]{2,1,0:T(2,128)(2,1)S(1)}, u32[]{:S(2)}, u32[]{:S(2)}) async-start(bf16[4,2,12288]{2,1,0:T(2,128)(2,1)} %reshape.196), calls=%async_computation.1 | async-start | bytes 393216 | tf_op jit(solution)/shard_map/all_to_all | solution.py:173
  78.7 2.4 %fusion.5 = bf16[128,768]{1,0:T(8,128)(2,1)} fusion(bf16[1024,768]{1,0:T(8,128)(2,1)S(1)} %constant_dynamic-update-slice_fusion.8, bf16[128,768]{1,0:T(8,128)(2,1)S(1)} %copy-done.2, f32[1024]{0:T(1024)S(1)} %copy-done.9, f32[128]{0:T(128)S(1)} %copy-done.17, s32[128]{0:T(128)S(1)} %copy-done.15, f32[]{:T(128)} %bitcast, s32[1024]{0:T(1024)S(1)} %fusion.47, ...), kind=kOutput, calls=%fused_computation.20 | convolution fusion | flops 404815872 | bytes 1976452 | tf_op jit(solution)/shard_map/dot_general | solution.py:160
  82.5 1.4 %all-to-all-done.1 = bf16[4,2,12288]{2,1,0:T(2,128)(2,1)S(1)} async-done(((bf16[4,2,12288]{2,1,0:T(2,128)(2,1)}), bf16[4,2,12288]{2,1,0:T(2,128)(2,1)S(1)}, u32[]{:S(2)}, u32[]{:S(2)}) %all-to-all-start.1) | async-done | bytes 196640 | tf_op jit(solution)/shard_map/all_to_all | solution.py:173
  83.9 0.2 reshape.197
  84.2 1.2 %gather_fusion.1 = bf16[4,32,768]{2,1,0:T(8,128)(2,1)} fusion(bf16[4,32,768]{2,1,0:T(8,128)(2,1)S(1)} %bitcast.50, s32[1024]{0:T(1024)S(1)} %pad_clamp_fusion), kind=kCustom, calls=%fused_computation.1 | custom fusion | bytes 393232 | tf_op jit(solution)/shard_map/gather | solution.py:176
  (71 shorter events, 0.6 us)
Async XLA Ops:
  0.6 4.5 %copy-start = (bf16[4,32,768]{2,1,0:T(8,128)(2,1)S(1)}, bf16[4,32,768]{2,1,0:T(8,128)(2,1)}, u32[]{:S(2)}) copy-start(bf16[4,32,768]{2,1,0:T(8,128)(2,1)} %param.11) | copy-start | bytes 589828
  0.6 12.8 %copy-start.16 = (s32[8]{0:T(128)S(1)}, s32[8]{0:T(128)}, u32[]{:S(2)}) copy-start(s32[8]{0:T(128)} %constant.220.clone) | copy-start | bytes 100
  0.7 18.1 %copy-start.3 = (s32[8]{0:T(128)S(1)}, s32[8]{0:T(128)}, u32[]{:S(2)}) copy-start(s32[8]{0:T(128)} %constant.219.clone) | copy-start | bytes 100
  0.7 12.7 %copy-start.1 = (bf16[128,768]{1,0:T(8,128)(2,1)S(1)}, bf16[128,768]{1,0:T(8,128)(2,1)}, u32[]{:S(2)}) copy-start(bf16[128,768]{1,0:T(8,128)(2,1)} %param.10) | copy-start | bytes 589828
  0.7 25.6 %copy-start.13 = (f32[4]{0:T(128)S(1)}, f32[4]{0:T(128)}, u32[]{:S(2)}) copy-start(f32[4]{0:T(128)} %param.15) | copy-start | bytes 52
  0.7 28.9 %collective-permute-start.7 = (bf16[128,768]{1,0:T(8,128)(2,1)}, bf16[128,768]{1,0:T(8,128)(2,1)}, u32[]{:S(2)}, u32[]{:S(2)}) collective-permute-start(bf16[128,768]{1,0:T(8,128)(2,1)} %param.10), channel_id=1, source_target_pairs={{0,2},{2,4},{4,6},{6,7},{7,5},{5,3},{3,1},{1,0},{8,10},{10,12},{12... | collective-permute-start | bytes 589832 | tf_op jit(solution)/shard_map/ppermute | solution.py:60
  3.8 27.9 %collective-permute-start.11 = (bf16[128,768]{1,0:T(8,128)(2,1)}, bf16[128,768]{1,0:T(8,128)(2,1)}, u32[]{:S(2)}, u32[]{:S(2)}) collective-permute-start(bf16[128,768]{1,0:T(8,128)(2,1)} %param.10), channel_id=1, source_target_pairs={{0,1},{2,0},{4,2},{6,4},{7,6},{5,7},{3,5},{1,3},{8,9},{10,8},{12,1... | collective-permute-start | bytes 589832 | tf_op jit(solution)/shard_map/ppermute | solution.py:60
  5.1 21.8 %copy-start.4 = (s32[1,1024]{1,0:T(1,128)S(1)}, s32[1,1024]{1,0:T(1,128)}, u32[]{:S(2)}) copy-start(s32[1,1024]{1,0:T(1,128)} %param.14) | copy-start | bytes 12292
  6.3 21.1 %all-to-all-start = ((bf16[4,32,768]{2,1,0:T(8,128)(2,1)}), bf16[4,32,768]{2,1,0:T(8,128)(2,1)S(1)}, u32[]{:S(2)}, u32[]{:S(2)}) async-start(bf16[4,32,768]{2,1,0:T(8,128)(2,1)} %gather_fusion), calls=%async_computation | async-start | bytes 393216 | tf_op jit(solution)/shard_map/all_to_all | solution.py:107
  11.7 17.7 %copy-start.11 = (pred[1024]{0:T(1024)(128)(4,1)}, pred[1024]{0:T(1024)(128)(4,1)S(1)}, u32[]{:S(2)}) copy-start(pred[1024]{0:T(1024)(128)(4,1)S(1)} %iota_compare_fusion) | copy-start | bytes 3076
  13.3 16.2 %copy-start.5 = (pred[1024]{0:T(1024)(128)(4,1)}, pred[1024]{0:T(1024)(128)(4,1)S(1)}, u32[]{:S(2)}) copy-start(pred[1024]{0:T(1024)(128)(4,1)S(1)} %broadcast_compare_fusion) | copy-start | bytes 3076
  27.4 7.8 %collective-permute-start = (bf16[128,768]{1,0:T(8,128)(2,1)S(1)}, bf16[128,768]{1,0:T(8,128)(2,1)S(1)}, u32[]{:S(2)}, u32[]{:S(2)}) collective-permute-start(bf16[128,768]{1,0:T(8,128)(2,1)S(1)} %bitcast.46), channel_id=1, source_target_pairs={{0,2},{2,4},{4,6},{6,7},{7,5},{5,3},{3,1},{1,0},{8,10},{10,12},{12... | collective-permute-start | bytes 589832 | tf_op jit(solution)/shard_map/ppermute | solution.py:60
  29.4 7.8 %collective-permute-start.4 = (bf16[128,768]{1,0:T(8,128)(2,1)S(1)}, bf16[128,768]{1,0:T(8,128)(2,1)S(1)}, u32[]{:S(2)}, u32[]{:S(2)}) collective-permute-start(bf16[128,768]{1,0:T(8,128)(2,1)S(1)} %bitcast.47), channel_id=1, source_target_pairs={{0,1},{2,0},{4,2},{6,4},{7,6},{5,7},{3,5},{1,3},{8,9},{10,8},{12,1... | collective-permute-start | bytes 589832 | tf_op jit(solution)/shard_map/ppermute | solution.py:60
  29.6 9.8 %collective-permute-start.8 = (bf16[128,768]{1,0:T(8,128)(2,1)}, bf16[128,768]{1,0:T(8,128)(2,1)S(1)}, u32[]{:S(2)}, u32[]{:S(2)}) collective-permute-start(bf16[128,768]{1,0:T(8,128)(2,1)} %collective-permute-done.7), channel_id=1, source_target_pairs={{0,2},{2,4},{4,6},{6,7},{7,5},{5,3},{3,1},{1,0},{8,10},{10,12},{12... | collective-permute-start | bytes 589832 | tf_op jit(solution)/shard_map/ppermute | solution.py:60
  31.7 9.8 %collective-permute-start.12 = (bf16[128,768]{1,0:T(8,128)(2,1)}, bf16[128,768]{1,0:T(8,128)(2,1)S(1)}, u32[]{:S(2)}, u32[]{:S(2)}) collective-permute-start(bf16[128,768]{1,0:T(8,128)(2,1)} %collective-permute-done.11), channel_id=1, source_target_pairs={{0,1},{2,0},{4,2},{6,4},{7,6},{5,7},{3,5},{1,3},{8,9},{10,8},{12,1... | collective-permute-start | bytes 589832 | tf_op jit(solution)/shard_map/ppermute | solution.py:60
  35.2 8.4 %collective-permute-start.1 = (bf16[128,768]{1,0:T(8,128)(2,1)S(1)}, bf16[128,768]{1,0:T(8,128)(2,1)S(1)}, u32[]{:S(2)}, u32[]{:S(2)}) collective-permute-start(bf16[128,768]{1,0:T(8,128)(2,1)S(1)} %collective-permute-done), channel_id=1, source_target_pairs={{0,2},{2,4},{4,6},{6,7},{7,5},{5,3},{3,1},{1,0},{8,10},{10,12},{12... | collective-permute-start | bytes 589832 | tf_op jit(solution)/shard_map/ppermute | solution.py:60
  37.2 8.4 %collective-permute-start.5 = (bf16[128,768]{1,0:T(8,128)(2,1)S(1)}, bf16[128,768]{1,0:T(8,128)(2,1)S(1)}, u32[]{:S(2)}, u32[]{:S(2)}) collective-permute-start(bf16[128,768]{1,0:T(8,128)(2,1)S(1)} %collective-permute-done.4), channel_id=1, source_target_pairs={{0,1},{2,0},{4,2},{6,4},{7,6},{5,7},{3,5},{1,3},{8,9},{10,8},{12,1... | collective-permute-start | bytes 589832 | tf_op jit(solution)/shard_map/ppermute | solution.py:60
  39.4 8.4 %collective-permute-start.9 = (bf16[128,768]{1,0:T(8,128)(2,1)S(1)}, bf16[128,768]{1,0:T(8,128)(2,1)S(1)}, u32[]{:S(2)}, u32[]{:S(2)}) collective-permute-start(bf16[128,768]{1,0:T(8,128)(2,1)S(1)} %collective-permute-done.8), channel_id=1, source_target_pairs={{0,2},{2,4},{4,6},{6,7},{7,5},{5,3},{3,1},{1,0},{8,10},{10,12},{12... | collective-permute-start | bytes 589832 | tf_op jit(solution)/shard_map/ppermute | solution.py:60
  41.4 15.8 %collective-permute-start.13 = (bf16[128,768]{1,0:T(8,128)(2,1)S(1)}, bf16[128,768]{1,0:T(8,128)(2,1)S(1)}, u32[]{:S(2)}, u32[]{:S(2)}) collective-permute-start(bf16[128,768]{1,0:T(8,128)(2,1)S(1)} %collective-permute-done.12), channel_id=1, source_target_pairs={{0,1},{2,0},{4,2},{6,4},{7,6},{5,7},{3,5},{1,3},{8,9},{10,8},{12,1... | collective-permute-start | bytes 589832 | tf_op jit(solution)/shard_map/ppermute | solution.py:60
  43.6 8.4 %collective-permute-start.2 = (bf16[128,768]{1,0:T(8,128)(2,1)S(1)}, bf16[128,768]{1,0:T(8,128)(2,1)S(1)}, u32[]{:S(2)}, u32[]{:S(2)}) collective-permute-start(bf16[128,768]{1,0:T(8,128)(2,1)S(1)} %collective-permute-done.1), channel_id=1, source_target_pairs={{0,2},{2,4},{4,6},{6,7},{7,5},{5,3},{3,1},{1,0},{8,10},{10,12},{12... | collective-permute-start | bytes 589832 | tf_op jit(solution)/shard_map/ppermute | solution.py:60
  45.6 14.6 %collective-permute-start.6 = (bf16[128,768]{1,0:T(8,128)(2,1)S(1)}, bf16[128,768]{1,0:T(8,128)(2,1)S(1)}, u32[]{:S(2)}, u32[]{:S(2)}) collective-permute-start(bf16[128,768]{1,0:T(8,128)(2,1)S(1)} %collective-permute-done.5), channel_id=1, source_target_pairs={{0,1},{2,0},{4,2},{6,4},{7,6},{5,7},{3,5},{1,3},{8,9},{10,8},{12,1... | collective-permute-start | bytes 589832 | tf_op jit(solution)/shard_map/ppermute | solution.py:60
  47.8 8.4 %collective-permute-start.10 = (bf16[128,768]{1,0:T(8,128)(2,1)S(1)}, bf16[128,768]{1,0:T(8,128)(2,1)S(1)}, u32[]{:S(2)}, u32[]{:S(2)}) collective-permute-start(bf16[128,768]{1,0:T(8,128)(2,1)S(1)} %collective-permute-done.9), channel_id=1, source_target_pairs={{0,2},{2,4},{4,6},{6,7},{7,5},{5,3},{3,1},{1,0},{8,10},{10,12},{12... | collective-permute-start | bytes 589832 | tf_op jit(solution)/shard_map/ppermute | solution.py:60
  52.0 8.1 %collective-permute-start.3 = (bf16[128,768]{1,0:T(8,128)(2,1)S(1)}, bf16[128,768]{1,0:T(8,128)(2,1)S(1)}, u32[]{:S(2)}, u32[]{:S(2)}) collective-permute-start(bf16[128,768]{1,0:T(8,128)(2,1)S(1)} %collective-permute-done.2), channel_id=1, source_target_pairs={{0,2},{2,4},{4,6},{6,7},{7,5},{5,3},{3,1},{1,0},{8,10},{10,12},{12... | collective-permute-start | bytes 589832 | tf_op jit(solution)/shard_map/ppermute | solution.py:60
  54.1 6.2 %copy-start.6 = (pred[1024]{0:T(1024)(128)(4,1)S(1)}, pred[1024]{0:T(1024)(128)(4,1)}, u32[]{:S(2)}) copy-start(pred[1024]{0:T(1024)(128)(4,1)} %copy-done.5) | copy-start | bytes 3076
  54.1 6.2 %copy-start.12 = (pred[1024]{0:T(1024)(128)(4,1)S(1)}, pred[1024]{0:T(1024)(128)(4,1)}, u32[]{:S(2)}) copy-start(pred[1024]{0:T(1024)(128)(4,1)} %copy-done.11) | copy-start | bytes 3076
  66.5 0.6 copy-start.8
  66.5 0.7 copy-start.10
  70.9 7.7 %copy-start.2 = (bf16[128,768]{1,0:T(8,128)(2,1)S(1)}, bf16[128,768]{1,0:T(8,128)(2,1)}, u32[]{:S(2)}) copy-start(bf16[128,768]{1,0:T(8,128)(2,1)} %param.10) | copy-start | bytes 589828
  70.9 7.7 %copy-start.7 = (pred[1024]{0:T(1024)(128)(4,1)S(1)}, pred[1024]{0:T(1024)(128)(4,1)}, u32[]{:S(2)}) copy-start(pred[1024]{0:T(1024)(128)(4,1)} %copy-done.5) | copy-start | bytes 3076
  70.9 7.8 %copy-start.9 = (f32[1024]{0:T(1024)S(1)}, f32[1024]{0:T(1024)}, u32[]{:S(2)}) copy-start(f32[1024]{0:T(1024)} %copy-done.8) | copy-start | bytes 12292
  70.9 7.8 %copy-start.14 = (pred[128]{0:T(512)(128)(4,1)S(1)}, pred[128]{0:T(512)(128)(4,1)}, u32[]{:S(2)}) copy-start(pred[128]{0:T(512)(128)(4,1)} %dynamic_slice.74) | copy-start | bytes 388
  70.9 7.8 %copy-start.15 = (s32[128]{0:T(128)S(1)}, s32[128]{0:T(128)}, u32[]{:S(2)}) copy-start(s32[128]{0:T(128)} %fusion.56) | copy-start | bytes 1540
  71.0 7.8 %copy-start.17 = (f32[128]{0:T(128)S(1)}, f32[128]{0:T(128)}, u32[]{:S(2)}) copy-start(f32[128]{0:T(128)} %dynamic_slice.92) | copy-start | bytes 1540
  75.3 8.6 %all-to-all-start.1 = ((bf16[4,2,12288]{2,1,0:T(2,128)(2,1)}), bf16[4,2,12288]{2,1,0:T(2,128)(2,1)S(1)}, u32[]{:S(2)}, u32[]{:S(2)}) async-start(bf16[4,2,12288]{2,1,0:T(2,128)(2,1)} %reshape.196), calls=%async_computation.1 | async-start | bytes 393216 | tf_op jit(solution)/shard_map/all_to_all | solution.py:173

commit v3 on v2

--- a/solution.py
+++ b/solution.py
@@ -114,8 +114,10 @@
     perm = target_index(pair_rows, row_count, per_slot, data_size)
     live_pos = (perm[None, :] == pair_align[:, None]) & row_live[:, None]
     col_live = jnp.max(live_pos.astype(jnp.int32), axis=0) > 0
-    x_all = ring_gather(src_emb, ring)
-    y_all = ring_gather(partner, ring)
+    both = ring_gather(jnp.concatenate([src_emb, partner], 0), ring)
+    both = both.reshape(data_size, 2, row_count, emb_width)
+    x_all = both[:, 0].reshape(pair_rows, emb_width)
+    y_all = both[:, 1].reshape(pair_rows, emb_width)
 
     block = max(1, min(pair_rows, BLOCK_BYTES // (4 * pair_rows)))
     steps = pair_rows // block
@@ -171,7 +173,7 @@
     )
     grad_local = (own_terms * inv_root).astype(jnp.bfloat16)
     returned = lax.all_to_all(
-        grad_local.reshape(1, row_count, emb_width), "lang", split_axis=1, concat_axis=0, tiled=True
+        grad_local.reshape(lang_size, per_slot, emb_width), "lang", split_axis=0, concat_axis=0, tiled=True
     )
     grad_tgt = returned[slot_group]
     return (grad_src, grad_tgt, pair_loss)

time: 87.2 us -> 96.3 us (1.10)
  waiting for transfers between devices: 17.7 us -> 28.6 us
  starting transfers between devices: 24.1 us -> 16 us
  local copies, waits for them, and re-layouts: 15.1 us -> 21.1 us
  matrix products: 7.97 us -> 9.15 us
  other arithmetic: 8.42 us -> 7.37 us
    ppermute x14 -> x7, starting transfers between devices: 17.3 us -> 8.34 us  [ring_gather(): cur = lax.ppermute(cur, 'dp', pairs)]
    ppermute x14 -> x7, waiting for transfers between devices: 16.3 us -> 22.8 us  [ring_gather(): cur = lax.ppermute(cur, 'dp', pairs)]
    all_to_all x1, waiting for transfers between devices: 0.01 us -> 5.3 us  [per_device(): lax.all_to_all(ordered, 'lang', split_axis=0, concat_axis=1, tiled=True)]
    dynamic_update_slice x14 -> x7, local copies, waits for them, and re-layouts: 2.13 us -> 6.19 us  [ring_gather(): out = lax.dynamic_update_slice_in_dim(out, cur, origin * rows, 0)]
    unnamed x1 -> x0, other arithmetic: 1.8 us -> none
    reshape x1 -> x0, local copies, waits for them, and re-layouts: 1.28 us -> none  [per_device(): grad_local.reshape(1, row_count, emb_width)]
    dot_general x1, matrix products: 2.44 us -> 3.47 us  [per_device(): jnp.dot(g_rows, y_all, preferred_element_type=jnp.float32) * inv_root]
    all_to_all x1, waiting for transfers between devices: 1.44 us -> 0.44 us  [per_device(): lax.all_to_all(grad_local.reshape(lang_size, per_slot, emb_width), 'lang'...]
  transfers between devices with their start and end apart: 16 -> 9, of which waited for: 8 -> 6; matrix products, arithmetic and copies ran while one was open for 17% -> 21% of each run, Pallas kernels for 0% -> 0%
where the time goes in v3:
time: 96.3 us; the launch traced here: 95.3 us
  waiting for transfers between devices  28.6 us (30%)
  local copies, waits for them, and re-layouts  21.1 us (22%)
  starting transfers between devices  16 us (17%)
  between operations  13.1 us (14%)
  matrix products  9.15 us (10%)
  other arithmetic  7.37 us (8%)
    ppermute x7, waiting for transfers between devices, ring_gather(): cur = lax.ppermute(cur, 'dp', pairs)  22.8 us
    ppermute x7, starting transfers between devices, ring_gather(): cur = lax.ppermute(cur, 'dp', pairs)  8.34 us
    dynamic_update_slice x7, local copies, waits for them, and re-layouts, ring_gather(): out = lax.dynamic_update_slice_in_dim(out, cur, origin * rows, 0)  6.19 us
    all_to_all x1, waiting for transfers between devices, per_device(): lax.all_to_all(ordered, 'lang', split_axis=0, concat_axis=1, tiled=True)  5.3 us
    all_to_all x1, starting transfers between devices, per_device(): lax.all_to_all(ordered, 'lang', split_axis=0, concat_axis=1, tiled=True)  4.24 us
    dot_general x1, matrix products, per_device(): jnp.dot(g_rows, y_all, preferred_element_type=jnp.float32) * inv_root  3.47 us
    all_to_all x1, starting transfers between devices, per_device(): lax.all_to_all(grad_local.reshape(lang_size, per_slot, emb_width), 'lang'...  3.44 us
    dot_general x1, matrix products, per_device(): lax.dot_general(g_cols, x_all, (((0,), (0,)), ((), ())), preferred_elemen...  3.28 us
  transfers between devices with their start and end apart: 9, of which 6 were waited for; matrix products, arithmetic and copies ran while one was open for 21% of the time, Pallas kernels for 0%

profile of v3, /device:TPU:0, one launch (start us, length us, event | category | flops | bytes accessed | tf_op | source)
XLA Modules:
  0.0 95.3 jit_solution(7641613226447588800)
XLA Ops:
  0.7 0.8 compare_select_fusion.5
  1.4 0.6 scatter_custom_fusion
  2.1 1.2 %gather_fusion = bf16[4,32,768]{2,1,0:T(8,128)(2,1)} fusion(bf16[4,32,768]{2,1,0:T(8,128)(2,1)S(1)} %copy-done, s32[1024]{0:T(1024)S(1)} %pad_clamp_fusion.1), kind=kCustom, calls=%fused_computation | custom fusion | bytes 393232 | tf_op jit(solution)/shard_map/gather | solution.py:106
  3.3 4.2 %all-to-all-start = ((bf16[4,32,768]{2,1,0:T(8,128)(2,1)}), bf16[4,32,768]{2,1,0:T(8,128)(2,1)S(1)}, u32[]{:S(2)}, u32[]{:S(2)}) async-start(bf16[4,32,768]{2,1,0:T(8,128)(2,1)} %gather_fusion), calls=%async_computation | async-start | bytes 393216 | tf_op jit(solution)/shard_map/all_to_all | solution.py:107
  7.5 5.3 %all-to-all-done = bf16[4,32,768]{2,1,0:T(8,128)(2,1)S(1)} async-done(((bf16[4,32,768]{2,1,0:T(8,128)(2,1)}), bf16[4,32,768]{2,1,0:T(8,128)(2,1)S(1)}, u32[]{:S(2)}, u32[]{:S(2)}) %all-to-all-start) | async-done | bytes 196640 | tf_op jit(solution)/shard_map/all_to_all | solution.py:107
  13.1 0.7 copy-done.6
  13.8 0.8 copy-done.5
  14.6 2.2 %collective-permute-start = (bf16[256,768]{1,0:T(8,128)(2,1)S(1)}, bf16[256,768]{1,0:T(8,128)(2,1)}, u32[]{:S(2)}, u32[]{:S(2)}) collective-permute-start(bf16[256,768]{1,0:T(8,128)(2,1)S(1)} %get-tuple-element.14), channel_id=1, source_target_pairs={{0,2},{2,4},{4,6},{6,7},{7,5},{5,3},{3,1},{1,0},{8,10},{10,12},{12... | collective-permute-start | bytes 1179656 | tf_op jit(solution)/shard_map/ppermute | solution.py:60
  16.8 8.6 %collective-permute-done = bf16[256,768]{1,0:T(8,128)(2,1)} collective-permute-done((bf16[256,768]{1,0:T(8,128)(2,1)S(1)}, bf16[256,768]{1,0:T(8,128)(2,1)}, u32[]{:S(2)}, u32[]{:S(2)}) %collective-permute-start) | collective-permute-done | bytes 393248 | tf_op jit(solution)/shard_map/ppermute | solution.py:60
  25.4 1.8 %collective-permute-start.1 = (bf16[256,768]{1,0:T(8,128)(2,1)}, bf16[256,768]{1,0:T(8,128)(2,1)}, u32[]{:S(2)}, u32[]{:S(2)}) collective-permute-start(bf16[256,768]{1,0:T(8,128)(2,1)} %collective-permute-done), channel_id=1, source_target_pairs={{0,2},{2,4},{4,6},{6,7},{7,5},{5,3},{3,1},{1,0},{8,10},{10,12},{12... | collective-permute-start | bytes 1179656 | tf_op jit(solution)/shard_map/ppermute | solution.py:60
  27.2 0.6 dynamic_slice.49
  27.8 0.2 collective-permute-start.4
  28.0 0.6 iota_compare_fusion
  28.7 6.7 %collective-permute-done.1 = bf16[256,768]{1,0:T(8,128)(2,1)} collective-permute-done((bf16[256,768]{1,0:T(8,128)(2,1)}, bf16[256,768]{1,0:T(8,128)(2,1)}, u32[]{:S(2)}, u32[]{:S(2)}) %collective-permute-start.1) | collective-permute-done | bytes 393248 | tf_op jit(solution)/shard_map/ppermute | solution.py:60
  35.4 1.5 %collective-permute-start.2 = (bf16[256,768]{1,0:T(8,128)(2,1)}, bf16[256,768]{1,0:T(8,128)(2,1)}, u32[]{:S(2)}, u32[]{:S(2)}) collective-permute-start(bf16[256,768]{1,0:T(8,128)(2,1)} %collective-permute-done.1), channel_id=1, source_target_pairs={{0,2},{2,4},{4,6},{6,7},{7,5},{5,3},{3,1},{1,0},{8,10},{10,12},{12... | collective-permute-start | bytes 1179656 | tf_op jit(solution)/shard_map/ppermute | solution.py:60
  37.0 0.8 convert_reduce_fusion
  37.8 0.6 collective-permute-start.5
  38.4 0.5 broadcast_compare_fusion
  38.9 0.7 pad_clamp_fusion
  39.6 5.1 %collective-permute-done.2 = bf16[256,768]{1,0:T(8,128)(2,1)} collective-permute-done((bf16[256,768]{1,0:T(8,128)(2,1)}, bf16[256,768]{1,0:T(8,128)(2,1)}, u32[]{:S(2)}, u32[]{:S(2)}) %collective-permute-start.2) | collective-permute-done | bytes 393248 | tf_op jit(solution)/shard_map/ppermute | solution.py:60
  44.7 1.5 %collective-permute-start.3 = (bf16[256,768]{1,0:T(8,128)(2,1)}, bf16[256,768]{1,0:T(8,128)(2,1)}, u32[]{:S(2)}, u32[]{:S(2)}) collective-permute-start(bf16[256,768]{1,0:T(8,128)(2,1)} %collective-permute-done.2), channel_id=1, source_target_pairs={{0,2},{2,4},{4,6},{6,7},{7,5},{5,3},{3,1},{1,0},{8,10},{10,12},{12... | collective-permute-start | bytes 1179656 | tf_op jit(solution)/shard_map/ppermute | solution.py:60
  46.2 1.2 %fusion.55 = s32[128]{0:T(128)} fusion(s32[1,1024]{1,0:T(1,128)} %param.12, s32[]{:T(128)S(6)} %select_n.181), kind=kLoop, calls=%fused_computation.107 | loop fusion | bytes 1028 | tf_op jit(solution)/shard_map/eq | solution.py:158
  47.4 1.2 %dynamic_slice.51 = s32[1]{0:T(128)} dynamic-slice(s32[8]{0:T(128)} %constant.182.clone, s32[]{:T(128)S(6)} %select_n.189), dynamic_slice_sizes={1} | dynamic-slice | bytes 12 | tf_op jit(solution)/shard_map/dynamic_slice | solution.py:51
  53.3 0.7 fusion.67
  59.0 0.6 dynamic_slice.62
  59.6 1.3 %dynamic_slice.50 = pred[128]{0:T(512)(128)(4,1)} dynamic-slice(pred[1024]{0:T(1024)(128)(4,1)} %copy-done.14, s32[]{:T(128)S(6)} %select_n.181), dynamic_slice_sizes={128} | dynamic-slice | bytes 260 | tf_op jit(solution)/shard_map/dynamic_slice | solution.py:156
  60.9 1.3 %dynamic_slice.61 = pred[128]{0:T(512)(128)(4,1)} dynamic-slice(pred[1024]{0:T(1024)(128)(4,1)} %broadcast_compare_fusion, s32[]{:T(128)S(6)} %select_n.181), dynamic_slice_sizes={128} | dynamic-slice | bytes 260 | tf_op jit(solution)/shard_map/dynamic_slice | solution.py:166
  62.2 1.3 %dynamic_slice.48 = f32[1]{0:T(128)} dynamic-slice(f32[4]{0:T(128)} %param.13, s32[]{:T(128)S(6)} %select_n.180), dynamic_slice_sizes={1} | dynamic-slice | bytes 12 | tf_op jit(solution)/shard_map/dynamic_slice | solution.py:110
  63.5 1.0 %constant_dynamic-update-slice_fusion.6 = bf16[2048,768]{1,0:T(8,128)(2,1)S(1)} fusion(bf16[2048,768]{1,0:T(8,128)(2,1)S(1)} %get-tuple-element.15, bf16[256,768]{1,0:T(8,128)(2,1)} %collective-permute-done, s32[]{:T(128)S(6)} %select_n.192), kind=kLoop, calls=%fused_computation.104 | loop fusion | bytes 786436 | tf_op jit(solution)/shard_map/dynamic_update_slice | solution.py:62
  64.5 0.6 collective-permute-start.6
  65.0 1.0 %constant_dynamic-update-slice_fusion.5 = bf16[2048,768]{1,0:T(8,128)(2,1)S(1)} fusion(bf16[2048,768]{1,0:T(8,128)(2,1)S(1)} %constant_dynamic-update-slice_fusion.6, bf16[256,768]{1,0:T(8,128)(2,1)} %collective-permute-done.1, s32[]{:T(128)S(6)} %select_n.195), kind=kLoop, calls=%fused_computation.103 | loop fusion | bytes 786436 | tf_op jit(solution)/shard_map/dynamic_update_slice | solution.py:62
  66.1 1.0 %constant_dynamic-update-slice_fusion.4 = bf16[2048,768]{1,0:T(8,128)(2,1)S(1)} fusion(bf16[2048,768]{1,0:T(8,128)(2,1)S(1)} %constant_dynamic-update-slice_fusion.5, bf16[256,768]{1,0:T(8,128)(2,1)} %collective-permute-done.2, s32[]{:T(128)S(6)} %select_n.198), kind=kLoop, calls=%fused_computation.102 | loop fusion | bytes 786436 | tf_op jit(solution)/shard_map/dynamic_update_slice | solution.py:62
  67.1 1.0 %constant_dynamic-update-slice_fusion.3 = bf16[2048,768]{1,0:T(8,128)(2,1)S(1)} fusion(bf16[2048,768]{1,0:T(8,128)(2,1)S(1)} %constant_dynamic-update-slice_fusion.4, bf16[256,768]{1,0:T(8,128)(2,1)} %collective-permute-done.3, s32[]{:T(128)S(6)} %select_n.201), kind=kLoop, calls=%fused_computation.101 | loop fusion | bytes 786436 | tf_op jit(solution)/shard_map/dynamic_update_slice | solution.py:62
  68.1 1.0 %constant_dynamic-update-slice_fusion.2 = bf16[2048,768]{1,0:T(8,128)(2,1)S(1)} fusion(bf16[2048,768]{1,0:T(8,128)(2,1)S(1)} %constant_dynamic-update-slice_fusion.3, bf16[256,768]{1,0:T(8,128)(2,1)} %collective-permute-done.4, s32[]{:T(128)S(6)} %select_n.204), kind=kLoop, calls=%fused_computation.100 | loop fusion | bytes 786436 | tf_op jit(solution)/shard_map/dynamic_update_slice | solution.py:62
  69.2 1.0 %constant_dynamic-update-slice_fusion.1 = bf16[2048,768]{1,0:T(8,128)(2,1)S(1)} fusion(bf16[2048,768]{1,0:T(8,128)(2,1)S(1)} %constant_dynamic-update-slice_fusion.2, bf16[256,768]{1,0:T(8,128)(2,1)} %collective-permute-done.5, s32[]{:T(128)S(6)} %select_n.207), kind=kLoop, calls=%fused_computation.99 | loop fusion | bytes 786436 | tf_op jit(solution)/shard_map/dynamic_update_slice | solution.py:62
  70.2 2.3 %collective-permute-done.6 = bf16[256,768]{1,0:T(8,128)(2,1)S(1)} collective-permute-done((bf16[256,768]{1,0:T(8,128)(2,1)}, bf16[256,768]{1,0:T(8,128)(2,1)S(1)}, u32[]{:S(2)}, u32[]{:S(2)}) %collective-permute-start.6) | collective-permute-done | bytes 393248 | tf_op jit(solution)/shard_map/ppermute | solution.py:60
  72.6 0.3 fusion.66
  72.9 0.4 copy-done.9
  73.3 2.4 %select_reduce_fusion.3 = (f32[1024]{0:T(1024)S(1)}, f32[1024]{0:T(1024)S(1)}, f32[1024,1024]{0,1:T(8,128)S(1)}) fusion(pred[1024]{0:T(1024)(128)(4,1)S(1)} %copy-done.10, pred[1024]{0:T(1024)(128)(4,1)S(1)} %copy-done.15, s32[1024]{0:T(1024)S(1)} %bitcast.51, s32[1024]{0:T(1024)S(1)} %fusion.46, bf16[1024,768]{1,0:T(8,128)(2,1)S(1)} %bitcast.44, ...), kind=kOutput, calls=%fused_computation.11 | convolution fusion | flops 1618999296 | bytes 7358464 | tf_op jit(solution)/shard_map/dot_general | solution.py:67
  75.7 2.4 %fusion.1 = (f32[1024]{0:T(1024)S(1)}, f32[1024]{0:T(1024)S(1)}, f32[1024]{0:T(1024)S(1)}) fusion(f32[1024,1024]{0,1:T(8,128)S(1)} %get-tuple-element.23, s32[1024]{0:T(1024)S(1)} %bitcast.52, s32[1024]{0:T(1024)S(1)} %fusion.46, f32[1024]{0:T(1024)S(1)} %get-tuple-element.7, pred[1024]{0:T(1024)(128)(4,1)S(1)} %copy-done.15, f32[1024]{0:T(1024)S(1)} %get-tuple-element.6, ...), kind=kLoop, calls=%fused_computation.7 | loop fusion | flops 9434112 | bytes 4225024 | tf_op jit(solution)/shard_map/reduce_sum | solution.py:79
  78.2 1.4 %select_reduce_fusion.4 = (f32[]{:T(128)}, f32[1024]{0:T(1024)S(1)}, f32[]{:T(128)}, f32[1024]{0:T(1024)S(1)}) fusion(f32[1024]{0:T(1024)S(1)} %get-tuple-element.7, f32[1024]{0:T(1024)S(1)} %get-tuple-element.4, f32[1024]{0:T(1024)S(1)} %get-tuple-element.3, f32[1024]{0:T(1024)S(1)} %get-tuple-element.6, f32[1024]{0:T(1024)S(1)} %get-tuple-element.5, ...), kind=kLoop, calls=%fused_computation.86 | loop fusion | flops 16382 | bytes 32780 | tf_op jit(solution)/shard_map/reduce_sum | solution.py:151
  79.6 0.6 copy-done.11
  80.2 0.6 dynamic_slice.63
  80.9 3.3 %fusion.6 = bf16[128,768]{1,0:T(8,128)(2,1)} fusion(bf16[1024,768]{1,0:T(8,128)(2,1)S(1)} %bitcast.45, bf16[128,768]{1,0:T(8,128)(2,1)S(1)} %bitcast.47, f32[128]{0:T(128)} %dynamic_slice.63, f32[1024]{0:T(1024)} %copy-done.13, s32[128]{0:T(128)} %dynamic_slice.62, f32[]{:T(128)} %bitcast, s32[1024]{0:T(1024)} %bitcast.49, ...), kind=kOutput, calls=%fused_computation.21 | convolution fusion | flops 404815872 | bytes 1976452 | tf_op jit(solution)/shard_map/dot_general | solution.py:171
  84.2 3.4 %all-to-all-start.1 = ((bf16[4,32,768]{2,1,0:T(8,128)(2,1)}), bf16[4,32,768]{2,1,0:T(8,128)(2,1)S(1)}, u32[]{:S(2)}, u32[]{:S(2)}) async-start(bf16[4,32,768]{2,1,0:T(8,128)(2,1)} %bitcast.48), calls=%async_computation.1 | async-start | bytes 393216 | tf_op jit(solution)/shard_map/all_to_all | solution.py:175
  87.6 3.5 %fusion.5 = bf16[128,768]{1,0:T(8,128)(2,1)} fusion(bf16[1024,768]{1,0:T(8,128)(2,1)S(1)} %bitcast.43, bf16[128,768]{1,0:T(8,128)(2,1)} %param.8, f32[1024]{0:T(1024)S(1)} %copy-done.12, f32[128]{0:T(128)S(1)} %dynamic_slice.60, s32[128]{0:T(128)} %fusion.55, f32[]{:T(128)} %bitcast, s32[1024]{0:T(1024)S(1)} %fusion.46, pred[128]{0:T(512)(128)(4,1)} %dynamic_slice.50, ...), kind=kOutput, calls=%fused_computation.20 | convolution fusion | flops 404815872 | bytes 1976452 | tf_op jit(solution)/shard_map/dot_general | solution.py:162
  92.5 0.4 all-to-all-done.1
  92.9 1.2 %gather_fusion.1 = bf16[4,32,768]{2,1,0:T(8,128)(2,1)} fusion(bf16[4,32,768]{2,1,0:T(8,128)(2,1)S(1)} %all-to-all-done.1, s32[1024]{0:T(1024)S(1)} %pad_clamp_fusion), kind=kCustom, calls=%fused_computation.1 | custom fusion | bytes 393232 | tf_op jit(solution)/shard_map/gather | solution.py:178
  (43 shorter events, 0.5 us)
Async XLA Ops:
  0.6 1.4 %copy-start = (bf16[4,32,768]{2,1,0:T(8,128)(2,1)S(1)}, bf16[4,32,768]{2,1,0:T(8,128)(2,1)}, u32[]{:S(2)}) copy-start(bf16[4,32,768]{2,1,0:T(8,128)(2,1)} %param.9) | copy-start | bytes 589828
  0.6 52.7 %copy-start.7 = (s32[8]{0:T(128)S(1)}, s32[8]{0:T(128)}, u32[]{:S(2)}) copy-start(s32[8]{0:T(128)} %constant.181.clone) | copy-start | bytes 100
  0.7 26.5 %copy-start.17 = (s32[4]{0:T(128)S(1)}, s32[4]{0:T(128)}, u32[]{:S(2)}) copy-start(s32[4]{0:T(128)} %param.11) | copy-start | bytes 52
  0.7 36.3 %copy-start.8 = (s32[1,1024]{1,0:T(1,128)S(1)}, s32[1,1024]{1,0:T(1,128)}, u32[]{:S(2)}) copy-start(s32[1,1024]{1,0:T(1,128)} %param.12) | copy-start | bytes 12292
  1.4 0.6 copy-start.16
  3.3 9.5 %all-to-all-start = ((bf16[4,32,768]{2,1,0:T(8,128)(2,1)}), bf16[4,32,768]{2,1,0:T(8,128)(2,1)S(1)}, u32[]{:S(2)}, u32[]{:S(2)}) async-start(bf16[4,32,768]{2,1,0:T(8,128)(2,1)} %gather_fusion), calls=%async_computation | async-start | bytes 393216 | tf_op jit(solution)/shard_map/all_to_all | solution.py:107
  12.9 0.9 copy-start.6
  13.8 0.8 copy-start.5
  14.6 10.8 %collective-permute-start = (bf16[256,768]{1,0:T(8,128)(2,1)S(1)}, bf16[256,768]{1,0:T(8,128)(2,1)}, u32[]{:S(2)}, u32[]{:S(2)}) collective-permute-start(bf16[256,768]{1,0:T(8,128)(2,1)S(1)} %get-tuple-element.14), channel_id=1, source_target_pairs={{0,2},{2,4},{4,6},{6,7},{7,5},{5,3},{3,1},{1,0},{8,10},{10,12},{12... | collective-permute-start | bytes 1179656 | tf_op jit(solution)/shard_map/ppermute | solution.py:60
  25.4 10.1 %collective-permute-start.1 = (bf16[256,768]{1,0:T(8,128)(2,1)}, bf16[256,768]{1,0:T(8,128)(2,1)}, u32[]{:S(2)}, u32[]{:S(2)}) collective-permute-start(bf16[256,768]{1,0:T(8,128)(2,1)} %collective-permute-done), channel_id=1, source_target_pairs={{0,2},{2,4},{4,6},{6,7},{7,5},{5,3},{3,1},{1,0},{8,10},{10,12},{12... | collective-permute-start | bytes 1179656 | tf_op jit(solution)/shard_map/ppermute | solution.py:60
  27.8 10.0 %collective-permute-start.4 = (bf16[256,768]{1,0:T(8,128)(2,1)}, bf16[256,768]{1,0:T(8,128)(2,1)}, u32[]{:S(2)}, u32[]{:S(2)}) collective-permute-start(bf16[256,768]{1,0:T(8,128)(2,1)} %copy-done.5), channel_id=1, source_target_pairs={{0,1},{2,0},{4,2},{6,4},{7,6},{5,7},{3,5},{1,3},{8,9},{10,8},{12,1... | collective-permute-start | bytes 1179656 | tf_op jit(solution)/shard_map/ppermute | solution.py:60
  28.7 9.1 %copy-start.14 = (pred[1024]{0:T(1024)(128)(4,1)}, pred[1024]{0:T(1024)(128)(4,1)S(1)}, u32[]{:S(2)}) copy-start(pred[1024]{0:T(1024)(128)(4,1)S(1)} %iota_compare_fusion) | copy-start | bytes 3076
  35.4 9.3 %collective-permute-start.2 = (bf16[256,768]{1,0:T(8,128)(2,1)}, bf16[256,768]{1,0:T(8,128)(2,1)}, u32[]{:S(2)}, u32[]{:S(2)}) collective-permute-start(bf16[256,768]{1,0:T(8,128)(2,1)} %collective-permute-done.1), channel_id=1, source_target_pairs={{0,2},{2,4},{4,6},{6,7},{7,5},{5,3},{3,1},{1,0},{8,10},{10,12},{12... | collective-permute-start | bytes 1179656 | tf_op jit(solution)/shard_map/ppermute | solution.py:60
  37.8 26.7 %collective-permute-start.5 = (bf16[256,768]{1,0:T(8,128)(2,1)}, bf16[256,768]{1,0:T(8,128)(2,1)}, u32[]{:S(2)}, u32[]{:S(2)}) collective-permute-start(bf16[256,768]{1,0:T(8,128)(2,1)} %collective-permute-done.4), channel_id=1, source_target_pairs={{0,1},{2,0},{4,2},{6,4},{7,6},{5,7},{3,5},{1,3},{8,9},{10,8},{12,1... | collective-permute-start | bytes 1179656 | tf_op jit(solution)/shard_map/ppermute | solution.py:60
  44.7 22.4 %collective-permute-start.3 = (bf16[256,768]{1,0:T(8,128)(2,1)}, bf16[256,768]{1,0:T(8,128)(2,1)}, u32[]{:S(2)}, u32[]{:S(2)}) collective-permute-start(bf16[256,768]{1,0:T(8,128)(2,1)} %collective-permute-done.2), channel_id=1, source_target_pairs={{0,2},{2,4},{4,6},{6,7},{7,5},{5,3},{3,1},{1,0},{8,10},{10,12},{12... | collective-permute-start | bytes 1179656 | tf_op jit(solution)/shard_map/ppermute | solution.py:60
  64.5 8.0 %collective-permute-start.6 = (bf16[256,768]{1,0:T(8,128)(2,1)}, bf16[256,768]{1,0:T(8,128)(2,1)S(1)}, u32[]{:S(2)}, u32[]{:S(2)}) collective-permute-start(bf16[256,768]{1,0:T(8,128)(2,1)} %collective-permute-done.5), channel_id=1, source_target_pairs={{0,1},{2,0},{4,2},{6,4},{7,6},{5,7},{3,5},{1,3},{8,9},{10,8},{12,1... | collective-permute-start | bytes 1179656 | tf_op jit(solution)/shard_map/ppermute | solution.py:60
  72.6 0.7 copy-start.9
  72.6 0.7 copy-start.10
  72.6 0.7 copy-start.15
  72.9 2.8 %copy-start.1 = (bf16[8,1,128,768]{3,2,1,0:T(8,128)(2,1)}, bf16[8,1,128,768]{3,2,1,0:T(8,128)(2,1)S(1)}, u32[]{:S(2)}) copy-start(bf16[8,1,128,768]{3,2,1,0:T(8,128)(2,1)S(1)} %get-tuple-element.13) | copy-start | bytes 4718596
  72.9 2.8 %copy-start.3 = (bf16[8,1,128,768]{3,2,1,0:T(8,128)(2,1)}, bf16[8,1,128,768]{3,2,1,0:T(8,128)(2,1)S(1)}, u32[]{:S(2)}) copy-start(bf16[8,1,128,768]{3,2,1,0:T(8,128)(2,1)S(1)} %get-tuple-element.12) | copy-start | bytes 4718596
  75.7 5.2 %copy-start.4 = (bf16[8,1,128,768]{3,2,1,0:T(8,128)(2,1)S(1)}, bf16[8,1,128,768]{3,2,1,0:T(8,128)(2,1)}, u32[]{:S(2)}) copy-start(bf16[8,1,128,768]{3,2,1,0:T(8,128)(2,1)} %copy-done.3) | copy-start | bytes 4718596
  78.1 9.5 %copy-start.2 = (bf16[8,1,128,768]{3,2,1,0:T(8,128)(2,1)S(1)}, bf16[8,1,128,768]{3,2,1,0:T(8,128)(2,1)}, u32[]{:S(2)}) copy-start(bf16[8,1,128,768]{3,2,1,0:T(8,128)(2,1)} %copy-done.1) | copy-start | bytes 4718596
  79.6 0.6 copy-start.11
  79.6 1.2 %copy-start.13 = (f32[1024]{0:T(1024)}, f32[1024]{0:T(1024)S(1)}, u32[]{:S(2)}) copy-start(f32[1024]{0:T(1024)S(1)} %get-tuple-element.25) | copy-start | bytes 12292
  80.8 6.8 %copy-start.12 = (f32[1024]{0:T(1024)S(1)}, f32[1024]{0:T(1024)}, u32[]{:S(2)}) copy-start(f32[1024]{0:T(1024)} %copy-done.11) | copy-start | bytes 12292
  84.2 8.7 %all-to-all-start.1 = ((bf16[4,32,768]{2,1,0:T(8,128)(2,1)}), bf16[4,32,768]{2,1,0:T(8,128)(2,1)S(1)}, u32[]{:S(2)}, u32[]{:S(2)}) async-start(bf16[4,32,768]{2,1,0:T(8,128)(2,1)} %bitcast.48), calls=%async_computation.1 | async-start | bytes 393216 | tf_op jit(solution)/shard_map/all_to_all | solution.py:175

commit v4 on v2

--- a/solution.py
+++ b/solution.py
@@ -103,9 +103,15 @@
     shard_index = lax.axis_index("dp")
     slot_ids = jnp.arange(lang_size, dtype=jnp.int32)
     slot_of_group = jnp.zeros((lang_size,), jnp.int32).at[slot_group].set(slot_ids)
-    ordered = tgt_emb[slot_of_group]
-    arrived = lax.all_to_all(ordered, "lang", split_axis=0, concat_axis=1, tiled=True)
-    partner = arrived[0]
+    partner = jnp.zeros((lang_size * per_slot, emb_width), tgt_emb.dtype)
+    own = lax.dynamic_index_in_dim(tgt_emb, slot_of_group[group_index], 0, keepdims=False)
+    partner = lax.dynamic_update_slice_in_dim(partner, own, group_index * per_slot, 0)
+    for k in range(1, lang_size):
+        dest = (group_index + k) % lang_size
+        sent = lax.dynamic_index_in_dim(tgt_emb, slot_of_group[dest], 0, keepdims=False)
+        got = lax.ppermute(sent, "lang", [(l, (l + k) % lang_size) for l in range(lang_size)])
+        origin = (group_index - k) % lang_size
+        partner = lax.dynamic_update_slice_in_dim(partner, got, origin * per_slot, 0)
     live_count = counts[group_index]
     weight = pair_weight[group_index]
     pair_align = align[0]
@@ -171,7 +177,7 @@
     )
     grad_local = (own_terms * inv_root).astype(jnp.bfloat16)
     returned = lax.all_to_all(
-        grad_local.reshape(1, row_count, emb_width), "lang", split_axis=1, concat_axis=0, tiled=True
+        grad_local.reshape(lang_size, per_slot, emb_width), "lang", split_axis=0, concat_axis=0, tiled=True
     )
     grad_tgt = returned[slot_group]
     return (grad_src, grad_tgt, pair_loss)

time: 87.2 us -> 91.8 us (1.053)
  between operations: 13.3 us -> 21.1 us
  waiting for transfers between devices: 17.7 us -> 16.4 us
  other arithmetic: 8.42 us -> 7.27 us
  local copies, waits for them, and re-layouts: 15.1 us -> 14.1 us
    ppermute x0 -> x3, starting transfers between devices: none -> 3.44 us  [per_device(): lax.ppermute(sent, 'lang', [(l, (l + k) % lang_size) for l in range(lang_...]
    all_to_all x2 -> x1, starting transfers between devices: 6.73 us -> 3.37 us  [per_device(): lax.all_to_all(grad_local.reshape(lang_size, per_slot, emb_width), 'lang'...]
    unnamed x40 -> x22, local copies, waits for them, and re-layouts: 2.12 us -> 0.05 us
    unnamed x1 -> x0, other arithmetic: 1.8 us -> none
    reshape x1 -> x0, local copies, waits for them, and re-layouts: 1.28 us -> none  [per_device(): grad_local.reshape(1, row_count, emb_width)]
    gather x1 -> x0, local copies, waits for them, and re-layouts: 1.24 us -> none  [per_device(): ordered = tgt_emb[slot_of_group]]
  transfers between devices with their start and end apart: 16 -> 18, of which waited for: 8 -> 8; matrix products, arithmetic and copies ran while one was open for 17% -> 19% of each run, Pallas kernels for 0% -> 0%
where the time goes in v4:
time: 91.8 us; the launch traced here: 91 us
  starting transfers between devices  23.3 us (25%)
  between operations  21.1 us (23%)
  waiting for transfers between devices  16.4 us (18%)
  local copies, waits for them, and re-layouts  14.1 us (15%)
  matrix products  8.78 us (10%)
  other arithmetic  7.27 us (8%)
    ppermute x14, starting transfers between devices, ring_gather(): cur = lax.ppermute(cur, 'dp', pairs)  16.5 us
    ppermute x14, waiting for transfers between devices, ring_gather(): cur = lax.ppermute(cur, 'dp', pairs)  15.6 us
    ppermute x3, starting transfers between devices, per_device(): lax.ppermute(sent, 'lang', [(l, (l + k) % lang_size) for l in range(lang_...  3.44 us
    all_to_all x1, starting transfers between devices, per_device(): lax.all_to_all(grad_local.reshape(lang_size, per_slot, emb_width), 'lang'...  3.37 us
    dot_general x1, matrix products, per_device(): lax.dot_general(g_cols, x_all, (((0,), (0,)), ((), ())), preferred_elemen...  3.2 us
    dot_general x1, matrix products, per_device(): jnp.dot(g_rows, y_all, preferred_element_type=jnp.float32) * inv_root  3.18 us
    reduce_sum x1, other arithmetic, block_stats(): pos_score = jnp.sum(jnp.where(is_pos, scores_f, 0.0), axis=1)  2.43 us
    dot_general x1, matrix products, scores_of(): lax.dot_general(x_rows, y_rows, (((1,), (1,)), ((), ())), preferred_eleme...  2.4 us
  transfers between devices with their start and end apart: 18, of which 8 were waited for; matrix products, arithmetic and copies ran while one was open for 19% of the time, Pallas kernels for 0%

profile of v4, /device:TPU:0, one launch (start us, length us, event | category | flops | bytes accessed | tf_op | source)
XLA Modules:
  0.0 91.0 jit_solution(13363861742990139242)
XLA Ops:
  0.7 3.1 %collective-permute-start.10 = (bf16[128,768]{1,0:T(8,128)(2,1)}, bf16[128,768]{1,0:T(8,128)(2,1)}, u32[]{:S(2)}, u32[]{:S(2)}) collective-permute-start(bf16[128,768]{1,0:T(8,128)(2,1)} %param.10), channel_id=1, source_target_pairs={{0,2},{2,4},{4,6},{6,7},{7,5},{5,3},{3,1},{1,0},{8,10},{10,12},{12... | collective-permute-start | bytes 589832 | tf_op jit(solution)/shard_map/ppermute | solution.py:60
  3.8 0.7 compare_select_fusion.4
  4.5 0.6 scatter_custom_fusion
  5.1 0.7 fusion.67
  11.5 0.9 dynamic-slice_bitcast_fusion
  12.5 2.0 %collective-permute-start.1 = (bf16[32,768]{1,0:T(8,128)(2,1)S(1)}, bf16[32,768]{1,0:T(8,128)(2,1)S(1)}, u32[]{:S(2)}, u32[]{:S(2)}) collective-permute-start(bf16[32,768]{1,0:T(8,128)(2,1)S(1)} %get-tuple-element.14), channel_id=1, source_target_pairs={{0,16},{8,24},{16,0},{24,8},{1,17},{9,25},{17,1},{25,9},{2,18},{10... | collective-permute-start | bytes 147464 | tf_op jit(solution)/shard_map/ppermute | solution.py:112
  14.5 1.4 %collective-permute-start.2 = (bf16[32,768]{1,0:T(8,128)(2,1)S(1)}, bf16[32,768]{1,0:T(8,128)(2,1)S(1)}, u32[]{:S(2)}, u32[]{:S(2)}) collective-permute-start(bf16[32,768]{1,0:T(8,128)(2,1)S(1)} %get-tuple-element.12), channel_id=1, source_target_pairs={{0,24},{8,0},{16,8},{24,16},{1,25},{9,1},{17,9},{25,17},{2,26},{10... | collective-permute-start | bytes 147464 | tf_op jit(solution)/shard_map/ppermute | solution.py:112
  17.3 1.3 %dynamic_slice.98 = s32[1]{0:T(128)} dynamic-slice(s32[4]{0:T(128)} %param.13, s32[]{:T(128)S(6)} %select_n.306), dynamic_slice_sizes={1} | dynamic-slice | bytes 12 | tf_op jit(solution)/shard_map/dynamic_slice | solution.py:115
  18.6 0.7 iota_compare_fusion
  19.3 1.5 %convert_reduce_fusion = s32[1024]{0:T(1024)S(1)} fusion(s32[1024]{0:T(1024)} %bitcast.50, s32[1024]{0:T(1024)S(1)} %fusion.46, pred[1024]{0:T(1024)(128)(4,1)S(1)} %iota_compare_fusion), kind=kLoop, calls=%fused_computation.11 | loop fusion | flops 4193280 | bytes 13312 | tf_op jit(solution)/shard_map/reduce_max | solution.py:122
  21.6 0.8 bitcast_dynamic-update-slice_fusion
  22.5 0.6 fusion.55
  23.0 0.6 dynamic_slice.108
  28.3 0.7 fusion.66
  34.1 0.6 dynamic_slice.127
  34.8 0.6 dynamic_slice.99
  35.4 0.6 dynamic_slice.126
  36.0 0.6 dynamic_slice.97
  36.6 1.6 %collective-permute-start.3 = (bf16[128,768]{1,0:T(8,128)(2,1)S(1)}, bf16[128,768]{1,0:T(8,128)(2,1)S(1)}, u32[]{:S(2)}, u32[]{:S(2)}) collective-permute-start(bf16[128,768]{1,0:T(8,128)(2,1)S(1)} %constant_dynamic-update-slice_fusion.15), channel_id=1, source_target_pairs={{0,2},{2,4},{4,6},{6,7},{7,5},{5,3},{3,1},{1,0},{8,10},{10,12},{12... | collective-permute-start | bytes 589832 | tf_op jit(solution)/shard_map/ppermute | solution.py:60
  38.3 0.5 collective-permute-start.7
  38.9 1.6 %collective-permute-start.11 = (bf16[128,768]{1,0:T(8,128)(2,1)}, bf16[128,768]{1,0:T(8,128)(2,1)S(1)}, u32[]{:S(2)}, u32[]{:S(2)}) collective-permute-start(bf16[128,768]{1,0:T(8,128)(2,1)} %collective-permute-done.10), channel_id=1, source_target_pairs={{0,2},{2,4},{4,6},{6,7},{7,5},{5,3},{3,1},{1,0},{8,10},{10,12},{12... | collective-permute-start | bytes 589832 | tf_op jit(solution)/shard_map/ppermute | solution.py:60
  40.5 0.5 collective-permute-start.15
  40.9 0.9 %constant_dynamic-update-slice_fusion = bf16[1024,768]{1,0:T(8,128)(2,1)S(1)} fusion(bf16[1024,768]{1,0:T(8,128)(2,1)S(1)} %constant_dynamic-update-slice_fusion.6, bf16[128,768]{1,0:T(8,128)(2,1)} %collective-permute-done.10, s32[]{:T(128)S(6)} %select_n.333), kind=kLoop, calls=%fused_computation.70 | loop fusion | bytes 393220 | tf_op jit(solution)/shard_map/dynamic_update_slice | solution.py:62
  41.9 2.6 %collective-permute-done.3 = bf16[128,768]{1,0:T(8,128)(2,1)S(1)} collective-permute-done((bf16[128,768]{1,0:T(8,128)(2,1)S(1)}, bf16[128,768]{1,0:T(8,128)(2,1)S(1)}, u32[]{:S(2)}, u32[]{:S(2)}) %collective-permute-start.3) | collective-permute-done | bytes 196640 | tf_op jit(solution)/shard_map/ppermute | solution.py:60
  44.5 1.6 %collective-permute-start.4 = (bf16[128,768]{1,0:T(8,128)(2,1)S(1)}, bf16[128,768]{1,0:T(8,128)(2,1)S(1)}, u32[]{:S(2)}, u32[]{:S(2)}) collective-permute-start(bf16[128,768]{1,0:T(8,128)(2,1)S(1)} %collective-permute-done.3), channel_id=1, source_target_pairs={{0,2},{2,4},{4,6},{6,7},{7,5},{5,3},{3,1},{1,0},{8,10},{10,12},{12... | collective-permute-start | bytes 589832 | tf_op jit(solution)/shard_map/ppermute | solution.py:60
  46.0 0.4 collective-permute-start.8
  46.5 2.2 %collective-permute-done.11 = bf16[128,768]{1,0:T(8,128)(2,1)S(1)} collective-permute-done((bf16[128,768]{1,0:T(8,128)(2,1)}, bf16[128,768]{1,0:T(8,128)(2,1)S(1)}, u32[]{:S(2)}, u32[]{:S(2)}) %collective-permute-start.11) | collective-permute-done | bytes 196640 | tf_op jit(solution)/shard_map/ppermute | solution.py:60
  48.7 1.6 %collective-permute-start.12 = (bf16[128,768]{1,0:T(8,128)(2,1)S(1)}, bf16[128,768]{1,0:T(8,128)(2,1)S(1)}, u32[]{:S(2)}, u32[]{:S(2)}) collective-permute-start(bf16[128,768]{1,0:T(8,128)(2,1)S(1)} %collective-permute-done.11), channel_id=1, source_target_pairs={{0,2},{2,4},{4,6},{6,7},{7,5},{5,3},{3,1},{1,0},{8,10},{10,12},{12... | collective-permute-start | bytes 589832 | tf_op jit(solution)/shard_map/ppermute | solution.py:60
  50.3 0.4 collective-permute-start.16
  50.7 2.2 %collective-permute-done.4 = bf16[128,768]{1,0:T(8,128)(2,1)S(1)} collective-permute-done((bf16[128,768]{1,0:T(8,128)(2,1)S(1)}, bf16[128,768]{1,0:T(8,128)(2,1)S(1)}, u32[]{:S(2)}, u32[]{:S(2)}) %collective-permute-start.4) | collective-permute-done | bytes 196640 | tf_op jit(solution)/shard_map/ppermute | solution.py:60
  52.9 1.6 %collective-permute-start.5 = (bf16[128,768]{1,0:T(8,128)(2,1)S(1)}, bf16[128,768]{1,0:T(8,128)(2,1)S(1)}, u32[]{:S(2)}, u32[]{:S(2)}) collective-permute-start(bf16[128,768]{1,0:T(8,128)(2,1)S(1)} %collective-permute-done.4), channel_id=1, source_target_pairs={{0,2},{2,4},{4,6},{6,7},{7,5},{5,3},{3,1},{1,0},{8,10},{10,12},{12... | collective-permute-start | bytes 589832 | tf_op jit(solution)/shard_map/ppermute | solution.py:60
  54.9 2.2 %collective-permute-done.12 = bf16[128,768]{1,0:T(8,128)(2,1)S(1)} collective-permute-done((bf16[128,768]{1,0:T(8,128)(2,1)S(1)}, bf16[128,768]{1,0:T(8,128)(2,1)S(1)}, u32[]{:S(2)}, u32[]{:S(2)}) %collective-permute-start.12) | collective-permute-done | bytes 196640 | tf_op jit(solution)/shard_map/ppermute | solution.py:60
  57.1 1.6 %collective-permute-start.13 = (bf16[128,768]{1,0:T(8,128)(2,1)S(1)}, bf16[128,768]{1,0:T(8,128)(2,1)S(1)}, u32[]{:S(2)}, u32[]{:S(2)}) collective-permute-start(bf16[128,768]{1,0:T(8,128)(2,1)S(1)} %collective-permute-done.12), channel_id=1, source_target_pairs={{0,2},{2,4},{4,6},{6,7},{7,5},{5,3},{3,1},{1,0},{8,10},{10,12},{12... | collective-permute-start | bytes 589832 | tf_op jit(solution)/shard_map/ppermute | solution.py:60
  58.7 2.6 %collective-permute-done.5 = bf16[128,768]{1,0:T(8,128)(2,1)S(1)} collective-permute-done((bf16[128,768]{1,0:T(8,128)(2,1)S(1)}, bf16[128,768]{1,0:T(8,128)(2,1)S(1)}, u32[]{:S(2)}, u32[]{:S(2)}) %collective-permute-start.5) | collective-permute-done | bytes 196640 | tf_op jit(solution)/shard_map/ppermute | solution.py:60
  61.3 1.6 %collective-permute-start.6 = (bf16[128,768]{1,0:T(8,128)(2,1)S(1)}, bf16[128,768]{1,0:T(8,128)(2,1)S(1)}, u32[]{:S(2)}, u32[]{:S(2)}) collective-permute-start(bf16[128,768]{1,0:T(8,128)(2,1)S(1)} %collective-permute-done.5), channel_id=1, source_target_pairs={{0,2},{2,4},{4,6},{6,7},{7,5},{5,3},{3,1},{1,0},{8,10},{10,12},{12... | collective-permute-start | bytes 589832 | tf_op jit(solution)/shard_map/ppermute | solution.py:60
  62.9 2.6 %collective-permute-done.13 = bf16[128,768]{1,0:T(8,128)(2,1)S(1)} collective-permute-done((bf16[128,768]{1,0:T(8,128)(2,1)S(1)}, bf16[128,768]{1,0:T(8,128)(2,1)S(1)}, u32[]{:S(2)}, u32[]{:S(2)}) %collective-permute-start.13) | collective-permute-done | bytes 196640 | tf_op jit(solution)/shard_map/ppermute | solution.py:60
  65.5 0.9 %constant_dynamic-update-slice_fusion.1 = bf16[1024,768]{1,0:T(8,128)(2,1)S(1)} fusion(bf16[1024,768]{1,0:T(8,128)(2,1)S(1)} %constant_dynamic-update-slice_fusion.2, bf16[128,768]{1,0:T(8,128)(2,1)} %collective-permute-done.14, s32[]{:T(128)S(6)} %select_n.345), kind=kLoop, calls=%fused_computation.71 | loop fusion | bytes 393220 | tf_op jit(solution)/shard_map/dynamic_update_slice | solution.py:62
  66.6 1.3 %collective-permute-done.6 = bf16[128,768]{1,0:T(8,128)(2,1)S(1)} collective-permute-done((bf16[128,768]{1,0:T(8,128)(2,1)S(1)}, bf16[128,768]{1,0:T(8,128)(2,1)S(1)}, u32[]{:S(2)}, u32[]{:S(2)}) %collective-permute-start.6) | collective-permute-done | bytes 196640 | tf_op jit(solution)/shard_map/ppermute | solution.py:60
  68.0 2.4 %select_reduce_fusion.3 = (f32[1024]{0:T(1024)S(1)}, f32[1024]{0:T(1024)S(1)}, f32[1024,1024]{0,1:T(8,128)S(1)}) fusion(pred[1024]{0:T(1024)(128)(4,1)S(1)} %copy-done.4, pred[1024]{0:T(1024)(128)(4,1)S(1)} %copy-done.8, s32[1024]{0:T(1024)S(1)} %bitcast.51, s32[1024]{0:T(1024)S(1)} %fusion.46, ...), kind=kOutput, calls=%fused_computation.10 | convolution fusion | flops 1618999296 | bytes 7358464 | tf_op jit(solution)/shard_map/dot_general | solution.py:67
  70.4 2.4 %fusion.1 = (f32[1024]{0:T(1024)S(1)}, f32[1024]{0:T(1024)S(1)}, f32[1024]{0:T(1024)S(1)}) fusion(f32[1024,1024]{0,1:T(8,128)S(1)} %get-tuple-element.26, s32[1024]{0:T(1024)S(1)} %bitcast.52, s32[1024]{0:T(1024)S(1)} %fusion.46, f32[1024]{0:T(1024)S(1)} %get-tuple-element.7, pred[1024]{0:T(1024)(128)(4,1)S(1)} %copy-done.8, f32[1024]{0:T(1024)S(1)} %get-tuple-element.6, ...), kind=kLoop, calls=%fused_computation.6 | loop fusion | flops 9434112 | bytes 4225024 | tf_op jit(solution)/shard_map/reduce_sum | solution.py:79
  72.9 1.9 %select_reduce_fusion.4 = (f32[]{:T(128)}, f32[1024]{0:T(1024)S(1)}, f32[]{:T(128)}, f32[1024]{0:T(1024)}) fusion(f32[1024]{0:T(1024)S(1)} %get-tuple-element.7, f32[1024]{0:T(1024)S(1)} %get-tuple-element.4, f32[1024]{0:T(1024)S(1)} %get-tuple-element.3, f32[1024]{0:T(1024)S(1)} %get-tuple-element.6, f32[1024]{0:T(1024)S(1)} %get-tuple-element.5, ...), kind=kLoop, calls=%fused_computation.107 | loop fusion | flops 16382 | bytes 32780 | tf_op jit(solution)/shard_map/reduce_sum | solution.py:155
  74.8 0.6 dynamic_slice.128
  75.4 1.3 %dynamic_slice.125 = f32[128]{0:T(128)} dynamic-slice(f32[1024]{0:T(1024)} %get-tuple-element.28, s32[]{:T(128)S(6)} %select_n.307), dynamic_slice_sizes={128} | dynamic-slice | bytes 1028 | tf_op jit(solution)/shard_map/dynamic_slice | solution.py:161
  76.8 3.2 %fusion.6 = bf16[128,768]{1,0:T(8,128)(2,1)} fusion(bf16[1024,768]{1,0:T(8,128)(2,1)S(1)} %constant_dynamic-update-slice_fusion.5, bf16[128,768]{1,0:T(8,128)(2,1)S(1)} %constant_dynamic-update-slice_fusion.15, f32[128]{0:T(128)} %dynamic_slice.128, f32[1024]{0:T(1024)} %get-tuple-element.28, s32[128]{0:T(128)} %dynamic_slice.127, f32[]{:T(128)} %bitcast, ...), kind=kOutput, calls=%fused_computation.20 | convolution fusion | flops 404815872 | bytes 1976452 | tf_op jit(solution)/shard_map/dot_general | solution.py:175
  80.0 3.4 %all-to-all-start = ((bf16[4,32,768]{2,1,0:T(8,128)(2,1)}), bf16[4,32,768]{2,1,0:T(8,128)(2,1)S(1)}, u32[]{:S(2)}, u32[]{:S(2)}) async-start(bf16[4,32,768]{2,1,0:T(8,128)(2,1)} %bitcast.49), calls=%async_computation | async-start | bytes 393216 | tf_op jit(solution)/shard_map/all_to_all | solution.py:179
  83.3 3.2 %fusion.5 = bf16[128,768]{1,0:T(8,128)(2,1)} fusion(bf16[1024,768]{1,0:T(8,128)(2,1)S(1)} %constant_dynamic-update-slice_fusion.7, bf16[128,768]{1,0:T(8,128)(2,1)S(1)} %copy-done, f32[1024]{0:T(1024)} %copy-done.6, f32[128]{0:T(128)} %dynamic_slice.125, s32[128]{0:T(128)} %fusion.55, f32[]{:T(128)} %bitcast, s32[1024]{0:T(1024)S(1)} %fusion.46, ...), kind=kOutput, calls=%fused_computation.19 | convolution fusion | flops 404815872 | bytes 1976452 | tf_op jit(solution)/shard_map/dot_general | solution.py:166
  87.8 0.8 all-to-all-done
  88.6 1.2 %gather_fusion = bf16[4,32,768]{2,1,0:T(8,128)(2,1)} fusion(bf16[4,32,768]{2,1,0:T(8,128)(2,1)S(1)} %all-to-all-done, s32[1024]{0:T(1024)S(1)} %pad_clamp_fusion), kind=kCustom, calls=%fused_computation | custom fusion | bytes 393232 | tf_op jit(solution)/shard_map/gather | solution.py:182
  (59 shorter events, 1.2 us)
Async XLA Ops:
  0.6 22.4 %copy-start.10 = (s32[8]{0:T(128)S(1)}, s32[8]{0:T(128)}, u32[]{:S(2)}) copy-start(s32[8]{0:T(128)} %constant.265.clone) | copy-start | bytes 100
  0.6 27.6 %copy-start.1 = (s32[8]{0:T(128)S(1)}, s32[8]{0:T(128)}, u32[]{:S(2)}) copy-start(s32[8]{0:T(128)} %constant.264.clone) | copy-start | bytes 100
  0.7 20.3 %copy-start = (bf16[128,768]{1,0:T(8,128)(2,1)S(1)}, bf16[128,768]{1,0:T(8,128)(2,1)}, u32[]{:S(2)}) copy-start(bf16[128,768]{1,0:T(8,128)(2,1)} %param.10) | copy-start | bytes 589828
  0.7 21.8 %copy-start.2 = (s32[1,1024]{1,0:T(1,128)S(1)}, s32[1,1024]{1,0:T(1,128)}, u32[]{:S(2)}) copy-start(s32[1,1024]{1,0:T(1,128)} %param.14) | copy-start | bytes 12292
  0.7 38.2 %collective-permute-start.10 = (bf16[128,768]{1,0:T(8,128)(2,1)}, bf16[128,768]{1,0:T(8,128)(2,1)}, u32[]{:S(2)}, u32[]{:S(2)}) collective-permute-start(bf16[128,768]{1,0:T(8,128)(2,1)} %param.10), channel_id=1, source_target_pairs={{0,2},{2,4},{4,6},{6,7},{7,5},{5,3},{3,1},{1,0},{8,10},{10,12},{12... | collective-permute-start | bytes 589832 | tf_op jit(solution)/shard_map/ppermute | solution.py:60
  3.8 36.7 %collective-permute-start.14 = (bf16[128,768]{1,0:T(8,128)(2,1)}, bf16[128,768]{1,0:T(8,128)(2,1)}, u32[]{:S(2)}, u32[]{:S(2)}) collective-permute-start(bf16[128,768]{1,0:T(8,128)(2,1)} %param.10), channel_id=1, source_target_pairs={{0,1},{2,0},{4,2},{6,4},{7,6},{5,7},{3,5},{1,3},{8,9},{10,8},{12,1... | collective-permute-start | bytes 589832 | tf_op jit(solution)/shard_map/ppermute | solution.py:60
  3.8 32.2 %copy-start.9 = (f32[4]{0:T(128)S(1)}, f32[4]{0:T(128)}, u32[]{:S(2)}) copy-start(f32[4]{0:T(128)} %param.15) | copy-start | bytes 52
  12.4 24.1 %collective-permute-start = (bf16[32,768]{1,0:T(8,128)(2,1)S(1)}, bf16[32,768]{1,0:T(8,128)(2,1)S(1)}, u32[]{:S(2)}, u32[]{:S(2)}) collective-permute-start(bf16[32,768]{1,0:T(8,128)(2,1)S(1)} %get-tuple-element.13), channel_id=1, source_target_pairs={{0,8},{8,16},{16,24},{24,0},{1,9},{9,17},{17,25},{25,1},{2,10},{10... | collective-permute-start | bytes 147464 | tf_op jit(solution)/shard_map/ppermute | solution.py:112
  12.5 24.1 %collective-permute-start.1 = (bf16[32,768]{1,0:T(8,128)(2,1)S(1)}, bf16[32,768]{1,0:T(8,128)(2,1)S(1)}, u32[]{:S(2)}, u32[]{:S(2)}) collective-permute-start(bf16[32,768]{1,0:T(8,128)(2,1)S(1)} %get-tuple-element.14), channel_id=1, source_target_pairs={{0,16},{8,24},{16,0},{24,8},{1,17},{9,25},{17,1},{25,9},{2,18},{10... | collective-permute-start | bytes 147464 | tf_op jit(solution)/shard_map/ppermute | solution.py:112
  14.5 22.1 %collective-permute-start.2 = (bf16[32,768]{1,0:T(8,128)(2,1)S(1)}, bf16[32,768]{1,0:T(8,128)(2,1)S(1)}, u32[]{:S(2)}, u32[]{:S(2)}) collective-permute-start(bf16[32,768]{1,0:T(8,128)(2,1)S(1)} %get-tuple-element.12), channel_id=1, source_target_pairs={{0,24},{8,0},{16,8},{24,16},{1,25},{9,1},{17,9},{25,17},{2,26},{10... | collective-permute-start | bytes 147464 | tf_op jit(solution)/shard_map/ppermute | solution.py:112
  19.2 19.0 %copy-start.7 = (pred[1024]{0:T(1024)(128)(4,1)}, pred[1024]{0:T(1024)(128)(4,1)S(1)}, u32[]{:S(2)}) copy-start(pred[1024]{0:T(1024)(128)(4,1)S(1)} %iota_compare_fusion) | copy-start | bytes 3076
  20.8 17.5 %copy-start.3 = (pred[1024]{0:T(1024)(128)(4,1)}, pred[1024]{0:T(1024)(128)(4,1)S(1)}, u32[]{:S(2)}) copy-start(pred[1024]{0:T(1024)(128)(4,1)S(1)} %broadcast_compare_fusion) | copy-start | bytes 3076
  36.6 7.8 %collective-permute-start.3 = (bf16[128,768]{1,0:T(8,128)(2,1)S(1)}, bf16[128,768]{1,0:T(8,128)(2,1)S(1)}, u32[]{:S(2)}, u32[]{:S(2)}) collective-permute-start(bf16[128,768]{1,0:T(8,128)(2,1)S(1)} %constant_dynamic-update-slice_fusion.15), channel_id=1, source_target_pairs={{0,2},{2,4},{4,6},{6,7},{7,5},{5,3},{3,1},{1,0},{8,10},{10,12},{12... | collective-permute-start | bytes 589832 | tf_op jit(solution)/shard_map/ppermute | solution.py:60
  38.3 7.8 %collective-permute-start.7 = (bf16[128,768]{1,0:T(8,128)(2,1)S(1)}, bf16[128,768]{1,0:T(8,128)(2,1)S(1)}, u32[]{:S(2)}, u32[]{:S(2)}) collective-permute-start(bf16[128,768]{1,0:T(8,128)(2,1)S(1)} %constant_dynamic-update-slice_fusion.15), channel_id=1, source_target_pairs={{0,1},{2,0},{4,2},{6,4},{7,6},{5,7},{3,5},{1,3},{8,9},{10,8},{12,1... | collective-permute-start | bytes 589832 | tf_op jit(solution)/shard_map/ppermute | solution.py:60
  38.9 9.8 %collective-permute-start.11 = (bf16[128,768]{1,0:T(8,128)(2,1)}, bf16[128,768]{1,0:T(8,128)(2,1)S(1)}, u32[]{:S(2)}, u32[]{:S(2)}) collective-permute-start(bf16[128,768]{1,0:T(8,128)(2,1)} %collective-permute-done.10), channel_id=1, source_target_pairs={{0,2},{2,4},{4,6},{6,7},{7,5},{5,3},{3,1},{1,0},{8,10},{10,12},{12... | collective-permute-start | bytes 589832 | tf_op jit(solution)/shard_map/ppermute | solution.py:60
  40.5 9.8 %collective-permute-start.15 = (bf16[128,768]{1,0:T(8,128)(2,1)}, bf16[128,768]{1,0:T(8,128)(2,1)S(1)}, u32[]{:S(2)}, u32[]{:S(2)}) collective-permute-start(bf16[128,768]{1,0:T(8,128)(2,1)} %collective-permute-done.14), channel_id=1, source_target_pairs={{0,1},{2,0},{4,2},{6,4},{7,6},{5,7},{3,5},{1,3},{8,9},{10,8},{12,1... | collective-permute-start | bytes 589832 | tf_op jit(solution)/shard_map/ppermute | solution.py:60
  44.5 8.4 %collective-permute-start.4 = (bf16[128,768]{1,0:T(8,128)(2,1)S(1)}, bf16[128,768]{1,0:T(8,128)(2,1)S(1)}, u32[]{:S(2)}, u32[]{:S(2)}) collective-permute-start(bf16[128,768]{1,0:T(8,128)(2,1)S(1)} %collective-permute-done.3), channel_id=1, source_target_pairs={{0,2},{2,4},{4,6},{6,7},{7,5},{5,3},{3,1},{1,0},{8,10},{10,12},{12... | collective-permute-start | bytes 589832 | tf_op jit(solution)/shard_map/ppermute | solution.py:60
  46.0 8.4 %collective-permute-start.8 = (bf16[128,768]{1,0:T(8,128)(2,1)S(1)}, bf16[128,768]{1,0:T(8,128)(2,1)S(1)}, u32[]{:S(2)}, u32[]{:S(2)}) collective-permute-start(bf16[128,768]{1,0:T(8,128)(2,1)S(1)} %collective-permute-done.7), channel_id=1, source_target_pairs={{0,1},{2,0},{4,2},{6,4},{7,6},{5,7},{3,5},{1,3},{8,9},{10,8},{12,1... | collective-permute-start | bytes 589832 | tf_op jit(solution)/shard_map/ppermute | solution.py:60
  48.7 8.4 %collective-permute-start.12 = (bf16[128,768]{1,0:T(8,128)(2,1)S(1)}, bf16[128,768]{1,0:T(8,128)(2,1)S(1)}, u32[]{:S(2)}, u32[]{:S(2)}) collective-permute-start(bf16[128,768]{1,0:T(8,128)(2,1)S(1)} %collective-permute-done.11), channel_id=1, source_target_pairs={{0,2},{2,4},{4,6},{6,7},{7,5},{5,3},{3,1},{1,0},{8,10},{10,12},{12... | collective-permute-start | bytes 589832 | tf_op jit(solution)/shard_map/ppermute | solution.py:60
  50.3 16.3 %collective-permute-start.16 = (bf16[128,768]{1,0:T(8,128)(2,1)S(1)}, bf16[128,768]{1,0:T(8,128)(2,1)S(1)}, u32[]{:S(2)}, u32[]{:S(2)}) collective-permute-start(bf16[128,768]{1,0:T(8,128)(2,1)S(1)} %collective-permute-done.15), channel_id=1, source_target_pairs={{0,1},{2,0},{4,2},{6,4},{7,6},{5,7},{3,5},{1,3},{8,9},{10,8},{12,1... | collective-permute-start | bytes 589832 | tf_op jit(solution)/shard_map/ppermute | solution.py:60
  52.9 8.4 %collective-permute-start.5 = (bf16[128,768]{1,0:T(8,128)(2,1)S(1)}, bf16[128,768]{1,0:T(8,128)(2,1)S(1)}, u32[]{:S(2)}, u32[]{:S(2)}) collective-permute-start(bf16[128,768]{1,0:T(8,128)(2,1)S(1)} %collective-permute-done.4), channel_id=1, source_target_pairs={{0,2},{2,4},{4,6},{6,7},{7,5},{5,3},{3,1},{1,0},{8,10},{10,12},{12... | collective-permute-start | bytes 589832 | tf_op jit(solution)/shard_map/ppermute | solution.py:60
  54.5 13.5 %collective-permute-start.9 = (bf16[128,768]{1,0:T(8,128)(2,1)S(1)}, bf16[128,768]{1,0:T(8,128)(2,1)S(1)}, u32[]{:S(2)}, u32[]{:S(2)}) collective-permute-start(bf16[128,768]{1,0:T(8,128)(2,1)S(1)} %collective-permute-done.8), channel_id=1, source_target_pairs={{0,1},{2,0},{4,2},{6,4},{7,6},{5,7},{3,5},{1,3},{8,9},{10,8},{12,1... | collective-permute-start | bytes 589832 | tf_op jit(solution)/shard_map/ppermute | solution.py:60
  57.1 8.4 %collective-permute-start.13 = (bf16[128,768]{1,0:T(8,128)(2,1)S(1)}, bf16[128,768]{1,0:T(8,128)(2,1)S(1)}, u32[]{:S(2)}, u32[]{:S(2)}) collective-permute-start(bf16[128,768]{1,0:T(8,128)(2,1)S(1)} %collective-permute-done.12), channel_id=1, source_target_pairs={{0,2},{2,4},{4,6},{6,7},{7,5},{5,3},{3,1},{1,0},{8,10},{10,12},{12... | collective-permute-start | bytes 589832 | tf_op jit(solution)/shard_map/ppermute | solution.py:60
  61.3 6.6 %collective-permute-start.6 = (bf16[128,768]{1,0:T(8,128)(2,1)S(1)}, bf16[128,768]{1,0:T(8,128)(2,1)S(1)}, u32[]{:S(2)}, u32[]{:S(2)}) collective-permute-start(bf16[128,768]{1,0:T(8,128)(2,1)S(1)} %collective-permute-done.5), channel_id=1, source_target_pairs={{0,2},{2,4},{4,6},{6,7},{7,5},{5,3},{3,1},{1,0},{8,10},{10,12},{12... | collective-permute-start | bytes 589832 | tf_op jit(solution)/shard_map/ppermute | solution.py:60
  62.9 5.1 %copy-start.4 = (pred[1024]{0:T(1024)(128)(4,1)S(1)}, pred[1024]{0:T(1024)(128)(4,1)}, u32[]{:S(2)}) copy-start(pred[1024]{0:T(1024)(128)(4,1)} %copy-done.3) | copy-start | bytes 3076
  62.9 5.1 %copy-start.8 = (pred[1024]{0:T(1024)(128)(4,1)S(1)}, pred[1024]{0:T(1024)(128)(4,1)}, u32[]{:S(2)}) copy-start(pred[1024]{0:T(1024)(128)(4,1)} %copy-done.7) | copy-start | bytes 3076
  74.8 1.9 %copy-start.6 = (f32[1024]{0:T(1024)}, f32[1024]{0:T(1024)S(1)}, u32[]{:S(2)}) copy-start(f32[1024]{0:T(1024)S(1)} %get-tuple-element.9) | copy-start | bytes 12292
  76.8 6.6 %copy-start.5 = (pred[1024]{0:T(1024)(128)(4,1)S(1)}, pred[1024]{0:T(1024)(128)(4,1)}, u32[]{:S(2)}) copy-start(pred[1024]{0:T(1024)(128)(4,1)} %copy-done.3) | copy-start | bytes 3076
  80.0 8.6 %all-to-all-start = ((bf16[4,32,768]{2,1,0:T(8,128)(2,1)}), bf16[4,32,768]{2,1,0:T(8,128)(2,1)S(1)}, u32[]{:S(2)}, u32[]{:S(2)}) async-start(bf16[4,32,768]{2,1,0:T(8,128)(2,1)} %bitcast.49), calls=%async_computation | async-start | bytes 393216 | tf_op jit(solution)/shard_map/all_to_all | solution.py:179

commit v5 on v4

--- a/solution.py
+++ b/solution.py
@@ -41,14 +41,27 @@
     return order
 
 
+def pick(table, index):
+    found = jnp.int32(table[0])
+    for k in range(1, len(table)):
+        found = jnp.where(index == k, jnp.int32(table[k]), found)
+    return found
+
+
+def slot_rows(tgt_emb, slot_group, group):
+    rows = tgt_emb[0]
+    for s in range(1, tgt_emb.shape[0]):
+        rows = jnp.where(slot_group[s] == group, tgt_emb[s], rows)
+    return rows
+
+
 def ring_gather(block, ring):
     count = len(ring)
     place = [0] * count
     for p, d in enumerate(ring):
         place[d] = p
-    ring_arr = jnp.array(ring, jnp.int32)
     my_dp = lax.axis_index("dp")
-    my_pos = jnp.array(place, jnp.int32)[my_dp]
+    my_pos = pick(place, my_dp)
     ahead = [(ring[p], ring[(p + 1) % count]) for p in range(count)]
     behind = [(ring[p], ring[(p - 1) % count]) for p in range(count)]
     rows = block.shape[0]
@@ -58,7 +71,7 @@
         cur = block
         for t in range(1, steps + 1):
             cur = lax.ppermute(cur, "dp", pairs)
-            origin = ring_arr[(my_pos + sign * t) % count]
+            origin = pick(ring, (my_pos + sign * t) % count)
             out = lax.dynamic_update_slice_in_dim(out, cur, origin * rows, 0)
     return out
 
@@ -101,14 +114,12 @@
     inv_root = 1.0 / math.sqrt(emb_width)
     group_index = lax.axis_index("lang")
     shard_index = lax.axis_index("dp")
-    slot_ids = jnp.arange(lang_size, dtype=jnp.int32)
-    slot_of_group = jnp.zeros((lang_size,), jnp.int32).at[slot_group].set(slot_ids)
     partner = jnp.zeros((lang_size * per_slot, emb_width), tgt_emb.dtype)
-    own = lax.dynamic_index_in_dim(tgt_emb, slot_of_group[group_index], 0, keepdims=False)
+    own = slot_rows(tgt_emb, slot_group, group_index)
     partner = lax.dynamic_update_slice_in_dim(partner, own, group_index * per_slot, 0)
     for k in range(1, lang_size):
         dest = (group_index + k) % lang_size
-        sent = lax.dynamic_index_in_dim(tgt_emb, slot_of_group[dest], 0, keepdims=False)
+        sent = slot_rows(tgt_emb, slot_group, dest)
         got = lax.ppermute(sent, "lang", [(l, (l + k) % lang_size) for l in range(lang_size)])
         origin = (group_index - k) % lang_size
         partner = lax.dynamic_update_slice_in_dim(partner, got, origin * per_slot, 0)
@@ -179,7 +190,9 @@
     returned = lax.all_to_all(
         grad_local.reshape(lang_size, per_slot, emb_width), "lang", split_axis=0, concat_axis=0, tiled=True
     )
-    grad_tgt = returned[slot_group]
+    grad_tgt = jnp.stack(
+        [slot_rows(returned, jnp.arange(lang_size, dtype=jnp.int32), slot_group[s]) for s in range(lang_size)]
+    )
     return (grad_src, grad_tgt, pair_loss)
 
 

time: 91.8 us -> 94.9 us (1.034)
  between operations: 21.1 us -> 26.7 us
  local copies, waits for them, and re-layouts: 14.1 us -> 10.5 us
  other arithmetic: 7.27 us -> 8.24 us
    slice x0 -> x2, local copies, waits for them, and re-layouts: none -> 2.02 us  [the longest x1 1.4 us: per_device(): slot_group[s]]
    dynamic_slice x3 -> x0, local copies, waits for them, and re-layouts: 1.93 us -> none  [the longest x1 0.68 us: ring_gather(): origin = ring_arr[(my_pos + sign * t) % count]]
    gather x1 -> x0, local copies, waits for them, and re-layouts: 1.23 us -> none  [per_device(): grad_tgt = returned[slot_group]]
    select_n x1 -> x4, other arithmetic: 0.67 us -> 1.81 us  [slot_rows(): rows = jnp.where(slot_group[s] == group, tgt_emb[s], rows)]
  transfers between devices with their start and end apart: 18 -> 18, of which waited for: 8 -> 8; matrix products, arithmetic and copies ran while one was open for 19% -> 17% of each run, Pallas kernels for 0% -> 0%
where the time goes in v5:
time: 94.9 us; the launch traced here: 94 us
  between operations  26.7 us (28%)
  starting transfers between devices  23.4 us (25%)
  waiting for transfers between devices  16.4 us (17%)
  local copies, waits for them, and re-layouts  10.5 us (11%)
  matrix products  8.78 us (9%)
  other arithmetic  8.24 us (9%)
    ppermute x14, starting transfers between devices, ring_gather(): cur = lax.ppermute(cur, 'dp', pairs)  16.5 us
    ppermute x14, waiting for transfers between devices, ring_gather(): cur = lax.ppermute(cur, 'dp', pairs)  15.6 us
    ppermute x3, starting transfers between devices, per_device(): lax.ppermute(sent, 'lang', [(l, (l + k) % lang_size) for l in range(lang_...  3.5 us
    all_to_all x1, starting transfers between devices, per_device(): lax.all_to_all(grad_local.reshape(lang_size, per_slot, emb_width), 'lang'...  3.37 us
    dot_general x1, matrix products, per_device(): lax.dot_general(g_cols, x_all, (((0,), (0,)), ((), ())), preferred_elemen...  3.21 us
    dot_general x1, matrix products, per_device(): jnp.dot(g_rows, y_all, preferred_element_type=jnp.float32) * inv_root  3.17 us
    reduce_sum x1, other arithmetic, block_stats(): pos_score = jnp.sum(jnp.where(is_pos, scores_f, 0.0), axis=1)  2.41 us
    dot_general x1, matrix products, scores_of(): lax.dot_general(x_rows, y_rows, (((1,), (1,)), ((), ())), preferred_eleme...  2.4 us
  transfers between devices with their start and end apart: 18, of which 8 were waited for; matrix products, arithmetic and copies ran while one was open for 17% of the time, Pallas kernels for 0%

profile of v5, /device:TPU:0, one launch (start us, length us, event | category | flops | bytes accessed | tf_op | source)
XLA Modules:
  0.0 94.0 jit_solution(14959228091487527333)
XLA Ops:
  0.7 3.1 %collective-permute-start.10 = (bf16[128,768]{1,0:T(8,128)(2,1)}, bf16[128,768]{1,0:T(8,128)(2,1)}, u32[]{:S(2)}, u32[]{:S(2)}) collective-permute-start(bf16[128,768]{1,0:T(8,128)(2,1)} %param.6), channel_id=1, source_target_pairs={{0,2},{2,4},{4,6},{6,7},{7,5},{5,3},{3,1},{1,0},{8,10},{10,12},{12... | collective-permute-start | bytes 589832 | tf_op jit(solution)/shard_map/ppermute | solution.py:73
  3.8 1.4 %fusion.64 = (s32[1]{0:T(128)}, s32[1]{0:T(128)}, s32[1]{0:T(128)}, s32[1]{0:T(128)}) fusion(s32[4]{0:T(128)} %param.8), kind=kLoop, calls=%fused_computation.128 | loop fusion | bytes 32 | tf_op jit(solution)/shard_map/slice | solution.py:194
  7.1 0.9 select_bitcast_fusion.2
  11.9 0.9 select_bitcast_fusion
  12.8 2.0 %collective-permute-start.1 = (bf16[32,768]{1,0:T(8,128)(2,1)S(1)}, bf16[32,768]{1,0:T(8,128)(2,1)S(1)}, u32[]{:S(2)}, u32[]{:S(2)}) collective-permute-start(bf16[32,768]{1,0:T(8,128)(2,1)S(1)} %get-tuple-element.17), channel_id=1, source_target_pairs={{0,16},{8,24},{16,0},{24,8},{1,17},{9,25},{17,1},{25,9},{2,18},{10... | collective-permute-start | bytes 147464 | tf_op jit(solution)/shard_map/ppermute | solution.py:123
  14.8 1.4 %collective-permute-start.2 = (bf16[32,768]{1,0:T(8,128)(2,1)S(1)}, bf16[32,768]{1,0:T(8,128)(2,1)S(1)}, u32[]{:S(2)}, u32[]{:S(2)}) collective-permute-start(bf16[32,768]{1,0:T(8,128)(2,1)S(1)} %get-tuple-element.16), channel_id=1, source_target_pairs={{0,24},{8,0},{16,8},{24,16},{1,25},{9,1},{17,9},{25,17},{2,26},{10... | collective-permute-start | bytes 147464 | tf_op jit(solution)/shard_map/ppermute | solution.py:123
  18.2 1.2 %dynamic_slice.25 = s32[1]{0:T(128)} dynamic-slice(s32[4]{0:T(128)} %param.9, s32[]{:T(128)S(6)} %select_n.607), dynamic_slice_sizes={1} | dynamic-slice | bytes 12 | tf_op jit(solution)/shard_map/dynamic_slice | solution.py:126
  19.4 0.6 iota_compare_fusion
  20.0 1.5 %convert_reduce_fusion = s32[1024]{0:T(1024)S(1)} fusion(s32[1024]{0:T(1024)} %bitcast.39, s32[1024]{0:T(1024)S(1)} %fusion.46, pred[1024]{0:T(1024)(128)(4,1)S(1)} %iota_compare_fusion), kind=kLoop, calls=%fused_computation.9 | loop fusion | flops 4193280 | bytes 13312 | tf_op jit(solution)/shard_map/reduce_max | solution.py:133
  21.6 0.6 fusion.65
  22.2 0.1 broadcast.224.clone.1
  22.4 0.6 fusion.55
  23.6 0.6 dynamic_slice.30
  39.3 0.6 dynamic_slice.26
  39.9 0.6 dynamic_slice.29
  40.5 0.6 dynamic_slice.24
  41.1 1.6 %collective-permute-start.3 = (bf16[128,768]{1,0:T(8,128)(2,1)S(1)}, bf16[128,768]{1,0:T(8,128)(2,1)S(1)}, u32[]{:S(2)}, u32[]{:S(2)}) collective-permute-start(bf16[128,768]{1,0:T(8,128)(2,1)S(1)} %constant_dynamic-update-slice_fusion.16), channel_id=1, source_target_pairs={{0,2},{2,4},{4,6},{6,7},{7,5},{5,3},{3,1},{1,0},{8,10},{10,12},{12... | collective-permute-start | bytes 589832 | tf_op jit(solution)/shard_map/ppermute | solution.py:73
  42.8 0.4 collective-permute-start.7
  43.4 1.6 %collective-permute-start.11 = (bf16[128,768]{1,0:T(8,128)(2,1)}, bf16[128,768]{1,0:T(8,128)(2,1)S(1)}, u32[]{:S(2)}, u32[]{:S(2)}) collective-permute-start(bf16[128,768]{1,0:T(8,128)(2,1)} %collective-permute-done.10), channel_id=1, source_target_pairs={{0,2},{2,4},{4,6},{6,7},{7,5},{5,3},{3,1},{1,0},{8,10},{10,12},{12... | collective-permute-start | bytes 589832 | tf_op jit(solution)/shard_map/ppermute | solution.py:73
  45.0 0.5 collective-permute-start.15
  45.4 0.9 %constant_dynamic-update-slice_fusion.6 = bf16[1024,768]{1,0:T(8,128)(2,1)S(1)} fusion(bf16[1024,768]{1,0:T(8,128)(2,1)S(1)} %constant_dynamic-update-slice_fusion.7, bf16[128,768]{1,0:T(8,128)(2,1)} %collective-permute-done.10, s32[]{:T(128)S(6)} %select_n.666), kind=kLoop, calls=%fused_computation.85 | loop fusion | bytes 393220 | tf_op jit(solution)/shard_map/dynamic_update_slice | solution.py:75
  46.4 2.6 %collective-permute-done.3 = bf16[128,768]{1,0:T(8,128)(2,1)S(1)} collective-permute-done((bf16[128,768]{1,0:T(8,128)(2,1)S(1)}, bf16[128,768]{1,0:T(8,128)(2,1)S(1)}, u32[]{:S(2)}, u32[]{:S(2)}) %collective-permute-start.3) | collective-permute-done | bytes 196640 | tf_op jit(solution)/shard_map/ppermute | solution.py:73
  49.0 1.6 %collective-permute-start.4 = (bf16[128,768]{1,0:T(8,128)(2,1)S(1)}, bf16[128,768]{1,0:T(8,128)(2,1)S(1)}, u32[]{:S(2)}, u32[]{:S(2)}) collective-permute-start(bf16[128,768]{1,0:T(8,128)(2,1)S(1)} %collective-permute-done.3), channel_id=1, source_target_pairs={{0,2},{2,4},{4,6},{6,7},{7,5},{5,3},{3,1},{1,0},{8,10},{10,12},{12... | collective-permute-start | bytes 589832 | tf_op jit(solution)/shard_map/ppermute | solution.py:73
  50.5 0.5 collective-permute-start.8
  51.0 2.2 %collective-permute-done.11 = bf16[128,768]{1,0:T(8,128)(2,1)S(1)} collective-permute-done((bf16[128,768]{1,0:T(8,128)(2,1)}, bf16[128,768]{1,0:T(8,128)(2,1)S(1)}, u32[]{:S(2)}, u32[]{:S(2)}) %collective-permute-start.11) | collective-permute-done | bytes 196640 | tf_op jit(solution)/shard_map/ppermute | solution.py:73
  53.2 1.6 %collective-permute-start.12 = (bf16[128,768]{1,0:T(8,128)(2,1)S(1)}, bf16[128,768]{1,0:T(8,128)(2,1)S(1)}, u32[]{:S(2)}, u32[]{:S(2)}) collective-permute-start(bf16[128,768]{1,0:T(8,128)(2,1)S(1)} %collective-permute-done.11), channel_id=1, source_target_pairs={{0,2},{2,4},{4,6},{6,7},{7,5},{5,3},{3,1},{1,0},{8,10},{10,12},{12... | collective-permute-start | bytes 589832 | tf_op jit(solution)/shard_map/ppermute | solution.py:73
  54.8 0.5 collective-permute-start.16
  55.2 2.2 %collective-permute-done.4 = bf16[128,768]{1,0:T(8,128)(2,1)S(1)} collective-permute-done((bf16[128,768]{1,0:T(8,128)(2,1)S(1)}, bf16[128,768]{1,0:T(8,128)(2,1)S(1)}, u32[]{:S(2)}, u32[]{:S(2)}) %collective-permute-start.4) | collective-permute-done | bytes 196640 | tf_op jit(solution)/shard_map/ppermute | solution.py:73
  57.4 1.6 %collective-permute-start.5 = (bf16[128,768]{1,0:T(8,128)(2,1)S(1)}, bf16[128,768]{1,0:T(8,128)(2,1)S(1)}, u32[]{:S(2)}, u32[]{:S(2)}) collective-permute-start(bf16[128,768]{1,0:T(8,128)(2,1)S(1)} %collective-permute-done.4), channel_id=1, source_target_pairs={{0,2},{2,4},{4,6},{6,7},{7,5},{5,3},{3,1},{1,0},{8,10},{10,12},{12... | collective-permute-start | bytes 589832 | tf_op jit(solution)/shard_map/ppermute | solution.py:73
  59.0 0.5 collective-permute-start.9
  59.4 2.2 %collective-permute-done.12 = bf16[128,768]{1,0:T(8,128)(2,1)S(1)} collective-permute-done((bf16[128,768]{1,0:T(8,128)(2,1)S(1)}, bf16[128,768]{1,0:T(8,128)(2,1)S(1)}, u32[]{:S(2)}, u32[]{:S(2)}) %collective-permute-start.12) | collective-permute-done | bytes 196640 | tf_op jit(solution)/shard_map/ppermute | solution.py:73
  61.6 1.6 %collective-permute-start.13 = (bf16[128,768]{1,0:T(8,128)(2,1)S(1)}, bf16[128,768]{1,0:T(8,128)(2,1)S(1)}, u32[]{:S(2)}, u32[]{:S(2)}) collective-permute-start(bf16[128,768]{1,0:T(8,128)(2,1)S(1)} %collective-permute-done.12), channel_id=1, source_target_pairs={{0,2},{2,4},{4,6},{6,7},{7,5},{5,3},{3,1},{1,0},{8,10},{10,12},{12... | collective-permute-start | bytes 589832 | tf_op jit(solution)/shard_map/ppermute | solution.py:73
  63.2 2.6 %collective-permute-done.5 = bf16[128,768]{1,0:T(8,128)(2,1)S(1)} collective-permute-done((bf16[128,768]{1,0:T(8,128)(2,1)S(1)}, bf16[128,768]{1,0:T(8,128)(2,1)S(1)}, u32[]{:S(2)}, u32[]{:S(2)}) %collective-permute-start.5) | collective-permute-done | bytes 196640 | tf_op jit(solution)/shard_map/ppermute | solution.py:73
  65.8 1.6 %collective-permute-start.6 = (bf16[128,768]{1,0:T(8,128)(2,1)S(1)}, bf16[128,768]{1,0:T(8,128)(2,1)S(1)}, u32[]{:S(2)}, u32[]{:S(2)}) collective-permute-start(bf16[128,768]{1,0:T(8,128)(2,1)S(1)} %collective-permute-done.5), channel_id=1, source_target_pairs={{0,2},{2,4},{4,6},{6,7},{7,5},{5,3},{3,1},{1,0},{8,10},{10,12},{12... | collective-permute-start | bytes 589832 | tf_op jit(solution)/shard_map/ppermute | solution.py:73
  67.4 2.6 %collective-permute-done.13 = bf16[128,768]{1,0:T(8,128)(2,1)S(1)} collective-permute-done((bf16[128,768]{1,0:T(8,128)(2,1)S(1)}, bf16[128,768]{1,0:T(8,128)(2,1)S(1)}, u32[]{:S(2)}, u32[]{:S(2)}) %collective-permute-start.13) | collective-permute-done | bytes 196640 | tf_op jit(solution)/shard_map/ppermute | solution.py:73
  70.1 0.9 %constant_dynamic-update-slice_fusion.2 = bf16[1024,768]{1,0:T(8,128)(2,1)S(1)} fusion(bf16[1024,768]{1,0:T(8,128)(2,1)S(1)} %constant_dynamic-update-slice_fusion.3, bf16[128,768]{1,0:T(8,128)(2,1)} %collective-permute-done.14, s32[]{:T(128)S(6)} %select_n.702), kind=kLoop, calls=%fused_computation.81 | loop fusion | bytes 393220 | tf_op jit(solution)/shard_map/dynamic_update_slice | solution.py:75
  71.1 1.3 %collective-permute-done.6 = bf16[128,768]{1,0:T(8,128)(2,1)S(1)} collective-permute-done((bf16[128,768]{1,0:T(8,128)(2,1)S(1)}, bf16[128,768]{1,0:T(8,128)(2,1)S(1)}, u32[]{:S(2)}, u32[]{:S(2)}) %collective-permute-start.6) | collective-permute-done | bytes 196640 | tf_op jit(solution)/shard_map/ppermute | solution.py:73
  72.5 2.4 %select_reduce_fusion.3 = (f32[1024]{0:T(1024)S(1)}, f32[1024]{0:T(1024)S(1)}, f32[1024,1024]{0,1:T(8,128)S(1)}) fusion(pred[1024]{0:T(1024)(128)(4,1)S(1)} %broadcast_compare_fusion, pred[1024]{0:T(1024)(128)(4,1)S(1)} %copy-done.7, s32[1024]{0:T(1024)S(1)} %bitcast.40, s32[1024]{0:T(1024)S(1)} %fusion.46, ...), kind=kOutput, calls=%fused_computation.8 | convolution fusion | flops 1618999296 | bytes 7358464 | tf_op jit(solution)/shard_map/dot_general | solution.py:80
  74.9 2.4 %fusion.1 = (f32[1024]{0:T(1024)S(1)}, f32[1024]{0:T(1024)S(1)}, f32[1024]{0:T(1024)S(1)}) fusion(f32[1024,1024]{0,1:T(8,128)S(1)} %get-tuple-element.25, s32[1024]{0:T(1024)S(1)} %bitcast.41, s32[1024]{0:T(1024)S(1)} %fusion.46, f32[1024]{0:T(1024)S(1)} %get-tuple-element.7, pred[1024]{0:T(1024)(128)(4,1)S(1)} %copy-done.7, f32[1024]{0:T(1024)S(1)} %get-tuple-element.6, ...), kind=kLoop, calls=%fused_computation.4 | loop fusion | flops 9434112 | bytes 4225024 | tf_op jit(solution)/shard_map/reduce_sum | solution.py:92
  77.3 1.2 %select_reduce_fusion.4 = (f32[]{:T(128)}, f32[1024]{0:T(1024)S(1)}, f32[]{:T(128)}, f32[1024]{0:T(1024)S(1)}) fusion(f32[1024]{0:T(1024)S(1)} %get-tuple-element.7, f32[1024]{0:T(1024)S(1)} %get-tuple-element.4, f32[1024]{0:T(1024)S(1)} %get-tuple-element.3, f32[1024]{0:T(1024)S(1)} %get-tuple-element.6, f32[1024]{0:T(1024)S(1)} %get-tuple-element.5, ...), kind=kLoop, calls=%fused_computation.109 | loop fusion | flops 16382 | bytes 32780 | tf_op jit(solution)/shard_map/reduce_sum | solution.py:166
  78.5 0.6 copy-done.3
  79.1 0.6 dynamic_slice.31
  79.7 0.6 dynamic_slice.28
  80.3 3.2 %fusion.6 = bf16[128,768]{1,0:T(8,128)(2,1)} fusion(bf16[1024,768]{1,0:T(8,128)(2,1)S(1)} %constant_dynamic-update-slice_fusion, bf16[128,768]{1,0:T(8,128)(2,1)S(1)} %constant_dynamic-update-slice_fusion.16, f32[128]{0:T(128)} %dynamic_slice.31, f32[1024]{0:T(1024)} %copy-done.5, s32[128]{0:T(128)} %dynamic_slice.30, f32[]{:T(128)} %bitcast, ...), kind=kOutput, calls=%fused_computation.18 | convolution fusion | flops 404815872 | bytes 1976452 | tf_op jit(solution)/shard_map/dot_general | solution.py:186
  83.5 3.4 %all-to-all-start = ((bf16[4,32,768]{2,1,0:T(8,128)(2,1)}), bf16[4,32,768]{2,1,0:T(8,128)(2,1)S(1)}, u32[]{:S(2)}, u32[]{:S(2)}) async-start(bf16[4,32,768]{2,1,0:T(8,128)(2,1)} %bitcast.38), calls=%async_computation | async-start | bytes 393216 | tf_op jit(solution)/shard_map/all_to_all | solution.py:190
  86.9 3.2 %fusion.5 = bf16[128,768]{1,0:T(8,128)(2,1)} fusion(bf16[1024,768]{1,0:T(8,128)(2,1)S(1)} %constant_dynamic-update-slice_fusion.8, bf16[128,768]{1,0:T(8,128)(2,1)S(1)} %copy-done.1, f32[1024]{0:T(1024)S(1)} %copy-done.4, f32[128]{0:T(128)} %dynamic_slice.28, s32[128]{0:T(128)} %fusion.55, f32[]{:T(128)} %bitcast, s32[1024]{0:T(1024)S(1)} %fusion.46, ...), kind=kOutput, calls=%fused_computation.17 | convolution fusion | flops 404815872 | bytes 1976452 | tf_op jit(solution)/shard_map/dot_general | solution.py:177
  91.3 0.8 all-to-all-done
  92.2 0.7 pad_maximum_fusion
  (54 shorter events, 0.6 us)
Async XLA Ops:
  0.6 21.7 %copy-start.1 = (bf16[128,768]{1,0:T(8,128)(2,1)S(1)}, bf16[128,768]{1,0:T(8,128)(2,1)}, u32[]{:S(2)}) copy-start(bf16[128,768]{1,0:T(8,128)(2,1)} %param.6) | copy-start | bytes 589828
  0.6 21.7 %copy-start = (bf16[4,32,768]{2,1,0:T(8,128)(2,1)S(1)}, bf16[4,32,768]{2,1,0:T(8,128)(2,1)}, u32[]{:S(2)}) copy-start(bf16[4,32,768]{2,1,0:T(8,128)(2,1)} %param.7) | copy-start | bytes 589828
  0.7 21.8 %copy-start.2 = (s32[1,1024]{1,0:T(1,128)S(1)}, s32[1,1024]{1,0:T(1,128)}, u32[]{:S(2)}) copy-start(s32[1,1024]{1,0:T(1,128)} %param.10) | copy-start | bytes 12292
  0.7 42.7 %collective-permute-start.10 = (bf16[128,768]{1,0:T(8,128)(2,1)}, bf16[128,768]{1,0:T(8,128)(2,1)}, u32[]{:S(2)}, u32[]{:S(2)}) collective-permute-start(bf16[128,768]{1,0:T(8,128)(2,1)} %param.6), channel_id=1, source_target_pairs={{0,2},{2,4},{4,6},{6,7},{7,5},{5,3},{3,1},{1,0},{8,10},{10,12},{12... | collective-permute-start | bytes 589832 | tf_op jit(solution)/shard_map/ppermute | solution.py:73
  3.8 41.2 %collective-permute-start.14 = (bf16[128,768]{1,0:T(8,128)(2,1)}, bf16[128,768]{1,0:T(8,128)(2,1)}, u32[]{:S(2)}, u32[]{:S(2)}) collective-permute-start(bf16[128,768]{1,0:T(8,128)(2,1)} %param.6), channel_id=1, source_target_pairs={{0,1},{2,0},{4,2},{6,4},{7,6},{5,7},{3,5},{1,3},{8,9},{10,8},{12,1... | collective-permute-start | bytes 589832 | tf_op jit(solution)/shard_map/ppermute | solution.py:73
  8.0 33.1 %collective-permute-start = (bf16[32,768]{1,0:T(8,128)(2,1)S(1)}, bf16[32,768]{1,0:T(8,128)(2,1)S(1)}, u32[]{:S(2)}, u32[]{:S(2)}) collective-permute-start(bf16[32,768]{1,0:T(8,128)(2,1)S(1)} %select_bitcast_fusion.2), channel_id=1, source_target_pairs={{0,8},{8,16},{16,24},{24,0},{1,9},{9,17},{17,25},{25,1},{2,10},{10... | collective-permute-start | bytes 147464 | tf_op jit(solution)/shard_map/ppermute | solution.py:123
  12.8 27.7 %copy-start.8 = (f32[4]{0:T(128)S(1)}, f32[4]{0:T(128)}, u32[]{:S(2)}) copy-start(f32[4]{0:T(128)} %param.11) | copy-start | bytes 52
  12.8 28.3 %collective-permute-start.1 = (bf16[32,768]{1,0:T(8,128)(2,1)S(1)}, bf16[32,768]{1,0:T(8,128)(2,1)S(1)}, u32[]{:S(2)}, u32[]{:S(2)}) collective-permute-start(bf16[32,768]{1,0:T(8,128)(2,1)S(1)} %get-tuple-element.17), channel_id=1, source_target_pairs={{0,16},{8,24},{16,0},{24,8},{1,17},{9,25},{17,1},{25,9},{2,18},{10... | collective-permute-start | bytes 147464 | tf_op jit(solution)/shard_map/ppermute | solution.py:123
  14.8 26.3 %collective-permute-start.2 = (bf16[32,768]{1,0:T(8,128)(2,1)S(1)}, bf16[32,768]{1,0:T(8,128)(2,1)S(1)}, u32[]{:S(2)}, u32[]{:S(2)}) collective-permute-start(bf16[32,768]{1,0:T(8,128)(2,1)S(1)} %get-tuple-element.16), channel_id=1, source_target_pairs={{0,24},{8,0},{16,8},{24,16},{1,25},{9,1},{17,9},{25,17},{2,26},{10... | collective-permute-start | bytes 147464 | tf_op jit(solution)/shard_map/ppermute | solution.py:123
  20.0 22.8 %copy-start.6 = (pred[1024]{0:T(1024)(128)(4,1)}, pred[1024]{0:T(1024)(128)(4,1)S(1)}, u32[]{:S(2)}) copy-start(pred[1024]{0:T(1024)(128)(4,1)S(1)} %iota_compare_fusion) | copy-start | bytes 3076
  41.1 7.8 %collective-permute-start.3 = (bf16[128,768]{1,0:T(8,128)(2,1)S(1)}, bf16[128,768]{1,0:T(8,128)(2,1)S(1)}, u32[]{:S(2)}, u32[]{:S(2)}) collective-permute-start(bf16[128,768]{1,0:T(8,128)(2,1)S(1)} %constant_dynamic-update-slice_fusion.16), channel_id=1, source_target_pairs={{0,2},{2,4},{4,6},{6,7},{7,5},{5,3},{3,1},{1,0},{8,10},{10,12},{12... | collective-permute-start | bytes 589832 | tf_op jit(solution)/shard_map/ppermute | solution.py:73
  42.8 7.8 %collective-permute-start.7 = (bf16[128,768]{1,0:T(8,128)(2,1)S(1)}, bf16[128,768]{1,0:T(8,128)(2,1)S(1)}, u32[]{:S(2)}, u32[]{:S(2)}) collective-permute-start(bf16[128,768]{1,0:T(8,128)(2,1)S(1)} %constant_dynamic-update-slice_fusion.16), channel_id=1, source_target_pairs={{0,1},{2,0},{4,2},{6,4},{7,6},{5,7},{3,5},{1,3},{8,9},{10,8},{12,1... | collective-permute-start | bytes 589832 | tf_op jit(solution)/shard_map/ppermute | solution.py:73
  43.4 9.8 %collective-permute-start.11 = (bf16[128,768]{1,0:T(8,128)(2,1)}, bf16[128,768]{1,0:T(8,128)(2,1)S(1)}, u32[]{:S(2)}, u32[]{:S(2)}) collective-permute-start(bf16[128,768]{1,0:T(8,128)(2,1)} %collective-permute-done.10), channel_id=1, source_target_pairs={{0,2},{2,4},{4,6},{6,7},{7,5},{5,3},{3,1},{1,0},{8,10},{10,12},{12... | collective-permute-start | bytes 589832 | tf_op jit(solution)/shard_map/ppermute | solution.py:73
  45.0 9.8 %collective-permute-start.15 = (bf16[128,768]{1,0:T(8,128)(2,1)}, bf16[128,768]{1,0:T(8,128)(2,1)S(1)}, u32[]{:S(2)}, u32[]{:S(2)}) collective-permute-start(bf16[128,768]{1,0:T(8,128)(2,1)} %collective-permute-done.14), channel_id=1, source_target_pairs={{0,1},{2,0},{4,2},{6,4},{7,6},{5,7},{3,5},{1,3},{8,9},{10,8},{12,1... | collective-permute-start | bytes 589832 | tf_op jit(solution)/shard_map/ppermute | solution.py:73
  49.0 8.4 %collective-permute-start.4 = (bf16[128,768]{1,0:T(8,128)(2,1)S(1)}, bf16[128,768]{1,0:T(8,128)(2,1)S(1)}, u32[]{:S(2)}, u32[]{:S(2)}) collective-permute-start(bf16[128,768]{1,0:T(8,128)(2,1)S(1)} %collective-permute-done.3), channel_id=1, source_target_pairs={{0,2},{2,4},{4,6},{6,7},{7,5},{5,3},{3,1},{1,0},{8,10},{10,12},{12... | collective-permute-start | bytes 589832 | tf_op jit(solution)/shard_map/ppermute | solution.py:73
  50.5 8.4 %collective-permute-start.8 = (bf16[128,768]{1,0:T(8,128)(2,1)S(1)}, bf16[128,768]{1,0:T(8,128)(2,1)S(1)}, u32[]{:S(2)}, u32[]{:S(2)}) collective-permute-start(bf16[128,768]{1,0:T(8,128)(2,1)S(1)} %collective-permute-done.7), channel_id=1, source_target_pairs={{0,1},{2,0},{4,2},{6,4},{7,6},{5,7},{3,5},{1,3},{8,9},{10,8},{12,1... | collective-permute-start | bytes 589832 | tf_op jit(solution)/shard_map/ppermute | solution.py:73
  53.2 8.4 %collective-permute-start.12 = (bf16[128,768]{1,0:T(8,128)(2,1)S(1)}, bf16[128,768]{1,0:T(8,128)(2,1)S(1)}, u32[]{:S(2)}, u32[]{:S(2)}) collective-permute-start(bf16[128,768]{1,0:T(8,128)(2,1)S(1)} %collective-permute-done.11), channel_id=1, source_target_pairs={{0,2},{2,4},{4,6},{6,7},{7,5},{5,3},{3,1},{1,0},{8,10},{10,12},{12... | collective-permute-start | bytes 589832 | tf_op jit(solution)/shard_map/ppermute | solution.py:73
  54.8 16.3 %collective-permute-start.16 = (bf16[128,768]{1,0:T(8,128)(2,1)S(1)}, bf16[128,768]{1,0:T(8,128)(2,1)S(1)}, u32[]{:S(2)}, u32[]{:S(2)}) collective-permute-start(bf16[128,768]{1,0:T(8,128)(2,1)S(1)} %collective-permute-done.15), channel_id=1, source_target_pairs={{0,1},{2,0},{4,2},{6,4},{7,6},{5,7},{3,5},{1,3},{8,9},{10,8},{12,1... | collective-permute-start | bytes 589832 | tf_op jit(solution)/shard_map/ppermute | solution.py:73
  57.4 8.4 %collective-permute-start.5 = (bf16[128,768]{1,0:T(8,128)(2,1)S(1)}, bf16[128,768]{1,0:T(8,128)(2,1)S(1)}, u32[]{:S(2)}, u32[]{:S(2)}) collective-permute-start(bf16[128,768]{1,0:T(8,128)(2,1)S(1)} %collective-permute-done.4), channel_id=1, source_target_pairs={{0,2},{2,4},{4,6},{6,7},{7,5},{5,3},{3,1},{1,0},{8,10},{10,12},{12... | collective-permute-start | bytes 589832 | tf_op jit(solution)/shard_map/ppermute | solution.py:73
  59.0 13.5 %collective-permute-start.9 = (bf16[128,768]{1,0:T(8,128)(2,1)S(1)}, bf16[128,768]{1,0:T(8,128)(2,1)S(1)}, u32[]{:S(2)}, u32[]{:S(2)}) collective-permute-start(bf16[128,768]{1,0:T(8,128)(2,1)S(1)} %collective-permute-done.8), channel_id=1, source_target_pairs={{0,1},{2,0},{4,2},{6,4},{7,6},{5,7},{3,5},{1,3},{8,9},{10,8},{12,1... | collective-permute-start | bytes 589832 | tf_op jit(solution)/shard_map/ppermute | solution.py:73
  61.6 8.4 %collective-permute-start.13 = (bf16[128,768]{1,0:T(8,128)(2,1)S(1)}, bf16[128,768]{1,0:T(8,128)(2,1)S(1)}, u32[]{:S(2)}, u32[]{:S(2)}) collective-permute-start(bf16[128,768]{1,0:T(8,128)(2,1)S(1)} %collective-permute-done.12), channel_id=1, source_target_pairs={{0,2},{2,4},{4,6},{6,7},{7,5},{5,3},{3,1},{1,0},{8,10},{10,12},{12... | collective-permute-start | bytes 589832 | tf_op jit(solution)/shard_map/ppermute | solution.py:73
  65.8 6.5 %collective-permute-start.6 = (bf16[128,768]{1,0:T(8,128)(2,1)S(1)}, bf16[128,768]{1,0:T(8,128)(2,1)S(1)}, u32[]{:S(2)}, u32[]{:S(2)}) collective-permute-start(bf16[128,768]{1,0:T(8,128)(2,1)S(1)} %collective-permute-done.5), channel_id=1, source_target_pairs={{0,2},{2,4},{4,6},{6,7},{7,5},{5,3},{3,1},{1,0},{8,10},{10,12},{12... | collective-permute-start | bytes 589832 | tf_op jit(solution)/shard_map/ppermute | solution.py:73
  67.4 5.0 %copy-start.7 = (pred[1024]{0:T(1024)(128)(4,1)S(1)}, pred[1024]{0:T(1024)(128)(4,1)}, u32[]{:S(2)}) copy-start(pred[1024]{0:T(1024)(128)(4,1)} %copy-done.6) | copy-start | bytes 3076
  78.5 0.6 copy-start.3
  78.5 1.8 %copy-start.5 = (f32[1024]{0:T(1024)}, f32[1024]{0:T(1024)S(1)}, u32[]{:S(2)}) copy-start(f32[1024]{0:T(1024)S(1)} %get-tuple-element.27) | copy-start | bytes 12292
  80.3 6.6 %copy-start.4 = (f32[1024]{0:T(1024)S(1)}, f32[1024]{0:T(1024)}, u32[]{:S(2)}) copy-start(f32[1024]{0:T(1024)} %copy-done.3) | copy-start | bytes 12292
  83.5 8.6 %all-to-all-start = ((bf16[4,32,768]{2,1,0:T(8,128)(2,1)}), bf16[4,32,768]{2,1,0:T(8,128)(2,1)S(1)}, u32[]{:S(2)}, u32[]{:S(2)}) async-start(bf16[4,32,768]{2,1,0:T(8,128)(2,1)} %bitcast.38), calls=%async_computation | async-start | bytes 393216 | tf_op jit(solution)/shard_map/all_to_all | solution.py:190

commit v6 on v5

--- a/solution.py
+++ b/solution.py
@@ -131,7 +131,8 @@
     perm = target_index(pair_rows, row_count, per_slot, data_size)
     live_pos = (perm[None, :] == pair_align[:, None]) & row_live[:, None]
     col_live = jnp.max(live_pos.astype(jnp.int32), axis=0) > 0
-    x_all = ring_gather(src_emb, ring)
+    after = src_emb + jnp.zeros_like(src_emb) * partner[:1, :1]
+    x_all = ring_gather(after, ring)
     y_all = ring_gather(partner, ring)
 
     block = max(1, min(pair_rows, BLOCK_BYTES // (4 * pair_rows)))

time: 94.9 us -> 98.8 us (1.041)
  waiting for transfers between devices: 16.4 us -> 20 us
  local copies, waits for them, and re-layouts: 10.5 us -> 9.27 us
  other arithmetic: 8.24 us -> 9.36 us
    ppermute x14, waiting for transfers between devices: 15.6 us -> 19.2 us  [ring_gather(): cur = lax.ppermute(cur, 'dp', pairs)]
    dynamic_update_slice x14, local copies, waits for them, and re-layouts: 2.12 us -> 0.28 us  [ring_gather(): out = lax.dynamic_update_slice_in_dim(out, cur, origin * rows, 0)]
    ppermute x14, starting transfers between devices: 16.5 us -> 15.4 us  [ring_gather(): cur = lax.ppermute(cur, 'dp', pairs)]
    ppermute x3, starting transfers between devices: 3.5 us -> 4.55 us  [per_device(): lax.ppermute(sent, 'lang', [(l, (l + k) % lang_size) for l in range(lang_...]
  transfers between devices with their start and end apart: 18 -> 18, of which waited for: 8 -> 9; matrix products, arithmetic and copies ran while one was open for 17% -> 13% of each run, Pallas kernels for 0% -> 0%
where the time goes in v6:
time: 98.8 us; the launch traced here: 97.9 us
  between operations  27.4 us (28%)
  starting transfers between devices  23.3 us (24%)
  waiting for transfers between devices  20 us (20%)
  other arithmetic  9.36 us (9%)
  local copies, waits for them, and re-layouts  9.27 us (9%)
  matrix products  8.62 us (9%)
    ppermute x14, waiting for transfers between devices, ring_gather(): cur = lax.ppermute(cur, 'dp', pairs)  19.2 us
    ppermute x14, starting transfers between devices, ring_gather(): cur = lax.ppermute(cur, 'dp', pairs)  15.4 us
    ppermute x3, starting transfers between devices, per_device(): lax.ppermute(sent, 'lang', [(l, (l + k) % lang_size) for l in range(lang_...  4.55 us
    all_to_all x1, starting transfers between devices, per_device(): lax.all_to_all(grad_local.reshape(lang_size, per_slot, emb_width), 'lang'...  3.37 us
    dot_general x1, matrix products, per_device(): lax.dot_general(g_cols, x_all, (((0,), (0,)), ((), ())), preferred_elemen...  3.14 us
    dot_general x1, matrix products, per_device(): jnp.dot(g_rows, y_all, preferred_element_type=jnp.float32) * inv_root  3.09 us
    reduce_sum x1, other arithmetic, block_stats(): pos_score = jnp.sum(jnp.where(is_pos, scores_f, 0.0), axis=1)  2.41 us
    dot_general x1, matrix products, scores_of(): lax.dot_general(x_rows, y_rows, (((1,), (1,)), ((), ())), preferred_eleme...  2.4 us
  transfers between devices with their start and end apart: 18, of which 9 were waited for; matrix products, arithmetic and copies ran while one was open for 13% of the time, Pallas kernels for 0%

profile of v6, /device:TPU:0, one launch (start us, length us, event | category | flops | bytes accessed | tf_op | source)
XLA Modules:
  0.0 97.9 jit_solution(2333826377552561219)
XLA Ops:
  0.7 1.4 %fusion.64 = (s32[1]{0:T(128)}, s32[1]{0:T(128)}, s32[1]{0:T(128)}, s32[1]{0:T(128)}) fusion(s32[4]{0:T(128)} %param.8), kind=kLoop, calls=%fused_computation.129 | loop fusion | bytes 32 | tf_op jit(solution)/shard_map/slice | solution.py:195
  4.0 0.9 select_bitcast_fusion.2
  4.9 0.5 collective-permute-start
  9.3 0.9 select_bitcast_fusion
  10.2 2.6 %collective-permute-start.1 = (bf16[32,768]{1,0:T(8,128)(2,1)S(1)}, bf16[32,768]{1,0:T(8,128)(2,1)S(1)}, u32[]{:S(2)}, u32[]{:S(2)}) collective-permute-start(bf16[32,768]{1,0:T(8,128)(2,1)S(1)} %get-tuple-element.19), channel_id=1, source_target_pairs={{0,16},{8,24},{16,0},{24,8},{1,17},{9,25},{17,1},{25,9},{2,18},{10... | collective-permute-start | bytes 147464 | tf_op jit(solution)/shard_map/ppermute | solution.py:123
  12.8 1.4 %collective-permute-start.2 = (bf16[32,768]{1,0:T(8,128)(2,1)S(1)}, bf16[32,768]{1,0:T(8,128)(2,1)S(1)}, u32[]{:S(2)}, u32[]{:S(2)}) collective-permute-start(bf16[32,768]{1,0:T(8,128)(2,1)S(1)} %get-tuple-element.18), channel_id=1, source_target_pairs={{0,24},{8,0},{16,8},{24,16},{1,25},{9,1},{17,9},{25,17},{2,26},{10... | collective-permute-start | bytes 147464 | tf_op jit(solution)/shard_map/ppermute | solution.py:123
  16.2 1.3 %dynamic_slice.25 = s32[1]{0:T(128)} dynamic-slice(s32[4]{0:T(128)} %param.9, s32[]{:T(128)S(6)} %select_n.607), dynamic_slice_sizes={1} | dynamic-slice | bytes 12 | tf_op jit(solution)/shard_map/dynamic_slice | solution.py:126
  17.5 0.6 iota_compare_fusion
  18.1 1.5 %convert_reduce_fusion = s32[1024]{0:T(1024)S(1)} fusion(s32[1024]{0:T(1024)} %bitcast.39, s32[1024]{0:T(1024)S(1)} %fusion.46, pred[1024]{0:T(1024)(128)(4,1)S(1)} %iota_compare_fusion), kind=kLoop, calls=%fused_computation.9 | loop fusion | flops 4193280 | bytes 13312 | tf_op jit(solution)/shard_map/reduce_max | solution.py:133
  19.7 0.9 bitcast_dynamic-update-slice_fusion
  20.6 0.7 fusion.65
  36.8 0.7 dynamic_slice.30
  37.5 0.6 dynamic_slice.26
  38.1 0.7 dynamic_slice.29
  38.8 0.6 dynamic_slice.24
  39.4 0.5 slice.48
  40.8 1.6 %collective-permute-start.10 = (bf16[128,768]{1,0:T(8,128)(2,1)S(1)}, bf16[128,768]{1,0:T(8,128)(2,1)S(1)}, u32[]{:S(2)}, u32[]{:S(2)}) collective-permute-start(bf16[128,768]{1,0:T(8,128)(2,1)S(1)} %get-tuple-element.13), channel_id=1, source_target_pairs={{0,2},{2,4},{4,6},{6,7},{7,5},{5,3},{3,1},{1,0},{8,10},{10,12},{12... | collective-permute-start | bytes 589832 | tf_op jit(solution)/shard_map/ppermute | solution.py:73
  42.8 1.6 %collective-permute-start.3 = (bf16[128,768]{1,0:T(8,128)(2,1)S(1)}, bf16[128,768]{1,0:T(8,128)(2,1)S(1)}, u32[]{:S(2)}, u32[]{:S(2)}) collective-permute-start(bf16[128,768]{1,0:T(8,128)(2,1)S(1)} %constant_dynamic-update-slice_fusion.16), channel_id=1, source_target_pairs={{0,2},{2,4},{4,6},{6,7},{7,5},{5,3},{3,1},{1,0},{8,10},{10,12},{12... | collective-permute-start | bytes 589832 | tf_op jit(solution)/shard_map/ppermute | solution.py:73
  44.9 0.5 fusion.55
  45.5 3.0 %collective-permute-done.10 = bf16[128,768]{1,0:T(8,128)(2,1)S(1)} collective-permute-done((bf16[128,768]{1,0:T(8,128)(2,1)S(1)}, bf16[128,768]{1,0:T(8,128)(2,1)S(1)}, u32[]{:S(2)}, u32[]{:S(2)}) %collective-permute-start.10) | collective-permute-done | bytes 196640 | tf_op jit(solution)/shard_map/ppermute | solution.py:73
  48.6 1.6 %collective-permute-start.11 = (bf16[128,768]{1,0:T(8,128)(2,1)S(1)}, bf16[128,768]{1,0:T(8,128)(2,1)S(1)}, u32[]{:S(2)}, u32[]{:S(2)}) collective-permute-start(bf16[128,768]{1,0:T(8,128)(2,1)S(1)} %collective-permute-done.10), channel_id=1, source_target_pairs={{0,2},{2,4},{4,6},{6,7},{7,5},{5,3},{3,1},{1,0},{8,10},{10,12},{12... | collective-permute-start | bytes 589832 | tf_op jit(solution)/shard_map/ppermute | solution.py:73
  50.2 0.5 collective-permute-start.15
  50.6 2.2 %collective-permute-done.3 = bf16[128,768]{1,0:T(8,128)(2,1)S(1)} collective-permute-done((bf16[128,768]{1,0:T(8,128)(2,1)S(1)}, bf16[128,768]{1,0:T(8,128)(2,1)S(1)}, u32[]{:S(2)}, u32[]{:S(2)}) %collective-permute-start.3) | collective-permute-done | bytes 196640 | tf_op jit(solution)/shard_map/ppermute | solution.py:73
  52.8 1.6 %collective-permute-start.4 = (bf16[128,768]{1,0:T(8,128)(2,1)S(1)}, bf16[128,768]{1,0:T(8,128)(2,1)S(1)}, u32[]{:S(2)}, u32[]{:S(2)}) collective-permute-start(bf16[128,768]{1,0:T(8,128)(2,1)S(1)} %collective-permute-done.3), channel_id=1, source_target_pairs={{0,2},{2,4},{4,6},{6,7},{7,5},{5,3},{3,1},{1,0},{8,10},{10,12},{12... | collective-permute-start | bytes 589832 | tf_op jit(solution)/shard_map/ppermute | solution.py:73
  54.4 0.5 collective-permute-start.8
  54.9 2.1 %collective-permute-done.11 = bf16[128,768]{1,0:T(8,128)(2,1)S(1)} collective-permute-done((bf16[128,768]{1,0:T(8,128)(2,1)S(1)}, bf16[128,768]{1,0:T(8,128)(2,1)S(1)}, u32[]{:S(2)}, u32[]{:S(2)}) %collective-permute-start.11) | collective-permute-done | bytes 196640 | tf_op jit(solution)/shard_map/ppermute | solution.py:73
  57.0 1.6 %collective-permute-start.12 = (bf16[128,768]{1,0:T(8,128)(2,1)S(1)}, bf16[128,768]{1,0:T(8,128)(2,1)S(1)}, u32[]{:S(2)}, u32[]{:S(2)}) collective-permute-start(bf16[128,768]{1,0:T(8,128)(2,1)S(1)} %collective-permute-done.11), channel_id=1, source_target_pairs={{0,2},{2,4},{4,6},{6,7},{7,5},{5,3},{3,1},{1,0},{8,10},{10,12},{12... | collective-permute-start | bytes 589832 | tf_op jit(solution)/shard_map/ppermute | solution.py:73
  58.6 0.5 collective-permute-start.16
  59.1 2.2 %collective-permute-done.4 = bf16[128,768]{1,0:T(8,128)(2,1)S(1)} collective-permute-done((bf16[128,768]{1,0:T(8,128)(2,1)S(1)}, bf16[128,768]{1,0:T(8,128)(2,1)S(1)}, u32[]{:S(2)}, u32[]{:S(2)}) %collective-permute-start.4) | collective-permute-done | bytes 196640 | tf_op jit(solution)/shard_map/ppermute | solution.py:73
  61.2 1.6 %collective-permute-start.5 = (bf16[128,768]{1,0:T(8,128)(2,1)S(1)}, bf16[128,768]{1,0:T(8,128)(2,1)S(1)}, u32[]{:S(2)}, u32[]{:S(2)}) collective-permute-start(bf16[128,768]{1,0:T(8,128)(2,1)S(1)} %collective-permute-done.4), channel_id=1, source_target_pairs={{0,2},{2,4},{4,6},{6,7},{7,5},{5,3},{3,1},{1,0},{8,10},{10,12},{12... | collective-permute-start | bytes 589832 | tf_op jit(solution)/shard_map/ppermute | solution.py:73
  62.8 0.5 collective-permute-start.9
  63.3 2.1 %collective-permute-done.12 = bf16[128,768]{1,0:T(8,128)(2,1)S(1)} collective-permute-done((bf16[128,768]{1,0:T(8,128)(2,1)S(1)}, bf16[128,768]{1,0:T(8,128)(2,1)S(1)}, u32[]{:S(2)}, u32[]{:S(2)}) %collective-permute-start.12) | collective-permute-done | bytes 196640 | tf_op jit(solution)/shard_map/ppermute | solution.py:73
  65.5 1.6 %collective-permute-start.13 = (bf16[128,768]{1,0:T(8,128)(2,1)S(1)}, bf16[128,768]{1,0:T(8,128)(2,1)S(1)}, u32[]{:S(2)}, u32[]{:S(2)}) collective-permute-start(bf16[128,768]{1,0:T(8,128)(2,1)S(1)} %collective-permute-done.12), channel_id=1, source_target_pairs={{0,2},{2,4},{4,6},{6,7},{7,5},{5,3},{3,1},{1,0},{8,10},{10,12},{12... | collective-permute-start | bytes 589832 | tf_op jit(solution)/shard_map/ppermute | solution.py:73
  67.0 2.6 %collective-permute-done.5 = bf16[128,768]{1,0:T(8,128)(2,1)S(1)} collective-permute-done((bf16[128,768]{1,0:T(8,128)(2,1)S(1)}, bf16[128,768]{1,0:T(8,128)(2,1)S(1)}, u32[]{:S(2)}, u32[]{:S(2)}) %collective-permute-start.5) | collective-permute-done | bytes 196640 | tf_op jit(solution)/shard_map/ppermute | solution.py:73
  69.7 1.6 %collective-permute-start.6 = (bf16[128,768]{1,0:T(8,128)(2,1)S(1)}, bf16[128,768]{1,0:T(8,128)(2,1)S(1)}, u32[]{:S(2)}, u32[]{:S(2)}) collective-permute-start(bf16[128,768]{1,0:T(8,128)(2,1)S(1)} %collective-permute-done.5), channel_id=1, source_target_pairs={{0,2},{2,4},{4,6},{6,7},{7,5},{5,3},{3,1},{1,0},{8,10},{10,12},{12... | collective-permute-start | bytes 589832 | tf_op jit(solution)/shard_map/ppermute | solution.py:73
  71.3 2.6 %collective-permute-done.13 = bf16[128,768]{1,0:T(8,128)(2,1)S(1)} collective-permute-done((bf16[128,768]{1,0:T(8,128)(2,1)S(1)}, bf16[128,768]{1,0:T(8,128)(2,1)S(1)}, u32[]{:S(2)}, u32[]{:S(2)}) %collective-permute-start.13) | collective-permute-done | bytes 196640 | tf_op jit(solution)/shard_map/ppermute | solution.py:73
  73.9 2.3 %collective-permute-done.6 = bf16[128,768]{1,0:T(8,128)(2,1)S(1)} collective-permute-done((bf16[128,768]{1,0:T(8,128)(2,1)S(1)}, bf16[128,768]{1,0:T(8,128)(2,1)S(1)}, u32[]{:S(2)}, u32[]{:S(2)}) %collective-permute-start.6) | collective-permute-done | bytes 196640 | tf_op jit(solution)/shard_map/ppermute | solution.py:73
  76.4 2.4 %select_reduce_fusion.3 = (f32[1024]{0:T(1024)S(1)}, f32[1024]{0:T(1024)S(1)}, f32[1024,1024]{0,1:T(8,128)S(1)}) fusion(pred[1024]{0:T(1024)(128)(4,1)S(1)} %broadcast_compare_fusion, pred[1024]{0:T(1024)(128)(4,1)S(1)} %copy-done.6, s32[1024]{0:T(1024)S(1)} %bitcast.40, s32[1024]{0:T(1024)S(1)} %fusion.46, ...), kind=kOutput, calls=%fused_computation.8 | convolution fusion | flops 1618999296 | bytes 7358464 | tf_op jit(solution)/shard_map/dot_general | solution.py:80
  78.8 2.4 %fusion.1 = (f32[1024]{0:T(1024)S(1)}, f32[1024]{0:T(1024)S(1)}, f32[1024]{0:T(1024)S(1)}) fusion(f32[1024,1024]{0,1:T(8,128)S(1)} %get-tuple-element.27, s32[1024]{0:T(1024)S(1)} %bitcast.41, s32[1024]{0:T(1024)S(1)} %fusion.46, f32[1024]{0:T(1024)S(1)} %get-tuple-element.7, pred[1024]{0:T(1024)(128)(4,1)S(1)} %copy-done.6, f32[1024]{0:T(1024)S(1)} %get-tuple-element.6, ...), kind=kLoop, calls=%fused_computation.4 | loop fusion | flops 9434112 | bytes 4225024 | tf_op jit(solution)/shard_map/reduce_sum | solution.py:92
  81.2 1.3 %select_reduce_fusion.4 = (f32[]{:T(128)}, f32[1024]{0:T(1024)S(1)}, f32[]{:T(128)}, f32[1024]{0:T(1024)S(1)}) fusion(f32[1024]{0:T(1024)S(1)} %get-tuple-element.7, f32[1024]{0:T(1024)S(1)} %get-tuple-element.4, f32[1024]{0:T(1024)S(1)} %get-tuple-element.3, f32[1024]{0:T(1024)S(1)} %get-tuple-element.6, f32[1024]{0:T(1024)S(1)} %get-tuple-element.5, ...), kind=kLoop, calls=%fused_computation.110 | loop fusion | flops 16382 | bytes 32780 | tf_op jit(solution)/shard_map/reduce_sum | solution.py:167
  82.5 0.6 copy-done.2
  83.1 0.6 dynamic_slice.31
  83.7 0.6 dynamic_slice.28
  84.3 3.1 %fusion.6 = bf16[128,768]{1,0:T(8,128)(2,1)} fusion(bf16[1024,768]{1,0:T(8,128)(2,1)S(1)} %constant_dynamic-update-slice_fusion, bf16[128,768]{1,0:T(8,128)(2,1)S(1)} %constant_dynamic-update-slice_fusion.16, f32[128]{0:T(128)} %dynamic_slice.31, f32[1024]{0:T(1024)} %copy-done.4, s32[128]{0:T(128)} %dynamic_slice.30, f32[]{:T(128)} %bitcast, ...), kind=kOutput, calls=%fused_computation.18 | convolution fusion | flops 404815872 | bytes 1976452 | tf_op jit(solution)/shard_map/dot_general | solution.py:187
  87.4 3.4 %all-to-all-start = ((bf16[4,32,768]{2,1,0:T(8,128)(2,1)}), bf16[4,32,768]{2,1,0:T(8,128)(2,1)S(1)}, u32[]{:S(2)}, u32[]{:S(2)}) async-start(bf16[4,32,768]{2,1,0:T(8,128)(2,1)} %bitcast.15), calls=%async_computation | async-start | bytes 393216 | tf_op jit(solution)/shard_map/all_to_all | solution.py:191
  90.8 3.1 %fusion.5 = bf16[128,768]{1,0:T(8,128)(2,1)} fusion(bf16[1024,768]{1,0:T(8,128)(2,1)S(1)} %constant_dynamic-update-slice_fusion.8, bf16[128,768]{1,0:T(8,128)(2,1)S(1)} %copy-done, f32[1024]{0:T(1024)S(1)} %copy-done.3, f32[128]{0:T(128)} %dynamic_slice.28, s32[128]{0:T(128)} %fusion.55, f32[]{:T(128)} %bitcast, s32[1024]{0:T(1024)S(1)} %fusion.46, ...), kind=kOutput, calls=%fused_computation.17 | convolution fusion | flops 404815872 | bytes 1976452 | tf_op jit(solution)/shard_map/dot_general | solution.py:178
  95.2 0.8 all-to-all-done
  96.1 0.7 pad_maximum_fusion
  (53 shorter events, 1.6 us)
Async XLA Ops:
  0.6 38.2 %copy-start.7 = (f32[4]{0:T(128)S(1)}, f32[4]{0:T(128)}, u32[]{:S(2)}) copy-start(f32[4]{0:T(128)} %param.11) | copy-start | bytes 52
  4.9 34.4 %collective-permute-start = (bf16[32,768]{1,0:T(8,128)(2,1)S(1)}, bf16[32,768]{1,0:T(8,128)(2,1)S(1)}, u32[]{:S(2)}, u32[]{:S(2)}) collective-permute-start(bf16[32,768]{1,0:T(8,128)(2,1)S(1)} %select_bitcast_fusion.2), channel_id=1, source_target_pairs={{0,8},{8,16},{16,24},{24,0},{1,9},{9,17},{17,25},{25,1},{2,10},{10... | collective-permute-start | bytes 147464 | tf_op jit(solution)/shard_map/ppermute | solution.py:123
  9.3 31.4 %copy-start = (bf16[128,768]{1,0:T(8,128)(2,1)S(1)}, bf16[128,768]{1,0:T(8,128)(2,1)}, u32[]{:S(2)}) copy-start(bf16[128,768]{1,0:T(8,128)(2,1)} %param.6) | copy-start | bytes 589828
  10.2 29.1 %collective-permute-start.1 = (bf16[32,768]{1,0:T(8,128)(2,1)S(1)}, bf16[32,768]{1,0:T(8,128)(2,1)S(1)}, u32[]{:S(2)}, u32[]{:S(2)}) collective-permute-start(bf16[32,768]{1,0:T(8,128)(2,1)S(1)} %get-tuple-element.19), channel_id=1, source_target_pairs={{0,16},{8,24},{16,0},{24,8},{1,17},{9,25},{17,1},{25,9},{2,18},{10... | collective-permute-start | bytes 147464 | tf_op jit(solution)/shard_map/ppermute | solution.py:123
  12.8 26.6 %collective-permute-start.2 = (bf16[32,768]{1,0:T(8,128)(2,1)S(1)}, bf16[32,768]{1,0:T(8,128)(2,1)S(1)}, u32[]{:S(2)}, u32[]{:S(2)}) collective-permute-start(bf16[32,768]{1,0:T(8,128)(2,1)S(1)} %get-tuple-element.18), channel_id=1, source_target_pairs={{0,24},{8,0},{16,8},{24,16},{1,25},{9,1},{17,9},{25,17},{2,26},{10... | collective-permute-start | bytes 147464 | tf_op jit(solution)/shard_map/ppermute | solution.py:123
  18.1 22.5 %copy-start.5 = (pred[1024]{0:T(1024)(128)(4,1)}, pred[1024]{0:T(1024)(128)(4,1)S(1)}, u32[]{:S(2)}) copy-start(pred[1024]{0:T(1024)(128)(4,1)S(1)} %iota_compare_fusion) | copy-start | bytes 3076
  20.6 24.3 %copy-start.1 = (s32[1,1024]{1,0:T(1,128)S(1)}, s32[1,1024]{1,0:T(1,128)}, u32[]{:S(2)}) copy-start(s32[1,1024]{1,0:T(1,128)} %param.10) | copy-start | bytes 12292
  40.8 7.8 %collective-permute-start.10 = (bf16[128,768]{1,0:T(8,128)(2,1)S(1)}, bf16[128,768]{1,0:T(8,128)(2,1)S(1)}, u32[]{:S(2)}, u32[]{:S(2)}) collective-permute-start(bf16[128,768]{1,0:T(8,128)(2,1)S(1)} %get-tuple-element.13), channel_id=1, source_target_pairs={{0,2},{2,4},{4,6},{6,7},{7,5},{5,3},{3,1},{1,0},{8,10},{10,12},{12... | collective-permute-start | bytes 589832 | tf_op jit(solution)/shard_map/ppermute | solution.py:73
  42.4 7.8 %collective-permute-start.14 = (bf16[128,768]{1,0:T(8,128)(2,1)S(1)}, bf16[128,768]{1,0:T(8,128)(2,1)S(1)}, u32[]{:S(2)}, u32[]{:S(2)}) collective-permute-start(bf16[128,768]{1,0:T(8,128)(2,1)S(1)} %get-tuple-element.13), channel_id=1, source_target_pairs={{0,1},{2,0},{4,2},{6,4},{7,6},{5,7},{3,5},{1,3},{8,9},{10,8},{12,1... | collective-permute-start | bytes 589832 | tf_op jit(solution)/shard_map/ppermute | solution.py:73
  42.8 10.0 %collective-permute-start.3 = (bf16[128,768]{1,0:T(8,128)(2,1)S(1)}, bf16[128,768]{1,0:T(8,128)(2,1)S(1)}, u32[]{:S(2)}, u32[]{:S(2)}) collective-permute-start(bf16[128,768]{1,0:T(8,128)(2,1)S(1)} %constant_dynamic-update-slice_fusion.16), channel_id=1, source_target_pairs={{0,2},{2,4},{4,6},{6,7},{7,5},{5,3},{3,1},{1,0},{8,10},{10,12},{12... | collective-permute-start | bytes 589832 | tf_op jit(solution)/shard_map/ppermute | solution.py:73
  44.4 10.0 %collective-permute-start.7 = (bf16[128,768]{1,0:T(8,128)(2,1)S(1)}, bf16[128,768]{1,0:T(8,128)(2,1)S(1)}, u32[]{:S(2)}, u32[]{:S(2)}) collective-permute-start(bf16[128,768]{1,0:T(8,128)(2,1)S(1)} %constant_dynamic-update-slice_fusion.16), channel_id=1, source_target_pairs={{0,1},{2,0},{4,2},{6,4},{7,6},{5,7},{3,5},{1,3},{8,9},{10,8},{12,1... | collective-permute-start | bytes 589832 | tf_op jit(solution)/shard_map/ppermute | solution.py:73
  48.6 8.4 %collective-permute-start.11 = (bf16[128,768]{1,0:T(8,128)(2,1)S(1)}, bf16[128,768]{1,0:T(8,128)(2,1)S(1)}, u32[]{:S(2)}, u32[]{:S(2)}) collective-permute-start(bf16[128,768]{1,0:T(8,128)(2,1)S(1)} %collective-permute-done.10), channel_id=1, source_target_pairs={{0,2},{2,4},{4,6},{6,7},{7,5},{5,3},{3,1},{1,0},{8,10},{10,12},{12... | collective-permute-start | bytes 589832 | tf_op jit(solution)/shard_map/ppermute | solution.py:73
  50.2 8.4 %collective-permute-start.15 = (bf16[128,768]{1,0:T(8,128)(2,1)S(1)}, bf16[128,768]{1,0:T(8,128)(2,1)S(1)}, u32[]{:S(2)}, u32[]{:S(2)}) collective-permute-start(bf16[128,768]{1,0:T(8,128)(2,1)S(1)} %collective-permute-done.14), channel_id=1, source_target_pairs={{0,1},{2,0},{4,2},{6,4},{7,6},{5,7},{3,5},{1,3},{8,9},{10,8},{12,1... | collective-permute-start | bytes 589832 | tf_op jit(solution)/shard_map/ppermute | solution.py:73
  52.8 8.4 %collective-permute-start.4 = (bf16[128,768]{1,0:T(8,128)(2,1)S(1)}, bf16[128,768]{1,0:T(8,128)(2,1)S(1)}, u32[]{:S(2)}, u32[]{:S(2)}) collective-permute-start(bf16[128,768]{1,0:T(8,128)(2,1)S(1)} %collective-permute-done.3), channel_id=1, source_target_pairs={{0,2},{2,4},{4,6},{6,7},{7,5},{5,3},{3,1},{1,0},{8,10},{10,12},{12... | collective-permute-start | bytes 589832 | tf_op jit(solution)/shard_map/ppermute | solution.py:73
  54.4 8.4 %collective-permute-start.8 = (bf16[128,768]{1,0:T(8,128)(2,1)S(1)}, bf16[128,768]{1,0:T(8,128)(2,1)S(1)}, u32[]{:S(2)}, u32[]{:S(2)}) collective-permute-start(bf16[128,768]{1,0:T(8,128)(2,1)S(1)} %collective-permute-done.7), channel_id=1, source_target_pairs={{0,1},{2,0},{4,2},{6,4},{7,6},{5,7},{3,5},{1,3},{8,9},{10,8},{12,1... | collective-permute-start | bytes 589832 | tf_op jit(solution)/shard_map/ppermute | solution.py:73
  57.0 8.4 %collective-permute-start.12 = (bf16[128,768]{1,0:T(8,128)(2,1)S(1)}, bf16[128,768]{1,0:T(8,128)(2,1)S(1)}, u32[]{:S(2)}, u32[]{:S(2)}) collective-permute-start(bf16[128,768]{1,0:T(8,128)(2,1)S(1)} %collective-permute-done.11), channel_id=1, source_target_pairs={{0,2},{2,4},{4,6},{6,7},{7,5},{5,3},{3,1},{1,0},{8,10},{10,12},{12... | collective-permute-start | bytes 589832 | tf_op jit(solution)/shard_map/ppermute | solution.py:73
  58.6 17.7 %collective-permute-start.16 = (bf16[128,768]{1,0:T(8,128)(2,1)S(1)}, bf16[128,768]{1,0:T(8,128)(2,1)S(1)}, u32[]{:S(2)}, u32[]{:S(2)}) collective-permute-start(bf16[128,768]{1,0:T(8,128)(2,1)S(1)} %collective-permute-done.15), channel_id=1, source_target_pairs={{0,1},{2,0},{4,2},{6,4},{7,6},{5,7},{3,5},{1,3},{8,9},{10,8},{12,1... | collective-permute-start | bytes 589832 | tf_op jit(solution)/shard_map/ppermute | solution.py:73
  61.2 8.4 %collective-permute-start.5 = (bf16[128,768]{1,0:T(8,128)(2,1)S(1)}, bf16[128,768]{1,0:T(8,128)(2,1)S(1)}, u32[]{:S(2)}, u32[]{:S(2)}) collective-permute-start(bf16[128,768]{1,0:T(8,128)(2,1)S(1)} %collective-permute-done.4), channel_id=1, source_target_pairs={{0,2},{2,4},{4,6},{6,7},{7,5},{5,3},{3,1},{1,0},{8,10},{10,12},{12... | collective-permute-start | bytes 589832 | tf_op jit(solution)/shard_map/ppermute | solution.py:73
  62.8 13.5 %collective-permute-start.9 = (bf16[128,768]{1,0:T(8,128)(2,1)S(1)}, bf16[128,768]{1,0:T(8,128)(2,1)S(1)}, u32[]{:S(2)}, u32[]{:S(2)}) collective-permute-start(bf16[128,768]{1,0:T(8,128)(2,1)S(1)} %collective-permute-done.8), channel_id=1, source_target_pairs={{0,1},{2,0},{4,2},{6,4},{7,6},{5,7},{3,5},{1,3},{8,9},{10,8},{12,1... | collective-permute-start | bytes 589832 | tf_op jit(solution)/shard_map/ppermute | solution.py:73
  65.5 8.4 %collective-permute-start.13 = (bf16[128,768]{1,0:T(8,128)(2,1)S(1)}, bf16[128,768]{1,0:T(8,128)(2,1)S(1)}, u32[]{:S(2)}, u32[]{:S(2)}) collective-permute-start(bf16[128,768]{1,0:T(8,128)(2,1)S(1)} %collective-permute-done.12), channel_id=1, source_target_pairs={{0,2},{2,4},{4,6},{6,7},{7,5},{5,3},{3,1},{1,0},{8,10},{10,12},{12... | collective-permute-start | bytes 589832 | tf_op jit(solution)/shard_map/ppermute | solution.py:73
  69.7 6.5 %collective-permute-start.6 = (bf16[128,768]{1,0:T(8,128)(2,1)S(1)}, bf16[128,768]{1,0:T(8,128)(2,1)S(1)}, u32[]{:S(2)}, u32[]{:S(2)}) collective-permute-start(bf16[128,768]{1,0:T(8,128)(2,1)S(1)} %collective-permute-done.5), channel_id=1, source_target_pairs={{0,2},{2,4},{4,6},{6,7},{7,5},{5,3},{3,1},{1,0},{8,10},{10,12},{12... | collective-permute-start | bytes 589832 | tf_op jit(solution)/shard_map/ppermute | solution.py:73
  71.3 5.1 %copy-start.6 = (pred[1024]{0:T(1024)(128)(4,1)S(1)}, pred[1024]{0:T(1024)(128)(4,1)}, u32[]{:S(2)}) copy-start(pred[1024]{0:T(1024)(128)(4,1)} %copy-done.5) | copy-start | bytes 3076
  82.5 0.6 copy-start.2
  82.5 1.8 %copy-start.4 = (f32[1024]{0:T(1024)}, f32[1024]{0:T(1024)S(1)}, u32[]{:S(2)}) copy-start(f32[1024]{0:T(1024)S(1)} %get-tuple-element.29) | copy-start | bytes 12292
  84.3 6.5 %copy-start.3 = (f32[1024]{0:T(1024)S(1)}, f32[1024]{0:T(1024)}, u32[]{:S(2)}) copy-start(f32[1024]{0:T(1024)} %copy-done.2) | copy-start | bytes 12292
  87.4 8.6 %all-to-all-start = ((bf16[4,32,768]{2,1,0:T(8,128)(2,1)}), bf16[4,32,768]{2,1,0:T(8,128)(2,1)S(1)}, u32[]{:S(2)}, u32[]{:S(2)}) async-start(bf16[4,32,768]{2,1,0:T(8,128)(2,1)} %bitcast.15), calls=%async_computation | async-start | bytes 393216 | tf_op jit(solution)/shard_map/all_to_all | solution.py:191

commit v7 on v5

--- a/solution.py
+++ b/solution.py
@@ -114,15 +114,9 @@
     inv_root = 1.0 / math.sqrt(emb_width)
     group_index = lax.axis_index("lang")
     shard_index = lax.axis_index("dp")
-    partner = jnp.zeros((lang_size * per_slot, emb_width), tgt_emb.dtype)
-    own = slot_rows(tgt_emb, slot_group, group_index)
-    partner = lax.dynamic_update_slice_in_dim(partner, own, group_index * per_slot, 0)
-    for k in range(1, lang_size):
-        dest = (group_index + k) % lang_size
-        sent = slot_rows(tgt_emb, slot_group, dest)
-        got = lax.ppermute(sent, "lang", [(l, (l + k) % lang_size) for l in range(lang_size)])
-        origin = (group_index - k) % lang_size
-        partner = lax.dynamic_update_slice_in_dim(partner, got, origin * per_slot, 0)
+    ordered = jnp.stack([slot_rows(tgt_emb, slot_group, g) for g in range(lang_size)])
+    arrived = lax.all_to_all(ordered, "lang", split_axis=0, concat_axis=1, tiled=True)
+    partner = arrived[0]
     live_count = counts[group_index]
     weight = pair_weight[group_index]
     pair_align = align[0]

time: 94.9 us -> 98 us (1.033)
  local copies, waits for them, and re-layouts: 10.5 us -> 11.7 us
    ppermute x3 -> x0, starting transfers between devices: 3.5 us -> none  [per_device(): lax.ppermute(sent, 'lang', [(l, (l + k) % lang_size) for l in range(lang_...]
    all_to_all x0 -> x1, starting transfers between devices: none -> 3.37 us  [per_device(): lax.all_to_all(ordered, 'lang', split_axis=0, concat_axis=1, tiled=True)]
    slice x1 -> x3, local copies, waits for them, and re-layouts: 0.62 us -> 1.84 us  [slot_rows(): rows = jnp.where(slot_group[s] == group, tgt_emb[s], rows)]
  transfers between devices with their start and end apart: 18 -> 16, of which waited for: 8 -> 8; matrix products, arithmetic and copies ran while one was open for 17% -> 18% of each run, Pallas kernels for 0% -> 0%
where the time goes in v7:
time: 98 us; the launch traced here: 97.1 us
  between operations  26.4 us (27%)
  starting transfers between devices  24.1 us (25%)
  waiting for transfers between devices  17.1 us (17%)
  local copies, waits for them, and re-layouts  11.7 us (12%)
  other arithmetic  9.1 us (9%)
  matrix products  8.79 us (9%)
    ppermute x14, starting transfers between devices, ring_gather(): cur = lax.ppermute(cur, 'dp', pairs)  17.3 us
    ppermute x14, waiting for transfers between devices, ring_gather(): cur = lax.ppermute(cur, 'dp', pairs)  16.3 us
    all_to_all x1, starting transfers between devices, per_device(): lax.all_to_all(grad_local.reshape(lang_size, per_slot, emb_width), 'lang'...  3.37 us
    all_to_all x1, starting transfers between devices, per_device(): lax.all_to_all(ordered, 'lang', split_axis=0, concat_axis=1, tiled=True)  3.37 us
    dot_general x1, matrix products, per_device(): lax.dot_general(g_cols, x_all, (((0,), (0,)), ((), ())), preferred_elemen...  3.25 us
    dot_general x1, matrix products, per_device(): jnp.dot(g_rows, y_all, preferred_element_type=jnp.float32) * inv_root  3.17 us
    reduce_sum x1, other arithmetic, block_stats(): pos_score = jnp.sum(jnp.where(is_pos, scores_f, 0.0), axis=1)  2.39 us
    dot_general x1, matrix products, scores_of(): lax.dot_general(x_rows, y_rows, (((1,), (1,)), ((), ())), preferred_eleme...  2.37 us
  transfers between devices with their start and end apart: 16, of which 8 were waited for; matrix products, arithmetic and copies ran while one was open for 18% of the time, Pallas kernels for 0%

profile of v7, /device:TPU:0, one launch (start us, length us, event | category | flops | bytes accessed | tf_op | source)
XLA Modules:
  0.0 97.1 jit_solution(5715402764972266771)
XLA Ops:
  0.6 3.1 %collective-permute-start.7 = (bf16[128,768]{1,0:T(8,128)(2,1)}, bf16[128,768]{1,0:T(8,128)(2,1)}, u32[]{:S(2)}, u32[]{:S(2)}) collective-permute-start(bf16[128,768]{1,0:T(8,128)(2,1)} %param.6), channel_id=1, source_target_pairs={{0,2},{2,4},{4,6},{6,7},{7,5},{5,3},{3,1},{1,0},{8,10},{10,12},{12... | collective-permute-start | bytes 589832 | tf_op jit(solution)/shard_map/ppermute | solution.py:73
  3.8 1.4 %fusion.64 = (s32[1]{0:T(128)}, s32[1]{0:T(128)}, s32[1]{0:T(128)}, s32[1]{0:T(128)}) fusion(s32[4]{0:T(128)} %param.8), kind=kLoop, calls=%fused_computation.126 | loop fusion | bytes 32 | tf_op jit(solution)/shard_map/slice | solution.py:188
  12.5 0.9 select_select_fusion.7
  13.4 0.9 select_select_fusion.6
  14.3 0.7 pad_maximum_fusion
  15.1 3.4 %all-to-all-start = ((bf16[4,32,768]{2,1,0:T(8,128)(2,1)}), bf16[4,32,768]{2,1,0:T(8,128)(2,1)S(1)}, u32[]{:S(2)}, u32[]{:S(2)}) async-start(bf16[4,32,768]{2,1,0:T(8,128)(2,1)} %pad_maximum_fusion), calls=%async_computation | async-start | bytes 393216 | tf_op jit(solution)/shard_map/all_to_all | solution.py:118
  18.5 1.3 %dynamic_slice.25 = s32[1]{0:T(128)} dynamic-slice(s32[4]{0:T(128)} %param.9, s32[]{:T(128)S(6)} %select_n.563), dynamic_slice_sizes={1} | dynamic-slice | bytes 12 | tf_op jit(solution)/shard_map/dynamic_slice | solution.py:120
  19.7 0.6 iota_compare_fusion
  20.4 1.5 %convert_reduce_fusion = s32[1024]{0:T(1024)S(1)} fusion(s32[1024]{0:T(1024)} %bitcast.53, s32[1024]{0:T(1024)S(1)} %fusion.46, pred[1024]{0:T(1024)(128)(4,1)S(1)} %iota_compare_fusion), kind=kLoop, calls=%fused_computation.9 | loop fusion | flops 4193280 | bytes 13312 | tf_op jit(solution)/shard_map/reduce_max | solution.py:127
  21.9 0.1 broadcast.206.clone.1
  23.0 0.6 dynamic_slice.30
  23.6 0.6 slice.55
  25.3 0.6 slice.58
  29.7 0.6 slice.120
  40.1 0.6 dynamic_slice.26
  40.7 0.6 dynamic_slice.29
  41.3 0.6 dynamic_slice.24
  41.9 0.6 fusion.55
  42.5 2.0 %collective-permute-start = (bf16[128,768]{1,0:T(8,128)(2,1)S(1)}, bf16[128,768]{1,0:T(8,128)(2,1)S(1)}, u32[]{:S(2)}, u32[]{:S(2)}) collective-permute-start(bf16[128,768]{1,0:T(8,128)(2,1)S(1)} %bitcast.48), channel_id=1, source_target_pairs={{0,2},{2,4},{4,6},{6,7},{7,5},{5,3},{3,1},{1,0},{8,10},{10,12},{12... | collective-permute-start | bytes 589832 | tf_op jit(solution)/shard_map/ppermute | solution.py:73
  44.5 0.1 broadcast.206.clone
  44.7 2.1 %collective-permute-start.8 = (bf16[128,768]{1,0:T(8,128)(2,1)}, bf16[128,768]{1,0:T(8,128)(2,1)S(1)}, u32[]{:S(2)}, u32[]{:S(2)}) collective-permute-start(bf16[128,768]{1,0:T(8,128)(2,1)} %collective-permute-done.7), channel_id=1, source_target_pairs={{0,2},{2,4},{4,6},{6,7},{7,5},{5,3},{3,1},{1,0},{8,10},{10,12},{12... | collective-permute-start | bytes 589832 | tf_op jit(solution)/shard_map/ppermute | solution.py:73
  46.8 0.0 collective-permute-start.12
  46.8 1.0 constant_dynamic-update-slice_fusion.6
  47.7 2.6 %collective-permute-done = bf16[128,768]{1,0:T(8,128)(2,1)S(1)} collective-permute-done((bf16[128,768]{1,0:T(8,128)(2,1)S(1)}, bf16[128,768]{1,0:T(8,128)(2,1)S(1)}, u32[]{:S(2)}, u32[]{:S(2)}) %collective-permute-start) | collective-permute-done | bytes 196640 | tf_op jit(solution)/shard_map/ppermute | solution.py:73
  50.3 2.0 %collective-permute-start.1 = (bf16[128,768]{1,0:T(8,128)(2,1)S(1)}, bf16[128,768]{1,0:T(8,128)(2,1)S(1)}, u32[]{:S(2)}, u32[]{:S(2)}) collective-permute-start(bf16[128,768]{1,0:T(8,128)(2,1)S(1)} %collective-permute-done), channel_id=1, source_target_pairs={{0,2},{2,4},{4,6},{6,7},{7,5},{5,3},{3,1},{1,0},{8,10},{10,12},{12... | collective-permute-start | bytes 589832 | tf_op jit(solution)/shard_map/ppermute | solution.py:73
  52.3 0.0 collective-permute-start.5
  52.3 2.2 %collective-permute-done.8 = bf16[128,768]{1,0:T(8,128)(2,1)S(1)} collective-permute-done((bf16[128,768]{1,0:T(8,128)(2,1)}, bf16[128,768]{1,0:T(8,128)(2,1)S(1)}, u32[]{:S(2)}, u32[]{:S(2)}) %collective-permute-start.8) | collective-permute-done | bytes 196640 | tf_op jit(solution)/shard_map/ppermute | solution.py:73
  54.5 2.0 %collective-permute-start.9 = (bf16[128,768]{1,0:T(8,128)(2,1)S(1)}, bf16[128,768]{1,0:T(8,128)(2,1)S(1)}, u32[]{:S(2)}, u32[]{:S(2)}) collective-permute-start(bf16[128,768]{1,0:T(8,128)(2,1)S(1)} %collective-permute-done.8), channel_id=1, source_target_pairs={{0,2},{2,4},{4,6},{6,7},{7,5},{5,3},{3,1},{1,0},{8,10},{10,12},{12... | collective-permute-start | bytes 589832 | tf_op jit(solution)/shard_map/ppermute | solution.py:73
  56.6 2.2 %collective-permute-done.1 = bf16[128,768]{1,0:T(8,128)(2,1)S(1)} collective-permute-done((bf16[128,768]{1,0:T(8,128)(2,1)S(1)}, bf16[128,768]{1,0:T(8,128)(2,1)S(1)}, u32[]{:S(2)}, u32[]{:S(2)}) %collective-permute-start.1) | collective-permute-done | bytes 196640 | tf_op jit(solution)/shard_map/ppermute | solution.py:73
  58.7 2.0 %collective-permute-start.2 = (bf16[128,768]{1,0:T(8,128)(2,1)S(1)}, bf16[128,768]{1,0:T(8,128)(2,1)S(1)}, u32[]{:S(2)}, u32[]{:S(2)}) collective-permute-start(bf16[128,768]{1,0:T(8,128)(2,1)S(1)} %collective-permute-done.1), channel_id=1, source_target_pairs={{0,2},{2,4},{4,6},{6,7},{7,5},{5,3},{3,1},{1,0},{8,10},{10,12},{12... | collective-permute-start | bytes 589832 | tf_op jit(solution)/shard_map/ppermute | solution.py:73
  60.8 2.2 %collective-permute-done.9 = bf16[128,768]{1,0:T(8,128)(2,1)S(1)} collective-permute-done((bf16[128,768]{1,0:T(8,128)(2,1)S(1)}, bf16[128,768]{1,0:T(8,128)(2,1)S(1)}, u32[]{:S(2)}, u32[]{:S(2)}) %collective-permute-start.9) | collective-permute-done | bytes 196640 | tf_op jit(solution)/shard_map/ppermute | solution.py:73
  62.9 2.0 %collective-permute-start.10 = (bf16[128,768]{1,0:T(8,128)(2,1)S(1)}, bf16[128,768]{1,0:T(8,128)(2,1)S(1)}, u32[]{:S(2)}, u32[]{:S(2)}) collective-permute-start(bf16[128,768]{1,0:T(8,128)(2,1)S(1)} %collective-permute-done.9), channel_id=1, source_target_pairs={{0,2},{2,4},{4,6},{6,7},{7,5},{5,3},{3,1},{1,0},{8,10},{10,12},{12... | collective-permute-start | bytes 589832 | tf_op jit(solution)/shard_map/ppermute | solution.py:73
  65.0 2.2 %collective-permute-done.2 = bf16[128,768]{1,0:T(8,128)(2,1)S(1)} collective-permute-done((bf16[128,768]{1,0:T(8,128)(2,1)S(1)}, bf16[128,768]{1,0:T(8,128)(2,1)S(1)}, u32[]{:S(2)}, u32[]{:S(2)}) %collective-permute-start.2) | collective-permute-done | bytes 196640 | tf_op jit(solution)/shard_map/ppermute | solution.py:73
  67.1 2.0 %collective-permute-start.3 = (bf16[128,768]{1,0:T(8,128)(2,1)S(1)}, bf16[128,768]{1,0:T(8,128)(2,1)S(1)}, u32[]{:S(2)}, u32[]{:S(2)}) collective-permute-start(bf16[128,768]{1,0:T(8,128)(2,1)S(1)} %collective-permute-done.2), channel_id=1, source_target_pairs={{0,2},{2,4},{4,6},{6,7},{7,5},{5,3},{3,1},{1,0},{8,10},{10,12},{12... | collective-permute-start | bytes 589832 | tf_op jit(solution)/shard_map/ppermute | solution.py:73
  69.2 2.2 %collective-permute-done.10 = bf16[128,768]{1,0:T(8,128)(2,1)S(1)} collective-permute-done((bf16[128,768]{1,0:T(8,128)(2,1)S(1)}, bf16[128,768]{1,0:T(8,128)(2,1)S(1)}, u32[]{:S(2)}, u32[]{:S(2)}) %collective-permute-start.10) | collective-permute-done | bytes 196640 | tf_op jit(solution)/shard_map/ppermute | solution.py:73
  71.4 0.9 constant_dynamic-update-slice_fusion.2
  72.4 2.9 %collective-permute-done.3 = bf16[128,768]{1,0:T(8,128)(2,1)S(1)} collective-permute-done((bf16[128,768]{1,0:T(8,128)(2,1)S(1)}, bf16[128,768]{1,0:T(8,128)(2,1)S(1)}, u32[]{:S(2)}, u32[]{:S(2)}) %collective-permute-start.3) | collective-permute-done | bytes 196640 | tf_op jit(solution)/shard_map/ppermute | solution.py:73
  75.4 2.4 %select_reduce_fusion.3 = (f32[1024]{0:T(1024)S(1)}, f32[1024]{0:T(1024)S(1)}, f32[1024,1024]{0,1:T(8,128)S(1)}) fusion(pred[1024]{0:T(1024)(128)(4,1)S(1)} %broadcast_compare_fusion, pred[1024]{0:T(1024)(128)(4,1)S(1)} %copy-done.6, s32[1024]{0:T(1024)S(1)} %bitcast.54, s32[1024]{0:T(1024)S(1)} %fusion.46, ...), kind=kOutput, calls=%fused_computation.8 | convolution fusion | flops 1618999296 | bytes 7358464 | tf_op jit(solution)/shard_map/dot_general | solution.py:80
  77.8 2.4 %fusion.1 = (f32[1024]{0:T(1024)S(1)}, f32[1024]{0:T(1024)S(1)}, f32[1024]{0:T(1024)S(1)}) fusion(f32[1024,1024]{0,1:T(8,128)S(1)} %get-tuple-element.24, s32[1024]{0:T(1024)S(1)} %bitcast.55, s32[1024]{0:T(1024)S(1)} %fusion.46, f32[1024]{0:T(1024)S(1)} %get-tuple-element.7, pred[1024]{0:T(1024)(128)(4,1)S(1)} %copy-done.6, f32[1024]{0:T(1024)S(1)} %get-tuple-element.6, ...), kind=kLoop, calls=%fused_computation.4 | loop fusion | flops 9434112 | bytes 4225024 | tf_op jit(solution)/shard_map/reduce_sum | solution.py:92
  80.2 1.3 %select_reduce_fusion.4 = (f32[]{:T(128)}, f32[1024]{0:T(1024)S(1)}, f32[]{:T(128)}, f32[1024]{0:T(1024)S(1)}) fusion(f32[1024]{0:T(1024)S(1)} %get-tuple-element.7, f32[1024]{0:T(1024)S(1)} %get-tuple-element.4, f32[1024]{0:T(1024)S(1)} %get-tuple-element.3, f32[1024]{0:T(1024)S(1)} %get-tuple-element.6, f32[1024]{0:T(1024)S(1)} %get-tuple-element.5, ...), kind=kLoop, calls=%fused_computation.107 | loop fusion | flops 16382 | bytes 32780 | tf_op jit(solution)/shard_map/reduce_sum | solution.py:160
  81.5 0.6 copy-done.2
  82.1 0.6 dynamic_slice.31
  82.7 0.6 dynamic_slice.28
  83.3 3.2 %fusion.6 = bf16[128,768]{1,0:T(8,128)(2,1)} fusion(bf16[1024,768]{1,0:T(8,128)(2,1)S(1)} %constant_dynamic-update-slice_fusion, bf16[128,768]{1,0:T(8,128)(2,1)S(1)} %bitcast.51, f32[128]{0:T(128)} %dynamic_slice.31, f32[1024]{0:T(1024)} %copy-done.4, s32[128]{0:T(128)} %dynamic_slice.30, f32[]{:T(128)} %bitcast, s32[1024]{0:T(1024)S(1)} %bitcast.56, ...), kind=kOutput, calls=%fused_computation.18 | convolution fusion | flops 404815872 | bytes 1976452 | tf_op jit(solution)/shard_map/dot_general | solution.py:180
  86.5 3.4 %all-to-all-start.1 = ((bf16[4,32,768]{2,1,0:T(8,128)(2,1)}), bf16[4,32,768]{2,1,0:T(8,128)(2,1)S(1)}, u32[]{:S(2)}, u32[]{:S(2)}) async-start(bf16[4,32,768]{2,1,0:T(8,128)(2,1)} %bitcast.52), calls=%async_computation.1 | async-start | bytes 393216 | tf_op jit(solution)/shard_map/all_to_all | solution.py:184
  89.9 3.2 %fusion.5 = bf16[128,768]{1,0:T(8,128)(2,1)} fusion(bf16[1024,768]{1,0:T(8,128)(2,1)S(1)} %constant_dynamic-update-slice_fusion.8, bf16[128,768]{1,0:T(8,128)(2,1)S(1)} %copy-done, f32[1024]{0:T(1024)S(1)} %copy-done.3, f32[128]{0:T(128)} %dynamic_slice.28, s32[128]{0:T(128)} %fusion.55, f32[]{:T(128)} %bitcast, s32[1024]{0:T(1024)S(1)} %fusion.46, ...), kind=kOutput, calls=%fused_computation.17 | convolution fusion | flops 404815872 | bytes 1976452 | tf_op jit(solution)/shard_map/dot_general | solution.py:171
  94.4 0.8 all-to-all-done.1
  95.2 0.7 pad_maximum_fusion.1
  (48 shorter events, 0.4 us)
Async XLA Ops:
  0.6 21.4 %copy-start = (bf16[128,768]{1,0:T(8,128)(2,1)S(1)}, bf16[128,768]{1,0:T(8,128)(2,1)}, u32[]{:S(2)}) copy-start(bf16[128,768]{1,0:T(8,128)(2,1)} %param.6) | copy-start | bytes 589828
  0.6 44.0 %collective-permute-start.7 = (bf16[128,768]{1,0:T(8,128)(2,1)}, bf16[128,768]{1,0:T(8,128)(2,1)}, u32[]{:S(2)}, u32[]{:S(2)}) collective-permute-start(bf16[128,768]{1,0:T(8,128)(2,1)} %param.6), channel_id=1, source_target_pairs={{0,2},{2,4},{4,6},{6,7},{7,5},{5,3},{3,1},{1,0},{8,10},{10,12},{12... | collective-permute-start | bytes 589832 | tf_op jit(solution)/shard_map/ppermute | solution.py:73
  3.7 43.0 %collective-permute-start.11 = (bf16[128,768]{1,0:T(8,128)(2,1)}, bf16[128,768]{1,0:T(8,128)(2,1)}, u32[]{:S(2)}, u32[]{:S(2)}) collective-permute-start(bf16[128,768]{1,0:T(8,128)(2,1)} %param.6), channel_id=1, source_target_pairs={{0,1},{2,0},{4,2},{6,4},{7,6},{5,7},{3,5},{1,3},{8,9},{10,8},{12,1... | collective-permute-start | bytes 589832 | tf_op jit(solution)/shard_map/ppermute | solution.py:73
  14.3 27.0 %copy-start.7 = (f32[4]{0:T(128)S(1)}, f32[4]{0:T(128)}, u32[]{:S(2)}) copy-start(f32[4]{0:T(128)} %param.11) | copy-start | bytes 52
  14.3 27.6 %copy-start.1 = (s32[1,1024]{1,0:T(1,128)S(1)}, s32[1,1024]{1,0:T(1,128)}, u32[]{:S(2)}) copy-start(s32[1,1024]{1,0:T(1,128)} %param.10) | copy-start | bytes 12292
  15.1 27.5 %all-to-all-start = ((bf16[4,32,768]{2,1,0:T(8,128)(2,1)}), bf16[4,32,768]{2,1,0:T(8,128)(2,1)S(1)}, u32[]{:S(2)}, u32[]{:S(2)}) async-start(bf16[4,32,768]{2,1,0:T(8,128)(2,1)} %pad_maximum_fusion), calls=%async_computation | async-start | bytes 393216 | tf_op jit(solution)/shard_map/all_to_all | solution.py:118
  20.4 24.2 %copy-start.5 = (pred[1024]{0:T(1024)(128)(4,1)}, pred[1024]{0:T(1024)(128)(4,1)S(1)}, u32[]{:S(2)}) copy-start(pred[1024]{0:T(1024)(128)(4,1)S(1)} %iota_compare_fusion) | copy-start | bytes 3076
  42.5 7.8 %collective-permute-start = (bf16[128,768]{1,0:T(8,128)(2,1)S(1)}, bf16[128,768]{1,0:T(8,128)(2,1)S(1)}, u32[]{:S(2)}, u32[]{:S(2)}) collective-permute-start(bf16[128,768]{1,0:T(8,128)(2,1)S(1)} %bitcast.48), channel_id=1, source_target_pairs={{0,2},{2,4},{4,6},{6,7},{7,5},{5,3},{3,1},{1,0},{8,10},{10,12},{12... | collective-permute-start | bytes 589832 | tf_op jit(solution)/shard_map/ppermute | solution.py:73
  44.5 7.8 %collective-permute-start.4 = (bf16[128,768]{1,0:T(8,128)(2,1)S(1)}, bf16[128,768]{1,0:T(8,128)(2,1)S(1)}, u32[]{:S(2)}, u32[]{:S(2)}) collective-permute-start(bf16[128,768]{1,0:T(8,128)(2,1)S(1)} %bitcast.49), channel_id=1, source_target_pairs={{0,1},{2,0},{4,2},{6,4},{7,6},{5,7},{3,5},{1,3},{8,9},{10,8},{12,1... | collective-permute-start | bytes 589832 | tf_op jit(solution)/shard_map/ppermute | solution.py:73
  44.7 9.8 %collective-permute-start.8 = (bf16[128,768]{1,0:T(8,128)(2,1)}, bf16[128,768]{1,0:T(8,128)(2,1)S(1)}, u32[]{:S(2)}, u32[]{:S(2)}) collective-permute-start(bf16[128,768]{1,0:T(8,128)(2,1)} %collective-permute-done.7), channel_id=1, source_target_pairs={{0,2},{2,4},{4,6},{6,7},{7,5},{5,3},{3,1},{1,0},{8,10},{10,12},{12... | collective-permute-start | bytes 589832 | tf_op jit(solution)/shard_map/ppermute | solution.py:73
  46.8 9.8 %collective-permute-start.12 = (bf16[128,768]{1,0:T(8,128)(2,1)}, bf16[128,768]{1,0:T(8,128)(2,1)S(1)}, u32[]{:S(2)}, u32[]{:S(2)}) collective-permute-start(bf16[128,768]{1,0:T(8,128)(2,1)} %collective-permute-done.11), channel_id=1, source_target_pairs={{0,1},{2,0},{4,2},{6,4},{7,6},{5,7},{3,5},{1,3},{8,9},{10,8},{12,1... | collective-permute-start | bytes 589832 | tf_op jit(solution)/shard_map/ppermute | solution.py:73
  50.3 8.4 %collective-permute-start.1 = (bf16[128,768]{1,0:T(8,128)(2,1)S(1)}, bf16[128,768]{1,0:T(8,128)(2,1)S(1)}, u32[]{:S(2)}, u32[]{:S(2)}) collective-permute-start(bf16[128,768]{1,0:T(8,128)(2,1)S(1)} %collective-permute-done), channel_id=1, source_target_pairs={{0,2},{2,4},{4,6},{6,7},{7,5},{5,3},{3,1},{1,0},{8,10},{10,12},{12... | collective-permute-start | bytes 589832 | tf_op jit(solution)/shard_map/ppermute | solution.py:73
  52.3 8.4 %collective-permute-start.5 = (bf16[128,768]{1,0:T(8,128)(2,1)S(1)}, bf16[128,768]{1,0:T(8,128)(2,1)S(1)}, u32[]{:S(2)}, u32[]{:S(2)}) collective-permute-start(bf16[128,768]{1,0:T(8,128)(2,1)S(1)} %collective-permute-done.4), channel_id=1, source_target_pairs={{0,1},{2,0},{4,2},{6,4},{7,6},{5,7},{3,5},{1,3},{8,9},{10,8},{12,1... | collective-permute-start | bytes 589832 | tf_op jit(solution)/shard_map/ppermute | solution.py:73
  54.5 8.4 %collective-permute-start.9 = (bf16[128,768]{1,0:T(8,128)(2,1)S(1)}, bf16[128,768]{1,0:T(8,128)(2,1)S(1)}, u32[]{:S(2)}, u32[]{:S(2)}) collective-permute-start(bf16[128,768]{1,0:T(8,128)(2,1)S(1)} %collective-permute-done.8), channel_id=1, source_target_pairs={{0,2},{2,4},{4,6},{6,7},{7,5},{5,3},{3,1},{1,0},{8,10},{10,12},{12... | collective-permute-start | bytes 589832 | tf_op jit(solution)/shard_map/ppermute | solution.py:73
  56.5 15.8 %collective-permute-start.13 = (bf16[128,768]{1,0:T(8,128)(2,1)S(1)}, bf16[128,768]{1,0:T(8,128)(2,1)S(1)}, u32[]{:S(2)}, u32[]{:S(2)}) collective-permute-start(bf16[128,768]{1,0:T(8,128)(2,1)S(1)} %collective-permute-done.12), channel_id=1, source_target_pairs={{0,1},{2,0},{4,2},{6,4},{7,6},{5,7},{3,5},{1,3},{8,9},{10,8},{12,1... | collective-permute-start | bytes 589832 | tf_op jit(solution)/shard_map/ppermute | solution.py:73
  58.7 8.4 %collective-permute-start.2 = (bf16[128,768]{1,0:T(8,128)(2,1)S(1)}, bf16[128,768]{1,0:T(8,128)(2,1)S(1)}, u32[]{:S(2)}, u32[]{:S(2)}) collective-permute-start(bf16[128,768]{1,0:T(8,128)(2,1)S(1)} %collective-permute-done.1), channel_id=1, source_target_pairs={{0,2},{2,4},{4,6},{6,7},{7,5},{5,3},{3,1},{1,0},{8,10},{10,12},{12... | collective-permute-start | bytes 589832 | tf_op jit(solution)/shard_map/ppermute | solution.py:73
  60.7 14.6 %collective-permute-start.6 = (bf16[128,768]{1,0:T(8,128)(2,1)S(1)}, bf16[128,768]{1,0:T(8,128)(2,1)S(1)}, u32[]{:S(2)}, u32[]{:S(2)}) collective-permute-start(bf16[128,768]{1,0:T(8,128)(2,1)S(1)} %collective-permute-done.5), channel_id=1, source_target_pairs={{0,1},{2,0},{4,2},{6,4},{7,6},{5,7},{3,5},{1,3},{8,9},{10,8},{12,1... | collective-permute-start | bytes 589832 | tf_op jit(solution)/shard_map/ppermute | solution.py:73
  62.9 8.4 %collective-permute-start.10 = (bf16[128,768]{1,0:T(8,128)(2,1)S(1)}, bf16[128,768]{1,0:T(8,128)(2,1)S(1)}, u32[]{:S(2)}, u32[]{:S(2)}) collective-permute-start(bf16[128,768]{1,0:T(8,128)(2,1)S(1)} %collective-permute-done.9), channel_id=1, source_target_pairs={{0,2},{2,4},{4,6},{6,7},{7,5},{5,3},{3,1},{1,0},{8,10},{10,12},{12... | collective-permute-start | bytes 589832 | tf_op jit(solution)/shard_map/ppermute | solution.py:73
  67.1 8.1 %collective-permute-start.3 = (bf16[128,768]{1,0:T(8,128)(2,1)S(1)}, bf16[128,768]{1,0:T(8,128)(2,1)S(1)}, u32[]{:S(2)}, u32[]{:S(2)}) collective-permute-start(bf16[128,768]{1,0:T(8,128)(2,1)S(1)} %collective-permute-done.2), channel_id=1, source_target_pairs={{0,2},{2,4},{4,6},{6,7},{7,5},{5,3},{3,1},{1,0},{8,10},{10,12},{12... | collective-permute-start | bytes 589832 | tf_op jit(solution)/shard_map/ppermute | solution.py:73
  69.2 6.2 %copy-start.6 = (pred[1024]{0:T(1024)(128)(4,1)S(1)}, pred[1024]{0:T(1024)(128)(4,1)}, u32[]{:S(2)}) copy-start(pred[1024]{0:T(1024)(128)(4,1)} %copy-done.5) | copy-start | bytes 3076
  81.5 0.6 copy-start.2
  81.5 1.8 %copy-start.4 = (f32[1024]{0:T(1024)}, f32[1024]{0:T(1024)S(1)}, u32[]{:S(2)}) copy-start(f32[1024]{0:T(1024)S(1)} %get-tuple-element.26) | copy-start | bytes 12292
  83.3 6.6 %copy-start.3 = (f32[1024]{0:T(1024)S(1)}, f32[1024]{0:T(1024)}, u32[]{:S(2)}) copy-start(f32[1024]{0:T(1024)} %copy-done.2) | copy-start | bytes 12292
  86.5 8.6 %all-to-all-start.1 = ((bf16[4,32,768]{2,1,0:T(8,128)(2,1)}), bf16[4,32,768]{2,1,0:T(8,128)(2,1)S(1)}, u32[]{:S(2)}, u32[]{:S(2)}) async-start(bf16[4,32,768]{2,1,0:T(8,128)(2,1)} %bitcast.52), calls=%async_computation.1 | async-start | bytes 393216 | tf_op jit(solution)/shard_map/all_to_all | solution.py:184

commit v8 on v2

--- a/solution.py
+++ b/solution.py
@@ -171,7 +171,7 @@
     )
     grad_local = (own_terms * inv_root).astype(jnp.bfloat16)
     returned = lax.all_to_all(
-        grad_local.reshape(1, row_count, emb_width), "lang", split_axis=1, concat_axis=0, tiled=True
+        grad_local.reshape(lang_size, per_slot, emb_width), "lang", split_axis=0, concat_axis=0, tiled=True
     )
     grad_tgt = returned[slot_group]
     return (grad_src, grad_tgt, pair_loss)

time: 87.2 us -> 83.8 us (0.961)
  local copies, waits for them, and re-layouts: 15.1 us -> 12.9 us
  other arithmetic: 8.42 us -> 7.11 us
  matrix products: 7.97 us -> 9.15 us
  waiting for transfers between devices: 17.7 us -> 16.7 us
    unnamed x40 -> x24, local copies, waits for them, and re-layouts: 2.12 us -> 0.06 us
    unnamed x1 -> x0, other arithmetic: 1.8 us -> none
    reshape x1 -> x0, local copies, waits for them, and re-layouts: 1.28 us -> none  [per_device(): grad_local.reshape(1, row_count, emb_width)]
    dot_general x1, matrix products: 2.44 us -> 3.48 us  [per_device(): jnp.dot(g_rows, y_all, preferred_element_type=jnp.float32) * inv_root]
    all_to_all x1, waiting for transfers between devices: 1.44 us -> 0.45 us  [per_device(): lax.all_to_all(grad_local.reshape(lang_size, per_slot, emb_width), 'lang'...]
  transfers between devices with their start and end apart: 16 -> 16, of which waited for: 8 -> 8; matrix products, arithmetic and copies ran while one was open for 17% -> 19% of each run, Pallas kernels for 0% -> 0%
where the time goes in v8:
time: 83.8 us; the launch traced here: 83.1 us
  starting transfers between devices  24.1 us (29%)
  waiting for transfers between devices  16.7 us (20%)
  between operations  13.1 us (16%)
  local copies, waits for them, and re-layouts  12.9 us (15%)
  matrix products  9.15 us (11%)
  other arithmetic  7.11 us (8%)
    ppermute x14, starting transfers between devices, ring_gather(): cur = lax.ppermute(cur, 'dp', pairs)  17.3 us
    ppermute x14, waiting for transfers between devices, ring_gather(): cur = lax.ppermute(cur, 'dp', pairs)  16.3 us
    dot_general x1, matrix products, per_device(): jnp.dot(g_rows, y_all, preferred_element_type=jnp.float32) * inv_root  3.48 us
    all_to_all x1, starting transfers between devices, per_device(): lax.all_to_all(ordered, 'lang', split_axis=0, concat_axis=1, tiled=True)  3.37 us
    all_to_all x1, starting transfers between devices, per_device(): lax.all_to_all(grad_local.reshape(lang_size, per_slot, emb_width), 'lang'...  3.37 us
    dot_general x1, matrix products, per_device(): lax.dot_general(g_cols, x_all, (((0,), (0,)), ((), ())), preferred_elemen...  3.26 us
    reduce_sum x1, other arithmetic, block_stats(): pos_score = jnp.sum(jnp.where(is_pos, scores_f, 0.0), axis=1)  2.43 us
    dot_general x1, matrix products, scores_of(): lax.dot_general(x_rows, y_rows, (((1,), (1,)), ((), ())), preferred_eleme...  2.4 us
  transfers between devices with their start and end apart: 16, of which 8 were waited for; matrix products, arithmetic and copies ran while one was open for 19% of the time, Pallas kernels for 0%

profile of v8, /device:TPU:0, one launch (start us, length us, event | category | flops | bytes accessed | tf_op | source)
XLA Modules:
  0.0 83.1 jit_solution(17320377136904404180)
XLA Ops:
  0.7 3.1 %collective-permute-start.7 = (bf16[128,768]{1,0:T(8,128)(2,1)}, bf16[128,768]{1,0:T(8,128)(2,1)}, u32[]{:S(2)}, u32[]{:S(2)}) collective-permute-start(bf16[128,768]{1,0:T(8,128)(2,1)} %param.10), channel_id=1, source_target_pairs={{0,2},{2,4},{4,6},{6,7},{7,5},{5,3},{3,1},{1,0},{8,10},{10,12},{12... | collective-permute-start | bytes 589832 | tf_op jit(solution)/shard_map/ppermute | solution.py:60
  3.8 0.7 compare_select_fusion.5
  4.5 0.6 scatter_custom_fusion
  5.1 1.2 %gather_fusion = bf16[4,32,768]{2,1,0:T(8,128)(2,1)} fusion(bf16[4,32,768]{2,1,0:T(8,128)(2,1)S(1)} %copy-done, s32[1024]{0:T(1024)S(1)} %pad_clamp_fusion.1), kind=kCustom, calls=%fused_computation | custom fusion | bytes 393232 | tf_op jit(solution)/shard_map/gather | solution.py:106
  6.3 3.4 %all-to-all-start = ((bf16[4,32,768]{2,1,0:T(8,128)(2,1)}), bf16[4,32,768]{2,1,0:T(8,128)(2,1)S(1)}, u32[]{:S(2)}, u32[]{:S(2)}) async-start(bf16[4,32,768]{2,1,0:T(8,128)(2,1)} %gather_fusion), calls=%async_computation | async-start | bytes 393216 | tf_op jit(solution)/shard_map/all_to_all | solution.py:107
  9.7 1.3 %dynamic_slice.73 = s32[1]{0:T(128)} dynamic-slice(s32[4]{0:T(128)} %param.13, s32[]{:T(128)S(6)} %select_n.250), dynamic_slice_sizes={1} | dynamic-slice | bytes 12 | tf_op jit(solution)/shard_map/dynamic_slice | solution.py:109
  11.0 0.6 iota_compare_fusion
  11.6 1.5 %convert_reduce_fusion = s32[1024]{0:T(1024)S(1)} fusion(s32[1024]{0:T(1024)} %bitcast.43, s32[1024]{0:T(1024)S(1)} %fusion.46, pred[1024]{0:T(1024)(128)(4,1)S(1)} %iota_compare_fusion), kind=kLoop, calls=%fused_computation.12 | loop fusion | flops 4193280 | bytes 13312 | tf_op jit(solution)/shard_map/reduce_max | solution.py:116
  13.2 0.1 broadcast.195.clone.1
  13.4 0.6 dynamic_slice.75
  18.6 0.7 fusion.66
  24.3 0.7 dynamic_slice.94
  25.0 0.6 dynamic_slice.74
  25.6 0.6 dynamic_slice.93
  26.1 0.6 dynamic_slice.72
  26.8 0.5 fusion.55
  27.3 2.0 %collective-permute-start = (bf16[128,768]{1,0:T(8,128)(2,1)S(1)}, bf16[128,768]{1,0:T(8,128)(2,1)S(1)}, u32[]{:S(2)}, u32[]{:S(2)}) collective-permute-start(bf16[128,768]{1,0:T(8,128)(2,1)S(1)} %bitcast.38), channel_id=1, source_target_pairs={{0,2},{2,4},{4,6},{6,7},{7,5},{5,3},{3,1},{1,0},{8,10},{10,12},{12... | collective-permute-start | bytes 589832 | tf_op jit(solution)/shard_map/ppermute | solution.py:60
  29.3 0.0 collective-permute-start.4
  29.3 0.1 broadcast.195.clone
  29.5 2.1 %collective-permute-start.8 = (bf16[128,768]{1,0:T(8,128)(2,1)}, bf16[128,768]{1,0:T(8,128)(2,1)S(1)}, u32[]{:S(2)}, u32[]{:S(2)}) collective-permute-start(bf16[128,768]{1,0:T(8,128)(2,1)} %collective-permute-done.7), channel_id=1, source_target_pairs={{0,2},{2,4},{4,6},{6,7},{7,5},{5,3},{3,1},{1,0},{8,10},{10,12},{12... | collective-permute-start | bytes 589832 | tf_op jit(solution)/shard_map/ppermute | solution.py:60
  31.6 0.0 collective-permute-start.12
  31.6 1.0 %constant_dynamic-update-slice_fusion.1 = bf16[1024,768]{1,0:T(8,128)(2,1)S(1)} fusion(bf16[1024,768]{1,0:T(8,128)(2,1)S(1)} %constant_dynamic-update-slice_fusion.7, bf16[128,768]{1,0:T(8,128)(2,1)} %collective-permute-done.7, s32[]{:T(128)S(6)} %select_n.261), kind=kLoop, calls=%fused_computation.74 | loop fusion | bytes 393220 | tf_op jit(solution)/shard_map/dynamic_update_slice | solution.py:62
  32.5 2.5 %collective-permute-done = bf16[128,768]{1,0:T(8,128)(2,1)S(1)} collective-permute-done((bf16[128,768]{1,0:T(8,128)(2,1)S(1)}, bf16[128,768]{1,0:T(8,128)(2,1)S(1)}, u32[]{:S(2)}, u32[]{:S(2)}) %collective-permute-start) | collective-permute-done | bytes 196640 | tf_op jit(solution)/shard_map/ppermute | solution.py:60
  35.1 2.0 %collective-permute-start.1 = (bf16[128,768]{1,0:T(8,128)(2,1)S(1)}, bf16[128,768]{1,0:T(8,128)(2,1)S(1)}, u32[]{:S(2)}, u32[]{:S(2)}) collective-permute-start(bf16[128,768]{1,0:T(8,128)(2,1)S(1)} %collective-permute-done), channel_id=1, source_target_pairs={{0,2},{2,4},{4,6},{6,7},{7,5},{5,3},{3,1},{1,0},{8,10},{10,12},{12... | collective-permute-start | bytes 589832 | tf_op jit(solution)/shard_map/ppermute | solution.py:60
  37.1 0.0 collective-permute-start.5
  37.1 2.2 %collective-permute-done.8 = bf16[128,768]{1,0:T(8,128)(2,1)S(1)} collective-permute-done((bf16[128,768]{1,0:T(8,128)(2,1)}, bf16[128,768]{1,0:T(8,128)(2,1)S(1)}, u32[]{:S(2)}, u32[]{:S(2)}) %collective-permute-start.8) | collective-permute-done | bytes 196640 | tf_op jit(solution)/shard_map/ppermute | solution.py:60
  39.3 2.0 %collective-permute-start.9 = (bf16[128,768]{1,0:T(8,128)(2,1)S(1)}, bf16[128,768]{1,0:T(8,128)(2,1)S(1)}, u32[]{:S(2)}, u32[]{:S(2)}) collective-permute-start(bf16[128,768]{1,0:T(8,128)(2,1)S(1)} %collective-permute-done.8), channel_id=1, source_target_pairs={{0,2},{2,4},{4,6},{6,7},{7,5},{5,3},{3,1},{1,0},{8,10},{10,12},{12... | collective-permute-start | bytes 589832 | tf_op jit(solution)/shard_map/ppermute | solution.py:60
  41.3 0.0 collective-permute-start.13
  41.4 2.2 %collective-permute-done.1 = bf16[128,768]{1,0:T(8,128)(2,1)S(1)} collective-permute-done((bf16[128,768]{1,0:T(8,128)(2,1)S(1)}, bf16[128,768]{1,0:T(8,128)(2,1)S(1)}, u32[]{:S(2)}, u32[]{:S(2)}) %collective-permute-start.1) | collective-permute-done | bytes 196640 | tf_op jit(solution)/shard_map/ppermute | solution.py:60
  43.5 2.0 %collective-permute-start.2 = (bf16[128,768]{1,0:T(8,128)(2,1)S(1)}, bf16[128,768]{1,0:T(8,128)(2,1)S(1)}, u32[]{:S(2)}, u32[]{:S(2)}) collective-permute-start(bf16[128,768]{1,0:T(8,128)(2,1)S(1)} %collective-permute-done.1), channel_id=1, source_target_pairs={{0,2},{2,4},{4,6},{6,7},{7,5},{5,3},{3,1},{1,0},{8,10},{10,12},{12... | collective-permute-start | bytes 589832 | tf_op jit(solution)/shard_map/ppermute | solution.py:60
  45.5 0.0 collective-permute-start.6
  45.6 2.2 %collective-permute-done.9 = bf16[128,768]{1,0:T(8,128)(2,1)S(1)} collective-permute-done((bf16[128,768]{1,0:T(8,128)(2,1)S(1)}, bf16[128,768]{1,0:T(8,128)(2,1)S(1)}, u32[]{:S(2)}, u32[]{:S(2)}) %collective-permute-start.9) | collective-permute-done | bytes 196640 | tf_op jit(solution)/shard_map/ppermute | solution.py:60
  47.7 2.0 %collective-permute-start.10 = (bf16[128,768]{1,0:T(8,128)(2,1)S(1)}, bf16[128,768]{1,0:T(8,128)(2,1)S(1)}, u32[]{:S(2)}, u32[]{:S(2)}) collective-permute-start(bf16[128,768]{1,0:T(8,128)(2,1)S(1)} %collective-permute-done.9), channel_id=1, source_target_pairs={{0,2},{2,4},{4,6},{6,7},{7,5},{5,3},{3,1},{1,0},{8,10},{10,12},{12... | collective-permute-start | bytes 589832 | tf_op jit(solution)/shard_map/ppermute | solution.py:60
  49.8 2.2 %collective-permute-done.2 = bf16[128,768]{1,0:T(8,128)(2,1)S(1)} collective-permute-done((bf16[128,768]{1,0:T(8,128)(2,1)S(1)}, bf16[128,768]{1,0:T(8,128)(2,1)S(1)}, u32[]{:S(2)}, u32[]{:S(2)}) %collective-permute-start.2) | collective-permute-done | bytes 196640 | tf_op jit(solution)/shard_map/ppermute | solution.py:60
  51.9 2.0 %collective-permute-start.3 = (bf16[128,768]{1,0:T(8,128)(2,1)S(1)}, bf16[128,768]{1,0:T(8,128)(2,1)S(1)}, u32[]{:S(2)}, u32[]{:S(2)}) collective-permute-start(bf16[128,768]{1,0:T(8,128)(2,1)S(1)} %collective-permute-done.2), channel_id=1, source_target_pairs={{0,2},{2,4},{4,6},{6,7},{7,5},{5,3},{3,1},{1,0},{8,10},{10,12},{12... | collective-permute-start | bytes 589832 | tf_op jit(solution)/shard_map/ppermute | solution.py:60
  54.0 2.2 %collective-permute-done.10 = bf16[128,768]{1,0:T(8,128)(2,1)S(1)} collective-permute-done((bf16[128,768]{1,0:T(8,128)(2,1)S(1)}, bf16[128,768]{1,0:T(8,128)(2,1)S(1)}, u32[]{:S(2)}, u32[]{:S(2)}) %collective-permute-start.10) | collective-permute-done | bytes 196640 | tf_op jit(solution)/shard_map/ppermute | solution.py:60
  56.2 0.9 %constant_dynamic-update-slice_fusion.2 = bf16[1024,768]{1,0:T(8,128)(2,1)S(1)} fusion(bf16[1024,768]{1,0:T(8,128)(2,1)S(1)} %constant_dynamic-update-slice_fusion.3, bf16[128,768]{1,0:T(8,128)(2,1)} %collective-permute-done.11, s32[]{:T(128)S(6)} %select_n.273), kind=kLoop, calls=%fused_computation.75 | loop fusion | bytes 393220 | tf_op jit(solution)/shard_map/dynamic_update_slice | solution.py:62
  57.2 2.9 %collective-permute-done.3 = bf16[128,768]{1,0:T(8,128)(2,1)S(1)} collective-permute-done((bf16[128,768]{1,0:T(8,128)(2,1)S(1)}, bf16[128,768]{1,0:T(8,128)(2,1)S(1)}, u32[]{:S(2)}, u32[]{:S(2)}) %collective-permute-start.3) | collective-permute-done | bytes 196640 | tf_op jit(solution)/shard_map/ppermute | solution.py:60
  60.2 2.4 %select_reduce_fusion.3 = (f32[1024]{0:T(1024)S(1)}, f32[1024]{0:T(1024)S(1)}, f32[1024,1024]{0,1:T(8,128)S(1)}) fusion(pred[1024]{0:T(1024)(128)(4,1)S(1)} %copy-done.5, pred[1024]{0:T(1024)(128)(4,1)S(1)} %copy-done.9, s32[1024]{0:T(1024)S(1)} %bitcast.44, s32[1024]{0:T(1024)S(1)} %fusion.46, ...), kind=kOutput, calls=%fused_computation.11 | convolution fusion | flops 1618999296 | bytes 7358464 | tf_op jit(solution)/shard_map/dot_general | solution.py:67
  62.6 2.4 %fusion.1 = (f32[1024]{0:T(1024)S(1)}, f32[1024]{0:T(1024)S(1)}, f32[1024]{0:T(1024)S(1)}) fusion(f32[1024,1024]{0,1:T(8,128)S(1)} %get-tuple-element.19, s32[1024]{0:T(1024)S(1)} %bitcast.45, s32[1024]{0:T(1024)S(1)} %fusion.46, f32[1024]{0:T(1024)S(1)} %get-tuple-element.7, pred[1024]{0:T(1024)(128)(4,1)S(1)} %copy-done.9, f32[1024]{0:T(1024)S(1)} %get-tuple-element.6, ...), kind=kLoop, calls=%fused_computation.7 | loop fusion | flops 9434112 | bytes 4225024 | tf_op jit(solution)/shard_map/reduce_sum | solution.py:79
  65.1 1.9 %select_reduce_fusion.4 = (f32[]{:T(128)}, f32[1024]{0:T(1024)S(1)}, f32[]{:T(128)}, f32[1024]{0:T(1024)}) fusion(f32[1024]{0:T(1024)S(1)} %get-tuple-element.7, f32[1024]{0:T(1024)S(1)} %get-tuple-element.4, f32[1024]{0:T(1024)S(1)} %get-tuple-element.3, f32[1024]{0:T(1024)S(1)} %get-tuple-element.6, f32[1024]{0:T(1024)S(1)} %get-tuple-element.5, ...), kind=kLoop, calls=%fused_computation.102 | loop fusion | flops 16382 | bytes 32780 | tf_op jit(solution)/shard_map/reduce_sum | solution.py:149
  66.9 0.6 dynamic_slice.95
  67.5 1.3 %dynamic_slice.92 = f32[128]{0:T(128)} dynamic-slice(f32[1024]{0:T(1024)} %get-tuple-element.21, s32[]{:T(128)S(6)} %select_n.251), dynamic_slice_sizes={128} | dynamic-slice | bytes 1028 | tf_op jit(solution)/shard_map/dynamic_slice | solution.py:155
  68.8 3.3 %fusion.6 = bf16[128,768]{1,0:T(8,128)(2,1)} fusion(bf16[1024,768]{1,0:T(8,128)(2,1)S(1)} %constant_dynamic-update-slice_fusion.6, bf16[128,768]{1,0:T(8,128)(2,1)S(1)} %bitcast.41, f32[128]{0:T(128)} %dynamic_slice.95, f32[1024]{0:T(1024)} %get-tuple-element.21, s32[128]{0:T(128)} %dynamic_slice.94, f32[]{:T(128)} %bitcast, s32[1024]{0:T(1024)S(1)} %bitcast.46, ...), kind=kOutput, calls=%fused_computation.21 | convolution fusion | flops 404815872 | bytes 1976452 | tf_op jit(solution)/shard_map/dot_general | solution.py:169
  72.1 3.4 %all-to-all-start.1 = ((bf16[4,32,768]{2,1,0:T(8,128)(2,1)}), bf16[4,32,768]{2,1,0:T(8,128)(2,1)S(1)}, u32[]{:S(2)}, u32[]{:S(2)}) async-start(bf16[4,32,768]{2,1,0:T(8,128)(2,1)} %bitcast.42), calls=%async_computation.1 | async-start | bytes 393216 | tf_op jit(solution)/shard_map/all_to_all | solution.py:173
  75.5 3.5 %fusion.5 = bf16[128,768]{1,0:T(8,128)(2,1)} fusion(bf16[1024,768]{1,0:T(8,128)(2,1)S(1)} %constant_dynamic-update-slice_fusion.8, bf16[128,768]{1,0:T(8,128)(2,1)} %param.10, f32[1024]{0:T(1024)} %copy-done.7, f32[128]{0:T(128)} %dynamic_slice.92, s32[128]{0:T(128)} %fusion.55, f32[]{:T(128)} %bitcast, s32[1024]{0:T(1024)S(1)} %fusion.46, ...), kind=kOutput, calls=%fused_computation.20 | convolution fusion | flops 404815872 | bytes 1976452 | tf_op jit(solution)/shard_map/dot_general | solution.py:160
  80.3 0.5 all-to-all-done.1
  80.7 1.2 %gather_fusion.1 = bf16[4,32,768]{2,1,0:T(8,128)(2,1)} fusion(bf16[4,32,768]{2,1,0:T(8,128)(2,1)S(1)} %all-to-all-done.1, s32[1024]{0:T(1024)S(1)} %pad_clamp_fusion), kind=kCustom, calls=%fused_computation.1 | custom fusion | bytes 393232 | tf_op jit(solution)/shard_map/gather | solution.py:176
  (53 shorter events, 0.4 us)
Async XLA Ops:
  0.6 4.5 %copy-start = (bf16[4,32,768]{2,1,0:T(8,128)(2,1)S(1)}, bf16[4,32,768]{2,1,0:T(8,128)(2,1)}, u32[]{:S(2)}) copy-start(bf16[4,32,768]{2,1,0:T(8,128)(2,1)} %param.11) | copy-start | bytes 589828
  0.6 12.7 %copy-start.11 = (s32[8]{0:T(128)S(1)}, s32[8]{0:T(128)}, u32[]{:S(2)}) copy-start(s32[8]{0:T(128)} %constant.220.clone) | copy-start | bytes 100
  0.7 18.0 %copy-start.2 = (s32[8]{0:T(128)S(1)}, s32[8]{0:T(128)}, u32[]{:S(2)}) copy-start(s32[8]{0:T(128)} %constant.219.clone) | copy-start | bytes 100
  0.7 12.6 %copy-start.1 = (bf16[128,768]{1,0:T(8,128)(2,1)S(1)}, bf16[128,768]{1,0:T(8,128)(2,1)}, u32[]{:S(2)}) copy-start(bf16[128,768]{1,0:T(8,128)(2,1)} %param.10) | copy-start | bytes 589828
  0.7 25.5 %copy-start.10 = (f32[4]{0:T(128)S(1)}, f32[4]{0:T(128)}, u32[]{:S(2)}) copy-start(f32[4]{0:T(128)} %param.15) | copy-start | bytes 52
  0.7 28.8 %collective-permute-start.7 = (bf16[128,768]{1,0:T(8,128)(2,1)}, bf16[128,768]{1,0:T(8,128)(2,1)}, u32[]{:S(2)}, u32[]{:S(2)}) collective-permute-start(bf16[128,768]{1,0:T(8,128)(2,1)} %param.10), channel_id=1, source_target_pairs={{0,2},{2,4},{4,6},{6,7},{7,5},{5,3},{3,1},{1,0},{8,10},{10,12},{12... | collective-permute-start | bytes 589832 | tf_op jit(solution)/shard_map/ppermute | solution.py:60
  3.8 27.8 %collective-permute-start.11 = (bf16[128,768]{1,0:T(8,128)(2,1)}, bf16[128,768]{1,0:T(8,128)(2,1)}, u32[]{:S(2)}, u32[]{:S(2)}) collective-permute-start(bf16[128,768]{1,0:T(8,128)(2,1)} %param.10), channel_id=1, source_target_pairs={{0,1},{2,0},{4,2},{6,4},{7,6},{5,7},{3,5},{1,3},{8,9},{10,8},{12,1... | collective-permute-start | bytes 589832 | tf_op jit(solution)/shard_map/ppermute | solution.py:60
  5.1 21.7 %copy-start.3 = (s32[1,1024]{1,0:T(1,128)S(1)}, s32[1,1024]{1,0:T(1,128)}, u32[]{:S(2)}) copy-start(s32[1,1024]{1,0:T(1,128)} %param.14) | copy-start | bytes 12292
  6.3 21.0 %all-to-all-start = ((bf16[4,32,768]{2,1,0:T(8,128)(2,1)}), bf16[4,32,768]{2,1,0:T(8,128)(2,1)S(1)}, u32[]{:S(2)}, u32[]{:S(2)}) async-start(bf16[4,32,768]{2,1,0:T(8,128)(2,1)} %gather_fusion), calls=%async_computation | async-start | bytes 393216 | tf_op jit(solution)/shard_map/all_to_all | solution.py:107
  11.6 17.7 %copy-start.8 = (pred[1024]{0:T(1024)(128)(4,1)}, pred[1024]{0:T(1024)(128)(4,1)S(1)}, u32[]{:S(2)}) copy-start(pred[1024]{0:T(1024)(128)(4,1)S(1)} %iota_compare_fusion) | copy-start | bytes 3076
  13.2 16.2 %copy-start.4 = (pred[1024]{0:T(1024)(128)(4,1)}, pred[1024]{0:T(1024)(128)(4,1)S(1)}, u32[]{:S(2)}) copy-start(pred[1024]{0:T(1024)(128)(4,1)S(1)} %broadcast_compare_fusion) | copy-start | bytes 3076
  27.3 7.8 %collective-permute-start = (bf16[128,768]{1,0:T(8,128)(2,1)S(1)}, bf16[128,768]{1,0:T(8,128)(2,1)S(1)}, u32[]{:S(2)}, u32[]{:S(2)}) collective-permute-start(bf16[128,768]{1,0:T(8,128)(2,1)S(1)} %bitcast.38), channel_id=1, source_target_pairs={{0,2},{2,4},{4,6},{6,7},{7,5},{5,3},{3,1},{1,0},{8,10},{10,12},{12... | collective-permute-start | bytes 589832 | tf_op jit(solution)/shard_map/ppermute | solution.py:60
  29.3 7.8 %collective-permute-start.4 = (bf16[128,768]{1,0:T(8,128)(2,1)S(1)}, bf16[128,768]{1,0:T(8,128)(2,1)S(1)}, u32[]{:S(2)}, u32[]{:S(2)}) collective-permute-start(bf16[128,768]{1,0:T(8,128)(2,1)S(1)} %bitcast.39), channel_id=1, source_target_pairs={{0,1},{2,0},{4,2},{6,4},{7,6},{5,7},{3,5},{1,3},{8,9},{10,8},{12,1... | collective-permute-start | bytes 589832 | tf_op jit(solution)/shard_map/ppermute | solution.py:60
  29.5 9.8 %collective-permute-start.8 = (bf16[128,768]{1,0:T(8,128)(2,1)}, bf16[128,768]{1,0:T(8,128)(2,1)S(1)}, u32[]{:S(2)}, u32[]{:S(2)}) collective-permute-start(bf16[128,768]{1,0:T(8,128)(2,1)} %collective-permute-done.7), channel_id=1, source_target_pairs={{0,2},{2,4},{4,6},{6,7},{7,5},{5,3},{3,1},{1,0},{8,10},{10,12},{12... | collective-permute-start | bytes 589832 | tf_op jit(solution)/shard_map/ppermute | solution.py:60
  31.6 9.8 %collective-permute-start.12 = (bf16[128,768]{1,0:T(8,128)(2,1)}, bf16[128,768]{1,0:T(8,128)(2,1)S(1)}, u32[]{:S(2)}, u32[]{:S(2)}) collective-permute-start(bf16[128,768]{1,0:T(8,128)(2,1)} %collective-permute-done.11), channel_id=1, source_target_pairs={{0,1},{2,0},{4,2},{6,4},{7,6},{5,7},{3,5},{1,3},{8,9},{10,8},{12,1... | collective-permute-start | bytes 589832 | tf_op jit(solution)/shard_map/ppermute | solution.py:60
  35.1 8.4 %collective-permute-start.1 = (bf16[128,768]{1,0:T(8,128)(2,1)S(1)}, bf16[128,768]{1,0:T(8,128)(2,1)S(1)}, u32[]{:S(2)}, u32[]{:S(2)}) collective-permute-start(bf16[128,768]{1,0:T(8,128)(2,1)S(1)} %collective-permute-done), channel_id=1, source_target_pairs={{0,2},{2,4},{4,6},{6,7},{7,5},{5,3},{3,1},{1,0},{8,10},{10,12},{12... | collective-permute-start | bytes 589832 | tf_op jit(solution)/shard_map/ppermute | solution.py:60
  37.1 8.4 %collective-permute-start.5 = (bf16[128,768]{1,0:T(8,128)(2,1)S(1)}, bf16[128,768]{1,0:T(8,128)(2,1)S(1)}, u32[]{:S(2)}, u32[]{:S(2)}) collective-permute-start(bf16[128,768]{1,0:T(8,128)(2,1)S(1)} %collective-permute-done.4), channel_id=1, source_target_pairs={{0,1},{2,0},{4,2},{6,4},{7,6},{5,7},{3,5},{1,3},{8,9},{10,8},{12,1... | collective-permute-start | bytes 589832 | tf_op jit(solution)/shard_map/ppermute | solution.py:60
  39.3 8.4 %collective-permute-start.9 = (bf16[128,768]{1,0:T(8,128)(2,1)S(1)}, bf16[128,768]{1,0:T(8,128)(2,1)S(1)}, u32[]{:S(2)}, u32[]{:S(2)}) collective-permute-start(bf16[128,768]{1,0:T(8,128)(2,1)S(1)} %collective-permute-done.8), channel_id=1, source_target_pairs={{0,2},{2,4},{4,6},{6,7},{7,5},{5,3},{3,1},{1,0},{8,10},{10,12},{12... | collective-permute-start | bytes 589832 | tf_op jit(solution)/shard_map/ppermute | solution.py:60
  41.3 15.8 %collective-permute-start.13 = (bf16[128,768]{1,0:T(8,128)(2,1)S(1)}, bf16[128,768]{1,0:T(8,128)(2,1)S(1)}, u32[]{:S(2)}, u32[]{:S(2)}) collective-permute-start(bf16[128,768]{1,0:T(8,128)(2,1)S(1)} %collective-permute-done.12), channel_id=1, source_target_pairs={{0,1},{2,0},{4,2},{6,4},{7,6},{5,7},{3,5},{1,3},{8,9},{10,8},{12,1... | collective-permute-start | bytes 589832 | tf_op jit(solution)/shard_map/ppermute | solution.py:60
  43.5 8.4 %collective-permute-start.2 = (bf16[128,768]{1,0:T(8,128)(2,1)S(1)}, bf16[128,768]{1,0:T(8,128)(2,1)S(1)}, u32[]{:S(2)}, u32[]{:S(2)}) collective-permute-start(bf16[128,768]{1,0:T(8,128)(2,1)S(1)} %collective-permute-done.1), channel_id=1, source_target_pairs={{0,2},{2,4},{4,6},{6,7},{7,5},{5,3},{3,1},{1,0},{8,10},{10,12},{12... | collective-permute-start | bytes 589832 | tf_op jit(solution)/shard_map/ppermute | solution.py:60
  45.5 14.6 %collective-permute-start.6 = (bf16[128,768]{1,0:T(8,128)(2,1)S(1)}, bf16[128,768]{1,0:T(8,128)(2,1)S(1)}, u32[]{:S(2)}, u32[]{:S(2)}) collective-permute-start(bf16[128,768]{1,0:T(8,128)(2,1)S(1)} %collective-permute-done.5), channel_id=1, source_target_pairs={{0,1},{2,0},{4,2},{6,4},{7,6},{5,7},{3,5},{1,3},{8,9},{10,8},{12,1... | collective-permute-start | bytes 589832 | tf_op jit(solution)/shard_map/ppermute | solution.py:60
  47.7 8.4 %collective-permute-start.10 = (bf16[128,768]{1,0:T(8,128)(2,1)S(1)}, bf16[128,768]{1,0:T(8,128)(2,1)S(1)}, u32[]{:S(2)}, u32[]{:S(2)}) collective-permute-start(bf16[128,768]{1,0:T(8,128)(2,1)S(1)} %collective-permute-done.9), channel_id=1, source_target_pairs={{0,2},{2,4},{4,6},{6,7},{7,5},{5,3},{3,1},{1,0},{8,10},{10,12},{12... | collective-permute-start | bytes 589832 | tf_op jit(solution)/shard_map/ppermute | solution.py:60
  51.9 8.1 %collective-permute-start.3 = (bf16[128,768]{1,0:T(8,128)(2,1)S(1)}, bf16[128,768]{1,0:T(8,128)(2,1)S(1)}, u32[]{:S(2)}, u32[]{:S(2)}) collective-permute-start(bf16[128,768]{1,0:T(8,128)(2,1)S(1)} %collective-permute-done.2), channel_id=1, source_target_pairs={{0,2},{2,4},{4,6},{6,7},{7,5},{5,3},{3,1},{1,0},{8,10},{10,12},{12... | collective-permute-start | bytes 589832 | tf_op jit(solution)/shard_map/ppermute | solution.py:60
  54.0 6.2 %copy-start.5 = (pred[1024]{0:T(1024)(128)(4,1)S(1)}, pred[1024]{0:T(1024)(128)(4,1)}, u32[]{:S(2)}) copy-start(pred[1024]{0:T(1024)(128)(4,1)} %copy-done.4) | copy-start | bytes 3076
  54.0 6.2 %copy-start.9 = (pred[1024]{0:T(1024)(128)(4,1)S(1)}, pred[1024]{0:T(1024)(128)(4,1)}, u32[]{:S(2)}) copy-start(pred[1024]{0:T(1024)(128)(4,1)} %copy-done.8) | copy-start | bytes 3076
  66.9 1.9 %copy-start.7 = (f32[1024]{0:T(1024)}, f32[1024]{0:T(1024)S(1)}, u32[]{:S(2)}) copy-start(f32[1024]{0:T(1024)S(1)} %get-tuple-element.9) | copy-start | bytes 12292
  68.8 6.6 %copy-start.6 = (pred[1024]{0:T(1024)(128)(4,1)S(1)}, pred[1024]{0:T(1024)(128)(4,1)}, u32[]{:S(2)}) copy-start(pred[1024]{0:T(1024)(128)(4,1)} %copy-done.4) | copy-start | bytes 3076
  72.1 8.6 %all-to-all-start.1 = ((bf16[4,32,768]{2,1,0:T(8,128)(2,1)}), bf16[4,32,768]{2,1,0:T(8,128)(2,1)S(1)}, u32[]{:S(2)}, u32[]{:S(2)}) async-start(bf16[4,32,768]{2,1,0:T(8,128)(2,1)} %bitcast.42), calls=%async_computation.1 | async-start | bytes 393216 | tf_op jit(solution)/shard_map/all_to_all | solution.py:173

commit v9 on v8

--- a/solution.py
+++ b/solution.py
@@ -39,6 +39,13 @@
         order += [at(r, c) for c in seq]
     order += [at(r, cols[0]) for r in rows[:0:-1]]
     return order
+
+
+def slot_rows(tgt_emb, slot_group, group):
+    rows = tgt_emb[0]
+    for s in range(1, tgt_emb.shape[0]):
+        rows = jnp.where(slot_group[s] == group, tgt_emb[s], rows)
+    return rows
 
 
 def ring_gather(block, ring):
@@ -170,10 +177,16 @@
         g_cols, x_all, (((0,), (0,)), ((), ())), preferred_element_type=jnp.float32
     )
     grad_local = (own_terms * inv_root).astype(jnp.bfloat16)
-    returned = lax.all_to_all(
-        grad_local.reshape(lang_size, per_slot, emb_width), "lang", split_axis=0, concat_axis=0, tiled=True
-    )
-    grad_tgt = returned[slot_group]
+    returned = jnp.zeros((lang_size, per_slot, emb_width), grad_local.dtype)
+    kept = lax.dynamic_slice_in_dim(grad_local, group_index * per_slot, per_slot)
+    returned = lax.dynamic_update_index_in_dim(returned, kept, group_index, 0)
+    for k in range(1, lang_size):
+        dest = (group_index + k) % lang_size
+        sent = lax.dynamic_slice_in_dim(grad_local, dest * per_slot, per_slot)
+        got = lax.ppermute(sent, "lang", [(l, (l + k) % lang_size) for l in range(lang_size)])
+        returned = lax.dynamic_update_index_in_dim(returned, got, (group_index - k) % lang_size, 0)
+    group_ids = jnp.arange(lang_size, dtype=jnp.int32)
+    grad_tgt = jnp.stack([slot_rows(returned, group_ids, slot_group[s]) for s in range(lang_size)])
     return (grad_src, grad_tgt, pair_loss)
 
 

time: 83.8 us -> 102 us (1.22)
  between operations: 13.1 us -> 28.6 us
  local copies, waits for them, and re-layouts: 12.9 us -> 15.8 us
    all_to_all x1 -> x0, starting transfers between devices: 3.37 us -> none  [per_device(): lax.all_to_all(grad_local.reshape(lang_size, per_slot, emb_width), 'lang'...]
    ppermute x0 -> x3, starting transfers between devices: none -> 3.14 us  [per_device(): lax.ppermute(sent, 'lang', [(l, (l + k) % lang_size) for l in range(lang_...]
    slice x0 -> x4, local copies, waits for them, and re-layouts: none -> 2.51 us  [the longest x3 1.86 us: slot_rows(): rows = jnp.where(slot_group[s] == group, tgt_emb[s], rows)]
    gather x1 -> x0, local copies, waits for them, and re-layouts: 1.23 us -> none  [per_device(): grad_tgt = returned[slot_group]]
  transfers between devices with their start and end apart: 16 -> 18, of which waited for: 8 -> 7; matrix products, arithmetic and copies ran while one was open for 19% -> 19% of each run, Pallas kernels for 0% -> 0%
where the time goes in v9:
time: 102 us; the launch traced here: 101 us
  between operations  28.6 us (28%)
  starting transfers between devices  24 us (24%)
  waiting for transfers between devices  16.3 us (16%)
  local copies, waits for them, and re-layouts  15.8 us (15%)
  matrix products  9.07 us (9%)
  other arithmetic  7.15 us (7%)
    ppermute x14, starting transfers between devices, ring_gather(): cur = lax.ppermute(cur, 'dp', pairs)  17.3 us
    ppermute x14, waiting for transfers between devices, ring_gather(): cur = lax.ppermute(cur, 'dp', pairs)  16.3 us
    all_to_all x1, starting transfers between devices, per_device(): lax.all_to_all(ordered, 'lang', split_axis=0, concat_axis=1, tiled=True)  3.5 us
    dot_general x1, matrix products, per_device(): jnp.dot(g_rows, y_all, preferred_element_type=jnp.float32) * inv_root  3.45 us
    dot_general x1, matrix products, per_device(): lax.dot_general(g_cols, x_all, (((0,), (0,)), ((), ())), preferred_elemen...  3.25 us
    ppermute x3, starting transfers between devices, per_device(): lax.ppermute(sent, 'lang', [(l, (l + k) % lang_size) for l in range(lang_...  3.14 us
    reduce_sum x1, other arithmetic, block_stats(): pos_score = jnp.sum(jnp.where(is_pos, scores_f, 0.0), axis=1)  2.39 us
    dot_general x1, matrix products, scores_of(): lax.dot_general(x_rows, y_rows, (((1,), (1,)), ((), ())), preferred_eleme...  2.38 us
  transfers between devices with their start and end apart: 18, of which 7 were waited for; matrix products, arithmetic and copies ran while one was open for 19% of the time, Pallas kernels for 0%

profile of v9, /device:TPU:0, one launch (start us, length us, event | category | flops | bytes accessed | tf_op | source)
XLA Modules:
  0.0 100.9 jit_solution(11101839658566055573)
XLA Ops:
  0.7 3.1 %collective-permute-start.7 = (bf16[128,768]{1,0:T(8,128)(2,1)}, bf16[128,768]{1,0:T(8,128)(2,1)}, u32[]{:S(2)}, u32[]{:S(2)}) collective-permute-start(bf16[128,768]{1,0:T(8,128)(2,1)} %param.10), channel_id=1, source_target_pairs={{0,2},{2,4},{4,6},{6,7},{7,5},{5,3},{3,1},{1,0},{8,10},{10,12},{12... | collective-permute-start | bytes 589832 | tf_op jit(solution)/shard_map/ppermute | solution.py:67
  3.8 0.7 compare_select_fusion.5
  4.5 0.6 scatter_custom_fusion
  5.1 1.2 %gather_fusion = bf16[4,32,768]{2,1,0:T(8,128)(2,1)} fusion(bf16[4,32,768]{2,1,0:T(8,128)(2,1)S(1)} %copy-done, s32[1024]{0:T(1024)S(1)} %pad_clamp_fusion), kind=kCustom, calls=%fused_computation | custom fusion | bytes 393232 | tf_op jit(solution)/shard_map/gather | solution.py:113
  6.3 3.5 %all-to-all-start = ((bf16[4,32,768]{2,1,0:T(8,128)(2,1)}), bf16[4,32,768]{2,1,0:T(8,128)(2,1)S(1)}, u32[]{:S(2)}, u32[]{:S(2)}) async-start(bf16[4,32,768]{2,1,0:T(8,128)(2,1)} %gather_fusion), calls=%async_computation | async-start | bytes 393216 | tf_op jit(solution)/shard_map/all_to_all | solution.py:114
  9.9 1.2 %dynamic_slice.85 = s32[1]{0:T(128)} dynamic-slice(s32[4]{0:T(128)} %param.13, s32[]{:T(128)S(6)} %select_n.382), dynamic_slice_sizes={1} | dynamic-slice | bytes 12 | tf_op jit(solution)/shard_map/dynamic_slice | solution.py:116
  11.1 0.6 iota_compare_fusion
  11.7 1.5 %convert_reduce_fusion = s32[1024]{0:T(1024)S(1)} fusion(s32[1024]{0:T(1024)} %bitcast.61, s32[1024]{0:T(1024)S(1)} %fusion.46, pred[1024]{0:T(1024)(128)(4,1)S(1)} %iota_compare_fusion), kind=kLoop, calls=%fused_computation.11 | loop fusion | flops 4193280 | bytes 13312 | tf_op jit(solution)/shard_map/reduce_max | solution.py:123
  13.4 0.6 fusion.66
  14.0 0.6 dynamic_slice.87
  19.3 0.7 fusion.67
  24.9 0.7 dynamic_slice.106
  25.6 0.6 slice.72
  26.2 0.6 slice.75
  31.9 0.6 slice.77
  42.9 0.6 dynamic_slice.86
  43.5 0.6 dynamic_slice.105
  44.2 0.6 dynamic_slice.84
  44.8 0.5 fusion.55
  45.3 2.0 %collective-permute-start = (bf16[128,768]{1,0:T(8,128)(2,1)S(1)}, bf16[128,768]{1,0:T(8,128)(2,1)S(1)}, u32[]{:S(2)}, u32[]{:S(2)}) collective-permute-start(bf16[128,768]{1,0:T(8,128)(2,1)S(1)} %bitcast.57), channel_id=1, source_target_pairs={{0,2},{2,4},{4,6},{6,7},{7,5},{5,3},{3,1},{1,0},{8,10},{10,12},{12... | collective-permute-start | bytes 589832 | tf_op jit(solution)/shard_map/ppermute | solution.py:67
  47.5 2.1 %collective-permute-start.8 = (bf16[128,768]{1,0:T(8,128)(2,1)}, bf16[128,768]{1,0:T(8,128)(2,1)S(1)}, u32[]{:S(2)}, u32[]{:S(2)}) collective-permute-start(bf16[128,768]{1,0:T(8,128)(2,1)} %collective-permute-done.7), channel_id=1, source_target_pairs={{0,2},{2,4},{4,6},{6,7},{7,5},{5,3},{3,1},{1,0},{8,10},{10,12},{12... | collective-permute-start | bytes 589832 | tf_op jit(solution)/shard_map/ppermute | solution.py:67
  49.6 1.0 constant_dynamic-update-slice_fusion.6
  50.5 2.6 %collective-permute-done = bf16[128,768]{1,0:T(8,128)(2,1)S(1)} collective-permute-done((bf16[128,768]{1,0:T(8,128)(2,1)S(1)}, bf16[128,768]{1,0:T(8,128)(2,1)S(1)}, u32[]{:S(2)}, u32[]{:S(2)}) %collective-permute-start) | collective-permute-done | bytes 196640 | tf_op jit(solution)/shard_map/ppermute | solution.py:67
  53.1 2.0 %collective-permute-start.1 = (bf16[128,768]{1,0:T(8,128)(2,1)S(1)}, bf16[128,768]{1,0:T(8,128)(2,1)S(1)}, u32[]{:S(2)}, u32[]{:S(2)}) collective-permute-start(bf16[128,768]{1,0:T(8,128)(2,1)S(1)} %collective-permute-done), channel_id=1, source_target_pairs={{0,2},{2,4},{4,6},{6,7},{7,5},{5,3},{3,1},{1,0},{8,10},{10,12},{12... | collective-permute-start | bytes 589832 | tf_op jit(solution)/shard_map/ppermute | solution.py:67
  55.1 2.2 %collective-permute-done.8 = bf16[128,768]{1,0:T(8,128)(2,1)S(1)} collective-permute-done((bf16[128,768]{1,0:T(8,128)(2,1)}, bf16[128,768]{1,0:T(8,128)(2,1)S(1)}, u32[]{:S(2)}, u32[]{:S(2)}) %collective-permute-start.8) | collective-permute-done | bytes 196640 | tf_op jit(solution)/shard_map/ppermute | solution.py:67
  57.3 2.0 %collective-permute-start.9 = (bf16[128,768]{1,0:T(8,128)(2,1)S(1)}, bf16[128,768]{1,0:T(8,128)(2,1)S(1)}, u32[]{:S(2)}, u32[]{:S(2)}) collective-permute-start(bf16[128,768]{1,0:T(8,128)(2,1)S(1)} %collective-permute-done.8), channel_id=1, source_target_pairs={{0,2},{2,4},{4,6},{6,7},{7,5},{5,3},{3,1},{1,0},{8,10},{10,12},{12... | collective-permute-start | bytes 589832 | tf_op jit(solution)/shard_map/ppermute | solution.py:67
  59.4 2.2 %collective-permute-done.1 = bf16[128,768]{1,0:T(8,128)(2,1)S(1)} collective-permute-done((bf16[128,768]{1,0:T(8,128)(2,1)S(1)}, bf16[128,768]{1,0:T(8,128)(2,1)S(1)}, u32[]{:S(2)}, u32[]{:S(2)}) %collective-permute-start.1) | collective-permute-done | bytes 196640 | tf_op jit(solution)/shard_map/ppermute | solution.py:67
  61.5 2.0 %collective-permute-start.2 = (bf16[128,768]{1,0:T(8,128)(2,1)S(1)}, bf16[128,768]{1,0:T(8,128)(2,1)S(1)}, u32[]{:S(2)}, u32[]{:S(2)}) collective-permute-start(bf16[128,768]{1,0:T(8,128)(2,1)S(1)} %collective-permute-done.1), channel_id=1, source_target_pairs={{0,2},{2,4},{4,6},{6,7},{7,5},{5,3},{3,1},{1,0},{8,10},{10,12},{12... | collective-permute-start | bytes 589832 | tf_op jit(solution)/shard_map/ppermute | solution.py:67
  63.6 2.2 %collective-permute-done.9 = bf16[128,768]{1,0:T(8,128)(2,1)S(1)} collective-permute-done((bf16[128,768]{1,0:T(8,128)(2,1)S(1)}, bf16[128,768]{1,0:T(8,128)(2,1)S(1)}, u32[]{:S(2)}, u32[]{:S(2)}) %collective-permute-start.9) | collective-permute-done | bytes 196640 | tf_op jit(solution)/shard_map/ppermute | solution.py:67
  65.7 2.0 %collective-permute-start.10 = (bf16[128,768]{1,0:T(8,128)(2,1)S(1)}, bf16[128,768]{1,0:T(8,128)(2,1)S(1)}, u32[]{:S(2)}, u32[]{:S(2)}) collective-permute-start(bf16[128,768]{1,0:T(8,128)(2,1)S(1)} %collective-permute-done.9), channel_id=1, source_target_pairs={{0,2},{2,4},{4,6},{6,7},{7,5},{5,3},{3,1},{1,0},{8,10},{10,12},{12... | collective-permute-start | bytes 589832 | tf_op jit(solution)/shard_map/ppermute | solution.py:67
  67.8 2.2 %collective-permute-done.2 = bf16[128,768]{1,0:T(8,128)(2,1)S(1)} collective-permute-done((bf16[128,768]{1,0:T(8,128)(2,1)S(1)}, bf16[128,768]{1,0:T(8,128)(2,1)S(1)}, u32[]{:S(2)}, u32[]{:S(2)}) %collective-permute-start.2) | collective-permute-done | bytes 196640 | tf_op jit(solution)/shard_map/ppermute | solution.py:67
  69.9 2.0 %collective-permute-start.3 = (bf16[128,768]{1,0:T(8,128)(2,1)S(1)}, bf16[128,768]{1,0:T(8,128)(2,1)S(1)}, u32[]{:S(2)}, u32[]{:S(2)}) collective-permute-start(bf16[128,768]{1,0:T(8,128)(2,1)S(1)} %collective-permute-done.2), channel_id=1, source_target_pairs={{0,2},{2,4},{4,6},{6,7},{7,5},{5,3},{3,1},{1,0},{8,10},{10,12},{12... | collective-permute-start | bytes 589832 | tf_op jit(solution)/shard_map/ppermute | solution.py:67
  72.0 2.2 %collective-permute-done.10 = bf16[128,768]{1,0:T(8,128)(2,1)S(1)} collective-permute-done((bf16[128,768]{1,0:T(8,128)(2,1)S(1)}, bf16[128,768]{1,0:T(8,128)(2,1)S(1)}, u32[]{:S(2)}, u32[]{:S(2)}) %collective-permute-start.10) | collective-permute-done | bytes 196640 | tf_op jit(solution)/shard_map/ppermute | solution.py:67
  74.2 0.9 constant_dynamic-update-slice_fusion.2
  75.2 2.9 %collective-permute-done.3 = bf16[128,768]{1,0:T(8,128)(2,1)S(1)} collective-permute-done((bf16[128,768]{1,0:T(8,128)(2,1)S(1)}, bf16[128,768]{1,0:T(8,128)(2,1)S(1)}, u32[]{:S(2)}, u32[]{:S(2)}) %collective-permute-start.3) | collective-permute-done | bytes 196640 | tf_op jit(solution)/shard_map/ppermute | solution.py:67
  78.2 2.4 %select_reduce_fusion.3 = (f32[1024]{0:T(1024)S(1)}, f32[1024]{0:T(1024)S(1)}, f32[1024,1024]{0,1:T(8,128)S(1)}) fusion(pred[1024]{0:T(1024)(128)(4,1)S(1)} %broadcast_compare_fusion, pred[1024]{0:T(1024)(128)(4,1)S(1)} %copy-done.9, s32[1024]{0:T(1024)S(1)} %bitcast.62, s32[1024]{0:T(1024)S(1)} %fusion.46, ...), kind=kOutput, calls=%fused_computation.10 | convolution fusion | flops 1618999296 | bytes 7358464 | tf_op jit(solution)/shard_map/dot_general | solution.py:74
  80.6 2.4 %fusion.1 = (f32[1024]{0:T(1024)S(1)}, f32[1024]{0:T(1024)S(1)}, f32[1024]{0:T(1024)S(1)}) fusion(f32[1024,1024]{0,1:T(8,128)S(1)} %get-tuple-element.30, s32[1024]{0:T(1024)S(1)} %bitcast.63, s32[1024]{0:T(1024)S(1)} %fusion.46, f32[1024]{0:T(1024)S(1)} %get-tuple-element.7, pred[1024]{0:T(1024)(128)(4,1)S(1)} %copy-done.9, f32[1024]{0:T(1024)S(1)} %get-tuple-element.6, ...), kind=kLoop, calls=%fused_computation.6 | loop fusion | flops 9434112 | bytes 4225024 | tf_op jit(solution)/shard_map/reduce_sum | solution.py:86
  83.0 1.2 %select_reduce_fusion.4 = (f32[]{:T(128)}, f32[1024]{0:T(1024)S(1)}, f32[]{:T(128)}, f32[1024]{0:T(1024)S(1)}) fusion(f32[1024]{0:T(1024)S(1)} %get-tuple-element.7, f32[1024]{0:T(1024)S(1)} %get-tuple-element.4, f32[1024]{0:T(1024)S(1)} %get-tuple-element.3, f32[1024]{0:T(1024)S(1)} %get-tuple-element.6, f32[1024]{0:T(1024)S(1)} %get-tuple-element.5, ...), kind=kLoop, calls=%fused_computation.112 | loop fusion | flops 16382 | bytes 32780 | tf_op jit(solution)/shard_map/reduce_sum | solution.py:156
  84.2 0.6 copy-done.5
  84.8 0.6 dynamic_slice.107
  85.4 0.6 dynamic_slice.104
  86.0 3.2 %fusion.6 = bf16[128,768]{1,0:T(8,128)(2,1)} fusion(bf16[1024,768]{1,0:T(8,128)(2,1)S(1)} %constant_dynamic-update-slice_fusion, bf16[128,768]{1,0:T(8,128)(2,1)S(1)} %bitcast.60, f32[128]{0:T(128)} %dynamic_slice.107, f32[1024]{0:T(1024)} %copy-done.7, s32[128]{0:T(128)} %dynamic_slice.106, f32[]{:T(128)} %bitcast, s32[1024]{0:T(1024)S(1)} %bitcast.64, ...), kind=kOutput, calls=%fused_computation.20 | convolution fusion | flops 404815872 | bytes 1976452 | tf_op jit(solution)/shard_map/dot_general | solution.py:176
  89.3 0.9 constant_dynamic-slice_fusion.2
  90.2 1.7 %collective-permute-start.15 = (bf16[32,768]{1,0:T(8,128)(2,1)S(1)}, bf16[32,768]{1,0:T(8,128)(2,1)S(1)}, u32[]{:S(2)}, u32[]{:S(2)}) collective-permute-start(bf16[32,768]{1,0:T(8,128)(2,1)S(1)} %get-tuple-element.17), channel_id=1, source_target_pairs={{0,16},{8,24},{16,0},{24,8},{1,17},{9,25},{17,1},{25,9},{2,18},{10... | collective-permute-start | bytes 147464 | tf_op jit(solution)/shard_map/ppermute | solution.py:186
  91.9 1.4 %collective-permute-start.16 = (bf16[32,768]{1,0:T(8,128)(2,1)S(1)}, bf16[32,768]{1,0:T(8,128)(2,1)S(1)}, u32[]{:S(2)}, u32[]{:S(2)}) collective-permute-start(bf16[32,768]{1,0:T(8,128)(2,1)S(1)} %get-tuple-element.16), channel_id=1, source_target_pairs={{0,24},{8,0},{16,8},{24,16},{1,25},{9,1},{17,9},{25,17},{2,26},{10... | collective-permute-start | bytes 147464 | tf_op jit(solution)/shard_map/ppermute | solution.py:186
  93.3 3.4 %fusion.5 = bf16[128,768]{1,0:T(8,128)(2,1)} fusion(bf16[1024,768]{1,0:T(8,128)(2,1)S(1)} %constant_dynamic-update-slice_fusion.8, bf16[128,768]{1,0:T(8,128)(2,1)} %param.10, f32[1024]{0:T(1024)S(1)} %copy-done.6, f32[128]{0:T(128)} %dynamic_slice.104, s32[128]{0:T(128)} %fusion.55, f32[]{:T(128)} %bitcast, s32[1024]{0:T(1024)S(1)} %fusion.46, ...), kind=kOutput, calls=%fused_computation.19 | convolution fusion | flops 404815872 | bytes 1976452 | tf_op jit(solution)/shard_map/dot_general | solution.py:167
  96.7 0.8 bitcast_dynamic-update-slice_fusion.3
  99.1 0.7 pad_maximum_fusion
  (71 shorter events, 0.8 us)
Async XLA Ops:
  0.6 4.5 %copy-start = (bf16[4,32,768]{2,1,0:T(8,128)(2,1)S(1)}, bf16[4,32,768]{2,1,0:T(8,128)(2,1)}, u32[]{:S(2)}) copy-start(bf16[4,32,768]{2,1,0:T(8,128)(2,1)} %param.11) | copy-start | bytes 589828
  0.6 13.4 %copy-start.11 = (s32[8]{0:T(128)S(1)}, s32[8]{0:T(128)}, u32[]{:S(2)}) copy-start(s32[8]{0:T(128)} %constant.265.clone) | copy-start | bytes 100
  0.7 18.6 %copy-start.2 = (s32[8]{0:T(128)S(1)}, s32[8]{0:T(128)}, u32[]{:S(2)}) copy-start(s32[8]{0:T(128)} %constant.264.clone) | copy-start | bytes 100
  0.7 12.7 %copy-start.1 = (bf16[128,768]{1,0:T(8,128)(2,1)S(1)}, bf16[128,768]{1,0:T(8,128)(2,1)}, u32[]{:S(2)}) copy-start(bf16[128,768]{1,0:T(8,128)(2,1)} %param.10) | copy-start | bytes 589828
  0.7 12.7 %copy-start.3 = (s32[4]{0:T(128)S(1)}, s32[4]{0:T(128)}, u32[]{:S(2)}) copy-start(s32[4]{0:T(128)} %param.12) | copy-start | bytes 52
  0.7 46.8 %collective-permute-start.7 = (bf16[128,768]{1,0:T(8,128)(2,1)}, bf16[128,768]{1,0:T(8,128)(2,1)}, u32[]{:S(2)}, u32[]{:S(2)}) collective-permute-start(bf16[128,768]{1,0:T(8,128)(2,1)} %param.10), channel_id=1, source_target_pairs={{0,2},{2,4},{4,6},{6,7},{7,5},{5,3},{3,1},{1,0},{8,10},{10,12},{12... | collective-permute-start | bytes 589832 | tf_op jit(solution)/shard_map/ppermute | solution.py:67
  3.8 45.8 %collective-permute-start.11 = (bf16[128,768]{1,0:T(8,128)(2,1)}, bf16[128,768]{1,0:T(8,128)(2,1)}, u32[]{:S(2)}, u32[]{:S(2)}) collective-permute-start(bf16[128,768]{1,0:T(8,128)(2,1)} %param.10), channel_id=1, source_target_pairs={{0,1},{2,0},{4,2},{6,4},{7,6},{5,7},{3,5},{1,3},{8,9},{10,8},{12,1... | collective-permute-start | bytes 589832 | tf_op jit(solution)/shard_map/ppermute | solution.py:67
  6.3 37.9 %copy-start.10 = (f32[4]{0:T(128)S(1)}, f32[4]{0:T(128)}, u32[]{:S(2)}) copy-start(f32[4]{0:T(128)} %param.15) | copy-start | bytes 52
  6.3 38.5 %copy-start.4 = (s32[1,1024]{1,0:T(1,128)S(1)}, s32[1,1024]{1,0:T(1,128)}, u32[]{:S(2)}) copy-start(s32[1,1024]{1,0:T(1,128)} %param.14) | copy-start | bytes 12292
  6.3 39.0 %all-to-all-start = ((bf16[4,32,768]{2,1,0:T(8,128)(2,1)}), bf16[4,32,768]{2,1,0:T(8,128)(2,1)S(1)}, u32[]{:S(2)}, u32[]{:S(2)}) async-start(bf16[4,32,768]{2,1,0:T(8,128)(2,1)} %gather_fusion), calls=%async_computation | async-start | bytes 393216 | tf_op jit(solution)/shard_map/all_to_all | solution.py:114
  11.7 35.7 %copy-start.8 = (pred[1024]{0:T(1024)(128)(4,1)}, pred[1024]{0:T(1024)(128)(4,1)S(1)}, u32[]{:S(2)}) copy-start(pred[1024]{0:T(1024)(128)(4,1)S(1)} %iota_compare_fusion) | copy-start | bytes 3076
  45.3 7.8 %collective-permute-start = (bf16[128,768]{1,0:T(8,128)(2,1)S(1)}, bf16[128,768]{1,0:T(8,128)(2,1)S(1)}, u32[]{:S(2)}, u32[]{:S(2)}) collective-permute-start(bf16[128,768]{1,0:T(8,128)(2,1)S(1)} %bitcast.57), channel_id=1, source_target_pairs={{0,2},{2,4},{4,6},{6,7},{7,5},{5,3},{3,1},{1,0},{8,10},{10,12},{12... | collective-permute-start | bytes 589832 | tf_op jit(solution)/shard_map/ppermute | solution.py:67
  47.3 7.8 %collective-permute-start.4 = (bf16[128,768]{1,0:T(8,128)(2,1)S(1)}, bf16[128,768]{1,0:T(8,128)(2,1)S(1)}, u32[]{:S(2)}, u32[]{:S(2)}) collective-permute-start(bf16[128,768]{1,0:T(8,128)(2,1)S(1)} %bitcast.58), channel_id=1, source_target_pairs={{0,1},{2,0},{4,2},{6,4},{7,6},{5,7},{3,5},{1,3},{8,9},{10,8},{12,1... | collective-permute-start | bytes 589832 | tf_op jit(solution)/shard_map/ppermute | solution.py:67
  47.5 9.8 %collective-permute-start.8 = (bf16[128,768]{1,0:T(8,128)(2,1)}, bf16[128,768]{1,0:T(8,128)(2,1)S(1)}, u32[]{:S(2)}, u32[]{:S(2)}) collective-permute-start(bf16[128,768]{1,0:T(8,128)(2,1)} %collective-permute-done.7), channel_id=1, source_target_pairs={{0,2},{2,4},{4,6},{6,7},{7,5},{5,3},{3,1},{1,0},{8,10},{10,12},{12... | collective-permute-start | bytes 589832 | tf_op jit(solution)/shard_map/ppermute | solution.py:67
  49.6 9.8 %collective-permute-start.12 = (bf16[128,768]{1,0:T(8,128)(2,1)}, bf16[128,768]{1,0:T(8,128)(2,1)S(1)}, u32[]{:S(2)}, u32[]{:S(2)}) collective-permute-start(bf16[128,768]{1,0:T(8,128)(2,1)} %collective-permute-done.11), channel_id=1, source_target_pairs={{0,1},{2,0},{4,2},{6,4},{7,6},{5,7},{3,5},{1,3},{8,9},{10,8},{12,1... | collective-permute-start | bytes 589832 | tf_op jit(solution)/shard_map/ppermute | solution.py:67
  53.1 8.4 %collective-permute-start.1 = (bf16[128,768]{1,0:T(8,128)(2,1)S(1)}, bf16[128,768]{1,0:T(8,128)(2,1)S(1)}, u32[]{:S(2)}, u32[]{:S(2)}) collective-permute-start(bf16[128,768]{1,0:T(8,128)(2,1)S(1)} %collective-permute-done), channel_id=1, source_target_pairs={{0,2},{2,4},{4,6},{6,7},{7,5},{5,3},{3,1},{1,0},{8,10},{10,12},{12... | collective-permute-start | bytes 589832 | tf_op jit(solution)/shard_map/ppermute | solution.py:67
  55.1 8.4 %collective-permute-start.5 = (bf16[128,768]{1,0:T(8,128)(2,1)S(1)}, bf16[128,768]{1,0:T(8,128)(2,1)S(1)}, u32[]{:S(2)}, u32[]{:S(2)}) collective-permute-start(bf16[128,768]{1,0:T(8,128)(2,1)S(1)} %collective-permute-done.4), channel_id=1, source_target_pairs={{0,1},{2,0},{4,2},{6,4},{7,6},{5,7},{3,5},{1,3},{8,9},{10,8},{12,1... | collective-permute-start | bytes 589832 | tf_op jit(solution)/shard_map/ppermute | solution.py:67
  57.3 8.4 %collective-permute-start.9 = (bf16[128,768]{1,0:T(8,128)(2,1)S(1)}, bf16[128,768]{1,0:T(8,128)(2,1)S(1)}, u32[]{:S(2)}, u32[]{:S(2)}) collective-permute-start(bf16[128,768]{1,0:T(8,128)(2,1)S(1)} %collective-permute-done.8), channel_id=1, source_target_pairs={{0,2},{2,4},{4,6},{6,7},{7,5},{5,3},{3,1},{1,0},{8,10},{10,12},{12... | collective-permute-start | bytes 589832 | tf_op jit(solution)/shard_map/ppermute | solution.py:67
  59.3 15.8 %collective-permute-start.13 = (bf16[128,768]{1,0:T(8,128)(2,1)S(1)}, bf16[128,768]{1,0:T(8,128)(2,1)S(1)}, u32[]{:S(2)}, u32[]{:S(2)}) collective-permute-start(bf16[128,768]{1,0:T(8,128)(2,1)S(1)} %collective-permute-done.12), channel_id=1, source_target_pairs={{0,1},{2,0},{4,2},{6,4},{7,6},{5,7},{3,5},{1,3},{8,9},{10,8},{12,1... | collective-permute-start | bytes 589832 | tf_op jit(solution)/shard_map/ppermute | solution.py:67
  61.5 8.4 %collective-permute-start.2 = (bf16[128,768]{1,0:T(8,128)(2,1)S(1)}, bf16[128,768]{1,0:T(8,128)(2,1)S(1)}, u32[]{:S(2)}, u32[]{:S(2)}) collective-permute-start(bf16[128,768]{1,0:T(8,128)(2,1)S(1)} %collective-permute-done.1), channel_id=1, source_target_pairs={{0,2},{2,4},{4,6},{6,7},{7,5},{5,3},{3,1},{1,0},{8,10},{10,12},{12... | collective-permute-start | bytes 589832 | tf_op jit(solution)/shard_map/ppermute | solution.py:67
  63.5 14.6 %collective-permute-start.6 = (bf16[128,768]{1,0:T(8,128)(2,1)S(1)}, bf16[128,768]{1,0:T(8,128)(2,1)S(1)}, u32[]{:S(2)}, u32[]{:S(2)}) collective-permute-start(bf16[128,768]{1,0:T(8,128)(2,1)S(1)} %collective-permute-done.5), channel_id=1, source_target_pairs={{0,1},{2,0},{4,2},{6,4},{7,6},{5,7},{3,5},{1,3},{8,9},{10,8},{12,1... | collective-permute-start | bytes 589832 | tf_op jit(solution)/shard_map/ppermute | solution.py:67
  65.7 8.4 %collective-permute-start.10 = (bf16[128,768]{1,0:T(8,128)(2,1)S(1)}, bf16[128,768]{1,0:T(8,128)(2,1)S(1)}, u32[]{:S(2)}, u32[]{:S(2)}) collective-permute-start(bf16[128,768]{1,0:T(8,128)(2,1)S(1)} %collective-permute-done.9), channel_id=1, source_target_pairs={{0,2},{2,4},{4,6},{6,7},{7,5},{5,3},{3,1},{1,0},{8,10},{10,12},{12... | collective-permute-start | bytes 589832 | tf_op jit(solution)/shard_map/ppermute | solution.py:67
  69.9 8.1 %collective-permute-start.3 = (bf16[128,768]{1,0:T(8,128)(2,1)S(1)}, bf16[128,768]{1,0:T(8,128)(2,1)S(1)}, u32[]{:S(2)}, u32[]{:S(2)}) collective-permute-start(bf16[128,768]{1,0:T(8,128)(2,1)S(1)} %collective-permute-done.2), channel_id=1, source_target_pairs={{0,2},{2,4},{4,6},{6,7},{7,5},{5,3},{3,1},{1,0},{8,10},{10,12},{12... | collective-permute-start | bytes 589832 | tf_op jit(solution)/shard_map/ppermute | solution.py:67
  72.0 6.2 %copy-start.9 = (pred[1024]{0:T(1024)(128)(4,1)S(1)}, pred[1024]{0:T(1024)(128)(4,1)}, u32[]{:S(2)}) copy-start(pred[1024]{0:T(1024)(128)(4,1)} %copy-done.8) | copy-start | bytes 3076
  84.2 0.6 copy-start.5
  84.2 1.8 %copy-start.7 = (f32[1024]{0:T(1024)}, f32[1024]{0:T(1024)S(1)}, u32[]{:S(2)}) copy-start(f32[1024]{0:T(1024)S(1)} %get-tuple-element.32) | copy-start | bytes 12292
  86.0 7.3 %copy-start.6 = (f32[1024]{0:T(1024)S(1)}, f32[1024]{0:T(1024)}, u32[]{:S(2)}) copy-start(f32[1024]{0:T(1024)} %copy-done.5) | copy-start | bytes 12292
  90.1 8.8 %collective-permute-start.14 = (bf16[32,768]{1,0:T(8,128)(2,1)S(1)}, bf16[32,768]{1,0:T(8,128)(2,1)S(1)}, u32[]{:S(2)}, u32[]{:S(2)}) collective-permute-start(bf16[32,768]{1,0:T(8,128)(2,1)S(1)} %get-tuple-element.18), channel_id=1, source_target_pairs={{0,8},{8,16},{16,24},{24,0},{1,9},{9,17},{17,25},{25,1},{2,10},{10... | collective-permute-start | bytes 147464 | tf_op jit(solution)/shard_map/ppermute | solution.py:186
  90.2 8.8 %collective-permute-start.15 = (bf16[32,768]{1,0:T(8,128)(2,1)S(1)}, bf16[32,768]{1,0:T(8,128)(2,1)S(1)}, u32[]{:S(2)}, u32[]{:S(2)}) collective-permute-start(bf16[32,768]{1,0:T(8,128)(2,1)S(1)} %get-tuple-element.17), channel_id=1, source_target_pairs={{0,16},{8,24},{16,0},{24,8},{1,17},{9,25},{17,1},{25,9},{2,18},{10... | collective-permute-start | bytes 147464 | tf_op jit(solution)/shard_map/ppermute | solution.py:186
  91.9 7.1 %collective-permute-start.16 = (bf16[32,768]{1,0:T(8,128)(2,1)S(1)}, bf16[32,768]{1,0:T(8,128)(2,1)S(1)}, u32[]{:S(2)}, u32[]{:S(2)}) collective-permute-start(bf16[32,768]{1,0:T(8,128)(2,1)S(1)} %get-tuple-element.16), channel_id=1, source_target_pairs={{0,24},{8,0},{16,8},{24,16},{1,25},{9,1},{17,9},{25,17},{2,26},{10... | collective-permute-start | bytes 147464 | tf_op jit(solution)/shard_map/ppermute | solution.py:186

commit v10 on v8

--- a/solution.py
+++ b/solution.py
@@ -114,7 +114,8 @@
     perm = target_index(pair_rows, row_count, per_slot, data_size)
     live_pos = (perm[None, :] == pair_align[:, None]) & row_live[:, None]
     col_live = jnp.max(live_pos.astype(jnp.int32), axis=0) > 0
-    x_all = ring_gather(src_emb, ring)
+    after = src_emb + jnp.zeros_like(src_emb) * partner[:1, :1]
+    x_all = ring_gather(after, ring)
     y_all = ring_gather(partner, ring)
 
     block = max(1, min(pair_rows, BLOCK_BYTES // (4 * pair_rows)))

time: 83.8 us -> 89.3 us (1.066)
  waiting for transfers between devices: 16.7 us -> 20 us
  local copies, waits for them, and re-layouts: 12.9 us -> 13.9 us
    ppermute x14, waiting for transfers between devices: 16.3 us -> 19.5 us  [ring_gather(): cur = lax.ppermute(cur, 'dp', pairs)]
    dynamic_update_slice x14, local copies, waits for them, and re-layouts: 2.13 us -> 0.28 us  [ring_gather(): out = lax.dynamic_update_slice_in_dim(out, cur, origin * rows, 0)]
    all_to_all x1, starting transfers between devices: 3.37 us -> 4.37 us  [per_device(): lax.all_to_all(ordered, 'lang', split_axis=0, concat_axis=1, tiled=True)]
    dynamic_slice x1, local copies, waits for them, and re-layouts: 0.68 us -> 1.6 us  [ring_gather(): origin = ring_arr[(my_pos + sign * t) % count]]
  transfers between devices with their start and end apart: 16 -> 16, of which waited for: 8 -> 9; matrix products, arithmetic and copies ran while one was open for 19% -> 16% of each run, Pallas kernels for 0% -> 0%
where the time goes in v10:
time: 89.3 us; the launch traced here: 88.6 us
  starting transfers between devices  24.5 us (27%)
  waiting for transfers between devices  20 us (22%)
  local copies, waits for them, and re-layouts  13.9 us (16%)
  between operations  13.8 us (15%)
  matrix products  9.06 us (10%)
  other arithmetic  7.34 us (8%)
    ppermute x14, waiting for transfers between devices, ring_gather(): cur = lax.ppermute(cur, 'dp', pairs)  19.5 us
    ppermute x14, starting transfers between devices, ring_gather(): cur = lax.ppermute(cur, 'dp', pairs)  16.8 us
    all_to_all x1, starting transfers between devices, per_device(): lax.all_to_all(ordered, 'lang', split_axis=0, concat_axis=1, tiled=True)  4.37 us
    dot_general x1, matrix products, per_device(): jnp.dot(g_rows, y_all, preferred_element_type=jnp.float32) * inv_root  3.44 us
    all_to_all x1, starting transfers between devices, per_device(): lax.all_to_all(grad_local.reshape(lang_size, per_slot, emb_width), 'lang'...  3.37 us
    dot_general x1, matrix products, per_device(): lax.dot_general(g_cols, x_all, (((0,), (0,)), ((), ())), preferred_elemen...  3.21 us
    reduce_sum x1, other arithmetic, block_stats(): pos_score = jnp.sum(jnp.where(is_pos, scores_f, 0.0), axis=1)  2.43 us
    dot_general x1, matrix products, scores_of(): lax.dot_general(x_rows, y_rows, (((1,), (1,)), ((), ())), preferred_eleme...  2.4 us
  transfers between devices with their start and end apart: 16, of which 9 were waited for; matrix products, arithmetic and copies ran while one was open for 16% of the time, Pallas kernels for 0%

profile of v10, /device:TPU:0, one launch (start us, length us, event | category | flops | bytes accessed | tf_op | source)
XLA Modules:
  0.0 88.6 jit_solution(2660183641695818927)
XLA Ops:
  0.6 0.0 copy-start
  0.7 0.7 compare_select_fusion.5
  1.4 0.6 scatter_custom_fusion
  2.0 1.2 %gather_fusion = bf16[4,32,768]{2,1,0:T(8,128)(2,1)} fusion(bf16[4,32,768]{2,1,0:T(8,128)(2,1)S(1)} %copy-done, s32[1024]{0:T(1024)S(1)} %pad_clamp_fusion.1), kind=kCustom, calls=%fused_computation | custom fusion | bytes 393232 | tf_op jit(solution)/shard_map/gather | solution.py:106
  3.2 4.4 %all-to-all-start = ((bf16[4,32,768]{2,1,0:T(8,128)(2,1)}), bf16[4,32,768]{2,1,0:T(8,128)(2,1)S(1)}, u32[]{:S(2)}, u32[]{:S(2)}) async-start(bf16[4,32,768]{2,1,0:T(8,128)(2,1)} %gather_fusion), calls=%async_computation | async-start | bytes 393216 | tf_op jit(solution)/shard_map/all_to_all | solution.py:107
  7.6 1.3 %dynamic_slice.73 = s32[1]{0:T(128)} dynamic-slice(s32[4]{0:T(128)} %param.13, s32[]{:T(128)S(6)} %select_n.250), dynamic_slice_sizes={1} | dynamic-slice | bytes 12 | tf_op jit(solution)/shard_map/dynamic_slice | solution.py:109
  8.9 0.7 iota_compare_fusion
  9.6 1.5 %convert_reduce_fusion = s32[1024]{0:T(1024)S(1)} fusion(s32[1024]{0:T(1024)} %bitcast.45, s32[1024]{0:T(1024)S(1)} %fusion.46, pred[1024]{0:T(1024)(128)(4,1)S(1)} %iota_compare_fusion), kind=kLoop, calls=%fused_computation.12 | loop fusion | flops 4193280 | bytes 13312 | tf_op jit(solution)/shard_map/reduce_max | solution.py:116
  11.2 1.2 %dynamic_slice.75 = s32[1]{0:T(128)} dynamic-slice(s32[8]{0:T(128)} %constant.223.clone, s32[]{:T(128)S(6)} %select_n.258), dynamic_slice_sizes={1} | dynamic-slice | bytes 12 | tf_op jit(solution)/shard_map/dynamic_slice | solution.py:51
  17.1 1.6 %fusion.66 = (s32[1]{0:T(128)}, s32[1]{0:T(128)}, s32[1]{0:T(128)}, s32[1]{0:T(128)}, s32[1]{0:T(128)}, /*index=5*/s32[1]{0:T(128)}, s32[1]{0:T(128)}) fusion(s32[8]{0:T(128)} %constant.222.clone, s32[]{:T(128)S(6)} %select_n.278, s32[]{:T(128)S(6)} %select_n.272, s32[]{:T(128)S(6)} %select_n.269, s32[]{:T(128)S(6)} %select_n.266, s32[]{:T(128)S(6)} %select_n.263, ...), kind=kLoop, calls=%fused_computation.126 | loop fusion | bytes 84 | tf_op jit(solution)/shard_map/dynamic_slice | solution.py:61
  23.8 0.7 dynamic_slice.94
  24.4 0.6 dynamic_slice.74
  25.1 0.6 dynamic_slice.93
  25.7 1.3 %dynamic_slice.72 = f32[1]{0:T(128)} dynamic-slice(f32[4]{0:T(128)} %param.15, s32[]{:T(128)S(6)} %select_n.250), dynamic_slice_sizes={1} | dynamic-slice | bytes 12 | tf_op jit(solution)/shard_map/dynamic_slice | solution.py:110
  26.9 0.5 slice.8
  28.1 0.1 broadcast.198.clone.1
  28.3 2.3 %collective-permute-start.7 = (bf16[128,768]{1,0:T(8,128)(2,1)S(1)}, bf16[128,768]{1,0:T(8,128)(2,1)S(1)}, u32[]{:S(2)}, u32[]{:S(2)}) collective-permute-start(bf16[128,768]{1,0:T(8,128)(2,1)S(1)} %get-tuple-element.13), channel_id=1, source_target_pairs={{0,2},{2,4},{4,6},{6,7},{7,5},{5,3},{3,1},{1,0},{8,10},{10,12},{12... | collective-permute-start | bytes 589832 | tf_op jit(solution)/shard_map/ppermute | solution.py:60
  30.5 0.0 collective-permute-start.11
  30.6 2.0 %collective-permute-start = (bf16[128,768]{1,0:T(8,128)(2,1)S(1)}, bf16[128,768]{1,0:T(8,128)(2,1)S(1)}, u32[]{:S(2)}, u32[]{:S(2)}) collective-permute-start(bf16[128,768]{1,0:T(8,128)(2,1)S(1)} %bitcast.40), channel_id=1, source_target_pairs={{0,2},{2,4},{4,6},{6,7},{7,5},{5,3},{3,1},{1,0},{8,10},{10,12},{12... | collective-permute-start | bytes 589832 | tf_op jit(solution)/shard_map/ppermute | solution.py:60
  32.6 0.0 collective-permute-start.4
  32.6 0.6 fusion.55
  33.1 0.1 broadcast.198.clone
  33.3 3.0 %collective-permute-done.7 = bf16[128,768]{1,0:T(8,128)(2,1)S(1)} collective-permute-done((bf16[128,768]{1,0:T(8,128)(2,1)S(1)}, bf16[128,768]{1,0:T(8,128)(2,1)S(1)}, u32[]{:S(2)}, u32[]{:S(2)}) %collective-permute-start.7) | collective-permute-done | bytes 196640 | tf_op jit(solution)/shard_map/ppermute | solution.py:60
  36.2 2.1 %collective-permute-start.8 = (bf16[128,768]{1,0:T(8,128)(2,1)S(1)}, bf16[128,768]{1,0:T(8,128)(2,1)S(1)}, u32[]{:S(2)}, u32[]{:S(2)}) collective-permute-start(bf16[128,768]{1,0:T(8,128)(2,1)S(1)} %collective-permute-done.7), channel_id=1, source_target_pairs={{0,2},{2,4},{4,6},{6,7},{7,5},{5,3},{3,1},{1,0},{8,10},{10,12},{12... | collective-permute-start | bytes 589832 | tf_op jit(solution)/shard_map/ppermute | solution.py:60
  38.3 0.0 collective-permute-start.12
  38.3 2.1 %collective-permute-done = bf16[128,768]{1,0:T(8,128)(2,1)S(1)} collective-permute-done((bf16[128,768]{1,0:T(8,128)(2,1)S(1)}, bf16[128,768]{1,0:T(8,128)(2,1)S(1)}, u32[]{:S(2)}, u32[]{:S(2)}) %collective-permute-start) | collective-permute-done | bytes 196640 | tf_op jit(solution)/shard_map/ppermute | solution.py:60
  40.5 2.1 %collective-permute-start.1 = (bf16[128,768]{1,0:T(8,128)(2,1)S(1)}, bf16[128,768]{1,0:T(8,128)(2,1)S(1)}, u32[]{:S(2)}, u32[]{:S(2)}) collective-permute-start(bf16[128,768]{1,0:T(8,128)(2,1)S(1)} %collective-permute-done), channel_id=1, source_target_pairs={{0,2},{2,4},{4,6},{6,7},{7,5},{5,3},{3,1},{1,0},{8,10},{10,12},{12... | collective-permute-start | bytes 589832 | tf_op jit(solution)/shard_map/ppermute | solution.py:60
  42.5 0.0 collective-permute-start.5
  42.6 2.1 %collective-permute-done.8 = bf16[128,768]{1,0:T(8,128)(2,1)S(1)} collective-permute-done((bf16[128,768]{1,0:T(8,128)(2,1)S(1)}, bf16[128,768]{1,0:T(8,128)(2,1)S(1)}, u32[]{:S(2)}, u32[]{:S(2)}) %collective-permute-start.8) | collective-permute-done | bytes 196640 | tf_op jit(solution)/shard_map/ppermute | solution.py:60
  44.7 2.1 %collective-permute-start.9 = (bf16[128,768]{1,0:T(8,128)(2,1)S(1)}, bf16[128,768]{1,0:T(8,128)(2,1)S(1)}, u32[]{:S(2)}, u32[]{:S(2)}) collective-permute-start(bf16[128,768]{1,0:T(8,128)(2,1)S(1)} %collective-permute-done.8), channel_id=1, source_target_pairs={{0,2},{2,4},{4,6},{6,7},{7,5},{5,3},{3,1},{1,0},{8,10},{10,12},{12... | collective-permute-start | bytes 589832 | tf_op jit(solution)/shard_map/ppermute | solution.py:60
  46.8 2.1 %collective-permute-done.1 = bf16[128,768]{1,0:T(8,128)(2,1)S(1)} collective-permute-done((bf16[128,768]{1,0:T(8,128)(2,1)S(1)}, bf16[128,768]{1,0:T(8,128)(2,1)S(1)}, u32[]{:S(2)}, u32[]{:S(2)}) %collective-permute-start.1) | collective-permute-done | bytes 196640 | tf_op jit(solution)/shard_map/ppermute | solution.py:60
  48.9 2.1 %collective-permute-start.2 = (bf16[128,768]{1,0:T(8,128)(2,1)S(1)}, bf16[128,768]{1,0:T(8,128)(2,1)S(1)}, u32[]{:S(2)}, u32[]{:S(2)}) collective-permute-start(bf16[128,768]{1,0:T(8,128)(2,1)S(1)} %collective-permute-done.1), channel_id=1, source_target_pairs={{0,2},{2,4},{4,6},{6,7},{7,5},{5,3},{3,1},{1,0},{8,10},{10,12},{12... | collective-permute-start | bytes 589832 | tf_op jit(solution)/shard_map/ppermute | solution.py:60
  51.0 2.1 %collective-permute-done.9 = bf16[128,768]{1,0:T(8,128)(2,1)S(1)} collective-permute-done((bf16[128,768]{1,0:T(8,128)(2,1)S(1)}, bf16[128,768]{1,0:T(8,128)(2,1)S(1)}, u32[]{:S(2)}, u32[]{:S(2)}) %collective-permute-start.9) | collective-permute-done | bytes 196640 | tf_op jit(solution)/shard_map/ppermute | solution.py:60
  53.1 2.1 %collective-permute-start.10 = (bf16[128,768]{1,0:T(8,128)(2,1)S(1)}, bf16[128,768]{1,0:T(8,128)(2,1)S(1)}, u32[]{:S(2)}, u32[]{:S(2)}) collective-permute-start(bf16[128,768]{1,0:T(8,128)(2,1)S(1)} %collective-permute-done.9), channel_id=1, source_target_pairs={{0,2},{2,4},{4,6},{6,7},{7,5},{5,3},{3,1},{1,0},{8,10},{10,12},{12... | collective-permute-start | bytes 589832 | tf_op jit(solution)/shard_map/ppermute | solution.py:60
  55.2 2.1 %collective-permute-done.2 = bf16[128,768]{1,0:T(8,128)(2,1)S(1)} collective-permute-done((bf16[128,768]{1,0:T(8,128)(2,1)S(1)}, bf16[128,768]{1,0:T(8,128)(2,1)S(1)}, u32[]{:S(2)}, u32[]{:S(2)}) %collective-permute-start.2) | collective-permute-done | bytes 196640 | tf_op jit(solution)/shard_map/ppermute | solution.py:60
  57.3 2.1 %collective-permute-start.3 = (bf16[128,768]{1,0:T(8,128)(2,1)S(1)}, bf16[128,768]{1,0:T(8,128)(2,1)S(1)}, u32[]{:S(2)}, u32[]{:S(2)}) collective-permute-start(bf16[128,768]{1,0:T(8,128)(2,1)S(1)} %collective-permute-done.2), channel_id=1, source_target_pairs={{0,2},{2,4},{4,6},{6,7},{7,5},{5,3},{3,1},{1,0},{8,10},{10,12},{12... | collective-permute-start | bytes 589832 | tf_op jit(solution)/shard_map/ppermute | solution.py:60
  59.5 2.1 %collective-permute-done.10 = bf16[128,768]{1,0:T(8,128)(2,1)S(1)} collective-permute-done((bf16[128,768]{1,0:T(8,128)(2,1)S(1)}, bf16[128,768]{1,0:T(8,128)(2,1)S(1)}, u32[]{:S(2)}, u32[]{:S(2)}) %collective-permute-start.10) | collective-permute-done | bytes 196640 | tf_op jit(solution)/shard_map/ppermute | solution.py:60
  61.6 3.9 %collective-permute-done.3 = bf16[128,768]{1,0:T(8,128)(2,1)S(1)} collective-permute-done((bf16[128,768]{1,0:T(8,128)(2,1)S(1)}, bf16[128,768]{1,0:T(8,128)(2,1)S(1)}, u32[]{:S(2)}, u32[]{:S(2)}) %collective-permute-start.3) | collective-permute-done | bytes 196640 | tf_op jit(solution)/shard_map/ppermute | solution.py:60
  65.7 2.4 %select_reduce_fusion.3 = (f32[1024]{0:T(1024)S(1)}, f32[1024]{0:T(1024)S(1)}, f32[1024,1024]{0,1:T(8,128)S(1)}) fusion(pred[1024]{0:T(1024)(128)(4,1)S(1)} %copy-done.4, pred[1024]{0:T(1024)(128)(4,1)S(1)} %copy-done.8, s32[1024]{0:T(1024)S(1)} %bitcast.46, s32[1024]{0:T(1024)S(1)} %fusion.46, ...), kind=kOutput, calls=%fused_computation.11 | convolution fusion | flops 1618999296 | bytes 7358464 | tf_op jit(solution)/shard_map/dot_general | solution.py:67
  68.1 2.4 %fusion.1 = (f32[1024]{0:T(1024)S(1)}, f32[1024]{0:T(1024)S(1)}, f32[1024]{0:T(1024)S(1)}) fusion(f32[1024,1024]{0,1:T(8,128)S(1)} %get-tuple-element.21, s32[1024]{0:T(1024)S(1)} %bitcast.47, s32[1024]{0:T(1024)S(1)} %fusion.46, f32[1024]{0:T(1024)S(1)} %get-tuple-element.7, pred[1024]{0:T(1024)(128)(4,1)S(1)} %copy-done.8, f32[1024]{0:T(1024)S(1)} %get-tuple-element.6, ...), kind=kLoop, calls=%fused_computation.7 | loop fusion | flops 9434112 | bytes 4225024 | tf_op jit(solution)/shard_map/reduce_sum | solution.py:79
  70.6 1.9 %select_reduce_fusion.4 = (f32[]{:T(128)}, f32[1024]{0:T(1024)S(1)}, f32[]{:T(128)}, f32[1024]{0:T(1024)}) fusion(f32[1024]{0:T(1024)S(1)} %get-tuple-element.7, f32[1024]{0:T(1024)S(1)} %get-tuple-element.4, f32[1024]{0:T(1024)S(1)} %get-tuple-element.3, f32[1024]{0:T(1024)S(1)} %get-tuple-element.6, f32[1024]{0:T(1024)S(1)} %get-tuple-element.5, ...), kind=kLoop, calls=%fused_computation.103 | loop fusion | flops 16382 | bytes 32780 | tf_op jit(solution)/shard_map/reduce_sum | solution.py:150
  72.5 0.6 dynamic_slice.95
  73.1 1.3 %dynamic_slice.92 = f32[128]{0:T(128)} dynamic-slice(f32[1024]{0:T(1024)} %get-tuple-element.23, s32[]{:T(128)S(6)} %select_n.251), dynamic_slice_sizes={128} | dynamic-slice | bytes 1028 | tf_op jit(solution)/shard_map/dynamic_slice | solution.py:156
  74.4 3.2 %fusion.6 = bf16[128,768]{1,0:T(8,128)(2,1)} fusion(bf16[1024,768]{1,0:T(8,128)(2,1)S(1)} %constant_dynamic-update-slice_fusion.6, bf16[128,768]{1,0:T(8,128)(2,1)S(1)} %bitcast.43, f32[128]{0:T(128)} %dynamic_slice.95, f32[1024]{0:T(1024)} %get-tuple-element.23, s32[128]{0:T(128)} %dynamic_slice.94, f32[]{:T(128)} %bitcast, s32[1024]{0:T(1024)S(1)} %bitcast.48, ...), kind=kOutput, calls=%fused_computation.21 | convolution fusion | flops 404815872 | bytes 1976452 | tf_op jit(solution)/shard_map/dot_general | solution.py:170
  77.6 3.4 %all-to-all-start.1 = ((bf16[4,32,768]{2,1,0:T(8,128)(2,1)}), bf16[4,32,768]{2,1,0:T(8,128)(2,1)S(1)}, u32[]{:S(2)}, u32[]{:S(2)}) async-start(bf16[4,32,768]{2,1,0:T(8,128)(2,1)} %bitcast.44), calls=%async_computation.1 | async-start | bytes 393216 | tf_op jit(solution)/shard_map/all_to_all | solution.py:174
  81.0 3.4 %fusion.5 = bf16[128,768]{1,0:T(8,128)(2,1)} fusion(bf16[1024,768]{1,0:T(8,128)(2,1)S(1)} %constant_dynamic-update-slice_fusion.8, bf16[128,768]{1,0:T(8,128)(2,1)} %param.10, f32[1024]{0:T(1024)} %copy-done.6, f32[128]{0:T(128)} %dynamic_slice.92, s32[128]{0:T(128)} %fusion.55, f32[]{:T(128)} %bitcast, s32[1024]{0:T(1024)S(1)} %fusion.46, ...), kind=kOutput, calls=%fused_computation.20 | convolution fusion | flops 404815872 | bytes 1976452 | tf_op jit(solution)/shard_map/dot_general | solution.py:161
  85.8 0.5 all-to-all-done.1
  86.3 1.2 %gather_fusion.1 = bf16[4,32,768]{2,1,0:T(8,128)(2,1)} fusion(bf16[4,32,768]{2,1,0:T(8,128)(2,1)S(1)} %all-to-all-done.1, s32[1024]{0:T(1024)S(1)} %pad_clamp_fusion), kind=kCustom, calls=%fused_computation.1 | custom fusion | bytes 393232 | tf_op jit(solution)/shard_map/gather | solution.py:177
  (48 shorter events, 0.4 us)
Async XLA Ops:
  0.6 1.4 %copy-start = (bf16[4,32,768]{2,1,0:T(8,128)(2,1)S(1)}, bf16[4,32,768]{2,1,0:T(8,128)(2,1)}, u32[]{:S(2)}) copy-start(bf16[4,32,768]{2,1,0:T(8,128)(2,1)} %param.11) | copy-start | bytes 589828
  0.6 27.6 %copy-start.1 = (bf16[128,768]{1,0:T(8,128)(2,1)S(1)}, bf16[128,768]{1,0:T(8,128)(2,1)}, u32[]{:S(2)}) copy-start(bf16[128,768]{1,0:T(8,128)(2,1)} %param.10) | copy-start | bytes 589828
  3.2 29.4 %copy-start.2 = (s32[1,1024]{1,0:T(1,128)S(1)}, s32[1,1024]{1,0:T(1,128)}, u32[]{:S(2)}) copy-start(s32[1,1024]{1,0:T(1,128)} %param.14) | copy-start | bytes 12292
  3.2 23.7 %all-to-all-start = ((bf16[4,32,768]{2,1,0:T(8,128)(2,1)}), bf16[4,32,768]{2,1,0:T(8,128)(2,1)S(1)}, u32[]{:S(2)}, u32[]{:S(2)}) async-start(bf16[4,32,768]{2,1,0:T(8,128)(2,1)} %gather_fusion), calls=%async_computation | async-start | bytes 393216 | tf_op jit(solution)/shard_map/all_to_all | solution.py:107
  9.6 22.9 %copy-start.7 = (pred[1024]{0:T(1024)(128)(4,1)}, pred[1024]{0:T(1024)(128)(4,1)S(1)}, u32[]{:S(2)}) copy-start(pred[1024]{0:T(1024)(128)(4,1)S(1)} %iota_compare_fusion) | copy-start | bytes 3076
  11.2 15.7 %copy-start.3 = (pred[1024]{0:T(1024)(128)(4,1)}, pred[1024]{0:T(1024)(128)(4,1)S(1)}, u32[]{:S(2)}) copy-start(pred[1024]{0:T(1024)(128)(4,1)S(1)} %broadcast_compare_fusion) | copy-start | bytes 3076
  28.3 7.9 %collective-permute-start.7 = (bf16[128,768]{1,0:T(8,128)(2,1)S(1)}, bf16[128,768]{1,0:T(8,128)(2,1)S(1)}, u32[]{:S(2)}, u32[]{:S(2)}) collective-permute-start(bf16[128,768]{1,0:T(8,128)(2,1)S(1)} %get-tuple-element.13), channel_id=1, source_target_pairs={{0,2},{2,4},{4,6},{6,7},{7,5},{5,3},{3,1},{1,0},{8,10},{10,12},{12... | collective-permute-start | bytes 589832 | tf_op jit(solution)/shard_map/ppermute | solution.py:60
  30.5 7.8 %collective-permute-start.11 = (bf16[128,768]{1,0:T(8,128)(2,1)S(1)}, bf16[128,768]{1,0:T(8,128)(2,1)S(1)}, u32[]{:S(2)}, u32[]{:S(2)}) collective-permute-start(bf16[128,768]{1,0:T(8,128)(2,1)S(1)} %get-tuple-element.13), channel_id=1, source_target_pairs={{0,1},{2,0},{4,2},{6,4},{7,6},{5,7},{3,5},{1,3},{8,9},{10,8},{12,1... | collective-permute-start | bytes 589832 | tf_op jit(solution)/shard_map/ppermute | solution.py:60
  30.6 9.9 %collective-permute-start = (bf16[128,768]{1,0:T(8,128)(2,1)S(1)}, bf16[128,768]{1,0:T(8,128)(2,1)S(1)}, u32[]{:S(2)}, u32[]{:S(2)}) collective-permute-start(bf16[128,768]{1,0:T(8,128)(2,1)S(1)} %bitcast.40), channel_id=1, source_target_pairs={{0,2},{2,4},{4,6},{6,7},{7,5},{5,3},{3,1},{1,0},{8,10},{10,12},{12... | collective-permute-start | bytes 589832 | tf_op jit(solution)/shard_map/ppermute | solution.py:60
  32.6 10.0 %collective-permute-start.4 = (bf16[128,768]{1,0:T(8,128)(2,1)S(1)}, bf16[128,768]{1,0:T(8,128)(2,1)S(1)}, u32[]{:S(2)}, u32[]{:S(2)}) collective-permute-start(bf16[128,768]{1,0:T(8,128)(2,1)S(1)} %bitcast.41), channel_id=1, source_target_pairs={{0,1},{2,0},{4,2},{6,4},{7,6},{5,7},{3,5},{1,3},{8,9},{10,8},{12,1... | collective-permute-start | bytes 589832 | tf_op jit(solution)/shard_map/ppermute | solution.py:60
  36.2 8.4 %collective-permute-start.8 = (bf16[128,768]{1,0:T(8,128)(2,1)S(1)}, bf16[128,768]{1,0:T(8,128)(2,1)S(1)}, u32[]{:S(2)}, u32[]{:S(2)}) collective-permute-start(bf16[128,768]{1,0:T(8,128)(2,1)S(1)} %collective-permute-done.7), channel_id=1, source_target_pairs={{0,2},{2,4},{4,6},{6,7},{7,5},{5,3},{3,1},{1,0},{8,10},{10,12},{12... | collective-permute-start | bytes 589832 | tf_op jit(solution)/shard_map/ppermute | solution.py:60
  38.3 8.4 %collective-permute-start.12 = (bf16[128,768]{1,0:T(8,128)(2,1)S(1)}, bf16[128,768]{1,0:T(8,128)(2,1)S(1)}, u32[]{:S(2)}, u32[]{:S(2)}) collective-permute-start(bf16[128,768]{1,0:T(8,128)(2,1)S(1)} %collective-permute-done.11), channel_id=1, source_target_pairs={{0,1},{2,0},{4,2},{6,4},{7,6},{5,7},{3,5},{1,3},{8,9},{10,8},{12,1... | collective-permute-start | bytes 589832 | tf_op jit(solution)/shard_map/ppermute | solution.py:60
  40.5 8.4 %collective-permute-start.1 = (bf16[128,768]{1,0:T(8,128)(2,1)S(1)}, bf16[128,768]{1,0:T(8,128)(2,1)S(1)}, u32[]{:S(2)}, u32[]{:S(2)}) collective-permute-start(bf16[128,768]{1,0:T(8,128)(2,1)S(1)} %collective-permute-done), channel_id=1, source_target_pairs={{0,2},{2,4},{4,6},{6,7},{7,5},{5,3},{3,1},{1,0},{8,10},{10,12},{12... | collective-permute-start | bytes 589832 | tf_op jit(solution)/shard_map/ppermute | solution.py:60
  42.5 8.4 %collective-permute-start.5 = (bf16[128,768]{1,0:T(8,128)(2,1)S(1)}, bf16[128,768]{1,0:T(8,128)(2,1)S(1)}, u32[]{:S(2)}, u32[]{:S(2)}) collective-permute-start(bf16[128,768]{1,0:T(8,128)(2,1)S(1)} %collective-permute-done.4), channel_id=1, source_target_pairs={{0,1},{2,0},{4,2},{6,4},{7,6},{5,7},{3,5},{1,3},{8,9},{10,8},{12,1... | collective-permute-start | bytes 589832 | tf_op jit(solution)/shard_map/ppermute | solution.py:60
  44.7 8.4 %collective-permute-start.9 = (bf16[128,768]{1,0:T(8,128)(2,1)S(1)}, bf16[128,768]{1,0:T(8,128)(2,1)S(1)}, u32[]{:S(2)}, u32[]{:S(2)}) collective-permute-start(bf16[128,768]{1,0:T(8,128)(2,1)S(1)} %collective-permute-done.8), channel_id=1, source_target_pairs={{0,2},{2,4},{4,6},{6,7},{7,5},{5,3},{3,1},{1,0},{8,10},{10,12},{12... | collective-permute-start | bytes 589832 | tf_op jit(solution)/shard_map/ppermute | solution.py:60
  46.7 18.9 %collective-permute-start.13 = (bf16[128,768]{1,0:T(8,128)(2,1)S(1)}, bf16[128,768]{1,0:T(8,128)(2,1)S(1)}, u32[]{:S(2)}, u32[]{:S(2)}) collective-permute-start(bf16[128,768]{1,0:T(8,128)(2,1)S(1)} %collective-permute-done.12), channel_id=1, source_target_pairs={{0,1},{2,0},{4,2},{6,4},{7,6},{5,7},{3,5},{1,3},{8,9},{10,8},{12,1... | collective-permute-start | bytes 589832 | tf_op jit(solution)/shard_map/ppermute | solution.py:60
  48.9 8.4 %collective-permute-start.2 = (bf16[128,768]{1,0:T(8,128)(2,1)S(1)}, bf16[128,768]{1,0:T(8,128)(2,1)S(1)}, u32[]{:S(2)}, u32[]{:S(2)}) collective-permute-start(bf16[128,768]{1,0:T(8,128)(2,1)S(1)} %collective-permute-done.1), channel_id=1, source_target_pairs={{0,2},{2,4},{4,6},{6,7},{7,5},{5,3},{3,1},{1,0},{8,10},{10,12},{12... | collective-permute-start | bytes 589832 | tf_op jit(solution)/shard_map/ppermute | solution.py:60
  51.0 14.7 %collective-permute-start.6 = (bf16[128,768]{1,0:T(8,128)(2,1)S(1)}, bf16[128,768]{1,0:T(8,128)(2,1)S(1)}, u32[]{:S(2)}, u32[]{:S(2)}) collective-permute-start(bf16[128,768]{1,0:T(8,128)(2,1)S(1)} %collective-permute-done.5), channel_id=1, source_target_pairs={{0,1},{2,0},{4,2},{6,4},{7,6},{5,7},{3,5},{1,3},{8,9},{10,8},{12,1... | collective-permute-start | bytes 589832 | tf_op jit(solution)/shard_map/ppermute | solution.py:60
  53.1 8.4 %collective-permute-start.10 = (bf16[128,768]{1,0:T(8,128)(2,1)S(1)}, bf16[128,768]{1,0:T(8,128)(2,1)S(1)}, u32[]{:S(2)}, u32[]{:S(2)}) collective-permute-start(bf16[128,768]{1,0:T(8,128)(2,1)S(1)} %collective-permute-done.9), channel_id=1, source_target_pairs={{0,2},{2,4},{4,6},{6,7},{7,5},{5,3},{3,1},{1,0},{8,10},{10,12},{12... | collective-permute-start | bytes 589832 | tf_op jit(solution)/shard_map/ppermute | solution.py:60
  57.3 8.2 %collective-permute-start.3 = (bf16[128,768]{1,0:T(8,128)(2,1)S(1)}, bf16[128,768]{1,0:T(8,128)(2,1)S(1)}, u32[]{:S(2)}, u32[]{:S(2)}) collective-permute-start(bf16[128,768]{1,0:T(8,128)(2,1)S(1)} %collective-permute-done.2), channel_id=1, source_target_pairs={{0,2},{2,4},{4,6},{6,7},{7,5},{5,3},{3,1},{1,0},{8,10},{10,12},{12... | collective-permute-start | bytes 589832 | tf_op jit(solution)/shard_map/ppermute | solution.py:60
  59.4 6.3 %copy-start.4 = (pred[1024]{0:T(1024)(128)(4,1)S(1)}, pred[1024]{0:T(1024)(128)(4,1)}, u32[]{:S(2)}) copy-start(pred[1024]{0:T(1024)(128)(4,1)} %copy-done.3) | copy-start | bytes 3076
  59.4 6.3 %copy-start.8 = (pred[1024]{0:T(1024)(128)(4,1)S(1)}, pred[1024]{0:T(1024)(128)(4,1)}, u32[]{:S(2)}) copy-start(pred[1024]{0:T(1024)(128)(4,1)} %copy-done.7) | copy-start | bytes 3076
  72.5 1.9 %copy-start.6 = (f32[1024]{0:T(1024)}, f32[1024]{0:T(1024)S(1)}, u32[]{:S(2)}) copy-start(f32[1024]{0:T(1024)S(1)} %get-tuple-element.9) | copy-start | bytes 12292
  74.4 6.6 %copy-start.5 = (pred[1024]{0:T(1024)(128)(4,1)S(1)}, pred[1024]{0:T(1024)(128)(4,1)}, u32[]{:S(2)}) copy-start(pred[1024]{0:T(1024)(128)(4,1)} %copy-done.3) | copy-start | bytes 3076
  77.6 8.6 %all-to-all-start.1 = ((bf16[4,32,768]{2,1,0:T(8,128)(2,1)}), bf16[4,32,768]{2,1,0:T(8,128)(2,1)S(1)}, u32[]{:S(2)}, u32[]{:S(2)}) async-start(bf16[4,32,768]{2,1,0:T(8,128)(2,1)} %bitcast.44), calls=%async_computation.1 | async-start | bytes 393216 | tf_op jit(solution)/shard_map/all_to_all | solution.py:174

commit v11 on v8

--- a/solution.py
+++ b/solution.py
@@ -41,7 +41,7 @@
     return order
 
 
-def ring_gather(block, ring):
+def ring_gather(block, ring, lang_size):
     count = len(ring)
     place = [0] * count
     for p, d in enumerate(ring):
@@ -49,16 +49,24 @@
     ring_arr = jnp.array(ring, jnp.int32)
     my_dp = lax.axis_index("dp")
     my_pos = jnp.array(place, jnp.int32)[my_dp]
-    ahead = [(ring[p], ring[(p + 1) % count]) for p in range(count)]
-    behind = [(ring[p], ring[(p - 1) % count]) for p in range(count)]
+    mirror = 1 - 2 * (lax.axis_index("lang") % 2)
+
+    def pairs_for(even_step):
+        out = []
+        for l in range(lang_size):
+            step = even_step if l % 2 == 0 else -even_step
+            out += [(l * count + ring[p], l * count + ring[(p + step) % count]) for p in range(count)]
+        return out
+
     rows = block.shape[0]
     out = jnp.zeros((count * rows,) + block.shape[1:], block.dtype)
     out = lax.dynamic_update_slice_in_dim(out, block, my_dp * rows, 0)
-    for pairs, steps, sign in ((ahead, count // 2, -1), (behind, count - 1 - count // 2, 1)):
+    for even_step, steps in ((1, count // 2), (-1, count - 1 - count // 2)):
+        pairs = pairs_for(even_step)
         cur = block
         for t in range(1, steps + 1):
-            cur = lax.ppermute(cur, "dp", pairs)
-            origin = ring_arr[(my_pos + sign * t) % count]
+            cur = lax.ppermute(cur, ("lang", "dp"), pairs)
+            origin = ring_arr[(my_pos - even_step * mirror * t) % count]
             out = lax.dynamic_update_slice_in_dim(out, cur, origin * rows, 0)
     return out
 
@@ -114,8 +122,8 @@
     perm = target_index(pair_rows, row_count, per_slot, data_size)
     live_pos = (perm[None, :] == pair_align[:, None]) & row_live[:, None]
     col_live = jnp.max(live_pos.astype(jnp.int32), axis=0) > 0
-    x_all = ring_gather(src_emb, ring)
-    y_all = ring_gather(partner, ring)
+    x_all = ring_gather(src_emb, ring, lang_size)
+    y_all = ring_gather(partner, ring, lang_size)
 
     block = max(1, min(pair_rows, BLOCK_BYTES // (4 * pair_rows)))
     steps = pair_rows // block

time: 83.8 us -> 80.7 us (0.963)
  waiting for transfers between devices: 16.7 us -> 11.2 us
  starting transfers between devices: 24.1 us -> 26.5 us
    ppermute x14, waiting for transfers between devices: 16.3 us -> 10.7 us  [ring_gather(): cur = lax.ppermute(cur, ('lang', 'dp'), pairs)]
    ppermute x14, starting transfers between devices: 17.3 us -> 19.6 us  [ring_gather(): cur = lax.ppermute(cur, ('lang', 'dp'), pairs)]
  transfers between devices with their start and end apart: 16 -> 16, of which waited for: 8 -> 8; matrix products, arithmetic and copies ran while one was open for 19% -> 20% of each run, Pallas kernels for 0% -> 0%
where the time goes in v11:
time: 80.7 us; the launch traced here: 80.1 us
  starting transfers between devices  26.5 us (33%)
  between operations  13.1 us (16%)
  local copies, waits for them, and re-layouts  12.9 us (16%)
  waiting for transfers between devices  11.2 us (14%)
  matrix products  9.15 us (11%)
  other arithmetic  7.11 us (9%)
    ppermute x14, starting transfers between devices, ring_gather(): cur = lax.ppermute(cur, ('lang', 'dp'), pairs)  19.6 us
    ppermute x14, waiting for transfers between devices, ring_gather(): cur = lax.ppermute(cur, ('lang', 'dp'), pairs)  10.7 us
    all_to_all x1, starting transfers between devices, per_device(): lax.all_to_all(grad_local.reshape(lang_size, per_slot, emb_width), 'lang'...  3.59 us
    dot_general x1, matrix products, per_device(): jnp.dot(g_rows, y_all, preferred_element_type=jnp.float32) * inv_root  3.48 us
    all_to_all x1, starting transfers between devices, per_device(): lax.all_to_all(ordered, 'lang', split_axis=0, concat_axis=1, tiled=True)  3.37 us
    dot_general x1, matrix products, per_device(): lax.dot_general(g_cols, x_all, (((0,), (0,)), ((), ())), preferred_elemen...  3.27 us
    reduce_sum x1, other arithmetic, block_stats(): pos_score = jnp.sum(jnp.where(is_pos, scores_f, 0.0), axis=1)  2.43 us
    dot_general x1, matrix products, scores_of(): lax.dot_general(x_rows, y_rows, (((1,), (1,)), ((), ())), preferred_eleme...  2.4 us
  transfers between devices with their start and end apart: 16, of which 8 were waited for; matrix products, arithmetic and copies ran while one was open for 20% of the time, Pallas kernels for 0%

profile of v11, /device:TPU:0, one launch (start us, length us, event | category | flops | bytes accessed | tf_op | source)
XLA Modules:
  0.0 80.1 jit_solution(12979332320661655334)
XLA Ops:
  0.7 3.1 %collective-permute-start.7 = (bf16[128,768]{1,0:T(8,128)(2,1)}, bf16[128,768]{1,0:T(8,128)(2,1)}, u32[]{:S(2)}, u32[]{:S(2)}) collective-permute-start(bf16[128,768]{1,0:T(8,128)(2,1)} %param.10), channel_id=1, source_target_pairs={{0,2},{2,4},{4,6},{6,7},{7,5},{5,3},{3,1},{1,0},{8,9},{10,8},{12,1... | collective-permute-start | bytes 589832 | tf_op jit(solution)/shard_map/ppermute | solution.py:68
  3.8 0.7 compare_select_fusion.5
  4.5 0.6 scatter_custom_fusion
  5.1 1.2 %gather_fusion = bf16[4,32,768]{2,1,0:T(8,128)(2,1)} fusion(bf16[4,32,768]{2,1,0:T(8,128)(2,1)S(1)} %copy-done, s32[1024]{0:T(1024)S(1)} %pad_clamp_fusion.1), kind=kCustom, calls=%fused_computation | custom fusion | bytes 393232 | tf_op jit(solution)/shard_map/gather | solution.py:114
  6.3 3.4 %all-to-all-start = ((bf16[4,32,768]{2,1,0:T(8,128)(2,1)}), bf16[4,32,768]{2,1,0:T(8,128)(2,1)S(1)}, u32[]{:S(2)}, u32[]{:S(2)}) async-start(bf16[4,32,768]{2,1,0:T(8,128)(2,1)} %gather_fusion), calls=%async_computation | async-start | bytes 393216 | tf_op jit(solution)/shard_map/all_to_all | solution.py:115
  9.7 1.3 %dynamic_slice.73 = s32[1]{0:T(128)} dynamic-slice(s32[4]{0:T(128)} %param.13, s32[]{:T(128)S(6)} %select_n.256), dynamic_slice_sizes={1} | dynamic-slice | bytes 12 | tf_op jit(solution)/shard_map/dynamic_slice | solution.py:117
  11.0 0.6 iota_compare_fusion
  11.7 1.5 %convert_reduce_fusion = s32[1024]{0:T(1024)S(1)} fusion(s32[1024]{0:T(1024)} %bitcast.37, s32[1024]{0:T(1024)S(1)} %fusion.46, pred[1024]{0:T(1024)(128)(4,1)S(1)} %iota_compare_fusion), kind=kLoop, calls=%fused_computation.12 | loop fusion | flops 4193280 | bytes 13312 | tf_op jit(solution)/shard_map/reduce_max | solution.py:124
  13.2 0.1 broadcast.196.clone.1
  13.4 0.6 dynamic_slice.75
  18.6 0.7 fusion.66
  24.3 0.7 dynamic_slice.94
  25.0 0.6 dynamic_slice.74
  25.6 0.6 dynamic_slice.93
  26.2 0.6 dynamic_slice.72
  26.8 0.5 fusion.55
  27.3 2.0 %collective-permute-start = (bf16[128,768]{1,0:T(8,128)(2,1)S(1)}, bf16[128,768]{1,0:T(8,128)(2,1)S(1)}, u32[]{:S(2)}, u32[]{:S(2)}) collective-permute-start(bf16[128,768]{1,0:T(8,128)(2,1)S(1)} %bitcast.32), channel_id=1, source_target_pairs={{0,2},{2,4},{4,6},{6,7},{7,5},{5,3},{3,1},{1,0},{8,9},{10,8},{12,1... | collective-permute-start | bytes 589832 | tf_op jit(solution)/shard_map/ppermute | solution.py:68
  29.4 0.0 collective-permute-start.4
  29.4 0.1 broadcast.196.clone
  29.5 2.1 %collective-permute-start.8 = (bf16[128,768]{1,0:T(8,128)(2,1)}, bf16[128,768]{1,0:T(8,128)(2,1)S(1)}, u32[]{:S(2)}, u32[]{:S(2)}) collective-permute-start(bf16[128,768]{1,0:T(8,128)(2,1)} %collective-permute-done.7), channel_id=1, source_target_pairs={{0,2},{2,4},{4,6},{6,7},{7,5},{5,3},{3,1},{1,0},{8,9},{10,8},{12,1... | collective-permute-start | bytes 589832 | tf_op jit(solution)/shard_map/ppermute | solution.py:68
  31.6 0.0 collective-permute-start.12
  31.6 1.0 %constant_dynamic-update-slice_fusion.1 = bf16[1024,768]{1,0:T(8,128)(2,1)S(1)} fusion(bf16[1024,768]{1,0:T(8,128)(2,1)S(1)} %constant_dynamic-update-slice_fusion.7, bf16[128,768]{1,0:T(8,128)(2,1)} %collective-permute-done.7, s32[]{:T(128)S(6)} %select_n.268), kind=kLoop, calls=%fused_computation.74 | loop fusion | bytes 393220 | tf_op jit(solution)/shard_map/dynamic_update_slice | solution.py:70
  32.6 2.1 %collective-permute-done = bf16[128,768]{1,0:T(8,128)(2,1)S(1)} collective-permute-done((bf16[128,768]{1,0:T(8,128)(2,1)S(1)}, bf16[128,768]{1,0:T(8,128)(2,1)S(1)}, u32[]{:S(2)}, u32[]{:S(2)}) %collective-permute-start) | collective-permute-done | bytes 196640 | tf_op jit(solution)/shard_map/ppermute | solution.py:68
  34.6 2.5 %collective-permute-start.1 = (bf16[128,768]{1,0:T(8,128)(2,1)S(1)}, bf16[128,768]{1,0:T(8,128)(2,1)S(1)}, u32[]{:S(2)}, u32[]{:S(2)}) collective-permute-start(bf16[128,768]{1,0:T(8,128)(2,1)S(1)} %collective-permute-done), channel_id=1, source_target_pairs={{0,2},{2,4},{4,6},{6,7},{7,5},{5,3},{3,1},{1,0},{8,9},{10,8},{12,1... | collective-permute-start | bytes 589832 | tf_op jit(solution)/shard_map/ppermute | solution.py:68
  37.1 0.0 collective-permute-start.5
  37.2 1.8 %collective-permute-done.8 = bf16[128,768]{1,0:T(8,128)(2,1)S(1)} collective-permute-done((bf16[128,768]{1,0:T(8,128)(2,1)}, bf16[128,768]{1,0:T(8,128)(2,1)S(1)}, u32[]{:S(2)}, u32[]{:S(2)}) %collective-permute-start.8) | collective-permute-done | bytes 196640 | tf_op jit(solution)/shard_map/ppermute | solution.py:68
  39.0 2.4 %collective-permute-start.9 = (bf16[128,768]{1,0:T(8,128)(2,1)S(1)}, bf16[128,768]{1,0:T(8,128)(2,1)S(1)}, u32[]{:S(2)}, u32[]{:S(2)}) collective-permute-start(bf16[128,768]{1,0:T(8,128)(2,1)S(1)} %collective-permute-done.8), channel_id=1, source_target_pairs={{0,2},{2,4},{4,6},{6,7},{7,5},{5,3},{3,1},{1,0},{8,9},{10,8},{12,1... | collective-permute-start | bytes 589832 | tf_op jit(solution)/shard_map/ppermute | solution.py:68
  41.3 0.0 collective-permute-start.13
  41.4 1.7 %collective-permute-done.1 = bf16[128,768]{1,0:T(8,128)(2,1)S(1)} collective-permute-done((bf16[128,768]{1,0:T(8,128)(2,1)S(1)}, bf16[128,768]{1,0:T(8,128)(2,1)S(1)}, u32[]{:S(2)}, u32[]{:S(2)}) %collective-permute-start.1) | collective-permute-done | bytes 196640 | tf_op jit(solution)/shard_map/ppermute | solution.py:68
  43.1 2.5 %collective-permute-start.2 = (bf16[128,768]{1,0:T(8,128)(2,1)S(1)}, bf16[128,768]{1,0:T(8,128)(2,1)S(1)}, u32[]{:S(2)}, u32[]{:S(2)}) collective-permute-start(bf16[128,768]{1,0:T(8,128)(2,1)S(1)} %collective-permute-done.1), channel_id=1, source_target_pairs={{0,2},{2,4},{4,6},{6,7},{7,5},{5,3},{3,1},{1,0},{8,9},{10,8},{12,1... | collective-permute-start | bytes 589832 | tf_op jit(solution)/shard_map/ppermute | solution.py:68
  45.6 0.0 collective-permute-start.6
  45.6 1.7 %collective-permute-done.9 = bf16[128,768]{1,0:T(8,128)(2,1)S(1)} collective-permute-done((bf16[128,768]{1,0:T(8,128)(2,1)S(1)}, bf16[128,768]{1,0:T(8,128)(2,1)S(1)}, u32[]{:S(2)}, u32[]{:S(2)}) %collective-permute-start.9) | collective-permute-done | bytes 196640 | tf_op jit(solution)/shard_map/ppermute | solution.py:68
  47.3 2.5 %collective-permute-start.10 = (bf16[128,768]{1,0:T(8,128)(2,1)S(1)}, bf16[128,768]{1,0:T(8,128)(2,1)S(1)}, u32[]{:S(2)}, u32[]{:S(2)}) collective-permute-start(bf16[128,768]{1,0:T(8,128)(2,1)S(1)} %collective-permute-done.9), channel_id=1, source_target_pairs={{0,2},{2,4},{4,6},{6,7},{7,5},{5,3},{3,1},{1,0},{8,9},{10,8},{12,1... | collective-permute-start | bytes 589832 | tf_op jit(solution)/shard_map/ppermute | solution.py:68
  49.8 1.3 %collective-permute-done.2 = bf16[128,768]{1,0:T(8,128)(2,1)S(1)} collective-permute-done((bf16[128,768]{1,0:T(8,128)(2,1)S(1)}, bf16[128,768]{1,0:T(8,128)(2,1)S(1)}, u32[]{:S(2)}, u32[]{:S(2)}) %collective-permute-start.2) | collective-permute-done | bytes 196640 | tf_op jit(solution)/shard_map/ppermute | solution.py:68
  51.1 2.5 %collective-permute-start.3 = (bf16[128,768]{1,0:T(8,128)(2,1)S(1)}, bf16[128,768]{1,0:T(8,128)(2,1)S(1)}, u32[]{:S(2)}, u32[]{:S(2)}) collective-permute-start(bf16[128,768]{1,0:T(8,128)(2,1)S(1)} %collective-permute-done.2), channel_id=1, source_target_pairs={{0,2},{2,4},{4,6},{6,7},{7,5},{5,3},{3,1},{1,0},{8,9},{10,8},{12,1... | collective-permute-start | bytes 589832 | tf_op jit(solution)/shard_map/ppermute | solution.py:68
  53.6 0.5 collective-permute-done.10
  54.1 0.9 %constant_dynamic-update-slice_fusion.2 = bf16[1024,768]{1,0:T(8,128)(2,1)S(1)} fusion(bf16[1024,768]{1,0:T(8,128)(2,1)S(1)} %constant_dynamic-update-slice_fusion.3, bf16[128,768]{1,0:T(8,128)(2,1)} %collective-permute-done.11, s32[]{:T(128)S(6)} %select_n.280), kind=kLoop, calls=%fused_computation.75 | loop fusion | bytes 393220 | tf_op jit(solution)/shard_map/dynamic_update_slice | solution.py:70
  55.1 1.7 %collective-permute-done.3 = bf16[128,768]{1,0:T(8,128)(2,1)S(1)} collective-permute-done((bf16[128,768]{1,0:T(8,128)(2,1)S(1)}, bf16[128,768]{1,0:T(8,128)(2,1)S(1)}, u32[]{:S(2)}, u32[]{:S(2)}) %collective-permute-start.3) | collective-permute-done | bytes 196640 | tf_op jit(solution)/shard_map/ppermute | solution.py:68
  56.9 2.4 %select_reduce_fusion.3 = (f32[1024]{0:T(1024)S(1)}, f32[1024]{0:T(1024)S(1)}, f32[1024,1024]{0,1:T(8,128)S(1)}) fusion(pred[1024]{0:T(1024)(128)(4,1)S(1)} %copy-done.5, pred[1024]{0:T(1024)(128)(4,1)S(1)} %copy-done.9, s32[1024]{0:T(1024)S(1)} %bitcast.38, s32[1024]{0:T(1024)S(1)} %fusion.46, ...), kind=kOutput, calls=%fused_computation.11 | convolution fusion | flops 1618999296 | bytes 7358464 | tf_op jit(solution)/shard_map/dot_general | solution.py:75
  59.3 2.4 %fusion.1 = (f32[1024]{0:T(1024)S(1)}, f32[1024]{0:T(1024)S(1)}, f32[1024]{0:T(1024)S(1)}) fusion(f32[1024,1024]{0,1:T(8,128)S(1)} %get-tuple-element.19, s32[1024]{0:T(1024)S(1)} %bitcast.39, s32[1024]{0:T(1024)S(1)} %fusion.46, f32[1024]{0:T(1024)S(1)} %get-tuple-element.7, pred[1024]{0:T(1024)(128)(4,1)S(1)} %copy-done.9, f32[1024]{0:T(1024)S(1)} %get-tuple-element.6, ...), kind=kLoop, calls=%fused_computation.7 | loop fusion | flops 9434112 | bytes 4225024 | tf_op jit(solution)/shard_map/reduce_sum | solution.py:87
  61.8 1.9 %select_reduce_fusion.4 = (f32[]{:T(128)}, f32[1024]{0:T(1024)S(1)}, f32[]{:T(128)}, f32[1024]{0:T(1024)}) fusion(f32[1024]{0:T(1024)S(1)} %get-tuple-element.7, f32[1024]{0:T(1024)S(1)} %get-tuple-element.4, f32[1024]{0:T(1024)S(1)} %get-tuple-element.3, f32[1024]{0:T(1024)S(1)} %get-tuple-element.6, f32[1024]{0:T(1024)S(1)} %get-tuple-element.5, ...), kind=kLoop, calls=%fused_computation.102 | loop fusion | flops 16382 | bytes 32780 | tf_op jit(solution)/shard_map/reduce_sum | solution.py:157
  63.6 0.6 dynamic_slice.95
  64.2 1.3 %dynamic_slice.92 = f32[128]{0:T(128)} dynamic-slice(f32[1024]{0:T(1024)} %get-tuple-element.21, s32[]{:T(128)S(6)} %select_n.257), dynamic_slice_sizes={128} | dynamic-slice | bytes 1028 | tf_op jit(solution)/shard_map/dynamic_slice | solution.py:163
  65.5 3.3 %fusion.6 = bf16[128,768]{1,0:T(8,128)(2,1)} fusion(bf16[1024,768]{1,0:T(8,128)(2,1)S(1)} %constant_dynamic-update-slice_fusion.6, bf16[128,768]{1,0:T(8,128)(2,1)S(1)} %bitcast.35, f32[128]{0:T(128)} %dynamic_slice.95, f32[1024]{0:T(1024)} %get-tuple-element.21, s32[128]{0:T(128)} %dynamic_slice.94, f32[]{:T(128)} %bitcast, s32[1024]{0:T(1024)S(1)} %bitcast.40, ...), kind=kOutput, calls=%fused_computation.21 | convolution fusion | flops 404815872 | bytes 1976452 | tf_op jit(solution)/shard_map/dot_general | solution.py:177
  68.8 3.6 %all-to-all-start.1 = ((bf16[4,32,768]{2,1,0:T(8,128)(2,1)}), bf16[4,32,768]{2,1,0:T(8,128)(2,1)S(1)}, u32[]{:S(2)}, u32[]{:S(2)}) async-start(bf16[4,32,768]{2,1,0:T(8,128)(2,1)} %bitcast.36), calls=%async_computation.1 | async-start | bytes 393216 | tf_op jit(solution)/shard_map/all_to_all | solution.py:181
  72.4 3.5 %fusion.5 = bf16[128,768]{1,0:T(8,128)(2,1)} fusion(bf16[1024,768]{1,0:T(8,128)(2,1)S(1)} %constant_dynamic-update-slice_fusion.8, bf16[128,768]{1,0:T(8,128)(2,1)} %param.10, f32[1024]{0:T(1024)} %copy-done.7, f32[128]{0:T(128)} %dynamic_slice.92, s32[128]{0:T(128)} %fusion.55, f32[]{:T(128)} %bitcast, s32[1024]{0:T(1024)S(1)} %fusion.46, ...), kind=kOutput, calls=%fused_computation.20 | convolution fusion | flops 404815872 | bytes 1976452 | tf_op jit(solution)/shard_map/dot_general | solution.py:168
  77.2 0.5 all-to-all-done.1
  77.7 1.2 %gather_fusion.1 = bf16[4,32,768]{2,1,0:T(8,128)(2,1)} fusion(bf16[4,32,768]{2,1,0:T(8,128)(2,1)S(1)} %all-to-all-done.1, s32[1024]{0:T(1024)S(1)} %pad_clamp_fusion), kind=kCustom, calls=%fused_computation.1 | custom fusion | bytes 393232 | tf_op jit(solution)/shard_map/gather | solution.py:184
  (53 shorter events, 0.4 us)
Async XLA Ops:
  0.6 4.4 %copy-start = (bf16[4,32,768]{2,1,0:T(8,128)(2,1)S(1)}, bf16[4,32,768]{2,1,0:T(8,128)(2,1)}, u32[]{:S(2)}) copy-start(bf16[4,32,768]{2,1,0:T(8,128)(2,1)} %param.11) | copy-start | bytes 589828
  0.6 12.7 %copy-start.11 = (s32[8]{0:T(128)S(1)}, s32[8]{0:T(128)}, u32[]{:S(2)}) copy-start(s32[8]{0:T(128)} %constant.211.clone) | copy-start | bytes 100
  0.7 18.0 %copy-start.2 = (s32[8]{0:T(128)S(1)}, s32[8]{0:T(128)}, u32[]{:S(2)}) copy-start(s32[8]{0:T(128)} %constant.210.clone) | copy-start | bytes 100
  0.7 12.6 %copy-start.1 = (bf16[128,768]{1,0:T(8,128)(2,1)S(1)}, bf16[128,768]{1,0:T(8,128)(2,1)}, u32[]{:S(2)}) copy-start(bf16[128,768]{1,0:T(8,128)(2,1)} %param.10) | copy-start | bytes 589828
  0.7 28.8 %collective-permute-start.7 = (bf16[128,768]{1,0:T(8,128)(2,1)}, bf16[128,768]{1,0:T(8,128)(2,1)}, u32[]{:S(2)}, u32[]{:S(2)}) collective-permute-start(bf16[128,768]{1,0:T(8,128)(2,1)} %param.10), channel_id=1, source_target_pairs={{0,2},{2,4},{4,6},{6,7},{7,5},{5,3},{3,1},{1,0},{8,9},{10,8},{12,1... | collective-permute-start | bytes 589832 | tf_op jit(solution)/shard_map/ppermute | solution.py:68
  3.8 27.8 %collective-permute-start.11 = (bf16[128,768]{1,0:T(8,128)(2,1)}, bf16[128,768]{1,0:T(8,128)(2,1)}, u32[]{:S(2)}, u32[]{:S(2)}) collective-permute-start(bf16[128,768]{1,0:T(8,128)(2,1)} %param.10), channel_id=1, source_target_pairs={{0,1},{2,0},{4,2},{6,4},{7,6},{5,7},{3,5},{1,3},{8,10},{10,12},{12... | collective-permute-start | bytes 589832 | tf_op jit(solution)/shard_map/ppermute | solution.py:68
  5.1 21.1 %copy-start.10 = (f32[4]{0:T(128)S(1)}, f32[4]{0:T(128)}, u32[]{:S(2)}) copy-start(f32[4]{0:T(128)} %param.15) | copy-start | bytes 52
  5.1 21.7 %copy-start.3 = (s32[1,1024]{1,0:T(1,128)S(1)}, s32[1,1024]{1,0:T(1,128)}, u32[]{:S(2)}) copy-start(s32[1,1024]{1,0:T(1,128)} %param.14) | copy-start | bytes 12292
  6.3 21.0 %all-to-all-start = ((bf16[4,32,768]{2,1,0:T(8,128)(2,1)}), bf16[4,32,768]{2,1,0:T(8,128)(2,1)S(1)}, u32[]{:S(2)}, u32[]{:S(2)}) async-start(bf16[4,32,768]{2,1,0:T(8,128)(2,1)} %gather_fusion), calls=%async_computation | async-start | bytes 393216 | tf_op jit(solution)/shard_map/all_to_all | solution.py:115
  11.6 17.7 %copy-start.8 = (pred[1024]{0:T(1024)(128)(4,1)}, pred[1024]{0:T(1024)(128)(4,1)S(1)}, u32[]{:S(2)}) copy-start(pred[1024]{0:T(1024)(128)(4,1)S(1)} %iota_compare_fusion) | copy-start | bytes 3076
  13.2 16.2 %copy-start.4 = (pred[1024]{0:T(1024)(128)(4,1)}, pred[1024]{0:T(1024)(128)(4,1)S(1)}, u32[]{:S(2)}) copy-start(pred[1024]{0:T(1024)(128)(4,1)S(1)} %broadcast_compare_fusion) | copy-start | bytes 3076
  27.3 7.3 %collective-permute-start = (bf16[128,768]{1,0:T(8,128)(2,1)S(1)}, bf16[128,768]{1,0:T(8,128)(2,1)S(1)}, u32[]{:S(2)}, u32[]{:S(2)}) collective-permute-start(bf16[128,768]{1,0:T(8,128)(2,1)S(1)} %bitcast.32), channel_id=1, source_target_pairs={{0,2},{2,4},{4,6},{6,7},{7,5},{5,3},{3,1},{1,0},{8,9},{10,8},{12,1... | collective-permute-start | bytes 589832 | tf_op jit(solution)/shard_map/ppermute | solution.py:68
  29.4 7.8 %collective-permute-start.4 = (bf16[128,768]{1,0:T(8,128)(2,1)S(1)}, bf16[128,768]{1,0:T(8,128)(2,1)S(1)}, u32[]{:S(2)}, u32[]{:S(2)}) collective-permute-start(bf16[128,768]{1,0:T(8,128)(2,1)S(1)} %bitcast.33), channel_id=1, source_target_pairs={{0,1},{2,0},{4,2},{6,4},{7,6},{5,7},{3,5},{1,3},{8,10},{10,12},{12... | collective-permute-start | bytes 589832 | tf_op jit(solution)/shard_map/ppermute | solution.py:68
  29.5 9.4 %collective-permute-start.8 = (bf16[128,768]{1,0:T(8,128)(2,1)}, bf16[128,768]{1,0:T(8,128)(2,1)S(1)}, u32[]{:S(2)}, u32[]{:S(2)}) collective-permute-start(bf16[128,768]{1,0:T(8,128)(2,1)} %collective-permute-done.7), channel_id=1, source_target_pairs={{0,2},{2,4},{4,6},{6,7},{7,5},{5,3},{3,1},{1,0},{8,9},{10,8},{12,1... | collective-permute-start | bytes 589832 | tf_op jit(solution)/shard_map/ppermute | solution.py:68
  31.6 9.8 %collective-permute-start.12 = (bf16[128,768]{1,0:T(8,128)(2,1)}, bf16[128,768]{1,0:T(8,128)(2,1)S(1)}, u32[]{:S(2)}, u32[]{:S(2)}) collective-permute-start(bf16[128,768]{1,0:T(8,128)(2,1)} %collective-permute-done.11), channel_id=1, source_target_pairs={{0,1},{2,0},{4,2},{6,4},{7,6},{5,7},{3,5},{1,3},{8,10},{10,12},{12... | collective-permute-start | bytes 589832 | tf_op jit(solution)/shard_map/ppermute | solution.py:68
  34.6 8.4 %collective-permute-start.1 = (bf16[128,768]{1,0:T(8,128)(2,1)S(1)}, bf16[128,768]{1,0:T(8,128)(2,1)S(1)}, u32[]{:S(2)}, u32[]{:S(2)}) collective-permute-start(bf16[128,768]{1,0:T(8,128)(2,1)S(1)} %collective-permute-done), channel_id=1, source_target_pairs={{0,2},{2,4},{4,6},{6,7},{7,5},{5,3},{3,1},{1,0},{8,9},{10,8},{12,1... | collective-permute-start | bytes 589832 | tf_op jit(solution)/shard_map/ppermute | solution.py:68
  37.1 8.4 %collective-permute-start.5 = (bf16[128,768]{1,0:T(8,128)(2,1)S(1)}, bf16[128,768]{1,0:T(8,128)(2,1)S(1)}, u32[]{:S(2)}, u32[]{:S(2)}) collective-permute-start(bf16[128,768]{1,0:T(8,128)(2,1)S(1)} %collective-permute-done.4), channel_id=1, source_target_pairs={{0,1},{2,0},{4,2},{6,4},{7,6},{5,7},{3,5},{1,3},{8,10},{10,12},{12... | collective-permute-start | bytes 589832 | tf_op jit(solution)/shard_map/ppermute | solution.py:68
  39.0 8.3 %collective-permute-start.9 = (bf16[128,768]{1,0:T(8,128)(2,1)S(1)}, bf16[128,768]{1,0:T(8,128)(2,1)S(1)}, u32[]{:S(2)}, u32[]{:S(2)}) collective-permute-start(bf16[128,768]{1,0:T(8,128)(2,1)S(1)} %collective-permute-done.8), channel_id=1, source_target_pairs={{0,2},{2,4},{4,6},{6,7},{7,5},{5,3},{3,1},{1,0},{8,9},{10,8},{12,1... | collective-permute-start | bytes 589832 | tf_op jit(solution)/shard_map/ppermute | solution.py:68
  41.3 13.7 %collective-permute-start.13 = (bf16[128,768]{1,0:T(8,128)(2,1)S(1)}, bf16[128,768]{1,0:T(8,128)(2,1)S(1)}, u32[]{:S(2)}, u32[]{:S(2)}) collective-permute-start(bf16[128,768]{1,0:T(8,128)(2,1)S(1)} %collective-permute-done.12), channel_id=1, source_target_pairs={{0,1},{2,0},{4,2},{6,4},{7,6},{5,7},{3,5},{1,3},{8,10},{10,12},{12... | collective-permute-start | bytes 589832 | tf_op jit(solution)/shard_map/ppermute | solution.py:68
  43.1 8.0 %collective-permute-start.2 = (bf16[128,768]{1,0:T(8,128)(2,1)S(1)}, bf16[128,768]{1,0:T(8,128)(2,1)S(1)}, u32[]{:S(2)}, u32[]{:S(2)}) collective-permute-start(bf16[128,768]{1,0:T(8,128)(2,1)S(1)} %collective-permute-done.1), channel_id=1, source_target_pairs={{0,2},{2,4},{4,6},{6,7},{7,5},{5,3},{3,1},{1,0},{8,9},{10,8},{12,1... | collective-permute-start | bytes 589832 | tf_op jit(solution)/shard_map/ppermute | solution.py:68
  45.6 11.3 %collective-permute-start.6 = (bf16[128,768]{1,0:T(8,128)(2,1)S(1)}, bf16[128,768]{1,0:T(8,128)(2,1)S(1)}, u32[]{:S(2)}, u32[]{:S(2)}) collective-permute-start(bf16[128,768]{1,0:T(8,128)(2,1)S(1)} %collective-permute-done.5), channel_id=1, source_target_pairs={{0,1},{2,0},{4,2},{6,4},{7,6},{5,7},{3,5},{1,3},{8,10},{10,12},{12... | collective-permute-start | bytes 589832 | tf_op jit(solution)/shard_map/ppermute | solution.py:68
  47.3 6.8 %collective-permute-start.10 = (bf16[128,768]{1,0:T(8,128)(2,1)S(1)}, bf16[128,768]{1,0:T(8,128)(2,1)S(1)}, u32[]{:S(2)}, u32[]{:S(2)}) collective-permute-start(bf16[128,768]{1,0:T(8,128)(2,1)S(1)} %collective-permute-done.9), channel_id=1, source_target_pairs={{0,2},{2,4},{4,6},{6,7},{7,5},{5,3},{3,1},{1,0},{8,9},{10,8},{12,1... | collective-permute-start | bytes 589832 | tf_op jit(solution)/shard_map/ppermute | solution.py:68
  51.1 5.7 %collective-permute-start.3 = (bf16[128,768]{1,0:T(8,128)(2,1)S(1)}, bf16[128,768]{1,0:T(8,128)(2,1)S(1)}, u32[]{:S(2)}, u32[]{:S(2)}) collective-permute-start(bf16[128,768]{1,0:T(8,128)(2,1)S(1)} %collective-permute-done.2), channel_id=1, source_target_pairs={{0,2},{2,4},{4,6},{6,7},{7,5},{5,3},{3,1},{1,0},{8,9},{10,8},{12,1... | collective-permute-start | bytes 589832 | tf_op jit(solution)/shard_map/ppermute | solution.py:68
  53.6 3.3 %copy-start.5 = (pred[1024]{0:T(1024)(128)(4,1)S(1)}, pred[1024]{0:T(1024)(128)(4,1)}, u32[]{:S(2)}) copy-start(pred[1024]{0:T(1024)(128)(4,1)} %copy-done.4) | copy-start | bytes 3076
  53.6 3.3 %copy-start.9 = (pred[1024]{0:T(1024)(128)(4,1)S(1)}, pred[1024]{0:T(1024)(128)(4,1)}, u32[]{:S(2)}) copy-start(pred[1024]{0:T(1024)(128)(4,1)} %copy-done.8) | copy-start | bytes 3076
  63.6 1.9 %copy-start.7 = (f32[1024]{0:T(1024)}, f32[1024]{0:T(1024)S(1)}, u32[]{:S(2)}) copy-start(f32[1024]{0:T(1024)S(1)} %get-tuple-element.9) | copy-start | bytes 12292
  65.5 6.9 %copy-start.6 = (pred[1024]{0:T(1024)(128)(4,1)S(1)}, pred[1024]{0:T(1024)(128)(4,1)}, u32[]{:S(2)}) copy-start(pred[1024]{0:T(1024)(128)(4,1)} %copy-done.4) | copy-start | bytes 3076
  68.8 8.9 %all-to-all-start.1 = ((bf16[4,32,768]{2,1,0:T(8,128)(2,1)}), bf16[4,32,768]{2,1,0:T(8,128)(2,1)S(1)}, u32[]{:S(2)}, u32[]{:S(2)}) async-start(bf16[4,32,768]{2,1,0:T(8,128)(2,1)} %bitcast.36), calls=%async_computation.1 | async-start | bytes 393216 | tf_op jit(solution)/shard_map/all_to_all | solution.py:181

commit v12 on v11

--- a/solution.py
+++ b/solution.py
@@ -61,6 +61,7 @@
     rows = block.shape[0]
     out = jnp.zeros((count * rows,) + block.shape[1:], block.dtype)
     out = lax.dynamic_update_slice_in_dim(out, block, my_dp * rows, 0)
+    arrivals = [(my_dp, block)]
     for even_step, steps in ((1, count // 2), (-1, count - 1 - count // 2)):
         pairs = pairs_for(even_step)
         cur = block
@@ -68,7 +69,8 @@
             cur = lax.ppermute(cur, ("lang", "dp"), pairs)
             origin = ring_arr[(my_pos - even_step * mirror * t) % count]
             out = lax.dynamic_update_slice_in_dim(out, cur, origin * rows, 0)
-    return out
+            arrivals.append((origin, cur))
+    return out, arrivals
 
 
 def scores_of(x_rows, y_rows, pos_mask, inv_root):
@@ -122,39 +124,64 @@
     perm = target_index(pair_rows, row_count, per_slot, data_size)
     live_pos = (perm[None, :] == pair_align[:, None]) & row_live[:, None]
     col_live = jnp.max(live_pos.astype(jnp.int32), axis=0) > 0
-    x_all = ring_gather(src_emb, ring, lang_size)
-    y_all = ring_gather(partner, ring, lang_size)
-
-    block = max(1, min(pair_rows, BLOCK_BYTES // (4 * pair_rows)))
-    steps = pair_rows // block
-    if steps == 1:
-        is_pos = perm[None, :] == pair_align[:, None]
-        scores_f = scores_of(x_all, y_all, is_pos, inv_root)
-        row_lse, pos_score, col_max, col_sum = block_stats(scores_f, is_pos, row_live, col_live)
+    x_all, _ = ring_gather(src_emb, ring, lang_size)
+    y_all, y_arrivals = ring_gather(partner, ring, lang_size)
+
+    if pair_rows * pair_rows * 4 <= BLOCK_BYTES:
+        row_f = row_live.astype(jnp.float32)
+        within = jnp.arange(row_count, dtype=jnp.int32)
+        run_max = jnp.full((pair_rows,), LOW_FILL, jnp.float32)
+        run_sum = jnp.zeros((pair_rows,), jnp.float32)
+        pos_score = jnp.zeros((pair_rows,), jnp.float32)
+        col_lse = jnp.zeros((pair_rows,), jnp.float32)
+        col_term = jnp.float32(0.0)
+        for origin, y_blk in y_arrivals:
+            perm_blk = (within // per_slot * data_size + origin) * per_slot + within % per_slot
+            pos_blk = perm_blk[None, :] == pair_align[:, None]
+            live_blk = jnp.max((pos_blk & row_live[:, None]).astype(jnp.int32), axis=0) > 0
+            s_blk = scores_of(x_all, y_blk, pos_blk, inv_root)
+            b_max = jnp.max(jnp.where(row_live[:, None], s_blk, LOW_FILL), axis=0)
+            b_sum = jnp.sum(jnp.where(row_live[:, None], jnp.exp(s_blk - b_max[None, :]), 0.0), axis=0)
+            b_lse = b_max + jnp.log(b_sum + (1.0 - live_blk.astype(jnp.float32)))
+            col_lse = lax.dynamic_update_slice_in_dim(col_lse, b_lse, origin * row_count, 0)
+            col_term = col_term + jnp.sum(live_blk.astype(jnp.float32) * b_lse)
+            r_max = jnp.max(jnp.where(live_blk[None, :], s_blk, LOW_FILL), axis=1)
+            top = jnp.maximum(run_max, r_max)
+            r_sum = jnp.sum(jnp.where(live_blk[None, :], jnp.exp(s_blk - top[:, None]), 0.0), axis=1)
+            run_sum = run_sum * jnp.exp(run_max - top) + r_sum
+            run_max = top
+            pos_score = pos_score + jnp.sum(jnp.where(pos_blk, s_blk, 0.0), axis=1)
+        row_lse = run_max + jnp.log(run_sum + (1.0 - row_f))
     else:
-        def one_block(k, carry):
-            row_lse, pos_score, col_max, col_sum = carry
-            start = k * block
-            x_blk = lax.dynamic_slice_in_dim(x_all, start, block)
-            a_blk = lax.dynamic_slice_in_dim(pair_align, start, block)
-            r_blk = lax.dynamic_slice_in_dim(row_live, start, block)
-            is_pos = perm[None, :] == a_blk[:, None]
-            s_blk = scores_of(x_blk, y_all, is_pos, inv_root)
-            b_lse, b_pos, b_max, b_sum = block_stats(s_blk, is_pos, r_blk, col_live)
-            top = jnp.maximum(col_max, b_max)
-            col_sum = col_sum * jnp.exp(col_max - top) + b_sum * jnp.exp(b_max - top)
-            row_lse = lax.dynamic_update_slice_in_dim(row_lse, b_lse, start, 0)
-            pos_score = lax.dynamic_update_slice_in_dim(pos_score, b_pos, start, 0)
-            return row_lse, pos_score, top, col_sum
-
-        zeros = jnp.zeros((pair_rows,), jnp.float32)
-        init = (zeros, zeros, jnp.full((pair_rows,), LOW_FILL, jnp.float32), zeros)
-        row_lse, pos_score, col_max, col_sum = lax.fori_loop(0, steps, one_block, init)
-    col_lse = col_max + jnp.log(col_sum + (1.0 - col_live.astype(jnp.float32)))
-
-    row_f = row_live.astype(jnp.float32)
-    col_f = col_live.astype(jnp.float32)
-    total = jnp.sum(row_f * (row_lse - 2.0 * pos_score)) + jnp.sum(col_f * col_lse)
+        block = max(1, min(pair_rows, BLOCK_BYTES // (4 * pair_rows)))
+        steps = pair_rows // block
+        if steps == 1:
+            is_pos = perm[None, :] == pair_align[:, None]
+            scores_f = scores_of(x_all, y_all, is_pos, inv_root)
+            row_lse, pos_score, col_max, col_sum = block_stats(scores_f, is_pos, row_live, col_live)
+        else:
+            def one_block(k, carry):
+                row_lse, pos_score, col_max, col_sum = carry
+                start = k * block
+                x_blk = lax.dynamic_slice_in_dim(x_all, start, block)
+                a_blk = lax.dynamic_slice_in_dim(pair_align, start, block)
+                r_blk = lax.dynamic_slice_in_dim(row_live, start, block)
+                is_pos = perm[None, :] == a_blk[:, None]
+                s_blk = scores_of(x_blk, y_all, is_pos, inv_root)
+                b_lse, b_pos, b_max, b_sum = block_stats(s_blk, is_pos, r_blk, col_live)
+                top = jnp.maximum(col_max, b_max)
+                col_sum = col_sum * jnp.exp(col_max - top) + b_sum * jnp.exp(b_max - top)
+                row_lse = lax.dynamic_update_slice_in_dim(row_lse, b_lse, start, 0)
+                pos_score = lax.dynamic_update_slice_in_dim(pos_score, b_pos, start, 0)
+                return row_lse, pos_score, top, col_sum
+
+            zeros = jnp.zeros((pair_rows,), jnp.float32)
+            init = (zeros, zeros, jnp.full((pair_rows,), LOW_FILL, jnp.float32), zeros)
+            row_lse, pos_score, col_max, col_sum = lax.fori_loop(0, steps, one_block, init)
+        col_lse = col_max + jnp.log(col_sum + (1.0 - col_live.astype(jnp.float32)))
+        row_f = row_live.astype(jnp.float32)
+        col_term = jnp.sum(col_live.astype(jnp.float32) * col_lse)
+    total = jnp.sum(row_f * (row_lse - 2.0 * pos_score)) + col_term
     pair_loss = (total / live_count.astype(jnp.float32)).reshape(1)
 
     mine = shard_index * row_count

time: 80.7 us -> 112 us (1.39)
  other arithmetic: 7.11 us -> 26 us
  between operations: 13.1 us -> 22.4 us
  local copies, waits for them, and re-layouts: 12.9 us -> 15.5 us
  matrix products: 9.15 us -> 11.6 us
  waiting for transfers between devices: 11.2 us -> 8.93 us
    reduce_sum x2 -> x12, other arithmetic: 4.3 us -> 12.5 us  [the longest x8 5.94 us: per_device(): col_term = col_term + jnp.sum(live_blk.astype(jnp.float32) * b_lse)]
    gt x0 -> x8, other arithmetic: none -> 4.33 us  [per_device(): jnp.max((pos_blk & row_live[:, None]).astype(jnp.int32), axis=0) > 0]
    add x0 -> x5, other arithmetic: none -> 4.31 us  [per_device(): (within // per_slot * data_size + origin) * per_slot + within % per_slot]
    dot_general x1 -> x8, matrix products: 2.4 us -> 6.63 us  [scores_of(): lax.dot_general(x_rows, y_rows, (((1,), (1,)), ((), ())), preferred_eleme...]
    dynamic_update_slice x14, local copies, waits for them, and re-layouts: 2.13 us -> 3.98 us  [ring_gather(): out = lax.dynamic_update_slice_in_dim(out, cur, origin * rows, 0)]
    ppermute x14, waiting for transfers between devices: 10.7 us -> 8.92 us  [ring_gather(): cur = lax.ppermute(cur, ('lang', 'dp'), pairs)]
    reduce_max x0 -> x1, other arithmetic: none -> 1.77 us  [per_device(): jnp.max((pos_blk & row_live[:, None]).astype(jnp.int32), axis=0) > 0]
  transfers between devices with their start and end apart: 16 -> 16, of which waited for: 8 -> 9; matrix products, arithmetic and copies ran while one was open for 20% -> 29% of each run, Pallas kernels for 0% -> 0%
where the time goes in v12:
time: 112 us; the launch traced here: 111 us
  starting transfers between devices  26.5 us (24%)
  other arithmetic  26 us (23%)
  between operations  22.4 us (20%)
  local copies, waits for them, and re-layouts  15.5 us (14%)
  matrix products  11.6 us (10%)
  waiting for transfers between devices  8.93 us (8%)
    ppermute x14, starting transfers between devices, ring_gather(): cur = lax.ppermute(cur, ('lang', 'dp'), pairs)  19.6 us
    ppermute x14, waiting for transfers between devices, ring_gather(): cur = lax.ppermute(cur, ('lang', 'dp'), pairs)  8.92 us
    dot_general x8, matrix products, scores_of(): lax.dot_general(x_rows, y_rows, (((1,), (1,)), ((), ())), preferred_eleme...  6.63 us
    reduce_sum x8, other arithmetic, per_device(): col_term = col_term + jnp.sum(live_blk.astype(jnp.float32) * b_lse)  5.94 us
    reduce_sum x3, other arithmetic, per_device(): pos_score = pos_score + jnp.sum(jnp.where(pos_blk, s_blk, 0.0), axis=1)  5.32 us
    gt x8, other arithmetic, per_device(): jnp.max((pos_blk & row_live[:, None]).astype(jnp.int32), axis=0) > 0  4.33 us
    add x5, other arithmetic, per_device(): (within // per_slot * data_size + origin) * per_slot + within % per_slot  4.31 us
    dynamic_update_slice x14, local copies, waits for them, and re-layouts, ring_gather(): out = lax.dynamic_update_slice_in_dim(out, cur, origin * rows, 0)  3.98 us
  transfers between devices with their start and end apart: 16, of which 9 were waited for; matrix products, arithmetic and copies ran while one was open for 29% of the time, Pallas kernels for 0%

profile of v12, /device:TPU:0, one launch (start us, length us, event | category | flops | bytes accessed | tf_op | source)
XLA Modules:
  0.0 110.9 jit_solution(7365635941399145418)
XLA Ops:
  0.7 3.1 %collective-permute-start.7 = (bf16[128,768]{1,0:T(8,128)(2,1)}, bf16[128,768]{1,0:T(8,128)(2,1)}, u32[]{:S(2)}, u32[]{:S(2)}) collective-permute-start(bf16[128,768]{1,0:T(8,128)(2,1)} %param.10), channel_id=1, source_target_pairs={{0,2},{2,4},{4,6},{6,7},{7,5},{5,3},{3,1},{1,0},{8,9},{10,8},{12,1... | collective-permute-start | bytes 589832 | tf_op jit(solution)/shard_map/ppermute | solution.py:69
  3.8 0.7 compare_select_fusion.19
  5.1 1.2 %gather_fusion = bf16[4,32,768]{2,1,0:T(8,128)(2,1)} fusion(bf16[4,32,768]{2,1,0:T(8,128)(2,1)S(1)} %copy-done, s32[1024]{0:T(1024)S(1)} %pad_clamp_fusion.1), kind=kCustom, calls=%fused_computation | custom fusion | bytes 393232 | tf_op jit(solution)/shard_map/gather | solution.py:116
  6.3 3.4 %all-to-all-start = ((bf16[4,32,768]{2,1,0:T(8,128)(2,1)}), bf16[4,32,768]{2,1,0:T(8,128)(2,1)S(1)}, u32[]{:S(2)}, u32[]{:S(2)}) async-start(bf16[4,32,768]{2,1,0:T(8,128)(2,1)} %gather_fusion), calls=%async_computation | async-start | bytes 393216 | tf_op jit(solution)/shard_map/all_to_all | solution.py:117
  9.7 1.2 %dynamic_slice.75 = s32[1]{0:T(128)} dynamic-slice(s32[8]{0:T(128)} %constant.291.clone, s32[]{:T(128)S(6)} %select_n.486), dynamic_slice_sizes={1} | dynamic-slice | bytes 12 | tf_op jit(solution)/shard_map/dynamic_slice | solution.py:51
  15.7 1.6 %fusion.91 = (s32[1]{0:T(128)}, s32[1]{0:T(128)}, s32[1]{0:T(128)}, s32[1]{0:T(128)}, s32[1]{0:T(128)}, /*index=5*/s32[1]{0:T(128)}, s32[1]{0:T(128)}) fusion(s32[8]{0:T(128)} %constant.290.clone, s32[]{:T(128)S(6)} %select_n.507, s32[]{:T(128)S(6)} %select_n.501, s32[]{:T(128)S(6)} %select_n.498, s32[]{:T(128)S(6)} %select_n.495, s32[]{:T(128)S(6)} %select_n.492, ...), kind=kLoop, calls=%fused_computation.248 | loop fusion | bytes 84 | tf_op jit(solution)/shard_map/dynamic_slice | solution.py:70
  17.3 0.7 multiply_add_fusion.6
  18.0 1.3 %dynamic_slice.73 = s32[1]{0:T(128)} dynamic-slice(s32[4]{0:T(128)} %param.13, s32[]{:T(128)S(6)} %select_n.478), dynamic_slice_sizes={1} | dynamic-slice | bytes 12 | tf_op jit(solution)/shard_map/dynamic_slice | solution.py:119
  19.9 1.2 %multiply_add_fusion = (s32[128]{0:T(128)S(1)}, s32[128]{0:T(128)S(1)}) fusion(s32[]{:T(128)} %bitcast.11, s32[]{:T(128)} %bitcast.10), kind=kLoop, calls=%fused_computation.213 | loop fusion | flops 2432 | bytes 1032 | tf_op jit(solution)/shard_map/add | solution.py:139
  21.2 1.2 %multiply_add_fusion.2 = (s32[128]{0:T(128)S(1)}, s32[128]{0:T(128)S(1)}) fusion(s32[]{:T(128)} %bitcast.9, s32[]{:T(128)} %bitcast.8), kind=kLoop, calls=%fused_computation.215 | loop fusion | flops 2432 | bytes 1032 | tf_op jit(solution)/shard_map/add | solution.py:139
  22.4 1.2 %multiply_add_fusion.4 = (s32[128]{0:T(128)S(1)}, s32[128]{0:T(128)S(1)}) fusion(s32[]{:T(128)} %bitcast.7, s32[]{:T(128)} %bitcast.6), kind=kLoop, calls=%fused_computation.217 | loop fusion | flops 2432 | bytes 1032 | tf_op jit(solution)/shard_map/add | solution.py:139
  23.6 1.8 %convert_reduce_fusion.1 = (s32[128]{0:T(128)S(1)}, s32[128]{0:T(128)S(1)}, s32[128]{0:T(128)S(1)}, s32[128]{0:T(128)S(1)}, s32[128]{0:T(128)S(1)}, /*index=5*/s32[128]{0:T(128)S(1)}, s32[128]{0:T(128)S(1)}, s32[128]{0:T(128)S(1)}) fusion(s32[128]{0:T(128)S(1)} %get-tuple-element.113, pred[1024]{0:T(1024)(128)(4,1)S(1)} %iota_compare_fusion, ...), kind=kLoop, calls=%fused_computation.101 | loop fusion | flops 4193280 | bytes 13312 | tf_op jit(solution)/shard_map/reduce_max | solution.py:141
  29.8 1.7 %convert_reduce_fusion = s32[1024]{0:T(1024)S(1)} fusion(s32[1024]{0:T(1024)S(1)} %fusion.60, s32[1024]{0:T(1024)} %bitcast.57, pred[1024]{0:T(1024)(128)(4,1)S(1)} %iota_compare_fusion), kind=kLoop, calls=%fused_computation.3 | loop fusion | flops 4193280 | bytes 13312 | tf_op jit(solution)/shard_map/reduce_max | solution.py:126
  43.9 2.0 %collective-permute-start = (bf16[128,768]{1,0:T(8,128)(2,1)S(1)}, bf16[128,768]{1,0:T(8,128)(2,1)S(1)}, u32[]{:S(2)}, u32[]{:S(2)}) collective-permute-start(bf16[128,768]{1,0:T(8,128)(2,1)S(1)} %bitcast.51), channel_id=1, source_target_pairs={{0,2},{2,4},{4,6},{6,7},{7,5},{5,3},{3,1},{1,0},{8,9},{10,8},{12,1... | collective-permute-start | bytes 589832 | tf_op jit(solution)/shard_map/ppermute | solution.py:69
  46.2 2.1 %collective-permute-start.8 = (bf16[128,768]{1,0:T(8,128)(2,1)}, bf16[128,768]{1,0:T(8,128)(2,1)S(1)}, u32[]{:S(2)}, u32[]{:S(2)}) collective-permute-start(bf16[128,768]{1,0:T(8,128)(2,1)} %collective-permute-done.7), channel_id=1, source_target_pairs={{0,2},{2,4},{4,6},{6,7},{7,5},{5,3},{3,1},{1,0},{8,9},{10,8},{12,1... | collective-permute-start | bytes 589832 | tf_op jit(solution)/shard_map/ppermute | solution.py:69
  48.3 1.0 constant_dynamic-update-slice_fusion.4
  49.3 1.9 %collective-permute-done = bf16[128,768]{1,0:T(8,128)(2,1)S(1)} collective-permute-done((bf16[128,768]{1,0:T(8,128)(2,1)S(1)}, bf16[128,768]{1,0:T(8,128)(2,1)S(1)}, u32[]{:S(2)}, u32[]{:S(2)}) %collective-permute-start) | collective-permute-done | bytes 196640 | tf_op jit(solution)/shard_map/ppermute | solution.py:69
  51.2 2.5 %collective-permute-start.1 = (bf16[128,768]{1,0:T(8,128)(2,1)S(1)}, bf16[128,768]{1,0:T(8,128)(2,1)S(1)}, u32[]{:S(2)}, u32[]{:S(2)}) collective-permute-start(bf16[128,768]{1,0:T(8,128)(2,1)S(1)} %collective-permute-done), channel_id=1, source_target_pairs={{0,2},{2,4},{4,6},{6,7},{7,5},{5,3},{3,1},{1,0},{8,9},{10,8},{12,1... | collective-permute-start | bytes 589832 | tf_op jit(solution)/shard_map/ppermute | solution.py:69
  53.9 1.6 %collective-permute-done.8 = bf16[128,768]{1,0:T(8,128)(2,1)S(1)} collective-permute-done((bf16[128,768]{1,0:T(8,128)(2,1)}, bf16[128,768]{1,0:T(8,128)(2,1)S(1)}, u32[]{:S(2)}, u32[]{:S(2)}) %collective-permute-start.8) | collective-permute-done | bytes 196640 | tf_op jit(solution)/shard_map/ppermute | solution.py:69
  55.5 2.4 %collective-permute-start.9 = (bf16[128,768]{1,0:T(8,128)(2,1)S(1)}, bf16[128,768]{1,0:T(8,128)(2,1)S(1)}, u32[]{:S(2)}, u32[]{:S(2)}) collective-permute-start(bf16[128,768]{1,0:T(8,128)(2,1)S(1)} %collective-permute-done.8), channel_id=1, source_target_pairs={{0,2},{2,4},{4,6},{6,7},{7,5},{5,3},{3,1},{1,0},{8,9},{10,8},{12,1... | collective-permute-start | bytes 589832 | tf_op jit(solution)/shard_map/ppermute | solution.py:69
  58.1 1.5 %collective-permute-done.1 = bf16[128,768]{1,0:T(8,128)(2,1)S(1)} collective-permute-done((bf16[128,768]{1,0:T(8,128)(2,1)S(1)}, bf16[128,768]{1,0:T(8,128)(2,1)S(1)}, u32[]{:S(2)}, u32[]{:S(2)}) %collective-permute-start.1) | collective-permute-done | bytes 196640 | tf_op jit(solution)/shard_map/ppermute | solution.py:69
  59.6 2.5 %collective-permute-start.2 = (bf16[128,768]{1,0:T(8,128)(2,1)S(1)}, bf16[128,768]{1,0:T(8,128)(2,1)S(1)}, u32[]{:S(2)}, u32[]{:S(2)}) collective-permute-start(bf16[128,768]{1,0:T(8,128)(2,1)S(1)} %collective-permute-done.1), channel_id=1, source_target_pairs={{0,2},{2,4},{4,6},{6,7},{7,5},{5,3},{3,1},{1,0},{8,9},{10,8},{12,1... | collective-permute-start | bytes 589832 | tf_op jit(solution)/shard_map/ppermute | solution.py:69
  62.3 1.5 %collective-permute-done.9 = bf16[128,768]{1,0:T(8,128)(2,1)S(1)} collective-permute-done((bf16[128,768]{1,0:T(8,128)(2,1)S(1)}, bf16[128,768]{1,0:T(8,128)(2,1)S(1)}, u32[]{:S(2)}, u32[]{:S(2)}) %collective-permute-start.9) | collective-permute-done | bytes 196640 | tf_op jit(solution)/shard_map/ppermute | solution.py:69
  63.8 2.5 %collective-permute-start.10 = (bf16[128,768]{1,0:T(8,128)(2,1)S(1)}, bf16[128,768]{1,0:T(8,128)(2,1)S(1)}, u32[]{:S(2)}, u32[]{:S(2)}) collective-permute-start(bf16[128,768]{1,0:T(8,128)(2,1)S(1)} %collective-permute-done.9), channel_id=1, source_target_pairs={{0,2},{2,4},{4,6},{6,7},{7,5},{5,3},{3,1},{1,0},{8,9},{10,8},{12,1... | collective-permute-start | bytes 589832 | tf_op jit(solution)/shard_map/ppermute | solution.py:69
  66.3 1.4 %collective-permute-done.2 = bf16[128,768]{1,0:T(8,128)(2,1)S(1)} collective-permute-done((bf16[128,768]{1,0:T(8,128)(2,1)S(1)}, bf16[128,768]{1,0:T(8,128)(2,1)S(1)}, u32[]{:S(2)}, u32[]{:S(2)}) %collective-permute-start.2) | collective-permute-done | bytes 196640 | tf_op jit(solution)/shard_map/ppermute | solution.py:69
  67.7 2.5 %collective-permute-start.3 = (bf16[128,768]{1,0:T(8,128)(2,1)S(1)}, bf16[128,768]{1,0:T(8,128)(2,1)}, u32[]{:S(2)}, u32[]{:S(2)}) collective-permute-start(bf16[128,768]{1,0:T(8,128)(2,1)S(1)} %collective-permute-done.2), channel_id=1, source_target_pairs={{0,2},{2,4},{4,6},{6,7},{7,5},{5,3},{3,1},{1,0},{8,9},{10,8},{12,1... | collective-permute-start | bytes 589832 | tf_op jit(solution)/shard_map/ppermute | solution.py:69
  70.6 0.9 constant_dynamic-update-slice_fusion
  71.7 0.7 select_reduce_fusion.31
  75.7 1.5 %fusion.3 = f32[1024,128]{1,0:T(8,128)S(1)} fusion(bf16[1024,768]{1,0:T(8,128)(2,1)S(1)} %constant_dynamic-update-slice_fusion.6, bf16[128,768]{1,0:T(8,128)(2,1)} %collective-permute-done.3, s32[128]{0:T(128)S(1)} %copy-done.20, s32[1024]{0:T(1024)S(1)} %bitcast.64), kind=kOutput, calls=%fused_computation.11 | convolution fusion | flops 201850880 | bytes 2298368 | tf_op jit(solution)/shard_map/dot_general | solution.py:77
  77.2 1.6 %select_reduce_fusion.30 = (f32[1024]{0:T(1024)S(1)}, f32[128]{0:T(128)S(1)}, f32[128]{0:T(128)S(1)}, f32[1024]{0:T(1024)S(1)}, f32[128]{0:T(128)S(1)}, /*index=...) fusion(pred[128]{0:T(512)(128)(4,1)S(1)} %copy-done.34, ...), kind=kOutput, calls=%fused_computation.112 | convolution fusion | flops 205512832 | bytes 5478272 | tf_op jit(solution)/shard_map/dot_general | solution.py:77
  78.9 1.9 %fusion.28 = (f32[1024]{0:T(1024)S(1)}, f32[128]{0:T(128)S(1)}, f32[1024]{0:T(1024)S(1)}, f32[1024]{0:T(1024)S(1)}, f32[128]{0:T(128)S(1)}, /*index=5*/f32[1024]...) fusion(f32[1024,128]{1,0:T(8,128)S(1)} %fusion, s32[128]{0:T(128)S(1)} %copy-done.22, ...), kind=kLoop, calls=%fused_computation.75 | loop fusion | flops 3663488 | bytes 1619328 | tf_op jit(solution)/shard_map/reduce_sum | solution.py:153
  80.9 1.6 %fusion.26 = (f32[1024]{0:T(1024)S(1)}, f32[128]{0:T(128)S(1)}, f32[1024]{0:T(1024)S(1)}, f32[1024]{0:T(1024)S(1)}, f32[128]{0:T(128)S(1)}, /*index=5*/f32[1024]{0:T(1024)S(1)}, f32[128]{0:T(128)S(1)}) fusion(f32[1024,128]{1,0:T(8,128)S(1)} %fusion.2, s32[128]{0:T(128)S(1)} %copy-done.18, s32[1024]{0:T(1024)S(1)} %bitcast.67, f32[128]{0:T(128)S(1)} %get-tuple-element.93, ...), kind=kLoop, calls=%fused_computation.73 | loop fusion | flops 3141248 | bytes 1607424 | tf_op jit(solution)/shard_map/reduce_sum | solution.py:153
  82.4 0.7 select_reduce_fusion.40
  83.2 0.8 select_reduce_fusion.39
  84.0 1.9 %fusion.27 = (f32[1024]{0:T(1024)S(1)}, f32[128]{0:T(128)S(1)}, f32[1024]{0:T(1024)S(1)}, f32[1024]{0:T(1024)S(1)}, f32[128]{0:T(128)S(1)}, /*index=5*/f32[1024]...) fusion(f32[1024,128]{1,0:T(8,128)S(1)} %fusion.1, s32[128]{0:T(128)S(1)} %copy-done.12, ...), kind=kLoop, calls=%fused_computation.74 | loop fusion | flops 3532416 | bytes 1619840 | tf_op jit(solution)/shard_map/reduce_sum | solution.py:153
  85.9 0.8 select_reduce_fusion.38
  86.7 0.7 select_reduce_fusion.37
  87.4 0.7 select_reduce_fusion.36
  88.1 0.7 select_reduce_fusion.35
  88.9 0.8 select_reduce_fusion.34
  89.6 0.7 select_reduce_fusion.33
  90.4 1.3 %select_reduce_fusion.32 = (f32[]{:T(128)}, f32[1024]{0:T(1024)S(1)}) fusion(f32[1024]{0:T(1024)S(1)} %get-tuple-element.24, f32[1024]{0:T(1024)S(1)} %get-tuple-element.21, f32[1024]{0:T(1024)S(1)} %get-tuple-element.18, f32[1024]{0:T(1024)S(1)} %get-tuple-element.55, f32[1024]{0:T(1024)S(1)} %get-tuple-element.52, f32[1024]{0:T(1024)S(1)} %get-tuple-element.49, ...), kind=kLoop, calls=%fused_computation.179 | loop fusion | flops 41983 | bytes 102408 | tf_op jit(solution)/shard_map/reduce_sum | solution.py:184
  92.3 2.4 %fusion.10 = bf16[128,768]{1,0:T(8,128)(2,1)} fusion(bf16[1024,768]{1,0:T(8,128)(2,1)S(1)} %constant_dynamic-update-slice_fusion.6, f32[1024,128]{1,0:T(8,128)S(1)} %get-tuple-element.112, f32[128]{0:T(128)S(1)} %dynamic_slice.95, f32[1024]{0:T(1024)S(1)} %get-tuple-element.66, s32[128]{0:T(128)S(1)} %copy-done.53, f32[]{:T(128)} %bitcast, ...), kind=kOutput, calls=%fused_computation.25 | convolution fusion | flops 203358208 | bytes 2304132 | tf_op jit(solution)/shard_map/dot_general | solution.py:204
  94.7 3.5 %all-to-all-start.1 = ((bf16[4,32,768]{2,1,0:T(8,128)(2,1)}), bf16[4,32,768]{2,1,0:T(8,128)(2,1)S(1)}, u32[]{:S(2)}, u32[]{:S(2)}) async-start(bf16[4,32,768]{2,1,0:T(8,128)(2,1)} %bitcast.55), calls=%async_computation.1 | async-start | bytes 393216 | tf_op jit(solution)/shard_map/all_to_all | solution.py:208
  98.2 0.9 constant_dynamic-update-slice_fusion.11
  99.2 0.9 constant_dynamic-update-slice_fusion.9
  100.3 2.6 %fusion.9 = bf16[128,768]{1,0:T(8,128)(2,1)} fusion(bf16[1024,768]{1,0:T(8,128)(2,1)S(1)} %constant_dynamic-update-slice_fusion.8, bf16[128,768]{1,0:T(8,128)(2,1)S(1)} %copy-done.2, f32[1024]{0:T(1024)S(1)} %get-tuple-element.76, f32[128]{0:T(128)S(1)} %copy-done.56, s32[128]{0:T(128)S(1)} %copy-done.55, f32[]{:T(128)} %bitcast, s32[1024]{0:T(1024)S(1)} %copy-done.10, ...), kind=kOutput, calls=%fused_computation.24 | convolution fusion | flops 404815872 | bytes 1976452 | tf_op jit(solution)/shard_map/dot_general | solution.py:195
  108.5 1.2 %gather_fusion.1 = bf16[4,32,768]{2,1,0:T(8,128)(2,1)} fusion(bf16[4,32,768]{2,1,0:T(8,128)(2,1)S(1)} %all-to-all-done.1, s32[1024]{0:T(1024)S(1)} %pad_clamp_fusion), kind=kCustom, calls=%fused_computation.1 | custom fusion | bytes 393232 | tf_op jit(solution)/shard_map/gather | solution.py:211
  (176 shorter events, 14.0 us)
Async XLA Ops:
  0.6 31.1 %copy-start.1 = (bf16[128,768]{1,0:T(8,128)(2,1)S(1)}, bf16[128,768]{1,0:T(8,128)(2,1)}, u32[]{:S(2)}) copy-start(bf16[128,768]{1,0:T(8,128)(2,1)} %param.10) | copy-start | bytes 589828
  0.7 45.6 %collective-permute-start.7 = (bf16[128,768]{1,0:T(8,128)(2,1)}, bf16[128,768]{1,0:T(8,128)(2,1)}, u32[]{:S(2)}, u32[]{:S(2)}) collective-permute-start(bf16[128,768]{1,0:T(8,128)(2,1)} %param.10), channel_id=1, source_target_pairs={{0,2},{2,4},{4,6},{6,7},{7,5},{5,3},{3,1},{1,0},{8,9},{10,8},{12,1... | collective-permute-start | bytes 589832 | tf_op jit(solution)/shard_map/ppermute | solution.py:69
  3.8 44.5 %collective-permute-start.11 = (bf16[128,768]{1,0:T(8,128)(2,1)}, bf16[128,768]{1,0:T(8,128)(2,1)}, u32[]{:S(2)}, u32[]{:S(2)}) collective-permute-start(bf16[128,768]{1,0:T(8,128)(2,1)} %param.10), channel_id=1, source_target_pairs={{0,1},{2,0},{4,2},{6,4},{7,6},{5,7},{3,5},{1,3},{8,10},{10,12},{12... | collective-permute-start | bytes 589832 | tf_op jit(solution)/shard_map/ppermute | solution.py:69
  5.1 37.7 %copy-start.51 = (f32[4]{0:T(128)S(1)}, f32[4]{0:T(128)}, u32[]{:S(2)}) copy-start(f32[4]{0:T(128)} %param.15) | copy-start | bytes 52
  5.1 38.3 %copy-start.8 = (s32[1,1024]{1,0:T(1,128)S(1)}, s32[1,1024]{1,0:T(1,128)}, u32[]{:S(2)}) copy-start(s32[1,1024]{1,0:T(1,128)} %param.14) | copy-start | bytes 12292
  6.3 37.6 %all-to-all-start = ((bf16[4,32,768]{2,1,0:T(8,128)(2,1)}), bf16[4,32,768]{2,1,0:T(8,128)(2,1)S(1)}, u32[]{:S(2)}, u32[]{:S(2)}) async-start(bf16[4,32,768]{2,1,0:T(8,128)(2,1)} %gather_fusion), calls=%async_computation | async-start | bytes 393216 | tf_op jit(solution)/shard_map/all_to_all | solution.py:117
  15.6 30.3 %copy-start.9 = (s32[1024]{0:T(1024)}, s32[1024]{0:T(1024)S(1)}, u32[]{:S(2)}) copy-start(s32[1024]{0:T(1024)S(1)} %fusion.60) | copy-start | bytes 12292
  18.0 11.8 %copy-start.28 = (s32[128]{0:T(128)}, s32[128]{0:T(128)S(1)}, u32[]{:S(2)}) copy-start(s32[128]{0:T(128)S(1)} %multiply_add_fusion.6) | copy-start | bytes 1540
  21.1 8.1 %copy-start.11 = (s32[128]{0:T(128)}, s32[128]{0:T(128)S(1)}, u32[]{:S(2)}) copy-start(s32[128]{0:T(128)S(1)} %get-tuple-element.114) | copy-start | bytes 1540
  21.2 24.8 %copy-start.21 = (s32[128]{0:T(128)}, s32[128]{0:T(128)S(1)}, u32[]{:S(2)}) copy-start(s32[128]{0:T(128)S(1)} %get-tuple-element.113) | copy-start | bytes 1540
  22.4 23.5 %copy-start.17 = (s32[128]{0:T(128)}, s32[128]{0:T(128)S(1)}, u32[]{:S(2)}) copy-start(s32[128]{0:T(128)S(1)} %get-tuple-element.115) | copy-start | bytes 1540
  22.4 23.5 %copy-start.19 = (s32[128]{0:T(128)}, s32[128]{0:T(128)S(1)}, u32[]{:S(2)}) copy-start(s32[128]{0:T(128)S(1)} %get-tuple-element.116) | copy-start | bytes 1540
  23.6 8.1 %copy-start.13 = (s32[128]{0:T(128)}, s32[128]{0:T(128)S(1)}, u32[]{:S(2)}) copy-start(s32[128]{0:T(128)S(1)} %get-tuple-element.117) | copy-start | bytes 1540
  23.6 22.3 %copy-start.15 = (s32[128]{0:T(128)}, s32[128]{0:T(128)S(1)}, u32[]{:S(2)}) copy-start(s32[128]{0:T(128)S(1)} %get-tuple-element.118) | copy-start | bytes 1540
  25.4 20.5 %copy-start.35 = (s32[128]{0:T(128)}, s32[128]{0:T(128)S(1)}, u32[]{:S(2)}) copy-start(s32[128]{0:T(128)S(1)} %get-tuple-element.57) | copy-start | bytes 1540
  25.4 20.5 %copy-start.37 = (s32[128]{0:T(128)}, s32[128]{0:T(128)S(1)}, u32[]{:S(2)}) copy-start(s32[128]{0:T(128)S(1)} %get-tuple-element.61) | copy-start | bytes 1540
  25.4 20.5 %copy-start.39 = (s32[128]{0:T(128)}, s32[128]{0:T(128)S(1)}, u32[]{:S(2)}) copy-start(s32[128]{0:T(128)S(1)} %get-tuple-element.60) | copy-start | bytes 1540
  25.4 20.5 %copy-start.41 = (s32[128]{0:T(128)}, s32[128]{0:T(128)S(1)}, u32[]{:S(2)}) copy-start(s32[128]{0:T(128)S(1)} %get-tuple-element.59) | copy-start | bytes 1540
  25.4 20.5 %copy-start.43 = (s32[128]{0:T(128)}, s32[128]{0:T(128)S(1)}, u32[]{:S(2)}) copy-start(s32[128]{0:T(128)S(1)} %get-tuple-element.58) | copy-start | bytes 1540
  25.4 20.5 %copy-start.45 = (s32[128]{0:T(128)}, s32[128]{0:T(128)S(1)}, u32[]{:S(2)}) copy-start(s32[128]{0:T(128)S(1)} %get-tuple-element.63) | copy-start | bytes 1540
  25.5 20.5 %copy-start.47 = (s32[128]{0:T(128)}, s32[128]{0:T(128)S(1)}, u32[]{:S(2)}) copy-start(s32[128]{0:T(128)S(1)} %get-tuple-element.62) | copy-start | bytes 1540
  25.5 20.5 %copy-start.49 = (s32[128]{0:T(128)}, s32[128]{0:T(128)S(1)}, u32[]{:S(2)}) copy-start(s32[128]{0:T(128)S(1)} %get-tuple-element.64) | copy-start | bytes 1540
  31.6 14.4 %copy-start.23 = (pred[1024]{0:T(1024)(128)(4,1)}, pred[1024]{0:T(1024)(128)(4,1)S(1)}, u32[]{:S(2)}) copy-start(pred[1024]{0:T(1024)(128)(4,1)S(1)} %broadcast_compare_fusion) | copy-start | bytes 3076
  43.9 7.3 %collective-permute-start = (bf16[128,768]{1,0:T(8,128)(2,1)S(1)}, bf16[128,768]{1,0:T(8,128)(2,1)S(1)}, u32[]{:S(2)}, u32[]{:S(2)}) collective-permute-start(bf16[128,768]{1,0:T(8,128)(2,1)S(1)} %bitcast.51), channel_id=1, source_target_pairs={{0,2},{2,4},{4,6},{6,7},{7,5},{5,3},{3,1},{1,0},{8,9},{10,8},{12,1... | collective-permute-start | bytes 589832 | tf_op jit(solution)/shard_map/ppermute | solution.py:69
  46.0 7.8 %collective-permute-start.4 = (bf16[128,768]{1,0:T(8,128)(2,1)S(1)}, bf16[128,768]{1,0:T(8,128)(2,1)S(1)}, u32[]{:S(2)}, u32[]{:S(2)}) collective-permute-start(bf16[128,768]{1,0:T(8,128)(2,1)S(1)} %bitcast.52), channel_id=1, source_target_pairs={{0,1},{2,0},{4,2},{6,4},{7,6},{5,7},{3,5},{1,3},{8,10},{10,12},{12... | collective-permute-start | bytes 589832 | tf_op jit(solution)/shard_map/ppermute | solution.py:69
  46.2 9.3 %collective-permute-start.8 = (bf16[128,768]{1,0:T(8,128)(2,1)}, bf16[128,768]{1,0:T(8,128)(2,1)S(1)}, u32[]{:S(2)}, u32[]{:S(2)}) collective-permute-start(bf16[128,768]{1,0:T(8,128)(2,1)} %collective-permute-done.7), channel_id=1, source_target_pairs={{0,2},{2,4},{4,6},{6,7},{7,5},{5,3},{3,1},{1,0},{8,9},{10,8},{12,1... | collective-permute-start | bytes 589832 | tf_op jit(solution)/shard_map/ppermute | solution.py:69
  48.3 9.8 %collective-permute-start.12 = (bf16[128,768]{1,0:T(8,128)(2,1)}, bf16[128,768]{1,0:T(8,128)(2,1)S(1)}, u32[]{:S(2)}, u32[]{:S(2)}) collective-permute-start(bf16[128,768]{1,0:T(8,128)(2,1)} %collective-permute-done.11), channel_id=1, source_target_pairs={{0,1},{2,0},{4,2},{6,4},{7,6},{5,7},{3,5},{1,3},{8,10},{10,12},{12... | collective-permute-start | bytes 589832 | tf_op jit(solution)/shard_map/ppermute | solution.py:69
  51.2 8.4 %collective-permute-start.1 = (bf16[128,768]{1,0:T(8,128)(2,1)S(1)}, bf16[128,768]{1,0:T(8,128)(2,1)S(1)}, u32[]{:S(2)}, u32[]{:S(2)}) collective-permute-start(bf16[128,768]{1,0:T(8,128)(2,1)S(1)} %collective-permute-done), channel_id=1, source_target_pairs={{0,2},{2,4},{4,6},{6,7},{7,5},{5,3},{3,1},{1,0},{8,9},{10,8},{12,1... | collective-permute-start | bytes 589832 | tf_op jit(solution)/shard_map/ppermute | solution.py:69
  53.8 20.4 %copy-start.3 = (bf16[128,768]{1,0:T(8,128)(2,1)}, bf16[128,768]{1,0:T(8,128)(2,1)S(1)}, u32[]{:S(2)}) copy-start(bf16[128,768]{1,0:T(8,128)(2,1)S(1)} %collective-permute-done.4) | copy-start | bytes 589828
  53.8 8.4 %collective-permute-start.5 = (bf16[128,768]{1,0:T(8,128)(2,1)S(1)}, bf16[128,768]{1,0:T(8,128)(2,1)S(1)}, u32[]{:S(2)}, u32[]{:S(2)}) collective-permute-start(bf16[128,768]{1,0:T(8,128)(2,1)S(1)} %collective-permute-done.4), channel_id=1, source_target_pairs={{0,1},{2,0},{4,2},{6,4},{7,6},{5,7},{3,5},{1,3},{8,10},{10,12},{12... | collective-permute-start | bytes 589832 | tf_op jit(solution)/shard_map/ppermute | solution.py:69
  53.9 17.8 %copy-start.32 = (pred[128]{0:T(512)(128)(4,1)S(1)}, pred[128]{0:T(512)(128)(4,1)}, u32[]{:S(2)}) copy-start(pred[128]{0:T(512)(128)(4,1)} %broadcast_compare_fusion.8) | copy-start | bytes 388
  55.5 8.3 %collective-permute-start.9 = (bf16[128,768]{1,0:T(8,128)(2,1)S(1)}, bf16[128,768]{1,0:T(8,128)(2,1)S(1)}, u32[]{:S(2)}, u32[]{:S(2)}) collective-permute-start(bf16[128,768]{1,0:T(8,128)(2,1)S(1)} %collective-permute-done.8), channel_id=1, source_target_pairs={{0,2},{2,4},{4,6},{6,7},{7,5},{5,3},{3,1},{1,0},{8,9},{10,8},{12,1... | collective-permute-start | bytes 589832 | tf_op jit(solution)/shard_map/ppermute | solution.py:69
  58.1 13.6 %collective-permute-start.13 = (bf16[128,768]{1,0:T(8,128)(2,1)S(1)}, bf16[128,768]{1,0:T(8,128)(2,1)S(1)}, u32[]{:S(2)}, u32[]{:S(2)}) collective-permute-start(bf16[128,768]{1,0:T(8,128)(2,1)S(1)} %collective-permute-done.12), channel_id=1, source_target_pairs={{0,1},{2,0},{4,2},{6,4},{7,6},{5,7},{3,5},{1,3},{8,10},{10,12},{12... | collective-permute-start | bytes 589832 | tf_op jit(solution)/shard_map/ppermute | solution.py:69
  59.6 8.1 %collective-permute-start.2 = (bf16[128,768]{1,0:T(8,128)(2,1)S(1)}, bf16[128,768]{1,0:T(8,128)(2,1)S(1)}, u32[]{:S(2)}, u32[]{:S(2)}) collective-permute-start(bf16[128,768]{1,0:T(8,128)(2,1)S(1)} %collective-permute-done.1), channel_id=1, source_target_pairs={{0,2},{2,4},{4,6},{6,7},{7,5},{5,3},{3,1},{1,0},{8,9},{10,8},{12,1... | collective-permute-start | bytes 589832 | tf_op jit(solution)/shard_map/ppermute | solution.py:69
  62.3 11.3 %copy-start.5 = (bf16[128,768]{1,0:T(8,128)(2,1)}, bf16[128,768]{1,0:T(8,128)(2,1)S(1)}, u32[]{:S(2)}) copy-start(bf16[128,768]{1,0:T(8,128)(2,1)S(1)} %collective-permute-done.5) | copy-start | bytes 589828
  62.3 12.6 %collective-permute-start.6 = (bf16[128,768]{1,0:T(8,128)(2,1)S(1)}, bf16[128,768]{1,0:T(8,128)(2,1)S(1)}, u32[]{:S(2)}, u32[]{:S(2)}) collective-permute-start(bf16[128,768]{1,0:T(8,128)(2,1)S(1)} %collective-permute-done.5), channel_id=1, source_target_pairs={{0,1},{2,0},{4,2},{6,4},{7,6},{5,7},{3,5},{1,3},{8,10},{10,12},{12... | collective-permute-start | bytes 589832 | tf_op jit(solution)/shard_map/ppermute | solution.py:69
  63.8 6.8 %collective-permute-start.10 = (bf16[128,768]{1,0:T(8,128)(2,1)S(1)}, bf16[128,768]{1,0:T(8,128)(2,1)S(1)}, u32[]{:S(2)}, u32[]{:S(2)}) collective-permute-start(bf16[128,768]{1,0:T(8,128)(2,1)S(1)} %collective-permute-done.9), channel_id=1, source_target_pairs={{0,2},{2,4},{4,6},{6,7},{7,5},{5,3},{3,1},{1,0},{8,9},{10,8},{12,1... | collective-permute-start | bytes 589832 | tf_op jit(solution)/shard_map/ppermute | solution.py:69
  67.7 7.9 %collective-permute-start.3 = (bf16[128,768]{1,0:T(8,128)(2,1)S(1)}, bf16[128,768]{1,0:T(8,128)(2,1)}, u32[]{:S(2)}, u32[]{:S(2)}) collective-permute-start(bf16[128,768]{1,0:T(8,128)(2,1)S(1)} %collective-permute-done.2), channel_id=1, source_target_pairs={{0,2},{2,4},{4,6},{6,7},{7,5},{5,3},{3,1},{1,0},{8,9},{10,8},{12,1... | collective-permute-start | bytes 589832 | tf_op jit(solution)/shard_map/ppermute | solution.py:69
  80.8 5.9 %copy-start.44 = (s32[128]{0:T(128)S(1)}, s32[128]{0:T(128)}, u32[]{:S(2)}) copy-start(s32[128]{0:T(128)} %copy-done.43) | copy-start | bytes 1540
  80.8 6.6 %copy-start.42 = (s32[128]{0:T(128)S(1)}, s32[128]{0:T(128)}, u32[]{:S(2)}) copy-start(s32[128]{0:T(128)} %copy-done.41) | copy-start | bytes 1540
  80.8 7.3 %copy-start.40 = (s32[128]{0:T(128)S(1)}, s32[128]{0:T(128)}, u32[]{:S(2)}) copy-start(s32[128]{0:T(128)} %copy-done.39) | copy-start | bytes 1540
  80.8 8.0 %copy-start.38 = (s32[128]{0:T(128)S(1)}, s32[128]{0:T(128)}, u32[]{:S(2)}) copy-start(s32[128]{0:T(128)} %copy-done.37) | copy-start | bytes 1540
  80.8 8.8 %copy-start.36 = (s32[128]{0:T(128)S(1)}, s32[128]{0:T(128)}, u32[]{:S(2)}) copy-start(s32[128]{0:T(128)} %copy-done.35) | copy-start | bytes 1540
  80.8 11.5 %copy-start.53 = (s32[128]{0:T(128)S(1)}, s32[128]{0:T(128)}, u32[]{:S(2)}) copy-start(s32[128]{0:T(128)} %dynamic_slice.94) | copy-start | bytes 1540
  80.8 11.4 %copy-start.54 = (pred[128]{0:T(512)(128)(4,1)S(1)}, pred[128]{0:T(512)(128)(4,1)}, u32[]{:S(2)}) copy-start(pred[128]{0:T(512)(128)(4,1)} %dynamic_slice.93) | copy-start | bytes 388
  92.3 6.9 %copy-start.4 = (bf16[128,768]{1,0:T(8,128)(2,1)S(1)}, bf16[128,768]{1,0:T(8,128)(2,1)}, u32[]{:S(2)}) copy-start(bf16[128,768]{1,0:T(8,128)(2,1)} %copy-done.3) | copy-start | bytes 589828
  94.7 5.6 %copy-start.52 = (pred[128]{0:T(512)(128)(4,1)S(1)}, pred[128]{0:T(512)(128)(4,1)}, u32[]{:S(2)}) copy-start(pred[128]{0:T(512)(128)(4,1)} %dynamic_slice.74) | copy-start | bytes 388
  94.7 13.8 %all-to-all-start.1 = ((bf16[4,32,768]{2,1,0:T(8,128)(2,1)}), bf16[4,32,768]{2,1,0:T(8,128)(2,1)S(1)}, u32[]{:S(2)}, u32[]{:S(2)}) async-start(bf16[4,32,768]{2,1,0:T(8,128)(2,1)} %bitcast.55), calls=%async_computation.1 | async-start | bytes 393216 | tf_op jit(solution)/shard_map/all_to_all | solution.py:208
  (25 other events, 68.4 us)

commit v13 on v11

--- a/solution.py
+++ b/solution.py
@@ -69,6 +69,13 @@
             origin = ring_arr[(my_pos - even_step * mirror * t) % count]
             out = lax.dynamic_update_slice_in_dim(out, cur, origin * rows, 0)
     return out
+
+
+def sum_free_pick(stack, group):
+    rows = stack[0]
+    for g in range(1, stack.shape[0]):
+        rows = jnp.where(group == g, stack[g], rows)
+    return rows
 
 
 def scores_of(x_rows, y_rows, pos_mask, inv_root):
@@ -181,7 +188,12 @@
     returned = lax.all_to_all(
         grad_local.reshape(lang_size, per_slot, emb_width), "lang", split_axis=0, concat_axis=0, tiled=True
     )
-    grad_tgt = returned[slot_group]
+    grad_tgt = jnp.stack(
+        [
+            sum_free_pick(returned, slot_group[slot])
+            for slot in range(lang_size)
+        ]
+    )
     return (grad_src, grad_tgt, pair_loss)
 
 

time: 80.7 us -> 87.7 us (1.087)
  between operations: 13.1 us -> 20.3 us
    gather x1 -> x0, local copies, waits for them, and re-layouts: 1.23 us -> none  [per_device(): grad_tgt = returned[slot_group]]
  transfers between devices with their start and end apart: 16 -> 16, of which waited for: 8 -> 8; matrix products, arithmetic and copies ran while one was open for 20% -> 19% of each run, Pallas kernels for 0% -> 0%
where the time goes in v13:
time: 87.7 us; the launch traced here: 86.9 us
  starting transfers between devices  26.5 us (30%)
  between operations  20.3 us (23%)
  local copies, waits for them, and re-layouts  12.4 us (14%)
  waiting for transfers between devices  11.3 us (13%)
  matrix products  9.12 us (10%)
  other arithmetic  7.37 us (8%)
    ppermute x14, starting transfers between devices, ring_gather(): cur = lax.ppermute(cur, ('lang', 'dp'), pairs)  19.5 us
    ppermute x14, waiting for transfers between devices, ring_gather(): cur = lax.ppermute(cur, ('lang', 'dp'), pairs)  10.7 us
    all_to_all x1, starting transfers between devices, per_device(): lax.all_to_all(grad_local.reshape(lang_size, per_slot, emb_width), 'lang'...  3.6 us
    dot_general x1, matrix products, per_device(): jnp.dot(g_rows, y_all, preferred_element_type=jnp.float32) * inv_root  3.48 us
    all_to_all x1, starting transfers between devices, per_device(): lax.all_to_all(ordered, 'lang', split_axis=0, concat_axis=1, tiled=True)  3.37 us
    dot_general x1, matrix products, per_device(): lax.dot_general(g_cols, x_all, (((0,), (0,)), ((), ())), preferred_elemen...  3.25 us
    reduce_sum x1, other arithmetic, block_stats(): pos_score = jnp.sum(jnp.where(is_pos, scores_f, 0.0), axis=1)  2.41 us
    dot_general x1, matrix products, scores_of(): lax.dot_general(x_rows, y_rows, (((1,), (1,)), ((), ())), preferred_eleme...  2.39 us
  transfers between devices with their start and end apart: 16, of which 8 were waited for; matrix products, arithmetic and copies ran while one was open for 19% of the time, Pallas kernels for 0%

profile of v13, /device:TPU:0, one launch (start us, length us, event | category | flops | bytes accessed | tf_op | source)
XLA Modules:
  0.0 86.9 jit_solution(7476751391689172349)
XLA Ops:
  0.7 3.1 %collective-permute-start.7 = (bf16[128,768]{1,0:T(8,128)(2,1)}, bf16[128,768]{1,0:T(8,128)(2,1)}, u32[]{:S(2)}, u32[]{:S(2)}) collective-permute-start(bf16[128,768]{1,0:T(8,128)(2,1)} %param.10), channel_id=1, source_target_pairs={{0,2},{2,4},{4,6},{6,7},{7,5},{5,3},{3,1},{1,0},{8,9},{10,8},{12,1... | collective-permute-start | bytes 589832 | tf_op jit(solution)/shard_map/ppermute | solution.py:68
  3.8 0.0 collective-permute-start.11
  3.8 0.7 compare_select_fusion.5
  4.5 0.6 scatter_custom_fusion
  5.1 1.2 %gather_fusion = bf16[4,32,768]{2,1,0:T(8,128)(2,1)} fusion(bf16[4,32,768]{2,1,0:T(8,128)(2,1)S(1)} %copy-done, s32[1024]{0:T(1024)S(1)} %pad_clamp_fusion), kind=kCustom, calls=%fused_computation | custom fusion | bytes 393232 | tf_op jit(solution)/shard_map/gather | solution.py:121
  6.4 3.4 %all-to-all-start = ((bf16[4,32,768]{2,1,0:T(8,128)(2,1)}), bf16[4,32,768]{2,1,0:T(8,128)(2,1)S(1)}, u32[]{:S(2)}, u32[]{:S(2)}) async-start(bf16[4,32,768]{2,1,0:T(8,128)(2,1)} %gather_fusion), calls=%async_computation | async-start | bytes 393216 | tf_op jit(solution)/shard_map/all_to_all | solution.py:122
  9.8 1.3 %dynamic_slice.73 = s32[1]{0:T(128)} dynamic-slice(s32[4]{0:T(128)} %param.13, s32[]{:T(128)S(6)} %select_n.341), dynamic_slice_sizes={1} | dynamic-slice | bytes 12 | tf_op jit(solution)/shard_map/dynamic_slice | solution.py:124
  11.1 0.7 iota_compare_fusion
  11.8 1.5 %convert_reduce_fusion = s32[1024]{0:T(1024)S(1)} fusion(s32[1024]{0:T(1024)} %bitcast.49, s32[1024]{0:T(1024)S(1)} %fusion.46, pred[1024]{0:T(1024)(128)(4,1)S(1)} %iota_compare_fusion), kind=kLoop, calls=%fused_computation.11 | loop fusion | flops 4193280 | bytes 13312 | tf_op jit(solution)/shard_map/reduce_max | solution.py:131
  13.3 0.1 broadcast.208.clone.1
  13.5 0.7 fusion.66
  14.1 0.6 dynamic_slice.75
  19.4 0.7 fusion.67
  25.2 0.6 dynamic_slice.94
  32.8 0.7 dynamic_slice.74
  33.5 0.6 dynamic_slice.93
  34.1 0.6 dynamic_slice.72
  34.8 0.5 fusion.55
  35.3 2.0 %collective-permute-start = (bf16[128,768]{1,0:T(8,128)(2,1)S(1)}, bf16[128,768]{1,0:T(8,128)(2,1)S(1)}, u32[]{:S(2)}, u32[]{:S(2)}) collective-permute-start(bf16[128,768]{1,0:T(8,128)(2,1)S(1)} %bitcast.44), channel_id=1, source_target_pairs={{0,2},{2,4},{4,6},{6,7},{7,5},{5,3},{3,1},{1,0},{8,9},{10,8},{12,1... | collective-permute-start | bytes 589832 | tf_op jit(solution)/shard_map/ppermute | solution.py:68
  37.4 0.0 collective-permute-start.4
  37.4 0.1 broadcast.208.clone
  37.5 2.1 %collective-permute-start.8 = (bf16[128,768]{1,0:T(8,128)(2,1)}, bf16[128,768]{1,0:T(8,128)(2,1)S(1)}, u32[]{:S(2)}, u32[]{:S(2)}) collective-permute-start(bf16[128,768]{1,0:T(8,128)(2,1)} %collective-permute-done.7), channel_id=1, source_target_pairs={{0,2},{2,4},{4,6},{6,7},{7,5},{5,3},{3,1},{1,0},{8,9},{10,8},{12,1... | collective-permute-start | bytes 589832 | tf_op jit(solution)/shard_map/ppermute | solution.py:68
  39.6 0.0 collective-permute-start.12
  39.6 1.0 %constant_dynamic-update-slice_fusion.1 = bf16[1024,768]{1,0:T(8,128)(2,1)S(1)} fusion(bf16[1024,768]{1,0:T(8,128)(2,1)S(1)} %constant_dynamic-update-slice_fusion.7, bf16[128,768]{1,0:T(8,128)(2,1)} %collective-permute-done.7, s32[]{:T(128)S(6)} %select_n.353), kind=kLoop, calls=%fused_computation.78 | loop fusion | bytes 393220 | tf_op jit(solution)/shard_map/dynamic_update_slice | solution.py:70
  40.6 2.1 %collective-permute-done = bf16[128,768]{1,0:T(8,128)(2,1)S(1)} collective-permute-done((bf16[128,768]{1,0:T(8,128)(2,1)S(1)}, bf16[128,768]{1,0:T(8,128)(2,1)S(1)}, u32[]{:S(2)}, u32[]{:S(2)}) %collective-permute-start) | collective-permute-done | bytes 196640 | tf_op jit(solution)/shard_map/ppermute | solution.py:68
  42.6 2.5 %collective-permute-start.1 = (bf16[128,768]{1,0:T(8,128)(2,1)S(1)}, bf16[128,768]{1,0:T(8,128)(2,1)S(1)}, u32[]{:S(2)}, u32[]{:S(2)}) collective-permute-start(bf16[128,768]{1,0:T(8,128)(2,1)S(1)} %collective-permute-done), channel_id=1, source_target_pairs={{0,2},{2,4},{4,6},{6,7},{7,5},{5,3},{3,1},{1,0},{8,9},{10,8},{12,1... | collective-permute-start | bytes 589832 | tf_op jit(solution)/shard_map/ppermute | solution.py:68
  45.2 1.8 %collective-permute-done.8 = bf16[128,768]{1,0:T(8,128)(2,1)S(1)} collective-permute-done((bf16[128,768]{1,0:T(8,128)(2,1)}, bf16[128,768]{1,0:T(8,128)(2,1)S(1)}, u32[]{:S(2)}, u32[]{:S(2)}) %collective-permute-start.8) | collective-permute-done | bytes 196640 | tf_op jit(solution)/shard_map/ppermute | solution.py:68
  47.0 2.4 %collective-permute-start.9 = (bf16[128,768]{1,0:T(8,128)(2,1)S(1)}, bf16[128,768]{1,0:T(8,128)(2,1)S(1)}, u32[]{:S(2)}, u32[]{:S(2)}) collective-permute-start(bf16[128,768]{1,0:T(8,128)(2,1)S(1)} %collective-permute-done.8), channel_id=1, source_target_pairs={{0,2},{2,4},{4,6},{6,7},{7,5},{5,3},{3,1},{1,0},{8,9},{10,8},{12,1... | collective-permute-start | bytes 589832 | tf_op jit(solution)/shard_map/ppermute | solution.py:68
  49.4 1.7 %collective-permute-done.1 = bf16[128,768]{1,0:T(8,128)(2,1)S(1)} collective-permute-done((bf16[128,768]{1,0:T(8,128)(2,1)S(1)}, bf16[128,768]{1,0:T(8,128)(2,1)S(1)}, u32[]{:S(2)}, u32[]{:S(2)}) %collective-permute-start.1) | collective-permute-done | bytes 196640 | tf_op jit(solution)/shard_map/ppermute | solution.py:68
  51.1 2.5 %collective-permute-start.2 = (bf16[128,768]{1,0:T(8,128)(2,1)S(1)}, bf16[128,768]{1,0:T(8,128)(2,1)S(1)}, u32[]{:S(2)}, u32[]{:S(2)}) collective-permute-start(bf16[128,768]{1,0:T(8,128)(2,1)S(1)} %collective-permute-done.1), channel_id=1, source_target_pairs={{0,2},{2,4},{4,6},{6,7},{7,5},{5,3},{3,1},{1,0},{8,9},{10,8},{12,1... | collective-permute-start | bytes 589832 | tf_op jit(solution)/shard_map/ppermute | solution.py:68
  53.6 1.7 %collective-permute-done.9 = bf16[128,768]{1,0:T(8,128)(2,1)S(1)} collective-permute-done((bf16[128,768]{1,0:T(8,128)(2,1)S(1)}, bf16[128,768]{1,0:T(8,128)(2,1)S(1)}, u32[]{:S(2)}, u32[]{:S(2)}) %collective-permute-start.9) | collective-permute-done | bytes 196640 | tf_op jit(solution)/shard_map/ppermute | solution.py:68
  55.3 2.5 %collective-permute-start.10 = (bf16[128,768]{1,0:T(8,128)(2,1)S(1)}, bf16[128,768]{1,0:T(8,128)(2,1)S(1)}, u32[]{:S(2)}, u32[]{:S(2)}) collective-permute-start(bf16[128,768]{1,0:T(8,128)(2,1)S(1)} %collective-permute-done.9), channel_id=1, source_target_pairs={{0,2},{2,4},{4,6},{6,7},{7,5},{5,3},{3,1},{1,0},{8,9},{10,8},{12,1... | collective-permute-start | bytes 589832 | tf_op jit(solution)/shard_map/ppermute | solution.py:68
  57.8 1.3 %collective-permute-done.2 = bf16[128,768]{1,0:T(8,128)(2,1)S(1)} collective-permute-done((bf16[128,768]{1,0:T(8,128)(2,1)S(1)}, bf16[128,768]{1,0:T(8,128)(2,1)S(1)}, u32[]{:S(2)}, u32[]{:S(2)}) %collective-permute-start.2) | collective-permute-done | bytes 196640 | tf_op jit(solution)/shard_map/ppermute | solution.py:68
  59.0 2.5 %collective-permute-start.3 = (bf16[128,768]{1,0:T(8,128)(2,1)S(1)}, bf16[128,768]{1,0:T(8,128)(2,1)S(1)}, u32[]{:S(2)}, u32[]{:S(2)}) collective-permute-start(bf16[128,768]{1,0:T(8,128)(2,1)S(1)} %collective-permute-done.2), channel_id=1, source_target_pairs={{0,2},{2,4},{4,6},{6,7},{7,5},{5,3},{3,1},{1,0},{8,9},{10,8},{12,1... | collective-permute-start | bytes 589832 | tf_op jit(solution)/shard_map/ppermute | solution.py:68
  61.6 0.5 collective-permute-done.10
  62.1 0.9 %constant_dynamic-update-slice_fusion.2 = bf16[1024,768]{1,0:T(8,128)(2,1)S(1)} fusion(bf16[1024,768]{1,0:T(8,128)(2,1)S(1)} %constant_dynamic-update-slice_fusion.3, bf16[128,768]{1,0:T(8,128)(2,1)} %collective-permute-done.11, s32[]{:T(128)S(6)} %select_n.365), kind=kLoop, calls=%fused_computation.79 | loop fusion | bytes 393220 | tf_op jit(solution)/shard_map/dynamic_update_slice | solution.py:70
  63.1 1.7 %collective-permute-done.3 = bf16[128,768]{1,0:T(8,128)(2,1)S(1)} collective-permute-done((bf16[128,768]{1,0:T(8,128)(2,1)S(1)}, bf16[128,768]{1,0:T(8,128)(2,1)S(1)}, u32[]{:S(2)}, u32[]{:S(2)}) %collective-permute-start.3) | collective-permute-done | bytes 196640 | tf_op jit(solution)/shard_map/ppermute | solution.py:68
  64.9 2.4 %select_reduce_fusion.3 = (f32[1024]{0:T(1024)S(1)}, f32[1024]{0:T(1024)S(1)}, f32[1024,1024]{0,1:T(8,128)S(1)}) fusion(pred[1024]{0:T(1024)(128)(4,1)S(1)} %broadcast_compare_fusion, pred[1024]{0:T(1024)(128)(4,1)S(1)} %copy-done.9, s32[1024]{0:T(1024)S(1)} %bitcast.50, s32[1024]{0:T(1024)S(1)} %fusion.46, ...), kind=kOutput, calls=%fused_computation.10 | convolution fusion | flops 1618999296 | bytes 7358464 | tf_op jit(solution)/shard_map/dot_general | solution.py:82
  67.3 2.4 %fusion.1 = (f32[1024]{0:T(1024)S(1)}, f32[1024]{0:T(1024)S(1)}, f32[1024]{0:T(1024)S(1)}) fusion(f32[1024,1024]{0,1:T(8,128)S(1)} %get-tuple-element.27, s32[1024]{0:T(1024)S(1)} %bitcast.51, s32[1024]{0:T(1024)S(1)} %fusion.46, f32[1024]{0:T(1024)S(1)} %get-tuple-element.7, pred[1024]{0:T(1024)(128)(4,1)S(1)} %copy-done.9, f32[1024]{0:T(1024)S(1)} %get-tuple-element.6, ...), kind=kLoop, calls=%fused_computation.6 | loop fusion | flops 9434112 | bytes 4225024 | tf_op jit(solution)/shard_map/reduce_sum | solution.py:94
  69.7 1.3 %select_reduce_fusion.4 = (f32[]{:T(128)}, f32[1024]{0:T(1024)S(1)}, f32[]{:T(128)}, f32[1024]{0:T(1024)S(1)}) fusion(f32[1024]{0:T(1024)S(1)} %get-tuple-element.7, f32[1024]{0:T(1024)S(1)} %get-tuple-element.4, f32[1024]{0:T(1024)S(1)} %get-tuple-element.3, f32[1024]{0:T(1024)S(1)} %get-tuple-element.6, f32[1024]{0:T(1024)S(1)} %get-tuple-element.5, ...), kind=kLoop, calls=%fused_computation.105 | loop fusion | flops 16382 | bytes 32780 | tf_op jit(solution)/shard_map/reduce_sum | solution.py:164
  71.1 0.6 copy-done.5
  71.7 0.6 dynamic_slice.95
  72.2 0.6 dynamic_slice.92
  72.9 3.3 %fusion.6 = bf16[128,768]{1,0:T(8,128)(2,1)} fusion(bf16[1024,768]{1,0:T(8,128)(2,1)S(1)} %constant_dynamic-update-slice_fusion.6, bf16[128,768]{1,0:T(8,128)(2,1)S(1)} %bitcast.47, f32[128]{0:T(128)} %dynamic_slice.95, f32[1024]{0:T(1024)} %copy-done.7, s32[128]{0:T(128)} %dynamic_slice.94, f32[]{:T(128)} %bitcast, s32[1024]{0:T(1024)S(1)} %bitcast.52, ...), kind=kOutput, calls=%fused_computation.20 | convolution fusion | flops 404815872 | bytes 1976452 | tf_op jit(solution)/shard_map/dot_general | solution.py:184
  76.1 3.6 %all-to-all-start.1 = ((bf16[4,32,768]{2,1,0:T(8,128)(2,1)}), bf16[4,32,768]{2,1,0:T(8,128)(2,1)S(1)}, u32[]{:S(2)}, u32[]{:S(2)}) async-start(bf16[4,32,768]{2,1,0:T(8,128)(2,1)} %bitcast.48), calls=%async_computation.1 | async-start | bytes 393216 | tf_op jit(solution)/shard_map/all_to_all | solution.py:188
  79.7 3.5 %fusion.5 = bf16[128,768]{1,0:T(8,128)(2,1)} fusion(bf16[1024,768]{1,0:T(8,128)(2,1)S(1)} %constant_dynamic-update-slice_fusion.8, bf16[128,768]{1,0:T(8,128)(2,1)} %param.10, f32[1024]{0:T(1024)S(1)} %copy-done.6, f32[128]{0:T(128)} %dynamic_slice.92, s32[128]{0:T(128)} %fusion.55, f32[]{:T(128)} %bitcast, s32[1024]{0:T(1024)S(1)} %fusion.46, ...), kind=kOutput, calls=%fused_computation.19 | convolution fusion | flops 404815872 | bytes 1976452 | tf_op jit(solution)/shard_map/dot_general | solution.py:175
  84.5 0.5 all-to-all-done.1
  85.1 0.7 pad_maximum_fusion
  (55 shorter events, 0.5 us)
Async XLA Ops:
  0.6 4.5 %copy-start = (bf16[4,32,768]{2,1,0:T(8,128)(2,1)S(1)}, bf16[4,32,768]{2,1,0:T(8,128)(2,1)}, u32[]{:S(2)}) copy-start(bf16[4,32,768]{2,1,0:T(8,128)(2,1)} %param.11) | copy-start | bytes 589828
  0.6 13.5 %copy-start.11 = (s32[8]{0:T(128)S(1)}, s32[8]{0:T(128)}, u32[]{:S(2)}) copy-start(s32[8]{0:T(128)} %constant.226.clone) | copy-start | bytes 100
  0.7 18.7 %copy-start.2 = (s32[8]{0:T(128)S(1)}, s32[8]{0:T(128)}, u32[]{:S(2)}) copy-start(s32[8]{0:T(128)} %constant.225.clone) | copy-start | bytes 100
  0.7 12.7 %copy-start.1 = (bf16[128,768]{1,0:T(8,128)(2,1)S(1)}, bf16[128,768]{1,0:T(8,128)(2,1)}, u32[]{:S(2)}) copy-start(bf16[128,768]{1,0:T(8,128)(2,1)} %param.10) | copy-start | bytes 589828
  0.7 12.8 %copy-start.3 = (s32[4]{0:T(128)S(1)}, s32[4]{0:T(128)}, u32[]{:S(2)}) copy-start(s32[4]{0:T(128)} %param.12) | copy-start | bytes 52
  0.7 36.8 %collective-permute-start.7 = (bf16[128,768]{1,0:T(8,128)(2,1)}, bf16[128,768]{1,0:T(8,128)(2,1)}, u32[]{:S(2)}, u32[]{:S(2)}) collective-permute-start(bf16[128,768]{1,0:T(8,128)(2,1)} %param.10), channel_id=1, source_target_pairs={{0,2},{2,4},{4,6},{6,7},{7,5},{5,3},{3,1},{1,0},{8,9},{10,8},{12,1... | collective-permute-start | bytes 589832 | tf_op jit(solution)/shard_map/ppermute | solution.py:68
  3.8 35.8 %collective-permute-start.11 = (bf16[128,768]{1,0:T(8,128)(2,1)}, bf16[128,768]{1,0:T(8,128)(2,1)}, u32[]{:S(2)}, u32[]{:S(2)}) collective-permute-start(bf16[128,768]{1,0:T(8,128)(2,1)} %param.10), channel_id=1, source_target_pairs={{0,1},{2,0},{4,2},{6,4},{7,6},{5,7},{3,5},{1,3},{8,10},{10,12},{12... | collective-permute-start | bytes 589832 | tf_op jit(solution)/shard_map/ppermute | solution.py:68
  5.1 29.1 %copy-start.10 = (f32[4]{0:T(128)S(1)}, f32[4]{0:T(128)}, u32[]{:S(2)}) copy-start(f32[4]{0:T(128)} %param.15) | copy-start | bytes 52
  5.1 29.7 %copy-start.4 = (s32[1,1024]{1,0:T(1,128)S(1)}, s32[1,1024]{1,0:T(1,128)}, u32[]{:S(2)}) copy-start(s32[1,1024]{1,0:T(1,128)} %param.14) | copy-start | bytes 12292
  6.4 29.0 %all-to-all-start = ((bf16[4,32,768]{2,1,0:T(8,128)(2,1)}), bf16[4,32,768]{2,1,0:T(8,128)(2,1)S(1)}, u32[]{:S(2)}, u32[]{:S(2)}) async-start(bf16[4,32,768]{2,1,0:T(8,128)(2,1)} %gather_fusion), calls=%async_computation | async-start | bytes 393216 | tf_op jit(solution)/shard_map/all_to_all | solution.py:122
  11.8 25.6 %copy-start.8 = (pred[1024]{0:T(1024)(128)(4,1)}, pred[1024]{0:T(1024)(128)(4,1)S(1)}, u32[]{:S(2)}) copy-start(pred[1024]{0:T(1024)(128)(4,1)S(1)} %iota_compare_fusion) | copy-start | bytes 3076
  35.3 7.3 %collective-permute-start = (bf16[128,768]{1,0:T(8,128)(2,1)S(1)}, bf16[128,768]{1,0:T(8,128)(2,1)S(1)}, u32[]{:S(2)}, u32[]{:S(2)}) collective-permute-start(bf16[128,768]{1,0:T(8,128)(2,1)S(1)} %bitcast.44), channel_id=1, source_target_pairs={{0,2},{2,4},{4,6},{6,7},{7,5},{5,3},{3,1},{1,0},{8,9},{10,8},{12,1... | collective-permute-start | bytes 589832 | tf_op jit(solution)/shard_map/ppermute | solution.py:68
  37.4 7.8 %collective-permute-start.4 = (bf16[128,768]{1,0:T(8,128)(2,1)S(1)}, bf16[128,768]{1,0:T(8,128)(2,1)S(1)}, u32[]{:S(2)}, u32[]{:S(2)}) collective-permute-start(bf16[128,768]{1,0:T(8,128)(2,1)S(1)} %bitcast.45), channel_id=1, source_target_pairs={{0,1},{2,0},{4,2},{6,4},{7,6},{5,7},{3,5},{1,3},{8,10},{10,12},{12... | collective-permute-start | bytes 589832 | tf_op jit(solution)/shard_map/ppermute | solution.py:68
  37.5 9.4 %collective-permute-start.8 = (bf16[128,768]{1,0:T(8,128)(2,1)}, bf16[128,768]{1,0:T(8,128)(2,1)S(1)}, u32[]{:S(2)}, u32[]{:S(2)}) collective-permute-start(bf16[128,768]{1,0:T(8,128)(2,1)} %collective-permute-done.7), channel_id=1, source_target_pairs={{0,2},{2,4},{4,6},{6,7},{7,5},{5,3},{3,1},{1,0},{8,9},{10,8},{12,1... | collective-permute-start | bytes 589832 | tf_op jit(solution)/shard_map/ppermute | solution.py:68
  39.6 9.8 %collective-permute-start.12 = (bf16[128,768]{1,0:T(8,128)(2,1)}, bf16[128,768]{1,0:T(8,128)(2,1)S(1)}, u32[]{:S(2)}, u32[]{:S(2)}) collective-permute-start(bf16[128,768]{1,0:T(8,128)(2,1)} %collective-permute-done.11), channel_id=1, source_target_pairs={{0,1},{2,0},{4,2},{6,4},{7,6},{5,7},{3,5},{1,3},{8,10},{10,12},{12... | collective-permute-start | bytes 589832 | tf_op jit(solution)/shard_map/ppermute | solution.py:68
  42.6 8.4 %collective-permute-start.1 = (bf16[128,768]{1,0:T(8,128)(2,1)S(1)}, bf16[128,768]{1,0:T(8,128)(2,1)S(1)}, u32[]{:S(2)}, u32[]{:S(2)}) collective-permute-start(bf16[128,768]{1,0:T(8,128)(2,1)S(1)} %collective-permute-done), channel_id=1, source_target_pairs={{0,2},{2,4},{4,6},{6,7},{7,5},{5,3},{3,1},{1,0},{8,9},{10,8},{12,1... | collective-permute-start | bytes 589832 | tf_op jit(solution)/shard_map/ppermute | solution.py:68
  45.1 8.4 %collective-permute-start.5 = (bf16[128,768]{1,0:T(8,128)(2,1)S(1)}, bf16[128,768]{1,0:T(8,128)(2,1)S(1)}, u32[]{:S(2)}, u32[]{:S(2)}) collective-permute-start(bf16[128,768]{1,0:T(8,128)(2,1)S(1)} %collective-permute-done.4), channel_id=1, source_target_pairs={{0,1},{2,0},{4,2},{6,4},{7,6},{5,7},{3,5},{1,3},{8,10},{10,12},{12... | collective-permute-start | bytes 589832 | tf_op jit(solution)/shard_map/ppermute | solution.py:68
  47.0 8.3 %collective-permute-start.9 = (bf16[128,768]{1,0:T(8,128)(2,1)S(1)}, bf16[128,768]{1,0:T(8,128)(2,1)S(1)}, u32[]{:S(2)}, u32[]{:S(2)}) collective-permute-start(bf16[128,768]{1,0:T(8,128)(2,1)S(1)} %collective-permute-done.8), channel_id=1, source_target_pairs={{0,2},{2,4},{4,6},{6,7},{7,5},{5,3},{3,1},{1,0},{8,9},{10,8},{12,1... | collective-permute-start | bytes 589832 | tf_op jit(solution)/shard_map/ppermute | solution.py:68
  49.3 13.7 %collective-permute-start.13 = (bf16[128,768]{1,0:T(8,128)(2,1)S(1)}, bf16[128,768]{1,0:T(8,128)(2,1)S(1)}, u32[]{:S(2)}, u32[]{:S(2)}) collective-permute-start(bf16[128,768]{1,0:T(8,128)(2,1)S(1)} %collective-permute-done.12), channel_id=1, source_target_pairs={{0,1},{2,0},{4,2},{6,4},{7,6},{5,7},{3,5},{1,3},{8,10},{10,12},{12... | collective-permute-start | bytes 589832 | tf_op jit(solution)/shard_map/ppermute | solution.py:68
  51.1 8.0 %collective-permute-start.2 = (bf16[128,768]{1,0:T(8,128)(2,1)S(1)}, bf16[128,768]{1,0:T(8,128)(2,1)S(1)}, u32[]{:S(2)}, u32[]{:S(2)}) collective-permute-start(bf16[128,768]{1,0:T(8,128)(2,1)S(1)} %collective-permute-done.1), channel_id=1, source_target_pairs={{0,2},{2,4},{4,6},{6,7},{7,5},{5,3},{3,1},{1,0},{8,9},{10,8},{12,1... | collective-permute-start | bytes 589832 | tf_op jit(solution)/shard_map/ppermute | solution.py:68
  53.6 11.3 %collective-permute-start.6 = (bf16[128,768]{1,0:T(8,128)(2,1)S(1)}, bf16[128,768]{1,0:T(8,128)(2,1)S(1)}, u32[]{:S(2)}, u32[]{:S(2)}) collective-permute-start(bf16[128,768]{1,0:T(8,128)(2,1)S(1)} %collective-permute-done.5), channel_id=1, source_target_pairs={{0,1},{2,0},{4,2},{6,4},{7,6},{5,7},{3,5},{1,3},{8,10},{10,12},{12... | collective-permute-start | bytes 589832 | tf_op jit(solution)/shard_map/ppermute | solution.py:68
  55.3 6.8 %collective-permute-start.10 = (bf16[128,768]{1,0:T(8,128)(2,1)S(1)}, bf16[128,768]{1,0:T(8,128)(2,1)S(1)}, u32[]{:S(2)}, u32[]{:S(2)}) collective-permute-start(bf16[128,768]{1,0:T(8,128)(2,1)S(1)} %collective-permute-done.9), channel_id=1, source_target_pairs={{0,2},{2,4},{4,6},{6,7},{7,5},{5,3},{3,1},{1,0},{8,9},{10,8},{12,1... | collective-permute-start | bytes 589832 | tf_op jit(solution)/shard_map/ppermute | solution.py:68
  59.0 5.7 %collective-permute-start.3 = (bf16[128,768]{1,0:T(8,128)(2,1)S(1)}, bf16[128,768]{1,0:T(8,128)(2,1)S(1)}, u32[]{:S(2)}, u32[]{:S(2)}) collective-permute-start(bf16[128,768]{1,0:T(8,128)(2,1)S(1)} %collective-permute-done.2), channel_id=1, source_target_pairs={{0,2},{2,4},{4,6},{6,7},{7,5},{5,3},{3,1},{1,0},{8,9},{10,8},{12,1... | collective-permute-start | bytes 589832 | tf_op jit(solution)/shard_map/ppermute | solution.py:68
  61.5 3.3 %copy-start.9 = (pred[1024]{0:T(1024)(128)(4,1)S(1)}, pred[1024]{0:T(1024)(128)(4,1)}, u32[]{:S(2)}) copy-start(pred[1024]{0:T(1024)(128)(4,1)} %copy-done.8) | copy-start | bytes 3076
  71.1 0.6 copy-start.5
  71.1 1.8 %copy-start.7 = (f32[1024]{0:T(1024)}, f32[1024]{0:T(1024)S(1)}, u32[]{:S(2)}) copy-start(f32[1024]{0:T(1024)S(1)} %get-tuple-element.29) | copy-start | bytes 12292
  72.9 6.9 %copy-start.6 = (f32[1024]{0:T(1024)S(1)}, f32[1024]{0:T(1024)}, u32[]{:S(2)}) copy-start(f32[1024]{0:T(1024)} %copy-done.5) | copy-start | bytes 12292
  76.1 8.9 %all-to-all-start.1 = ((bf16[4,32,768]{2,1,0:T(8,128)(2,1)}), bf16[4,32,768]{2,1,0:T(8,128)(2,1)S(1)}, u32[]{:S(2)}, u32[]{:S(2)}) async-start(bf16[4,32,768]{2,1,0:T(8,128)(2,1)} %bitcast.48), calls=%async_computation.1 | async-start | bytes 393216 | tf_op jit(solution)/shard_map/all_to_all | solution.py:188

commit v14 on v11

--- a/solution.py
+++ b/solution.py
@@ -155,7 +155,6 @@
     row_f = row_live.astype(jnp.float32)
     col_f = col_live.astype(jnp.float32)
     total = jnp.sum(row_f * (row_lse - 2.0 * pos_score)) + jnp.sum(col_f * col_lse)
-    pair_loss = (total / live_count.astype(jnp.float32)).reshape(1)
 
     mine = shard_index * row_count
     a_my = lax.dynamic_slice_in_dim(pair_align, mine, row_count)
@@ -178,6 +177,8 @@
         g_cols, x_all, (((0,), (0,)), ((), ())), preferred_element_type=jnp.float32
     )
     grad_local = (own_terms * inv_root).astype(jnp.bfloat16)
+    total = total + 0.0 * grad_local[0, 0].astype(jnp.float32)
+    pair_loss = (total / live_count.astype(jnp.float32)).reshape(1)
     returned = lax.all_to_all(
         grad_local.reshape(lang_size, per_slot, emb_width), "lang", split_axis=0, concat_axis=0, tiled=True
     )

time: 80.7 us -> 82.4 us (1.021)
  local copies, waits for them, and re-layouts: 12.9 us -> 14.2 us
    slice x0 -> x1, local copies, waits for them, and re-layouts: none -> 1.26 us  [per_device(): total = total + 0.0 * grad_local[0, 0].astype(jnp.float32)]
  transfers between devices with their start and end apart: 16 -> 16, of which waited for: 8 -> 7; matrix products, arithmetic and copies ran while one was open for 20% -> 21% of each run, Pallas kernels for 0% -> 0%
where the time goes in v14:
time: 82.4 us; the launch traced here: 81.5 us
  starting transfers between devices  26.5 us (32%)
  local copies, waits for them, and re-layouts  14.2 us (17%)
  between operations  13.8 us (17%)
  waiting for transfers between devices  10.7 us (13%)
  matrix products  9.15 us (11%)
  other arithmetic  7.11 us (9%)
    ppermute x14, starting transfers between devices, ring_gather(): cur = lax.ppermute(cur, ('lang', 'dp'), pairs)  19.6 us
    ppermute x14, waiting for transfers between devices, ring_gather(): cur = lax.ppermute(cur, ('lang', 'dp'), pairs)  10.7 us
    all_to_all x1, starting transfers between devices, per_device(): lax.all_to_all(grad_local.reshape(lang_size, per_slot, emb_width), 'lang'...  3.58 us
    dot_general x1, matrix products, per_device(): jnp.dot(g_rows, y_all, preferred_element_type=jnp.float32) * inv_root  3.48 us
    all_to_all x1, starting transfers between devices, per_device(): lax.all_to_all(ordered, 'lang', split_axis=0, concat_axis=1, tiled=True)  3.37 us
    dot_general x1, matrix products, per_device(): lax.dot_general(g_cols, x_all, (((0,), (0,)), ((), ())), preferred_elemen...  3.27 us
    reduce_sum x1, other arithmetic, block_stats(): pos_score = jnp.sum(jnp.where(is_pos, scores_f, 0.0), axis=1)  2.43 us
    dot_general x1, matrix products, scores_of(): lax.dot_general(x_rows, y_rows, (((1,), (1,)), ((), ())), preferred_eleme...  2.4 us
  transfers between devices with their start and end apart: 16, of which 7 were waited for; matrix products, arithmetic and copies ran while one was open for 21% of the time, Pallas kernels for 0%

profile of v14, /device:TPU:0, one launch (start us, length us, event | category | flops | bytes accessed | tf_op | source)
XLA Modules:
  0.0 81.5 jit_solution(17372679056448153422)
XLA Ops:
  0.7 3.1 %collective-permute-start.7 = (bf16[128,768]{1,0:T(8,128)(2,1)}, bf16[128,768]{1,0:T(8,128)(2,1)}, u32[]{:S(2)}, u32[]{:S(2)}) collective-permute-start(bf16[128,768]{1,0:T(8,128)(2,1)} %param.10), channel_id=1, source_target_pairs={{0,2},{2,4},{4,6},{6,7},{7,5},{5,3},{3,1},{1,0},{8,9},{10,8},{12,1... | collective-permute-start | bytes 589832 | tf_op jit(solution)/shard_map/ppermute | solution.py:68
  3.8 0.7 compare_select_fusion.5
  4.5 0.6 scatter_custom_fusion
  5.1 1.2 %gather_fusion = bf16[4,32,768]{2,1,0:T(8,128)(2,1)} fusion(bf16[4,32,768]{2,1,0:T(8,128)(2,1)S(1)} %copy-done, s32[1024]{0:T(1024)S(1)} %pad_clamp_fusion.1), kind=kCustom, calls=%fused_computation | custom fusion | bytes 393232 | tf_op jit(solution)/shard_map/gather | solution.py:114
  6.3 3.4 %all-to-all-start = ((bf16[4,32,768]{2,1,0:T(8,128)(2,1)}), bf16[4,32,768]{2,1,0:T(8,128)(2,1)S(1)}, u32[]{:S(2)}, u32[]{:S(2)}) async-start(bf16[4,32,768]{2,1,0:T(8,128)(2,1)} %gather_fusion), calls=%async_computation | async-start | bytes 393216 | tf_op jit(solution)/shard_map/all_to_all | solution.py:115
  9.7 1.3 %dynamic_slice.73 = s32[1]{0:T(128)} dynamic-slice(s32[4]{0:T(128)} %param.13, s32[]{:T(128)S(6)} %select_n.256), dynamic_slice_sizes={1} | dynamic-slice | bytes 12 | tf_op jit(solution)/shard_map/dynamic_slice | solution.py:117
  11.0 0.6 iota_compare_fusion
  11.7 1.5 %convert_reduce_fusion = s32[1024]{0:T(1024)S(1)} fusion(s32[1024]{0:T(1024)} %bitcast.38, s32[1024]{0:T(1024)S(1)} %fusion.46, pred[1024]{0:T(1024)(128)(4,1)S(1)} %iota_compare_fusion), kind=kLoop, calls=%fused_computation.12 | loop fusion | flops 4193280 | bytes 13312 | tf_op jit(solution)/shard_map/reduce_max | solution.py:124
  13.2 0.1 broadcast.196.clone.1
  13.4 0.6 dynamic_slice.75
  18.6 0.7 fusion.66
  23.7 0.7 dynamic_slice.94
  25.0 0.6 dynamic_slice.74
  25.6 0.6 dynamic_slice.93
  26.2 0.6 dynamic_slice.72
  26.8 0.5 fusion.55
  27.3 2.0 %collective-permute-start = (bf16[128,768]{1,0:T(8,128)(2,1)S(1)}, bf16[128,768]{1,0:T(8,128)(2,1)S(1)}, u32[]{:S(2)}, u32[]{:S(2)}) collective-permute-start(bf16[128,768]{1,0:T(8,128)(2,1)S(1)} %bitcast.33), channel_id=1, source_target_pairs={{0,2},{2,4},{4,6},{6,7},{7,5},{5,3},{3,1},{1,0},{8,9},{10,8},{12,1... | collective-permute-start | bytes 589832 | tf_op jit(solution)/shard_map/ppermute | solution.py:68
  29.4 0.0 collective-permute-start.4
  29.4 0.1 broadcast.196.clone
  29.5 2.1 %collective-permute-start.8 = (bf16[128,768]{1,0:T(8,128)(2,1)}, bf16[128,768]{1,0:T(8,128)(2,1)S(1)}, u32[]{:S(2)}, u32[]{:S(2)}) collective-permute-start(bf16[128,768]{1,0:T(8,128)(2,1)} %collective-permute-done.7), channel_id=1, source_target_pairs={{0,2},{2,4},{4,6},{6,7},{7,5},{5,3},{3,1},{1,0},{8,9},{10,8},{12,1... | collective-permute-start | bytes 589832 | tf_op jit(solution)/shard_map/ppermute | solution.py:68
  31.6 0.0 collective-permute-start.12
  31.6 1.0 %constant_dynamic-update-slice_fusion.1 = bf16[1024,768]{1,0:T(8,128)(2,1)S(1)} fusion(bf16[1024,768]{1,0:T(8,128)(2,1)S(1)} %constant_dynamic-update-slice_fusion.7, bf16[128,768]{1,0:T(8,128)(2,1)} %collective-permute-done.7, s32[]{:T(128)S(6)} %select_n.268), kind=kLoop, calls=%fused_computation.74 | loop fusion | bytes 393220 | tf_op jit(solution)/shard_map/dynamic_update_slice | solution.py:70
  32.6 2.1 %collective-permute-done = bf16[128,768]{1,0:T(8,128)(2,1)S(1)} collective-permute-done((bf16[128,768]{1,0:T(8,128)(2,1)S(1)}, bf16[128,768]{1,0:T(8,128)(2,1)S(1)}, u32[]{:S(2)}, u32[]{:S(2)}) %collective-permute-start) | collective-permute-done | bytes 196640 | tf_op jit(solution)/shard_map/ppermute | solution.py:68
  34.7 2.5 %collective-permute-start.1 = (bf16[128,768]{1,0:T(8,128)(2,1)S(1)}, bf16[128,768]{1,0:T(8,128)(2,1)S(1)}, u32[]{:S(2)}, u32[]{:S(2)}) collective-permute-start(bf16[128,768]{1,0:T(8,128)(2,1)S(1)} %collective-permute-done), channel_id=1, source_target_pairs={{0,2},{2,4},{4,6},{6,7},{7,5},{5,3},{3,1},{1,0},{8,9},{10,8},{12,1... | collective-permute-start | bytes 589832 | tf_op jit(solution)/shard_map/ppermute | solution.py:68
  37.1 0.0 collective-permute-start.5
  37.2 1.8 %collective-permute-done.8 = bf16[128,768]{1,0:T(8,128)(2,1)S(1)} collective-permute-done((bf16[128,768]{1,0:T(8,128)(2,1)}, bf16[128,768]{1,0:T(8,128)(2,1)S(1)}, u32[]{:S(2)}, u32[]{:S(2)}) %collective-permute-start.8) | collective-permute-done | bytes 196640 | tf_op jit(solution)/shard_map/ppermute | solution.py:68
  39.0 2.4 %collective-permute-start.9 = (bf16[128,768]{1,0:T(8,128)(2,1)S(1)}, bf16[128,768]{1,0:T(8,128)(2,1)S(1)}, u32[]{:S(2)}, u32[]{:S(2)}) collective-permute-start(bf16[128,768]{1,0:T(8,128)(2,1)S(1)} %collective-permute-done.8), channel_id=1, source_target_pairs={{0,2},{2,4},{4,6},{6,7},{7,5},{5,3},{3,1},{1,0},{8,9},{10,8},{12,1... | collective-permute-start | bytes 589832 | tf_op jit(solution)/shard_map/ppermute | solution.py:68
  41.4 0.0 collective-permute-start.13
  41.4 1.7 %collective-permute-done.1 = bf16[128,768]{1,0:T(8,128)(2,1)S(1)} collective-permute-done((bf16[128,768]{1,0:T(8,128)(2,1)S(1)}, bf16[128,768]{1,0:T(8,128)(2,1)S(1)}, u32[]{:S(2)}, u32[]{:S(2)}) %collective-permute-start.1) | collective-permute-done | bytes 196640 | tf_op jit(solution)/shard_map/ppermute | solution.py:68
  43.1 2.5 %collective-permute-start.2 = (bf16[128,768]{1,0:T(8,128)(2,1)S(1)}, bf16[128,768]{1,0:T(8,128)(2,1)S(1)}, u32[]{:S(2)}, u32[]{:S(2)}) collective-permute-start(bf16[128,768]{1,0:T(8,128)(2,1)S(1)} %collective-permute-done.1), channel_id=1, source_target_pairs={{0,2},{2,4},{4,6},{6,7},{7,5},{5,3},{3,1},{1,0},{8,9},{10,8},{12,1... | collective-permute-start | bytes 589832 | tf_op jit(solution)/shard_map/ppermute | solution.py:68
  45.6 0.0 collective-permute-start.6
  45.6 1.7 %collective-permute-done.9 = bf16[128,768]{1,0:T(8,128)(2,1)S(1)} collective-permute-done((bf16[128,768]{1,0:T(8,128)(2,1)S(1)}, bf16[128,768]{1,0:T(8,128)(2,1)S(1)}, u32[]{:S(2)}, u32[]{:S(2)}) %collective-permute-start.9) | collective-permute-done | bytes 196640 | tf_op jit(solution)/shard_map/ppermute | solution.py:68
  47.3 2.5 %collective-permute-start.10 = (bf16[128,768]{1,0:T(8,128)(2,1)S(1)}, bf16[128,768]{1,0:T(8,128)(2,1)S(1)}, u32[]{:S(2)}, u32[]{:S(2)}) collective-permute-start(bf16[128,768]{1,0:T(8,128)(2,1)S(1)} %collective-permute-done.9), channel_id=1, source_target_pairs={{0,2},{2,4},{4,6},{6,7},{7,5},{5,3},{3,1},{1,0},{8,9},{10,8},{12,1... | collective-permute-start | bytes 589832 | tf_op jit(solution)/shard_map/ppermute | solution.py:68
  49.8 1.3 %collective-permute-done.2 = bf16[128,768]{1,0:T(8,128)(2,1)S(1)} collective-permute-done((bf16[128,768]{1,0:T(8,128)(2,1)S(1)}, bf16[128,768]{1,0:T(8,128)(2,1)S(1)}, u32[]{:S(2)}, u32[]{:S(2)}) %collective-permute-start.2) | collective-permute-done | bytes 196640 | tf_op jit(solution)/shard_map/ppermute | solution.py:68
  51.1 2.5 %collective-permute-start.3 = (bf16[128,768]{1,0:T(8,128)(2,1)S(1)}, bf16[128,768]{1,0:T(8,128)(2,1)S(1)}, u32[]{:S(2)}, u32[]{:S(2)}) collective-permute-start(bf16[128,768]{1,0:T(8,128)(2,1)S(1)} %collective-permute-done.2), channel_id=1, source_target_pairs={{0,2},{2,4},{4,6},{6,7},{7,5},{5,3},{3,1},{1,0},{8,9},{10,8},{12,1... | collective-permute-start | bytes 589832 | tf_op jit(solution)/shard_map/ppermute | solution.py:68
  53.6 0.5 collective-permute-done.10
  54.1 0.9 %constant_dynamic-update-slice_fusion.2 = bf16[1024,768]{1,0:T(8,128)(2,1)S(1)} fusion(bf16[1024,768]{1,0:T(8,128)(2,1)S(1)} %constant_dynamic-update-slice_fusion.3, bf16[128,768]{1,0:T(8,128)(2,1)} %collective-permute-done.11, s32[]{:T(128)S(6)} %select_n.280), kind=kLoop, calls=%fused_computation.75 | loop fusion | bytes 393220 | tf_op jit(solution)/shard_map/dynamic_update_slice | solution.py:70
  55.1 1.7 %collective-permute-done.3 = bf16[128,768]{1,0:T(8,128)(2,1)S(1)} collective-permute-done((bf16[128,768]{1,0:T(8,128)(2,1)S(1)}, bf16[128,768]{1,0:T(8,128)(2,1)S(1)}, u32[]{:S(2)}, u32[]{:S(2)}) %collective-permute-start.3) | collective-permute-done | bytes 196640 | tf_op jit(solution)/shard_map/ppermute | solution.py:68
  56.9 2.4 %select_reduce_fusion.3 = (f32[1024]{0:T(1024)S(1)}, f32[1024]{0:T(1024)S(1)}, f32[1024,1024]{0,1:T(8,128)S(1)}) fusion(pred[1024]{0:T(1024)(128)(4,1)S(1)} %copy-done.5, pred[1024]{0:T(1024)(128)(4,1)S(1)} %copy-done.9, s32[1024]{0:T(1024)S(1)} %bitcast.39, s32[1024]{0:T(1024)S(1)} %fusion.46, ...), kind=kOutput, calls=%fused_computation.11 | convolution fusion | flops 1618999296 | bytes 7358464 | tf_op jit(solution)/shard_map/dot_general | solution.py:75
  59.3 2.4 %fusion.1 = (f32[1024]{0:T(1024)S(1)}, f32[1024]{0:T(1024)S(1)}, f32[1024]{0:T(1024)S(1)}) fusion(f32[1024,1024]{0,1:T(8,128)S(1)} %get-tuple-element.19, s32[1024]{0:T(1024)S(1)} %bitcast.40, s32[1024]{0:T(1024)S(1)} %fusion.46, f32[1024]{0:T(1024)S(1)} %get-tuple-element.7, pred[1024]{0:T(1024)(128)(4,1)S(1)} %copy-done.9, f32[1024]{0:T(1024)S(1)} %get-tuple-element.6, ...), kind=kLoop, calls=%fused_computation.7 | loop fusion | flops 9434112 | bytes 4225024 | tf_op jit(solution)/shard_map/reduce_sum | solution.py:87
  61.8 1.9 %select_reduce_fusion.4 = (f32[]{:T(128)}, f32[1024]{0:T(1024)S(1)}, f32[]{:T(128)}, f32[1024]{0:T(1024)}) fusion(f32[1024]{0:T(1024)S(1)} %get-tuple-element.7, f32[1024]{0:T(1024)S(1)} %get-tuple-element.4, f32[1024]{0:T(1024)S(1)} %get-tuple-element.3, f32[1024]{0:T(1024)S(1)} %get-tuple-element.6, f32[1024]{0:T(1024)S(1)} %get-tuple-element.5, ...), kind=kLoop, calls=%fused_computation.102 | loop fusion | flops 16382 | bytes 32780 | tf_op jit(solution)/shard_map/reduce_sum | solution.py:157
  63.6 0.6 dynamic_slice.95
  64.2 1.3 %dynamic_slice.92 = f32[128]{0:T(128)} dynamic-slice(f32[1024]{0:T(1024)} %get-tuple-element.21, s32[]{:T(128)S(6)} %select_n.257), dynamic_slice_sizes={128} | dynamic-slice | bytes 1028 | tf_op jit(solution)/shard_map/dynamic_slice | solution.py:162
  65.5 3.3 %fusion.6 = bf16[128,768]{1,0:T(8,128)(2,1)} fusion(bf16[1024,768]{1,0:T(8,128)(2,1)S(1)} %constant_dynamic-update-slice_fusion.6, bf16[128,768]{1,0:T(8,128)(2,1)S(1)} %bitcast.36, f32[128]{0:T(128)} %dynamic_slice.95, f32[1024]{0:T(1024)} %get-tuple-element.21, s32[128]{0:T(128)} %dynamic_slice.94, f32[]{:T(128)} %bitcast, s32[1024]{0:T(1024)S(1)} %bitcast.41, ...), kind=kOutput, calls=%fused_computation.21 | convolution fusion | flops 404815872 | bytes 1976452 | tf_op jit(solution)/shard_map/dot_general | solution.py:176
  68.8 3.6 %all-to-all-start.1 = ((bf16[4,32,768]{2,1,0:T(8,128)(2,1)}), bf16[4,32,768]{2,1,0:T(8,128)(2,1)S(1)}, u32[]{:S(2)}, u32[]{:S(2)}) async-start(bf16[4,32,768]{2,1,0:T(8,128)(2,1)} %bitcast.37), calls=%async_computation.1 | async-start | bytes 393216 | tf_op jit(solution)/shard_map/all_to_all | solution.py:182
  72.4 3.5 %fusion.5 = bf16[128,768]{1,0:T(8,128)(2,1)} fusion(bf16[1024,768]{1,0:T(8,128)(2,1)S(1)} %constant_dynamic-update-slice_fusion.8, bf16[128,768]{1,0:T(8,128)(2,1)} %param.10, f32[1024]{0:T(1024)} %copy-done.7, f32[128]{0:T(128)} %dynamic_slice.92, s32[128]{0:T(128)} %fusion.55, f32[]{:T(128)} %bitcast, s32[1024]{0:T(1024)S(1)} %fusion.46, ...), kind=kOutput, calls=%fused_computation.20 | convolution fusion | flops 404815872 | bytes 1976452 | tf_op jit(solution)/shard_map/dot_general | solution.py:167
  75.9 1.3 %slice.8 = bf16[1,1]{1,0:T(2,128)(2,1)} slice(bf16[128,768]{1,0:T(8,128)(2,1)} %fusion.6), slice={[0:1], [0:1]} | slice | bytes 4 | tf_op jit(solution)/shard_map/slice | solution.py:180
  79.2 1.2 %gather_fusion.1 = bf16[4,32,768]{2,1,0:T(8,128)(2,1)} fusion(bf16[4,32,768]{2,1,0:T(8,128)(2,1)S(1)} %all-to-all-done.1, s32[1024]{0:T(1024)S(1)} %pad_clamp_fusion), kind=kCustom, calls=%fused_computation.1 | custom fusion | bytes 393232 | tf_op jit(solution)/shard_map/gather | solution.py:185
  (54 shorter events, 0.4 us)
Async XLA Ops:
  0.6 4.4 %copy-start = (bf16[4,32,768]{2,1,0:T(8,128)(2,1)S(1)}, bf16[4,32,768]{2,1,0:T(8,128)(2,1)}, u32[]{:S(2)}) copy-start(bf16[4,32,768]{2,1,0:T(8,128)(2,1)} %param.11) | copy-start | bytes 589828
  0.6 12.7 %copy-start.11 = (s32[8]{0:T(128)S(1)}, s32[8]{0:T(128)}, u32[]{:S(2)}) copy-start(s32[8]{0:T(128)} %constant.213.clone) | copy-start | bytes 100
  0.7 18.0 %copy-start.2 = (s32[8]{0:T(128)S(1)}, s32[8]{0:T(128)}, u32[]{:S(2)}) copy-start(s32[8]{0:T(128)} %constant.212.clone) | copy-start | bytes 100
  0.7 12.6 %copy-start.1 = (bf16[128,768]{1,0:T(8,128)(2,1)S(1)}, bf16[128,768]{1,0:T(8,128)(2,1)}, u32[]{:S(2)}) copy-start(bf16[128,768]{1,0:T(8,128)(2,1)} %param.10) | copy-start | bytes 589828
  0.7 28.8 %collective-permute-start.7 = (bf16[128,768]{1,0:T(8,128)(2,1)}, bf16[128,768]{1,0:T(8,128)(2,1)}, u32[]{:S(2)}, u32[]{:S(2)}) collective-permute-start(bf16[128,768]{1,0:T(8,128)(2,1)} %param.10), channel_id=1, source_target_pairs={{0,2},{2,4},{4,6},{6,7},{7,5},{5,3},{3,1},{1,0},{8,9},{10,8},{12,1... | collective-permute-start | bytes 589832 | tf_op jit(solution)/shard_map/ppermute | solution.py:68
  3.8 27.8 %collective-permute-start.11 = (bf16[128,768]{1,0:T(8,128)(2,1)}, bf16[128,768]{1,0:T(8,128)(2,1)}, u32[]{:S(2)}, u32[]{:S(2)}) collective-permute-start(bf16[128,768]{1,0:T(8,128)(2,1)} %param.10), channel_id=1, source_target_pairs={{0,1},{2,0},{4,2},{6,4},{7,6},{5,7},{3,5},{1,3},{8,10},{10,12},{12... | collective-permute-start | bytes 589832 | tf_op jit(solution)/shard_map/ppermute | solution.py:68
  5.1 21.1 %copy-start.10 = (f32[4]{0:T(128)S(1)}, f32[4]{0:T(128)}, u32[]{:S(2)}) copy-start(f32[4]{0:T(128)} %param.15) | copy-start | bytes 52
  5.1 21.7 %copy-start.3 = (s32[1,1024]{1,0:T(1,128)S(1)}, s32[1,1024]{1,0:T(1,128)}, u32[]{:S(2)}) copy-start(s32[1,1024]{1,0:T(1,128)} %param.14) | copy-start | bytes 12292
  6.3 21.0 %all-to-all-start = ((bf16[4,32,768]{2,1,0:T(8,128)(2,1)}), bf16[4,32,768]{2,1,0:T(8,128)(2,1)S(1)}, u32[]{:S(2)}, u32[]{:S(2)}) async-start(bf16[4,32,768]{2,1,0:T(8,128)(2,1)} %gather_fusion), calls=%async_computation | async-start | bytes 393216 | tf_op jit(solution)/shard_map/all_to_all | solution.py:115
  11.6 17.7 %copy-start.8 = (pred[1024]{0:T(1024)(128)(4,1)}, pred[1024]{0:T(1024)(128)(4,1)S(1)}, u32[]{:S(2)}) copy-start(pred[1024]{0:T(1024)(128)(4,1)S(1)} %iota_compare_fusion) | copy-start | bytes 3076
  13.2 16.2 %copy-start.4 = (pred[1024]{0:T(1024)(128)(4,1)}, pred[1024]{0:T(1024)(128)(4,1)S(1)}, u32[]{:S(2)}) copy-start(pred[1024]{0:T(1024)(128)(4,1)S(1)} %broadcast_compare_fusion) | copy-start | bytes 3076
  27.3 7.3 %collective-permute-start = (bf16[128,768]{1,0:T(8,128)(2,1)S(1)}, bf16[128,768]{1,0:T(8,128)(2,1)S(1)}, u32[]{:S(2)}, u32[]{:S(2)}) collective-permute-start(bf16[128,768]{1,0:T(8,128)(2,1)S(1)} %bitcast.33), channel_id=1, source_target_pairs={{0,2},{2,4},{4,6},{6,7},{7,5},{5,3},{3,1},{1,0},{8,9},{10,8},{12,1... | collective-permute-start | bytes 589832 | tf_op jit(solution)/shard_map/ppermute | solution.py:68
  29.4 7.8 %collective-permute-start.4 = (bf16[128,768]{1,0:T(8,128)(2,1)S(1)}, bf16[128,768]{1,0:T(8,128)(2,1)S(1)}, u32[]{:S(2)}, u32[]{:S(2)}) collective-permute-start(bf16[128,768]{1,0:T(8,128)(2,1)S(1)} %bitcast.34), channel_id=1, source_target_pairs={{0,1},{2,0},{4,2},{6,4},{7,6},{5,7},{3,5},{1,3},{8,10},{10,12},{12... | collective-permute-start | bytes 589832 | tf_op jit(solution)/shard_map/ppermute | solution.py:68
  29.5 9.4 %collective-permute-start.8 = (bf16[128,768]{1,0:T(8,128)(2,1)}, bf16[128,768]{1,0:T(8,128)(2,1)S(1)}, u32[]{:S(2)}, u32[]{:S(2)}) collective-permute-start(bf16[128,768]{1,0:T(8,128)(2,1)} %collective-permute-done.7), channel_id=1, source_target_pairs={{0,2},{2,4},{4,6},{6,7},{7,5},{5,3},{3,1},{1,0},{8,9},{10,8},{12,1... | collective-permute-start | bytes 589832 | tf_op jit(solution)/shard_map/ppermute | solution.py:68
  31.6 9.8 %collective-permute-start.12 = (bf16[128,768]{1,0:T(8,128)(2,1)}, bf16[128,768]{1,0:T(8,128)(2,1)S(1)}, u32[]{:S(2)}, u32[]{:S(2)}) collective-permute-start(bf16[128,768]{1,0:T(8,128)(2,1)} %collective-permute-done.11), channel_id=1, source_target_pairs={{0,1},{2,0},{4,2},{6,4},{7,6},{5,7},{3,5},{1,3},{8,10},{10,12},{12... | collective-permute-start | bytes 589832 | tf_op jit(solution)/shard_map/ppermute | solution.py:68
  34.7 8.4 %collective-permute-start.1 = (bf16[128,768]{1,0:T(8,128)(2,1)S(1)}, bf16[128,768]{1,0:T(8,128)(2,1)S(1)}, u32[]{:S(2)}, u32[]{:S(2)}) collective-permute-start(bf16[128,768]{1,0:T(8,128)(2,1)S(1)} %collective-permute-done), channel_id=1, source_target_pairs={{0,2},{2,4},{4,6},{6,7},{7,5},{5,3},{3,1},{1,0},{8,9},{10,8},{12,1... | collective-permute-start | bytes 589832 | tf_op jit(solution)/shard_map/ppermute | solution.py:68
  37.1 8.4 %collective-permute-start.5 = (bf16[128,768]{1,0:T(8,128)(2,1)S(1)}, bf16[128,768]{1,0:T(8,128)(2,1)S(1)}, u32[]{:S(2)}, u32[]{:S(2)}) collective-permute-start(bf16[128,768]{1,0:T(8,128)(2,1)S(1)} %collective-permute-done.4), channel_id=1, source_target_pairs={{0,1},{2,0},{4,2},{6,4},{7,6},{5,7},{3,5},{1,3},{8,10},{10,12},{12... | collective-permute-start | bytes 589832 | tf_op jit(solution)/shard_map/ppermute | solution.py:68
  39.0 8.3 %collective-permute-start.9 = (bf16[128,768]{1,0:T(8,128)(2,1)S(1)}, bf16[128,768]{1,0:T(8,128)(2,1)S(1)}, u32[]{:S(2)}, u32[]{:S(2)}) collective-permute-start(bf16[128,768]{1,0:T(8,128)(2,1)S(1)} %collective-permute-done.8), channel_id=1, source_target_pairs={{0,2},{2,4},{4,6},{6,7},{7,5},{5,3},{3,1},{1,0},{8,9},{10,8},{12,1... | collective-permute-start | bytes 589832 | tf_op jit(solution)/shard_map/ppermute | solution.py:68
  41.4 13.7 %collective-permute-start.13 = (bf16[128,768]{1,0:T(8,128)(2,1)S(1)}, bf16[128,768]{1,0:T(8,128)(2,1)S(1)}, u32[]{:S(2)}, u32[]{:S(2)}) collective-permute-start(bf16[128,768]{1,0:T(8,128)(2,1)S(1)} %collective-permute-done.12), channel_id=1, source_target_pairs={{0,1},{2,0},{4,2},{6,4},{7,6},{5,7},{3,5},{1,3},{8,10},{10,12},{12... | collective-permute-start | bytes 589832 | tf_op jit(solution)/shard_map/ppermute | solution.py:68
  43.1 8.0 %collective-permute-start.2 = (bf16[128,768]{1,0:T(8,128)(2,1)S(1)}, bf16[128,768]{1,0:T(8,128)(2,1)S(1)}, u32[]{:S(2)}, u32[]{:S(2)}) collective-permute-start(bf16[128,768]{1,0:T(8,128)(2,1)S(1)} %collective-permute-done.1), channel_id=1, source_target_pairs={{0,2},{2,4},{4,6},{6,7},{7,5},{5,3},{3,1},{1,0},{8,9},{10,8},{12,1... | collective-permute-start | bytes 589832 | tf_op jit(solution)/shard_map/ppermute | solution.py:68
  45.6 11.3 %collective-permute-start.6 = (bf16[128,768]{1,0:T(8,128)(2,1)S(1)}, bf16[128,768]{1,0:T(8,128)(2,1)S(1)}, u32[]{:S(2)}, u32[]{:S(2)}) collective-permute-start(bf16[128,768]{1,0:T(8,128)(2,1)S(1)} %collective-permute-done.5), channel_id=1, source_target_pairs={{0,1},{2,0},{4,2},{6,4},{7,6},{5,7},{3,5},{1,3},{8,10},{10,12},{12... | collective-permute-start | bytes 589832 | tf_op jit(solution)/shard_map/ppermute | solution.py:68
  47.3 6.8 %collective-permute-start.10 = (bf16[128,768]{1,0:T(8,128)(2,1)S(1)}, bf16[128,768]{1,0:T(8,128)(2,1)S(1)}, u32[]{:S(2)}, u32[]{:S(2)}) collective-permute-start(bf16[128,768]{1,0:T(8,128)(2,1)S(1)} %collective-permute-done.9), channel_id=1, source_target_pairs={{0,2},{2,4},{4,6},{6,7},{7,5},{5,3},{3,1},{1,0},{8,9},{10,8},{12,1... | collective-permute-start | bytes 589832 | tf_op jit(solution)/shard_map/ppermute | solution.py:68
  51.1 5.7 %collective-permute-start.3 = (bf16[128,768]{1,0:T(8,128)(2,1)S(1)}, bf16[128,768]{1,0:T(8,128)(2,1)S(1)}, u32[]{:S(2)}, u32[]{:S(2)}) collective-permute-start(bf16[128,768]{1,0:T(8,128)(2,1)S(1)} %collective-permute-done.2), channel_id=1, source_target_pairs={{0,2},{2,4},{4,6},{6,7},{7,5},{5,3},{3,1},{1,0},{8,9},{10,8},{12,1... | collective-permute-start | bytes 589832 | tf_op jit(solution)/shard_map/ppermute | solution.py:68
  53.6 3.3 %copy-start.5 = (pred[1024]{0:T(1024)(128)(4,1)S(1)}, pred[1024]{0:T(1024)(128)(4,1)}, u32[]{:S(2)}) copy-start(pred[1024]{0:T(1024)(128)(4,1)} %copy-done.4) | copy-start | bytes 3076
  53.6 3.3 %copy-start.9 = (pred[1024]{0:T(1024)(128)(4,1)S(1)}, pred[1024]{0:T(1024)(128)(4,1)}, u32[]{:S(2)}) copy-start(pred[1024]{0:T(1024)(128)(4,1)} %copy-done.8) | copy-start | bytes 3076
  63.6 1.9 %copy-start.7 = (f32[1024]{0:T(1024)}, f32[1024]{0:T(1024)S(1)}, u32[]{:S(2)}) copy-start(f32[1024]{0:T(1024)S(1)} %get-tuple-element.9) | copy-start | bytes 12292
  65.5 6.9 %copy-start.6 = (pred[1024]{0:T(1024)(128)(4,1)S(1)}, pred[1024]{0:T(1024)(128)(4,1)}, u32[]{:S(2)}) copy-start(pred[1024]{0:T(1024)(128)(4,1)} %copy-done.4) | copy-start | bytes 3076
  68.8 10.3 %all-to-all-start.1 = ((bf16[4,32,768]{2,1,0:T(8,128)(2,1)}), bf16[4,32,768]{2,1,0:T(8,128)(2,1)S(1)}, u32[]{:S(2)}, u32[]{:S(2)}) async-start(bf16[4,32,768]{2,1,0:T(8,128)(2,1)} %bitcast.37), calls=%async_computation.1 | async-start | bytes 393216 | tf_op jit(solution)/shard_map/all_to_all | solution.py:182

commit v15 on v11

--- a/solution.py
+++ b/solution.py
@@ -159,7 +159,7 @@
 
     mine = shard_index * row_count
     a_my = lax.dynamic_slice_in_dim(pair_align, mine, row_count)
-    r_my = lax.dynamic_slice_in_dim(row_live, mine, row_count)
+    r_my = (mine + jnp.arange(row_count, dtype=jnp.int32)) < live_count
     lse_my = lax.dynamic_slice_in_dim(row_lse, mine, row_count)
     pos_rows = perm[None, :] == a_my[:, None]
     s_rows = scores_of(src_emb, y_all, pos_rows, inv_root)
@@ -168,10 +168,11 @@
         jnp.dot(g_rows, y_all, preferred_element_type=jnp.float32) * inv_root
     ).astype(jnp.bfloat16)
 
-    p_my = lax.dynamic_slice_in_dim(perm, mine, row_count)
-    c_my = lax.dynamic_slice_in_dim(col_live, mine, row_count)
+    q_my = jnp.arange(row_count, dtype=jnp.int32)
+    p_my = (q_my // per_slot * data_size + shard_index) * per_slot + q_my % per_slot
     clse_my = lax.dynamic_slice_in_dim(col_lse, mine, row_count)
     pos_cols = p_my[None, :] == pair_align[:, None]
+    c_my = jnp.max((pos_cols & row_live[:, None]).astype(jnp.int32), axis=0) > 0
     s_cols = scores_of(x_all, partner, pos_cols, inv_root)
     g_cols = grad_of(s_cols, pos_cols, row_live, c_my, row_lse, clse_my, weight)
     own_terms = lax.dot_general(

time: 80.7 us -> 80.7 us (level)
  other arithmetic: 7.11 us -> 9.56 us
  local copies, waits for them, and re-layouts: 12.9 us -> 10.5 us
    dynamic_slice x3 -> x0, local copies, waits for them, and re-layouts: 1.81 us -> none  [the longest x1 0.65 us: per_device(): p_my = lax.dynamic_slice_in_dim(perm, mine, row_count)]
    lt x0 -> x1, other arithmetic: none -> 1.06 us  [per_device(): r_my = mine + jnp.arange(row_count, dtype=jnp.int32) < live_count]
    reduce_max x0 -> x1, other arithmetic: none -> 1.03 us  [per_device(): c_my = jnp.max((pos_cols & row_live[:, None]).astype(jnp.int32), axis=0) > 0]
  transfers between devices with their start and end apart: 16 -> 16, of which waited for: 8 -> 8; matrix products, arithmetic and copies ran while one was open for 20% -> 22% of each run, Pallas kernels for 0% -> 0%
where the time goes in v15:
time: 80.7 us; the launch traced here: 80 us
  starting transfers between devices  26.5 us (33%)
  between operations  13 us (16%)
  waiting for transfers between devices  11.3 us (14%)
  local copies, waits for them, and re-layouts  10.5 us (13%)
  other arithmetic  9.56 us (12%)
  matrix products  9.15 us (11%)
    ppermute x14, starting transfers between devices, ring_gather(): cur = lax.ppermute(cur, ('lang', 'dp'), pairs)  19.6 us
    ppermute x14, waiting for transfers between devices, ring_gather(): cur = lax.ppermute(cur, ('lang', 'dp'), pairs)  10.7 us
    all_to_all x1, starting transfers between devices, per_device(): lax.all_to_all(grad_local.reshape(lang_size, per_slot, emb_width), 'lang'...  3.59 us
    dot_general x1, matrix products, per_device(): jnp.dot(g_rows, y_all, preferred_element_type=jnp.float32) * inv_root  3.48 us
    all_to_all x1, starting transfers between devices, per_device(): lax.all_to_all(ordered, 'lang', split_axis=0, concat_axis=1, tiled=True)  3.37 us
    dot_general x1, matrix products, per_device(): lax.dot_general(g_cols, x_all, (((0,), (0,)), ((), ())), preferred_elemen...  3.27 us
    reduce_sum x1, other arithmetic, block_stats(): pos_score = jnp.sum(jnp.where(is_pos, scores_f, 0.0), axis=1)  2.43 us
    dot_general x1, matrix products, scores_of(): lax.dot_general(x_rows, y_rows, (((1,), (1,)), ((), ())), preferred_eleme...  2.4 us
  transfers between devices with their start and end apart: 16, of which 8 were waited for; matrix products, arithmetic and copies ran while one was open for 22% of the time, Pallas kernels for 0%

profile of v15, /device:TPU:0, one launch (start us, length us, event | category | flops | bytes accessed | tf_op | source)
XLA Modules:
  0.0 80.0 jit_solution(10804633454166885154)
XLA Ops:
  0.7 3.1 %collective-permute-start.7 = (bf16[128,768]{1,0:T(8,128)(2,1)}, bf16[128,768]{1,0:T(8,128)(2,1)}, u32[]{:S(2)}, u32[]{:S(2)}) collective-permute-start(bf16[128,768]{1,0:T(8,128)(2,1)} %param.10), channel_id=1, source_target_pairs={{0,2},{2,4},{4,6},{6,7},{7,5},{5,3},{3,1},{1,0},{8,9},{10,8},{12,1... | collective-permute-start | bytes 589832 | tf_op jit(solution)/shard_map/ppermute | solution.py:68
  3.8 0.7 compare_select_fusion.5
  4.5 0.6 scatter_custom_fusion
  5.1 1.2 %gather_fusion = bf16[4,32,768]{2,1,0:T(8,128)(2,1)} fusion(bf16[4,32,768]{2,1,0:T(8,128)(2,1)S(1)} %copy-done, s32[1024]{0:T(1024)S(1)} %pad_clamp_fusion.1), kind=kCustom, calls=%fused_computation | custom fusion | bytes 393232 | tf_op jit(solution)/shard_map/gather | solution.py:114
  6.3 3.4 %all-to-all-start = ((bf16[4,32,768]{2,1,0:T(8,128)(2,1)}), bf16[4,32,768]{2,1,0:T(8,128)(2,1)S(1)}, u32[]{:S(2)}, u32[]{:S(2)}) async-start(bf16[4,32,768]{2,1,0:T(8,128)(2,1)} %gather_fusion), calls=%async_computation | async-start | bytes 393216 | tf_op jit(solution)/shard_map/all_to_all | solution.py:115
  9.8 1.2 %dynamic_slice.64 = s32[1]{0:T(128)} dynamic-slice(s32[4]{0:T(128)} %param.13, s32[]{:T(128)S(6)} %select_n.264), dynamic_slice_sizes={1} | dynamic-slice | bytes 12 | tf_op jit(solution)/shard_map/dynamic_slice | solution.py:117
  11.0 0.6 iota_compare_fusion
  11.6 1.5 %convert_reduce_fusion = s32[1024]{0:T(1024)S(1)} fusion(s32[1024]{0:T(1024)} %bitcast.37, s32[1024]{0:T(1024)S(1)} %fusion.49, pred[1024]{0:T(1024)(128)(4,1)S(1)} %iota_compare_fusion), kind=kLoop, calls=%fused_computation.12 | loop fusion | flops 4193280 | bytes 13312 | tf_op jit(solution)/shard_map/reduce_max | solution.py:124
  13.1 0.6 broadcast_compare_fusion
  13.7 1.0 %fusion.9 = s32[128]{0:T(128)S(1)} fusion(s32[128]{0:T(128)S(1)} %fusion.58, s32[1024]{0:T(1024)} %bitcast.38, pred[1024]{0:T(1024)(128)(4,1)S(1)} %iota_compare_fusion), kind=kLoop, calls=%fused_computation.32 | loop fusion | flops 524160 | bytes 6144 | tf_op jit(solution)/shard_map/reduce_max | solution.py:175
  14.7 0.6 broadcast_compare_fusion.1
  15.3 0.1 broadcast.262.clone.1
  15.4 1.1 %add_compare_fusion = pred[128]{0:T(512)(128)(4,1)} fusion(s32[]{:T(128)} %bitcast.1, s32[]{:T(128)S(6)} %mul.241), kind=kLoop, calls=%fused_computation.127 | loop fusion | flops 256 | bytes 136 | tf_op jit(solution)/shard_map/lt | solution.py:162
  16.5 0.6 dynamic_slice.65
  21.7 0.7 fusion.73
  27.4 0.7 dynamic_slice.63
  28.1 0.6 fusion.62
  28.7 2.0 %collective-permute-start = (bf16[128,768]{1,0:T(8,128)(2,1)S(1)}, bf16[128,768]{1,0:T(8,128)(2,1)S(1)}, u32[]{:S(2)}, u32[]{:S(2)}) collective-permute-start(bf16[128,768]{1,0:T(8,128)(2,1)S(1)} %bitcast.32), channel_id=1, source_target_pairs={{0,2},{2,4},{4,6},{6,7},{7,5},{5,3},{3,1},{1,0},{8,9},{10,8},{12,1... | collective-permute-start | bytes 589832 | tf_op jit(solution)/shard_map/ppermute | solution.py:68
  30.7 0.0 collective-permute-start.4
  30.7 0.1 broadcast.262.clone
  30.8 2.1 %collective-permute-start.8 = (bf16[128,768]{1,0:T(8,128)(2,1)}, bf16[128,768]{1,0:T(8,128)(2,1)S(1)}, u32[]{:S(2)}, u32[]{:S(2)}) collective-permute-start(bf16[128,768]{1,0:T(8,128)(2,1)} %collective-permute-done.7), channel_id=1, source_target_pairs={{0,2},{2,4},{4,6},{6,7},{7,5},{5,3},{3,1},{1,0},{8,9},{10,8},{12,1... | collective-permute-start | bytes 589832 | tf_op jit(solution)/shard_map/ppermute | solution.py:68
  32.9 0.0 collective-permute-start.12
  32.9 1.0 %constant_dynamic-update-slice_fusion.2 = bf16[1024,768]{1,0:T(8,128)(2,1)S(1)} fusion(bf16[1024,768]{1,0:T(8,128)(2,1)S(1)} %constant_dynamic-update-slice_fusion.7, bf16[128,768]{1,0:T(8,128)(2,1)} %collective-permute-done.7, s32[]{:T(128)S(6)} %select_n.276), kind=kLoop, calls=%fused_computation.78 | loop fusion | bytes 393220 | tf_op jit(solution)/shard_map/dynamic_update_slice | solution.py:70
  33.9 2.1 %collective-permute-done = bf16[128,768]{1,0:T(8,128)(2,1)S(1)} collective-permute-done((bf16[128,768]{1,0:T(8,128)(2,1)S(1)}, bf16[128,768]{1,0:T(8,128)(2,1)S(1)}, u32[]{:S(2)}, u32[]{:S(2)}) %collective-permute-start) | collective-permute-done | bytes 196640 | tf_op jit(solution)/shard_map/ppermute | solution.py:68
  36.0 2.5 %collective-permute-start.1 = (bf16[128,768]{1,0:T(8,128)(2,1)S(1)}, bf16[128,768]{1,0:T(8,128)(2,1)S(1)}, u32[]{:S(2)}, u32[]{:S(2)}) collective-permute-start(bf16[128,768]{1,0:T(8,128)(2,1)S(1)} %collective-permute-done), channel_id=1, source_target_pairs={{0,2},{2,4},{4,6},{6,7},{7,5},{5,3},{3,1},{1,0},{8,9},{10,8},{12,1... | collective-permute-start | bytes 589832 | tf_op jit(solution)/shard_map/ppermute | solution.py:68
  38.5 0.0 collective-permute-start.5
  38.5 1.8 %collective-permute-done.8 = bf16[128,768]{1,0:T(8,128)(2,1)S(1)} collective-permute-done((bf16[128,768]{1,0:T(8,128)(2,1)}, bf16[128,768]{1,0:T(8,128)(2,1)S(1)}, u32[]{:S(2)}, u32[]{:S(2)}) %collective-permute-start.8) | collective-permute-done | bytes 196640 | tf_op jit(solution)/shard_map/ppermute | solution.py:68
  40.3 2.4 %collective-permute-start.9 = (bf16[128,768]{1,0:T(8,128)(2,1)S(1)}, bf16[128,768]{1,0:T(8,128)(2,1)S(1)}, u32[]{:S(2)}, u32[]{:S(2)}) collective-permute-start(bf16[128,768]{1,0:T(8,128)(2,1)S(1)} %collective-permute-done.8), channel_id=1, source_target_pairs={{0,2},{2,4},{4,6},{6,7},{7,5},{5,3},{3,1},{1,0},{8,9},{10,8},{12,1... | collective-permute-start | bytes 589832 | tf_op jit(solution)/shard_map/ppermute | solution.py:68
  42.7 0.0 collective-permute-start.13
  42.7 1.7 %collective-permute-done.1 = bf16[128,768]{1,0:T(8,128)(2,1)S(1)} collective-permute-done((bf16[128,768]{1,0:T(8,128)(2,1)S(1)}, bf16[128,768]{1,0:T(8,128)(2,1)S(1)}, u32[]{:S(2)}, u32[]{:S(2)}) %collective-permute-start.1) | collective-permute-done | bytes 196640 | tf_op jit(solution)/shard_map/ppermute | solution.py:68
  44.4 2.5 %collective-permute-start.2 = (bf16[128,768]{1,0:T(8,128)(2,1)S(1)}, bf16[128,768]{1,0:T(8,128)(2,1)S(1)}, u32[]{:S(2)}, u32[]{:S(2)}) collective-permute-start(bf16[128,768]{1,0:T(8,128)(2,1)S(1)} %collective-permute-done.1), channel_id=1, source_target_pairs={{0,2},{2,4},{4,6},{6,7},{7,5},{5,3},{3,1},{1,0},{8,9},{10,8},{12,1... | collective-permute-start | bytes 589832 | tf_op jit(solution)/shard_map/ppermute | solution.py:68
  46.9 1.7 %collective-permute-done.9 = bf16[128,768]{1,0:T(8,128)(2,1)S(1)} collective-permute-done((bf16[128,768]{1,0:T(8,128)(2,1)S(1)}, bf16[128,768]{1,0:T(8,128)(2,1)S(1)}, u32[]{:S(2)}, u32[]{:S(2)}) %collective-permute-start.9) | collective-permute-done | bytes 196640 | tf_op jit(solution)/shard_map/ppermute | solution.py:68
  48.6 2.5 %collective-permute-start.10 = (bf16[128,768]{1,0:T(8,128)(2,1)S(1)}, bf16[128,768]{1,0:T(8,128)(2,1)S(1)}, u32[]{:S(2)}, u32[]{:S(2)}) collective-permute-start(bf16[128,768]{1,0:T(8,128)(2,1)S(1)} %collective-permute-done.9), channel_id=1, source_target_pairs={{0,2},{2,4},{4,6},{6,7},{7,5},{5,3},{3,1},{1,0},{8,9},{10,8},{12,1... | collective-permute-start | bytes 589832 | tf_op jit(solution)/shard_map/ppermute | solution.py:68
  51.1 1.3 %collective-permute-done.2 = bf16[128,768]{1,0:T(8,128)(2,1)S(1)} collective-permute-done((bf16[128,768]{1,0:T(8,128)(2,1)S(1)}, bf16[128,768]{1,0:T(8,128)(2,1)S(1)}, u32[]{:S(2)}, u32[]{:S(2)}) %collective-permute-start.2) | collective-permute-done | bytes 196640 | tf_op jit(solution)/shard_map/ppermute | solution.py:68
  52.4 2.5 %collective-permute-start.3 = (bf16[128,768]{1,0:T(8,128)(2,1)S(1)}, bf16[128,768]{1,0:T(8,128)(2,1)S(1)}, u32[]{:S(2)}, u32[]{:S(2)}) collective-permute-start(bf16[128,768]{1,0:T(8,128)(2,1)S(1)} %collective-permute-done.2), channel_id=1, source_target_pairs={{0,2},{2,4},{4,6},{6,7},{7,5},{5,3},{3,1},{1,0},{8,9},{10,8},{12,1... | collective-permute-start | bytes 589832 | tf_op jit(solution)/shard_map/ppermute | solution.py:68
  54.9 0.5 collective-permute-done.10
  55.4 0.9 %constant_dynamic-update-slice_fusion = bf16[1024,768]{1,0:T(8,128)(2,1)S(1)} fusion(bf16[1024,768]{1,0:T(8,128)(2,1)S(1)} %constant_dynamic-update-slice_fusion.4, bf16[128,768]{1,0:T(8,128)(2,1)} %collective-permute-done.11, s32[]{:T(128)S(6)} %select_n.288), kind=kLoop, calls=%fused_computation.76 | loop fusion | bytes 393220 | tf_op jit(solution)/shard_map/dynamic_update_slice | solution.py:70
  56.4 1.7 %collective-permute-done.3 = bf16[128,768]{1,0:T(8,128)(2,1)S(1)} collective-permute-done((bf16[128,768]{1,0:T(8,128)(2,1)S(1)}, bf16[128,768]{1,0:T(8,128)(2,1)S(1)}, u32[]{:S(2)}, u32[]{:S(2)}) %collective-permute-start.3) | collective-permute-done | bytes 196640 | tf_op jit(solution)/shard_map/ppermute | solution.py:68
  58.2 2.4 %select_reduce_fusion.3 = (f32[1024]{0:T(1024)S(1)}, f32[1024]{0:T(1024)S(1)}, f32[1024,1024]{0,1:T(8,128)S(1)}) fusion(pred[1024]{0:T(1024)(128)(4,1)S(1)} %copy-done.4, pred[1024]{0:T(1024)(128)(4,1)S(1)} %copy-done.7, s32[1024]{0:T(1024)S(1)} %bitcast.39, s32[1024]{0:T(1024)S(1)} %fusion.49, ...), kind=kOutput, calls=%fused_computation.11 | convolution fusion | flops 1618999296 | bytes 7358464 | tf_op jit(solution)/shard_map/dot_general | solution.py:75
  60.6 2.4 %fusion.1 = (f32[1024]{0:T(1024)S(1)}, f32[1024]{0:T(1024)S(1)}, f32[1024]{0:T(1024)S(1)}) fusion(f32[1024,1024]{0,1:T(8,128)S(1)} %get-tuple-element.19, s32[1024]{0:T(1024)S(1)} %bitcast.40, s32[1024]{0:T(1024)S(1)} %fusion.49, f32[1024]{0:T(1024)S(1)} %get-tuple-element.7, pred[1024]{0:T(1024)(128)(4,1)S(1)} %copy-done.7, f32[1024]{0:T(1024)S(1)} %get-tuple-element.6, ...), kind=kLoop, calls=%fused_computation.7 | loop fusion | flops 9434112 | bytes 4225024 | tf_op jit(solution)/shard_map/reduce_sum | solution.py:87
  63.1 1.2 %select_reduce_fusion.4 = (f32[]{:T(128)}, f32[1024]{0:T(1024)S(1)}, f32[]{:T(128)}, f32[1024]{0:T(1024)S(1)}) fusion(f32[1024]{0:T(1024)S(1)} %get-tuple-element.7, f32[1024]{0:T(1024)S(1)} %get-tuple-element.4, f32[1024]{0:T(1024)S(1)} %get-tuple-element.3, f32[1024]{0:T(1024)S(1)} %get-tuple-element.6, f32[1024]{0:T(1024)S(1)} %get-tuple-element.5, ...), kind=kLoop, calls=%fused_computation.105 | loop fusion | flops 16382 | bytes 32780 | tf_op jit(solution)/shard_map/reduce_sum | solution.py:157
  64.2 0.7 dynamic_slice.83
  64.9 0.6 dynamic_slice.82
  65.5 3.3 %fusion.6 = bf16[128,768]{1,0:T(8,128)(2,1)} fusion(bf16[1024,768]{1,0:T(8,128)(2,1)S(1)} %constant_dynamic-update-slice_fusion.6, bf16[128,768]{1,0:T(8,128)(2,1)S(1)} %bitcast.35, f32[128]{0:T(128)} %dynamic_slice.83, f32[1024]{0:T(1024)} %copy-done.9, s32[128]{0:T(128)} %copy-done.10, f32[]{:T(128)} %bitcast, s32[1024]{0:T(1024)S(1)} %bitcast.41, ...), kind=kOutput, calls=%fused_computation.21 | convolution fusion | flops 404815872 | bytes 1976452 | tf_op jit(solution)/shard_map/dot_general | solution.py:178
  68.7 3.6 %all-to-all-start.1 = ((bf16[4,32,768]{2,1,0:T(8,128)(2,1)}), bf16[4,32,768]{2,1,0:T(8,128)(2,1)S(1)}, u32[]{:S(2)}, u32[]{:S(2)}) async-start(bf16[4,32,768]{2,1,0:T(8,128)(2,1)} %bitcast.36), calls=%async_computation.1 | async-start | bytes 393216 | tf_op jit(solution)/shard_map/all_to_all | solution.py:182
  72.3 3.5 %fusion.5 = bf16[128,768]{1,0:T(8,128)(2,1)} fusion(bf16[1024,768]{1,0:T(8,128)(2,1)S(1)} %constant_dynamic-update-slice_fusion.8, bf16[128,768]{1,0:T(8,128)(2,1)} %param.10, f32[1024]{0:T(1024)} %copy-done.8, f32[128]{0:T(128)} %dynamic_slice.82, s32[128]{0:T(128)} %fusion.62, f32[]{:T(128)} %bitcast, s32[1024]{0:T(1024)S(1)} %fusion.49, ...), kind=kOutput, calls=%fused_computation.20 | convolution fusion | flops 404815872 | bytes 1976452 | tf_op jit(solution)/shard_map/dot_general | solution.py:168
  77.1 0.6 all-to-all-done.1
  77.6 1.2 %gather_fusion.1 = bf16[4,32,768]{2,1,0:T(8,128)(2,1)} fusion(bf16[4,32,768]{2,1,0:T(8,128)(2,1)S(1)} %all-to-all-done.1, s32[1024]{0:T(1024)S(1)} %pad_clamp_fusion), kind=kCustom, calls=%fused_computation.1 | custom fusion | bytes 393232 | tf_op jit(solution)/shard_map/gather | solution.py:185
  (56 shorter events, 0.4 us)
Async XLA Ops:
  0.6 4.4 %copy-start = (bf16[4,32,768]{2,1,0:T(8,128)(2,1)S(1)}, bf16[4,32,768]{2,1,0:T(8,128)(2,1)}, u32[]{:S(2)}) copy-start(bf16[4,32,768]{2,1,0:T(8,128)(2,1)} %param.11) | copy-start | bytes 589828
  0.6 15.8 %copy-start.12 = (s32[8]{0:T(128)S(1)}, s32[8]{0:T(128)}, u32[]{:S(2)}) copy-start(s32[8]{0:T(128)} %constant.227.clone) | copy-start | bytes 100
  0.7 21.1 %copy-start.2 = (s32[8]{0:T(128)S(1)}, s32[8]{0:T(128)}, u32[]{:S(2)}) copy-start(s32[8]{0:T(128)} %constant.226.clone) | copy-start | bytes 100
  0.7 14.7 %copy-start.1 = (bf16[128,768]{1,0:T(8,128)(2,1)S(1)}, bf16[128,768]{1,0:T(8,128)(2,1)}, u32[]{:S(2)}) copy-start(bf16[128,768]{1,0:T(8,128)(2,1)} %param.10) | copy-start | bytes 589828
  0.7 30.1 %collective-permute-start.7 = (bf16[128,768]{1,0:T(8,128)(2,1)}, bf16[128,768]{1,0:T(8,128)(2,1)}, u32[]{:S(2)}, u32[]{:S(2)}) collective-permute-start(bf16[128,768]{1,0:T(8,128)(2,1)} %param.10), channel_id=1, source_target_pairs={{0,2},{2,4},{4,6},{6,7},{7,5},{5,3},{3,1},{1,0},{8,9},{10,8},{12,1... | collective-permute-start | bytes 589832 | tf_op jit(solution)/shard_map/ppermute | solution.py:68
  3.8 29.1 %collective-permute-start.11 = (bf16[128,768]{1,0:T(8,128)(2,1)}, bf16[128,768]{1,0:T(8,128)(2,1)}, u32[]{:S(2)}, u32[]{:S(2)}) collective-permute-start(bf16[128,768]{1,0:T(8,128)(2,1)} %param.10), channel_id=1, source_target_pairs={{0,1},{2,0},{4,2},{6,4},{7,6},{5,7},{3,5},{1,3},{8,10},{10,12},{12... | collective-permute-start | bytes 589832 | tf_op jit(solution)/shard_map/ppermute | solution.py:68
  5.1 22.3 %copy-start.11 = (f32[4]{0:T(128)S(1)}, f32[4]{0:T(128)}, u32[]{:S(2)}) copy-start(f32[4]{0:T(128)} %param.15) | copy-start | bytes 52
  5.1 23.0 %copy-start.3 = (s32[1,1024]{1,0:T(1,128)S(1)}, s32[1,1024]{1,0:T(1,128)}, u32[]{:S(2)}) copy-start(s32[1,1024]{1,0:T(1,128)} %param.14) | copy-start | bytes 12292
  6.3 22.3 %all-to-all-start = ((bf16[4,32,768]{2,1,0:T(8,128)(2,1)}), bf16[4,32,768]{2,1,0:T(8,128)(2,1)S(1)}, u32[]{:S(2)}, u32[]{:S(2)}) async-start(bf16[4,32,768]{2,1,0:T(8,128)(2,1)} %gather_fusion), calls=%async_computation | async-start | bytes 393216 | tf_op jit(solution)/shard_map/all_to_all | solution.py:115
  9.8 20.9 %copy-start.10 = (s32[128]{0:T(128)}, s32[128]{0:T(128)S(1)}, u32[]{:S(2)}) copy-start(s32[128]{0:T(128)S(1)} %fusion.58) | copy-start | bytes 1540
  11.6 19.1 %copy-start.6 = (pred[1024]{0:T(1024)(128)(4,1)}, pred[1024]{0:T(1024)(128)(4,1)S(1)}, u32[]{:S(2)}) copy-start(pred[1024]{0:T(1024)(128)(4,1)S(1)} %iota_compare_fusion) | copy-start | bytes 3076
  28.7 7.3 %collective-permute-start = (bf16[128,768]{1,0:T(8,128)(2,1)S(1)}, bf16[128,768]{1,0:T(8,128)(2,1)S(1)}, u32[]{:S(2)}, u32[]{:S(2)}) collective-permute-start(bf16[128,768]{1,0:T(8,128)(2,1)S(1)} %bitcast.32), channel_id=1, source_target_pairs={{0,2},{2,4},{4,6},{6,7},{7,5},{5,3},{3,1},{1,0},{8,9},{10,8},{12,1... | collective-permute-start | bytes 589832 | tf_op jit(solution)/shard_map/ppermute | solution.py:68
  30.7 7.8 %collective-permute-start.4 = (bf16[128,768]{1,0:T(8,128)(2,1)S(1)}, bf16[128,768]{1,0:T(8,128)(2,1)S(1)}, u32[]{:S(2)}, u32[]{:S(2)}) collective-permute-start(bf16[128,768]{1,0:T(8,128)(2,1)S(1)} %bitcast.33), channel_id=1, source_target_pairs={{0,1},{2,0},{4,2},{6,4},{7,6},{5,7},{3,5},{1,3},{8,10},{10,12},{12... | collective-permute-start | bytes 589832 | tf_op jit(solution)/shard_map/ppermute | solution.py:68
  30.8 9.4 %collective-permute-start.8 = (bf16[128,768]{1,0:T(8,128)(2,1)}, bf16[128,768]{1,0:T(8,128)(2,1)S(1)}, u32[]{:S(2)}, u32[]{:S(2)}) collective-permute-start(bf16[128,768]{1,0:T(8,128)(2,1)} %collective-permute-done.7), channel_id=1, source_target_pairs={{0,2},{2,4},{4,6},{6,7},{7,5},{5,3},{3,1},{1,0},{8,9},{10,8},{12,1... | collective-permute-start | bytes 589832 | tf_op jit(solution)/shard_map/ppermute | solution.py:68
  32.9 9.8 %collective-permute-start.12 = (bf16[128,768]{1,0:T(8,128)(2,1)}, bf16[128,768]{1,0:T(8,128)(2,1)S(1)}, u32[]{:S(2)}, u32[]{:S(2)}) collective-permute-start(bf16[128,768]{1,0:T(8,128)(2,1)} %collective-permute-done.11), channel_id=1, source_target_pairs={{0,1},{2,0},{4,2},{6,4},{7,6},{5,7},{3,5},{1,3},{8,10},{10,12},{12... | collective-permute-start | bytes 589832 | tf_op jit(solution)/shard_map/ppermute | solution.py:68
  36.0 8.4 %collective-permute-start.1 = (bf16[128,768]{1,0:T(8,128)(2,1)S(1)}, bf16[128,768]{1,0:T(8,128)(2,1)S(1)}, u32[]{:S(2)}, u32[]{:S(2)}) collective-permute-start(bf16[128,768]{1,0:T(8,128)(2,1)S(1)} %collective-permute-done), channel_id=1, source_target_pairs={{0,2},{2,4},{4,6},{6,7},{7,5},{5,3},{3,1},{1,0},{8,9},{10,8},{12,1... | collective-permute-start | bytes 589832 | tf_op jit(solution)/shard_map/ppermute | solution.py:68
  38.5 8.4 %collective-permute-start.5 = (bf16[128,768]{1,0:T(8,128)(2,1)S(1)}, bf16[128,768]{1,0:T(8,128)(2,1)S(1)}, u32[]{:S(2)}, u32[]{:S(2)}) collective-permute-start(bf16[128,768]{1,0:T(8,128)(2,1)S(1)} %collective-permute-done.4), channel_id=1, source_target_pairs={{0,1},{2,0},{4,2},{6,4},{7,6},{5,7},{3,5},{1,3},{8,10},{10,12},{12... | collective-permute-start | bytes 589832 | tf_op jit(solution)/shard_map/ppermute | solution.py:68
  40.3 8.3 %collective-permute-start.9 = (bf16[128,768]{1,0:T(8,128)(2,1)S(1)}, bf16[128,768]{1,0:T(8,128)(2,1)S(1)}, u32[]{:S(2)}, u32[]{:S(2)}) collective-permute-start(bf16[128,768]{1,0:T(8,128)(2,1)S(1)} %collective-permute-done.8), channel_id=1, source_target_pairs={{0,2},{2,4},{4,6},{6,7},{7,5},{5,3},{3,1},{1,0},{8,9},{10,8},{12,1... | collective-permute-start | bytes 589832 | tf_op jit(solution)/shard_map/ppermute | solution.py:68
  42.7 13.7 %collective-permute-start.13 = (bf16[128,768]{1,0:T(8,128)(2,1)S(1)}, bf16[128,768]{1,0:T(8,128)(2,1)S(1)}, u32[]{:S(2)}, u32[]{:S(2)}) collective-permute-start(bf16[128,768]{1,0:T(8,128)(2,1)S(1)} %collective-permute-done.12), channel_id=1, source_target_pairs={{0,1},{2,0},{4,2},{6,4},{7,6},{5,7},{3,5},{1,3},{8,10},{10,12},{12... | collective-permute-start | bytes 589832 | tf_op jit(solution)/shard_map/ppermute | solution.py:68
  44.4 8.0 %collective-permute-start.2 = (bf16[128,768]{1,0:T(8,128)(2,1)S(1)}, bf16[128,768]{1,0:T(8,128)(2,1)S(1)}, u32[]{:S(2)}, u32[]{:S(2)}) collective-permute-start(bf16[128,768]{1,0:T(8,128)(2,1)S(1)} %collective-permute-done.1), channel_id=1, source_target_pairs={{0,2},{2,4},{4,6},{6,7},{7,5},{5,3},{3,1},{1,0},{8,9},{10,8},{12,1... | collective-permute-start | bytes 589832 | tf_op jit(solution)/shard_map/ppermute | solution.py:68
  46.9 11.3 %collective-permute-start.6 = (bf16[128,768]{1,0:T(8,128)(2,1)S(1)}, bf16[128,768]{1,0:T(8,128)(2,1)S(1)}, u32[]{:S(2)}, u32[]{:S(2)}) collective-permute-start(bf16[128,768]{1,0:T(8,128)(2,1)S(1)} %collective-permute-done.5), channel_id=1, source_target_pairs={{0,1},{2,0},{4,2},{6,4},{7,6},{5,7},{3,5},{1,3},{8,10},{10,12},{12... | collective-permute-start | bytes 589832 | tf_op jit(solution)/shard_map/ppermute | solution.py:68
  48.6 6.8 %collective-permute-start.10 = (bf16[128,768]{1,0:T(8,128)(2,1)S(1)}, bf16[128,768]{1,0:T(8,128)(2,1)S(1)}, u32[]{:S(2)}, u32[]{:S(2)}) collective-permute-start(bf16[128,768]{1,0:T(8,128)(2,1)S(1)} %collective-permute-done.9), channel_id=1, source_target_pairs={{0,2},{2,4},{4,6},{6,7},{7,5},{5,3},{3,1},{1,0},{8,9},{10,8},{12,1... | collective-permute-start | bytes 589832 | tf_op jit(solution)/shard_map/ppermute | solution.py:68
  52.4 5.7 %collective-permute-start.3 = (bf16[128,768]{1,0:T(8,128)(2,1)S(1)}, bf16[128,768]{1,0:T(8,128)(2,1)S(1)}, u32[]{:S(2)}, u32[]{:S(2)}) collective-permute-start(bf16[128,768]{1,0:T(8,128)(2,1)S(1)} %collective-permute-done.2), channel_id=1, source_target_pairs={{0,2},{2,4},{4,6},{6,7},{7,5},{5,3},{3,1},{1,0},{8,9},{10,8},{12,1... | collective-permute-start | bytes 589832 | tf_op jit(solution)/shard_map/ppermute | solution.py:68
  54.9 3.3 %copy-start.4 = (pred[1024]{0:T(1024)(128)(4,1)S(1)}, pred[1024]{0:T(1024)(128)(4,1)}, u32[]{:S(2)}) copy-start(pred[1024]{0:T(1024)(128)(4,1)} %broadcast_compare_fusion) | copy-start | bytes 3076
  54.9 3.3 %copy-start.7 = (pred[1024]{0:T(1024)(128)(4,1)S(1)}, pred[1024]{0:T(1024)(128)(4,1)}, u32[]{:S(2)}) copy-start(pred[1024]{0:T(1024)(128)(4,1)} %copy-done.6) | copy-start | bytes 3076
  64.2 1.2 %copy-start.8 = (f32[1024]{0:T(1024)}, f32[1024]{0:T(1024)S(1)}, u32[]{:S(2)}) copy-start(f32[1024]{0:T(1024)S(1)} %get-tuple-element.9) | copy-start | bytes 12292
  64.2 1.2 %copy-start.9 = (f32[1024]{0:T(1024)}, f32[1024]{0:T(1024)S(1)}, u32[]{:S(2)}) copy-start(f32[1024]{0:T(1024)S(1)} %get-tuple-element.21) | copy-start | bytes 12292
  65.5 6.9 %copy-start.5 = (pred[1024]{0:T(1024)(128)(4,1)S(1)}, pred[1024]{0:T(1024)(128)(4,1)}, u32[]{:S(2)}) copy-start(pred[1024]{0:T(1024)(128)(4,1)} %broadcast_compare_fusion) | copy-start | bytes 3076
  68.7 8.9 %all-to-all-start.1 = ((bf16[4,32,768]{2,1,0:T(8,128)(2,1)}), bf16[4,32,768]{2,1,0:T(8,128)(2,1)S(1)}, u32[]{:S(2)}, u32[]{:S(2)}) async-start(bf16[4,32,768]{2,1,0:T(8,128)(2,1)} %bitcast.36), calls=%async_computation.1 | async-start | bytes 393216 | tf_op jit(solution)/shard_map/all_to_all | solution.py:182

commit v16 on v15

--- a/solution.py
+++ b/solution.py
@@ -182,7 +182,10 @@
     returned = lax.all_to_all(
         grad_local.reshape(lang_size, per_slot, emb_width), "lang", split_axis=0, concat_axis=0, tiled=True
     )
-    grad_tgt = returned[slot_group]
+    choose = (slot_group[:, None] == jnp.arange(lang_size, dtype=jnp.int32)[None, :]).astype(returned.dtype)
+    grad_tgt = jnp.einsum(
+        "sg,grd->srd", choose, returned, preferred_element_type=jnp.float32
+    ).astype(returned.dtype)
     return (grad_src, grad_tgt, pair_loss)
 
 

time: 80.7 us -> 80.6 us (level)
    unnamed x26 -> x27, local copies, waits for them, and re-layouts: 0.07 us -> 1.35 us
    gather x1 -> x0, local copies, waits for them, and re-layouts: 1.23 us -> none  [per_device(): grad_tgt = returned[slot_group]]
  transfers between devices with their start and end apart: 16 -> 16, of which waited for: 8 -> 8; matrix products, arithmetic and copies ran while one was open for 22% -> 21% of each run, Pallas kernels for 0% -> 0%
where the time goes in v16:
time: 80.6 us; the launch traced here: 79.9 us
  starting transfers between devices  26.5 us (33%)
  between operations  13 us (16%)
  waiting for transfers between devices  11.4 us (14%)
  local copies, waits for them, and re-layouts  10.5 us (13%)
  other arithmetic  9.3 us (12%)
  matrix products  9.24 us (11%)
    ppermute x14, starting transfers between devices, ring_gather(): cur = lax.ppermute(cur, ('lang', 'dp'), pairs)  19.6 us
    ppermute x14, waiting for transfers between devices, ring_gather(): cur = lax.ppermute(cur, ('lang', 'dp'), pairs)  10.7 us
    all_to_all x1, starting transfers between devices, per_device(): lax.all_to_all(grad_local.reshape(lang_size, per_slot, emb_width), 'lang'...  3.58 us
    dot_general x1, matrix products, per_device(): jnp.dot(g_rows, y_all, preferred_element_type=jnp.float32) * inv_root  3.38 us
    all_to_all x1, starting transfers between devices, per_device(): lax.all_to_all(ordered, 'lang', split_axis=0, concat_axis=1, tiled=True)  3.37 us
    dot_general x1, matrix products, per_device(): lax.dot_general(g_cols, x_all, (((0,), (0,)), ((), ())), preferred_elemen...  3.14 us
    reduce_sum x1, other arithmetic, block_stats(): pos_score = jnp.sum(jnp.where(is_pos, scores_f, 0.0), axis=1)  2.43 us
    dot_general x1, matrix products, scores_of(): lax.dot_general(x_rows, y_rows, (((1,), (1,)), ((), ())), preferred_eleme...  2.4 us
  transfers between devices with their start and end apart: 16, of which 8 were waited for; matrix products, arithmetic and copies ran while one was open for 21% of the time, Pallas kernels for 0%

profile of v16, /device:TPU:0, one launch (start us, length us, event | category | flops | bytes accessed | tf_op | source)
XLA Modules:
  0.0 79.9 jit_solution(10609330405166338243)
XLA Ops:
  0.7 3.1 %collective-permute-start.7 = (bf16[128,768]{1,0:T(8,128)(2,1)}, bf16[128,768]{1,0:T(8,128)(2,1)}, u32[]{:S(2)}, u32[]{:S(2)}) collective-permute-start(bf16[128,768]{1,0:T(8,128)(2,1)} %param.10), channel_id=1, source_target_pairs={{0,2},{2,4},{4,6},{6,7},{7,5},{5,3},{3,1},{1,0},{8,9},{10,8},{12,1... | collective-permute-start | bytes 589832 | tf_op jit(solution)/shard_map/ppermute | solution.py:68
  3.8 0.7 compare_select_fusion.5
  4.5 0.6 scatter_custom_fusion
  5.1 1.2 %gather_fusion = bf16[4,32,768]{2,1,0:T(8,128)(2,1)} fusion(bf16[4,32,768]{2,1,0:T(8,128)(2,1)S(1)} %copy-done, s32[1024]{0:T(1024)S(1)} %pad_clamp_fusion), kind=kCustom, calls=%fused_computation | custom fusion | bytes 393232 | tf_op jit(solution)/shard_map/gather | solution.py:114
  6.3 3.4 %all-to-all-start = ((bf16[4,32,768]{2,1,0:T(8,128)(2,1)}), bf16[4,32,768]{2,1,0:T(8,128)(2,1)S(1)}, u32[]{:S(2)}, u32[]{:S(2)}) async-start(bf16[4,32,768]{2,1,0:T(8,128)(2,1)} %gather_fusion), calls=%async_computation | async-start | bytes 393216 | tf_op jit(solution)/shard_map/all_to_all | solution.py:115
  9.8 1.3 %dynamic_slice.64 = s32[1]{0:T(128)} dynamic-slice(s32[4]{0:T(128)} %param.13, s32[]{:T(128)S(6)} %select_n.263), dynamic_slice_sizes={1} | dynamic-slice | bytes 12 | tf_op jit(solution)/shard_map/dynamic_slice | solution.py:117
  11.0 0.6 iota_compare_fusion
  11.7 1.5 %convert_reduce_fusion = s32[1024]{0:T(1024)S(1)} fusion(s32[1024]{0:T(1024)} %bitcast.40, s32[1024]{0:T(1024)S(1)} %fusion.50, pred[1024]{0:T(1024)(128)(4,1)S(1)} %iota_compare_fusion), kind=kLoop, calls=%fused_computation.11 | loop fusion | flops 4193280 | bytes 13312 | tf_op jit(solution)/shard_map/reduce_max | solution.py:124
  13.2 1.0 %fusion.9 = s32[128]{0:T(128)S(1)} fusion(s32[128]{0:T(128)S(1)} %fusion.62, s32[1024]{0:T(1024)} %bitcast.41, pred[1024]{0:T(1024)(128)(4,1)S(1)} %iota_compare_fusion), kind=kLoop, calls=%fused_computation.32 | loop fusion | flops 524160 | bytes 6144 | tf_op jit(solution)/shard_map/reduce_max | solution.py:175
  14.2 0.6 broadcast_compare_fusion.1
  14.8 0.1 broadcast.263.clone.1
  15.0 1.2 %add_compare_fusion = pred[128]{0:T(512)(128)(4,1)} fusion(s32[]{:T(128)} %bitcast.1, s32[]{:T(128)S(6)} %mul.241), kind=kLoop, calls=%fused_computation.130 | loop fusion | flops 256 | bytes 136 | tf_op jit(solution)/shard_map/lt | solution.py:162
  16.2 0.6 dynamic_slice.65
  21.5 0.7 fusion.77
  27.1 0.6 dynamic_slice.63
  27.7 0.6 fusion.66
  28.3 2.0 %collective-permute-start = (bf16[128,768]{1,0:T(8,128)(2,1)S(1)}, bf16[128,768]{1,0:T(8,128)(2,1)S(1)}, u32[]{:S(2)}, u32[]{:S(2)}) collective-permute-start(bf16[128,768]{1,0:T(8,128)(2,1)S(1)} %bitcast.35), channel_id=1, source_target_pairs={{0,2},{2,4},{4,6},{6,7},{7,5},{5,3},{3,1},{1,0},{8,9},{10,8},{12,1... | collective-permute-start | bytes 589832 | tf_op jit(solution)/shard_map/ppermute | solution.py:68
  30.3 0.1 broadcast.263.clone
  30.4 2.1 %collective-permute-start.8 = (bf16[128,768]{1,0:T(8,128)(2,1)}, bf16[128,768]{1,0:T(8,128)(2,1)S(1)}, u32[]{:S(2)}, u32[]{:S(2)}) collective-permute-start(bf16[128,768]{1,0:T(8,128)(2,1)} %collective-permute-done.7), channel_id=1, source_target_pairs={{0,2},{2,4},{4,6},{6,7},{7,5},{5,3},{3,1},{1,0},{8,9},{10,8},{12,1... | collective-permute-start | bytes 589832 | tf_op jit(solution)/shard_map/ppermute | solution.py:68
  32.5 0.0 collective-permute-start.12
  32.5 1.0 %constant_dynamic-update-slice_fusion.2 = bf16[1024,768]{1,0:T(8,128)(2,1)S(1)} fusion(bf16[1024,768]{1,0:T(8,128)(2,1)S(1)} %constant_dynamic-update-slice_fusion.7, bf16[128,768]{1,0:T(8,128)(2,1)} %collective-permute-done.7, s32[]{:T(128)S(6)} %select_n.275), kind=kLoop, calls=%fused_computation.79 | loop fusion | bytes 393220 | tf_op jit(solution)/shard_map/dynamic_update_slice | solution.py:70
  33.5 2.1 %collective-permute-done = bf16[128,768]{1,0:T(8,128)(2,1)S(1)} collective-permute-done((bf16[128,768]{1,0:T(8,128)(2,1)S(1)}, bf16[128,768]{1,0:T(8,128)(2,1)S(1)}, u32[]{:S(2)}, u32[]{:S(2)}) %collective-permute-start) | collective-permute-done | bytes 196640 | tf_op jit(solution)/shard_map/ppermute | solution.py:68
  35.6 2.5 %collective-permute-start.1 = (bf16[128,768]{1,0:T(8,128)(2,1)S(1)}, bf16[128,768]{1,0:T(8,128)(2,1)S(1)}, u32[]{:S(2)}, u32[]{:S(2)}) collective-permute-start(bf16[128,768]{1,0:T(8,128)(2,1)S(1)} %collective-permute-done), channel_id=1, source_target_pairs={{0,2},{2,4},{4,6},{6,7},{7,5},{5,3},{3,1},{1,0},{8,9},{10,8},{12,1... | collective-permute-start | bytes 589832 | tf_op jit(solution)/shard_map/ppermute | solution.py:68
  38.1 1.8 %collective-permute-done.8 = bf16[128,768]{1,0:T(8,128)(2,1)S(1)} collective-permute-done((bf16[128,768]{1,0:T(8,128)(2,1)}, bf16[128,768]{1,0:T(8,128)(2,1)S(1)}, u32[]{:S(2)}, u32[]{:S(2)}) %collective-permute-start.8) | collective-permute-done | bytes 196640 | tf_op jit(solution)/shard_map/ppermute | solution.py:68
  39.9 2.4 %collective-permute-start.9 = (bf16[128,768]{1,0:T(8,128)(2,1)S(1)}, bf16[128,768]{1,0:T(8,128)(2,1)S(1)}, u32[]{:S(2)}, u32[]{:S(2)}) collective-permute-start(bf16[128,768]{1,0:T(8,128)(2,1)S(1)} %collective-permute-done.8), channel_id=1, source_target_pairs={{0,2},{2,4},{4,6},{6,7},{7,5},{5,3},{3,1},{1,0},{8,9},{10,8},{12,1... | collective-permute-start | bytes 589832 | tf_op jit(solution)/shard_map/ppermute | solution.py:68
  42.3 0.0 collective-permute-start.13
  42.3 1.7 %collective-permute-done.1 = bf16[128,768]{1,0:T(8,128)(2,1)S(1)} collective-permute-done((bf16[128,768]{1,0:T(8,128)(2,1)S(1)}, bf16[128,768]{1,0:T(8,128)(2,1)S(1)}, u32[]{:S(2)}, u32[]{:S(2)}) %collective-permute-start.1) | collective-permute-done | bytes 196640 | tf_op jit(solution)/shard_map/ppermute | solution.py:68
  44.0 2.5 %collective-permute-start.2 = (bf16[128,768]{1,0:T(8,128)(2,1)S(1)}, bf16[128,768]{1,0:T(8,128)(2,1)S(1)}, u32[]{:S(2)}, u32[]{:S(2)}) collective-permute-start(bf16[128,768]{1,0:T(8,128)(2,1)S(1)} %collective-permute-done.1), channel_id=1, source_target_pairs={{0,2},{2,4},{4,6},{6,7},{7,5},{5,3},{3,1},{1,0},{8,9},{10,8},{12,1... | collective-permute-start | bytes 589832 | tf_op jit(solution)/shard_map/ppermute | solution.py:68
  46.5 0.0 collective-permute-start.6
  46.5 1.7 %collective-permute-done.9 = bf16[128,768]{1,0:T(8,128)(2,1)S(1)} collective-permute-done((bf16[128,768]{1,0:T(8,128)(2,1)S(1)}, bf16[128,768]{1,0:T(8,128)(2,1)S(1)}, u32[]{:S(2)}, u32[]{:S(2)}) %collective-permute-start.9) | collective-permute-done | bytes 196640 | tf_op jit(solution)/shard_map/ppermute | solution.py:68
  48.2 2.5 %collective-permute-start.10 = (bf16[128,768]{1,0:T(8,128)(2,1)S(1)}, bf16[128,768]{1,0:T(8,128)(2,1)S(1)}, u32[]{:S(2)}, u32[]{:S(2)}) collective-permute-start(bf16[128,768]{1,0:T(8,128)(2,1)S(1)} %collective-permute-done.9), channel_id=1, source_target_pairs={{0,2},{2,4},{4,6},{6,7},{7,5},{5,3},{3,1},{1,0},{8,9},{10,8},{12,1... | collective-permute-start | bytes 589832 | tf_op jit(solution)/shard_map/ppermute | solution.py:68
  50.7 1.3 %collective-permute-done.2 = bf16[128,768]{1,0:T(8,128)(2,1)S(1)} collective-permute-done((bf16[128,768]{1,0:T(8,128)(2,1)S(1)}, bf16[128,768]{1,0:T(8,128)(2,1)S(1)}, u32[]{:S(2)}, u32[]{:S(2)}) %collective-permute-start.2) | collective-permute-done | bytes 196640 | tf_op jit(solution)/shard_map/ppermute | solution.py:68
  52.0 2.5 %collective-permute-start.3 = (bf16[128,768]{1,0:T(8,128)(2,1)S(1)}, bf16[128,768]{1,0:T(8,128)(2,1)S(1)}, u32[]{:S(2)}, u32[]{:S(2)}) collective-permute-start(bf16[128,768]{1,0:T(8,128)(2,1)S(1)} %collective-permute-done.2), channel_id=1, source_target_pairs={{0,2},{2,4},{4,6},{6,7},{7,5},{5,3},{3,1},{1,0},{8,9},{10,8},{12,1... | collective-permute-start | bytes 589832 | tf_op jit(solution)/shard_map/ppermute | solution.py:68
  54.5 0.5 collective-permute-done.10
  55.0 0.9 %constant_dynamic-update-slice_fusion = bf16[1024,768]{1,0:T(8,128)(2,1)S(1)} fusion(bf16[1024,768]{1,0:T(8,128)(2,1)S(1)} %constant_dynamic-update-slice_fusion.4, bf16[128,768]{1,0:T(8,128)(2,1)} %collective-permute-done.11, s32[]{:T(128)S(6)} %select_n.287), kind=kLoop, calls=%fused_computation.77 | loop fusion | bytes 393220 | tf_op jit(solution)/shard_map/dynamic_update_slice | solution.py:70
  56.0 1.7 %collective-permute-done.3 = bf16[128,768]{1,0:T(8,128)(2,1)S(1)} collective-permute-done((bf16[128,768]{1,0:T(8,128)(2,1)S(1)}, bf16[128,768]{1,0:T(8,128)(2,1)S(1)}, u32[]{:S(2)}, u32[]{:S(2)}) %collective-permute-start.3) | collective-permute-done | bytes 196640 | tf_op jit(solution)/shard_map/ppermute | solution.py:68
  57.8 2.4 %select_reduce_fusion.3 = (f32[1024]{0:T(1024)S(1)}, f32[1024]{0:T(1024)S(1)}, f32[1024,1024]{0,1:T(8,128)S(1)}) fusion(pred[1024]{0:T(1024)(128)(4,1)S(1)} %broadcast_compare_fusion, pred[1024]{0:T(1024)(128)(4,1)S(1)} %copy-done.5, s32[1024]{0:T(1024)S(1)} %bitcast.42, s32[1024]{0:T(1024)S(1)} %fusion.50, ...), kind=kOutput, calls=%fused_computation.10 | convolution fusion | flops 1618999296 | bytes 7358464 | tf_op jit(solution)/shard_map/dot_general | solution.py:75
  60.2 2.4 %fusion.1 = (f32[1024]{0:T(1024)S(1)}, f32[1024]{0:T(1024)S(1)}, f32[1024]{0:T(1024)S(1)}) fusion(f32[1024,1024]{0,1:T(8,128)S(1)} %get-tuple-element.25, s32[1024]{0:T(1024)S(1)} %bitcast.43, s32[1024]{0:T(1024)S(1)} %fusion.50, f32[1024]{0:T(1024)S(1)} %get-tuple-element.13, pred[1024]{0:T(1024)(128)(4,1)S(1)} %copy-done.5, f32[1024]{0:T(1024)S(1)} %get-tuple-element.12, ...), kind=kLoop, calls=%fused_computation.6 | loop fusion | flops 9434112 | bytes 4225024 | tf_op jit(solution)/shard_map/reduce_sum | solution.py:87
  62.7 1.2 %select_reduce_fusion.4 = (f32[]{:T(128)}, f32[1024]{0:T(1024)S(1)}, f32[]{:T(128)}, f32[1024]{0:T(1024)S(1)}) fusion(f32[1024]{0:T(1024)S(1)} %get-tuple-element.13, f32[1024]{0:T(1024)S(1)} %get-tuple-element.10, f32[1024]{0:T(1024)S(1)} %get-tuple-element.9, f32[1024]{0:T(1024)S(1)} %get-tuple-element.12, f32[1024]{0:T(1024)S(1)} %get-tuple-element.11, ...), kind=kLoop, calls=%fused_computation.105 | loop fusion | flops 16382 | bytes 32780 | tf_op jit(solution)/shard_map/reduce_sum | solution.py:157
  63.9 0.6 copy-done.6
  64.5 0.7 dynamic_slice.83
  65.1 0.6 dynamic_slice.82
  65.8 3.1 %fusion.6 = bf16[128,768]{1,0:T(8,128)(2,1)} fusion(bf16[1024,768]{1,0:T(8,128)(2,1)S(1)} %constant_dynamic-update-slice_fusion.6, bf16[128,768]{1,0:T(8,128)(2,1)S(1)} %bitcast.38, f32[128]{0:T(128)} %dynamic_slice.83, f32[1024]{0:T(1024)} %copy-done.8, s32[128]{0:T(128)} %copy-done.9, f32[]{:T(128)} %bitcast, s32[1024]{0:T(1024)S(1)} %bitcast.44, ...), kind=kOutput, calls=%fused_computation.20 | convolution fusion | flops 404815872 | bytes 1976452 | tf_op jit(solution)/shard_map/dot_general | solution.py:178
  68.9 3.6 %all-to-all-start.1 = ((bf16[4,32,768]{2,1,0:T(8,128)(2,1)}), bf16[4,32,768]{2,1,0:T(8,128)(2,1)S(1)}, u32[]{:S(2)}, u32[]{:S(2)}) async-start(bf16[4,32,768]{2,1,0:T(8,128)(2,1)} %bitcast.39), calls=%async_computation.1 | async-start | bytes 393216 | tf_op jit(solution)/shard_map/all_to_all | solution.py:182
  72.5 3.4 %fusion.5 = bf16[128,768]{1,0:T(8,128)(2,1)} fusion(bf16[1024,768]{1,0:T(8,128)(2,1)S(1)} %constant_dynamic-update-slice_fusion.8, bf16[128,768]{1,0:T(8,128)(2,1)} %param.10, f32[1024]{0:T(1024)S(1)} %copy-done.7, f32[128]{0:T(128)} %dynamic_slice.82, s32[128]{0:T(128)} %fusion.66, f32[]{:T(128)} %bitcast, s32[1024]{0:T(1024)S(1)} %fusion.50, ...), kind=kOutput, calls=%fused_computation.19 | convolution fusion | flops 404815872 | bytes 1976452 | tf_op jit(solution)/shard_map/dot_general | solution.py:168
  77.1 0.7 all-to-all-done.1
  77.8 0.3 convolution_convert_fusion
  78.1 0.7 copy.16
  (56 shorter events, 0.4 us)
Async XLA Ops:
  0.6 4.4 %copy-start = (bf16[4,32,768]{2,1,0:T(8,128)(2,1)S(1)}, bf16[4,32,768]{2,1,0:T(8,128)(2,1)}, u32[]{:S(2)}) copy-start(bf16[4,32,768]{2,1,0:T(8,128)(2,1)} %param.11) | copy-start | bytes 589828
  0.6 15.5 %copy-start.12 = (s32[8]{0:T(128)S(1)}, s32[8]{0:T(128)}, u32[]{:S(2)}) copy-start(s32[8]{0:T(128)} %constant.227.clone) | copy-start | bytes 100
  0.7 20.8 %copy-start.2 = (s32[8]{0:T(128)S(1)}, s32[8]{0:T(128)}, u32[]{:S(2)}) copy-start(s32[8]{0:T(128)} %constant.226.clone) | copy-start | bytes 100
  0.7 14.3 %copy-start.1 = (bf16[128,768]{1,0:T(8,128)(2,1)S(1)}, bf16[128,768]{1,0:T(8,128)(2,1)}, u32[]{:S(2)}) copy-start(bf16[128,768]{1,0:T(8,128)(2,1)} %param.10) | copy-start | bytes 589828
  0.7 29.8 %collective-permute-start.7 = (bf16[128,768]{1,0:T(8,128)(2,1)}, bf16[128,768]{1,0:T(8,128)(2,1)}, u32[]{:S(2)}, u32[]{:S(2)}) collective-permute-start(bf16[128,768]{1,0:T(8,128)(2,1)} %param.10), channel_id=1, source_target_pairs={{0,2},{2,4},{4,6},{6,7},{7,5},{5,3},{3,1},{1,0},{8,9},{10,8},{12,1... | collective-permute-start | bytes 589832 | tf_op jit(solution)/shard_map/ppermute | solution.py:68
  3.8 28.7 %collective-permute-start.11 = (bf16[128,768]{1,0:T(8,128)(2,1)}, bf16[128,768]{1,0:T(8,128)(2,1)}, u32[]{:S(2)}, u32[]{:S(2)}) collective-permute-start(bf16[128,768]{1,0:T(8,128)(2,1)} %param.10), channel_id=1, source_target_pairs={{0,1},{2,0},{4,2},{6,4},{7,6},{5,7},{3,5},{1,3},{8,10},{10,12},{12... | collective-permute-start | bytes 589832 | tf_op jit(solution)/shard_map/ppermute | solution.py:68
  5.1 22.0 %copy-start.10 = (f32[4]{0:T(128)S(1)}, f32[4]{0:T(128)}, u32[]{:S(2)}) copy-start(f32[4]{0:T(128)} %param.15) | copy-start | bytes 52
  5.1 22.6 %copy-start.3 = (s32[1,1024]{1,0:T(1,128)S(1)}, s32[1,1024]{1,0:T(1,128)}, u32[]{:S(2)}) copy-start(s32[1,1024]{1,0:T(1,128)} %param.14) | copy-start | bytes 12292
  6.3 21.9 %all-to-all-start = ((bf16[4,32,768]{2,1,0:T(8,128)(2,1)}), bf16[4,32,768]{2,1,0:T(8,128)(2,1)S(1)}, u32[]{:S(2)}, u32[]{:S(2)}) async-start(bf16[4,32,768]{2,1,0:T(8,128)(2,1)} %gather_fusion), calls=%async_computation | async-start | bytes 393216 | tf_op jit(solution)/shard_map/all_to_all | solution.py:115
  9.8 20.5 %copy-start.9 = (s32[128]{0:T(128)}, s32[128]{0:T(128)S(1)}, u32[]{:S(2)}) copy-start(s32[128]{0:T(128)S(1)} %fusion.62) | copy-start | bytes 1540
  11.7 18.6 %copy-start.4 = (pred[1024]{0:T(1024)(128)(4,1)}, pred[1024]{0:T(1024)(128)(4,1)S(1)}, u32[]{:S(2)}) copy-start(pred[1024]{0:T(1024)(128)(4,1)S(1)} %iota_compare_fusion) | copy-start | bytes 3076
  28.3 7.3 %collective-permute-start = (bf16[128,768]{1,0:T(8,128)(2,1)S(1)}, bf16[128,768]{1,0:T(8,128)(2,1)S(1)}, u32[]{:S(2)}, u32[]{:S(2)}) collective-permute-start(bf16[128,768]{1,0:T(8,128)(2,1)S(1)} %bitcast.35), channel_id=1, source_target_pairs={{0,2},{2,4},{4,6},{6,7},{7,5},{5,3},{3,1},{1,0},{8,9},{10,8},{12,1... | collective-permute-start | bytes 589832 | tf_op jit(solution)/shard_map/ppermute | solution.py:68
  30.3 7.8 %collective-permute-start.4 = (bf16[128,768]{1,0:T(8,128)(2,1)S(1)}, bf16[128,768]{1,0:T(8,128)(2,1)S(1)}, u32[]{:S(2)}, u32[]{:S(2)}) collective-permute-start(bf16[128,768]{1,0:T(8,128)(2,1)S(1)} %bitcast.36), channel_id=1, source_target_pairs={{0,1},{2,0},{4,2},{6,4},{7,6},{5,7},{3,5},{1,3},{8,10},{10,12},{12... | collective-permute-start | bytes 589832 | tf_op jit(solution)/shard_map/ppermute | solution.py:68
  30.4 9.4 %collective-permute-start.8 = (bf16[128,768]{1,0:T(8,128)(2,1)}, bf16[128,768]{1,0:T(8,128)(2,1)S(1)}, u32[]{:S(2)}, u32[]{:S(2)}) collective-permute-start(bf16[128,768]{1,0:T(8,128)(2,1)} %collective-permute-done.7), channel_id=1, source_target_pairs={{0,2},{2,4},{4,6},{6,7},{7,5},{5,3},{3,1},{1,0},{8,9},{10,8},{12,1... | collective-permute-start | bytes 589832 | tf_op jit(solution)/shard_map/ppermute | solution.py:68
  32.5 9.8 %collective-permute-start.12 = (bf16[128,768]{1,0:T(8,128)(2,1)}, bf16[128,768]{1,0:T(8,128)(2,1)S(1)}, u32[]{:S(2)}, u32[]{:S(2)}) collective-permute-start(bf16[128,768]{1,0:T(8,128)(2,1)} %collective-permute-done.11), channel_id=1, source_target_pairs={{0,1},{2,0},{4,2},{6,4},{7,6},{5,7},{3,5},{1,3},{8,10},{10,12},{12... | collective-permute-start | bytes 589832 | tf_op jit(solution)/shard_map/ppermute | solution.py:68
  35.6 8.4 %collective-permute-start.1 = (bf16[128,768]{1,0:T(8,128)(2,1)S(1)}, bf16[128,768]{1,0:T(8,128)(2,1)S(1)}, u32[]{:S(2)}, u32[]{:S(2)}) collective-permute-start(bf16[128,768]{1,0:T(8,128)(2,1)S(1)} %collective-permute-done), channel_id=1, source_target_pairs={{0,2},{2,4},{4,6},{6,7},{7,5},{5,3},{3,1},{1,0},{8,9},{10,8},{12,1... | collective-permute-start | bytes 589832 | tf_op jit(solution)/shard_map/ppermute | solution.py:68
  38.1 8.4 %collective-permute-start.5 = (bf16[128,768]{1,0:T(8,128)(2,1)S(1)}, bf16[128,768]{1,0:T(8,128)(2,1)S(1)}, u32[]{:S(2)}, u32[]{:S(2)}) collective-permute-start(bf16[128,768]{1,0:T(8,128)(2,1)S(1)} %collective-permute-done.4), channel_id=1, source_target_pairs={{0,1},{2,0},{4,2},{6,4},{7,6},{5,7},{3,5},{1,3},{8,10},{10,12},{12... | collective-permute-start | bytes 589832 | tf_op jit(solution)/shard_map/ppermute | solution.py:68
  39.9 8.3 %collective-permute-start.9 = (bf16[128,768]{1,0:T(8,128)(2,1)S(1)}, bf16[128,768]{1,0:T(8,128)(2,1)S(1)}, u32[]{:S(2)}, u32[]{:S(2)}) collective-permute-start(bf16[128,768]{1,0:T(8,128)(2,1)S(1)} %collective-permute-done.8), channel_id=1, source_target_pairs={{0,2},{2,4},{4,6},{6,7},{7,5},{5,3},{3,1},{1,0},{8,9},{10,8},{12,1... | collective-permute-start | bytes 589832 | tf_op jit(solution)/shard_map/ppermute | solution.py:68
  42.3 13.7 %collective-permute-start.13 = (bf16[128,768]{1,0:T(8,128)(2,1)S(1)}, bf16[128,768]{1,0:T(8,128)(2,1)S(1)}, u32[]{:S(2)}, u32[]{:S(2)}) collective-permute-start(bf16[128,768]{1,0:T(8,128)(2,1)S(1)} %collective-permute-done.12), channel_id=1, source_target_pairs={{0,1},{2,0},{4,2},{6,4},{7,6},{5,7},{3,5},{1,3},{8,10},{10,12},{12... | collective-permute-start | bytes 589832 | tf_op jit(solution)/shard_map/ppermute | solution.py:68
  44.0 8.0 %collective-permute-start.2 = (bf16[128,768]{1,0:T(8,128)(2,1)S(1)}, bf16[128,768]{1,0:T(8,128)(2,1)S(1)}, u32[]{:S(2)}, u32[]{:S(2)}) collective-permute-start(bf16[128,768]{1,0:T(8,128)(2,1)S(1)} %collective-permute-done.1), channel_id=1, source_target_pairs={{0,2},{2,4},{4,6},{6,7},{7,5},{5,3},{3,1},{1,0},{8,9},{10,8},{12,1... | collective-permute-start | bytes 589832 | tf_op jit(solution)/shard_map/ppermute | solution.py:68
  46.5 11.3 %collective-permute-start.6 = (bf16[128,768]{1,0:T(8,128)(2,1)S(1)}, bf16[128,768]{1,0:T(8,128)(2,1)S(1)}, u32[]{:S(2)}, u32[]{:S(2)}) collective-permute-start(bf16[128,768]{1,0:T(8,128)(2,1)S(1)} %collective-permute-done.5), channel_id=1, source_target_pairs={{0,1},{2,0},{4,2},{6,4},{7,6},{5,7},{3,5},{1,3},{8,10},{10,12},{12... | collective-permute-start | bytes 589832 | tf_op jit(solution)/shard_map/ppermute | solution.py:68
  48.2 6.8 %collective-permute-start.10 = (bf16[128,768]{1,0:T(8,128)(2,1)S(1)}, bf16[128,768]{1,0:T(8,128)(2,1)S(1)}, u32[]{:S(2)}, u32[]{:S(2)}) collective-permute-start(bf16[128,768]{1,0:T(8,128)(2,1)S(1)} %collective-permute-done.9), channel_id=1, source_target_pairs={{0,2},{2,4},{4,6},{6,7},{7,5},{5,3},{3,1},{1,0},{8,9},{10,8},{12,1... | collective-permute-start | bytes 589832 | tf_op jit(solution)/shard_map/ppermute | solution.py:68
  52.0 5.7 %collective-permute-start.3 = (bf16[128,768]{1,0:T(8,128)(2,1)S(1)}, bf16[128,768]{1,0:T(8,128)(2,1)S(1)}, u32[]{:S(2)}, u32[]{:S(2)}) collective-permute-start(bf16[128,768]{1,0:T(8,128)(2,1)S(1)} %collective-permute-done.2), channel_id=1, source_target_pairs={{0,2},{2,4},{4,6},{6,7},{7,5},{5,3},{3,1},{1,0},{8,9},{10,8},{12,1... | collective-permute-start | bytes 589832 | tf_op jit(solution)/shard_map/ppermute | solution.py:68
  54.5 3.3 %copy-start.5 = (pred[1024]{0:T(1024)(128)(4,1)S(1)}, pred[1024]{0:T(1024)(128)(4,1)}, u32[]{:S(2)}) copy-start(pred[1024]{0:T(1024)(128)(4,1)} %copy-done.4) | copy-start | bytes 3076
  63.9 0.6 copy-start.6
  63.9 1.9 %copy-start.8 = (f32[1024]{0:T(1024)}, f32[1024]{0:T(1024)S(1)}, u32[]{:S(2)}) copy-start(f32[1024]{0:T(1024)S(1)} %get-tuple-element.27) | copy-start | bytes 12292
  65.8 6.7 %copy-start.7 = (f32[1024]{0:T(1024)S(1)}, f32[1024]{0:T(1024)}, u32[]{:S(2)}) copy-start(f32[1024]{0:T(1024)} %copy-done.6) | copy-start | bytes 12292
  68.9 8.9 %all-to-all-start.1 = ((bf16[4,32,768]{2,1,0:T(8,128)(2,1)}), bf16[4,32,768]{2,1,0:T(8,128)(2,1)S(1)}, u32[]{:S(2)}, u32[]{:S(2)}) async-start(bf16[4,32,768]{2,1,0:T(8,128)(2,1)} %bitcast.39), calls=%async_computation.1 | async-start | bytes 393216 | tf_op jit(solution)/shard_map/all_to_all | solution.py:182
  72.5 5.3 %copy-start.11 = (s32[4]{0:T(128)S(1)}, s32[4]{0:T(128)}, u32[]{:S(2)}) copy-start(s32[4]{0:T(128)} %param.12) | copy-start | bytes 52

commit v17 on v16

--- a/solution.py
+++ b/solution.py
@@ -162,7 +162,10 @@
     r_my = (mine + jnp.arange(row_count, dtype=jnp.int32)) < live_count
     lse_my = lax.dynamic_slice_in_dim(row_lse, mine, row_count)
     pos_rows = perm[None, :] == a_my[:, None]
-    s_rows = scores_of(src_emb, y_all, pos_rows, inv_root)
+    if steps == 1:
+        s_rows = lax.dynamic_slice_in_dim(scores_f, mine, row_count, 0)
+    else:
+        s_rows = scores_of(src_emb, y_all, pos_rows, inv_root)
     g_rows = grad_of(s_rows, pos_rows, r_my, col_live, lse_my, col_lse, weight)
     grad_src = (
         jnp.dot(g_rows, y_all, preferred_element_type=jnp.float32) * inv_root
@@ -173,7 +176,10 @@
     clse_my = lax.dynamic_slice_in_dim(col_lse, mine, row_count)
     pos_cols = p_my[None, :] == pair_align[:, None]
     c_my = jnp.max((pos_cols & row_live[:, None]).astype(jnp.int32), axis=0) > 0
-    s_cols = scores_of(x_all, partner, pos_cols, inv_root)
+    if steps == 1:
+        s_cols = lax.dynamic_slice_in_dim(scores_f, mine, row_count, 1)
+    else:
+        s_cols = scores_of(x_all, partner, pos_cols, inv_root)
     g_cols = grad_of(s_cols, pos_cols, row_live, c_my, row_lse, clse_my, weight)
     own_terms = lax.dot_general(
         g_cols, x_all, (((0,), (0,)), ((), ())), preferred_element_type=jnp.float32

time: 80.6 us -> 78 us (0.968)
  waiting for transfers between devices: 11.4 us -> 14.3 us
  starting transfers between devices: 26.5 us -> 23.8 us
  local copies, waits for them, and re-layouts: 10.5 us -> 8.91 us
  matrix products: 9.24 us -> 8.17 us
    ppermute x14, waiting for transfers between devices: 10.7 us -> 13.8 us  [ring_gather(): cur = lax.ppermute(cur, ('lang', 'dp'), pairs)]
    ppermute x14, starting transfers between devices: 19.6 us -> 17.1 us  [ring_gather(): cur = lax.ppermute(cur, ('lang', 'dp'), pairs)]
    dot_general x1, matrix products: 3.14 us -> 2.04 us  [per_device(): lax.dot_general(g_cols, x_all, (((0,), (0,)), ((), ())), preferred_elemen...]
  transfers between devices with their start and end apart: 16 -> 16, of which waited for: 8 -> 8; matrix products, arithmetic and copies ran while one was open for 21% -> 22% of each run, Pallas kernels for 0% -> 0%
where the time goes in v17:
time: 78 us; the launch traced here: 77.3 us
  starting transfers between devices  23.8 us (31%)
  waiting for transfers between devices  14.3 us (18%)
  between operations  13.2 us (17%)
  other arithmetic  8.99 us (12%)
  local copies, waits for them, and re-layouts  8.91 us (11%)
  matrix products  8.17 us (10%)
    ppermute x14, starting transfers between devices, ring_gather(): cur = lax.ppermute(cur, ('lang', 'dp'), pairs)  17.1 us
    ppermute x14, waiting for transfers between devices, ring_gather(): cur = lax.ppermute(cur, ('lang', 'dp'), pairs)  13.8 us
    dot_general x1, matrix products, per_device(): jnp.dot(g_rows, y_all, preferred_element_type=jnp.float32) * inv_root  3.41 us
    all_to_all x1, starting transfers between devices, per_device(): lax.all_to_all(ordered, 'lang', split_axis=0, concat_axis=1, tiled=True)  3.37 us
    all_to_all x1, starting transfers between devices, per_device(): lax.all_to_all(grad_local.reshape(lang_size, per_slot, emb_width), 'lang'...  3.37 us
    reduce_sum x1, other arithmetic, block_stats(): pos_score = jnp.sum(jnp.where(is_pos, scores_f, 0.0), axis=1)  2.43 us
    dot_general x1, matrix products, scores_of(): lax.dot_general(x_rows, y_rows, (((1,), (1,)), ((), ())), preferred_eleme...  2.4 us
    dynamic_update_slice x14, local copies, waits for them, and re-layouts, ring_gather(): out = lax.dynamic_update_slice_in_dim(out, cur, origin * rows, 0)  2.15 us
  transfers between devices with their start and end apart: 16, of which 8 were waited for; matrix products, arithmetic and copies ran while one was open for 22% of the time, Pallas kernels for 0%

profile of v17, /device:TPU:0, one launch (start us, length us, event | category | flops | bytes accessed | tf_op | source)
XLA Modules:
  0.0 77.3 jit_solution(13396814966231801332)
XLA Ops:
  0.7 3.0 %collective-permute-start.4 = (bf16[128,768]{1,0:T(8,128)(2,1)}, bf16[128,768]{1,0:T(8,128)(2,1)}, u32[]{:S(2)}, u32[]{:S(2)}) collective-permute-start(bf16[128,768]{1,0:T(8,128)(2,1)} %param.10), channel_id=1, source_target_pairs={{0,1},{2,0},{4,2},{6,4},{7,6},{5,7},{3,5},{1,3},{8,10},{10,12},{12... | collective-permute-start | bytes 589832 | tf_op jit(solution)/shard_map/ppermute | solution.py:68
  3.7 0.1 collective-permute-start
  3.9 0.7 compare_select_fusion.3
  4.5 0.6 scatter_custom_fusion
  5.2 1.2 %gather_fusion = bf16[4,32,768]{2,1,0:T(8,128)(2,1)} fusion(bf16[4,32,768]{2,1,0:T(8,128)(2,1)S(1)} %copy-done, s32[1024]{0:T(1024)S(1)} %pad_clamp_fusion), kind=kCustom, calls=%fused_computation | custom fusion | bytes 393232 | tf_op jit(solution)/shard_map/gather | solution.py:114
  6.4 3.4 %all-to-all-start = ((bf16[4,32,768]{2,1,0:T(8,128)(2,1)}), bf16[4,32,768]{2,1,0:T(8,128)(2,1)S(1)}, u32[]{:S(2)}, u32[]{:S(2)}) async-start(bf16[4,32,768]{2,1,0:T(8,128)(2,1)} %gather_fusion), calls=%async_computation | async-start | bytes 393216 | tf_op jit(solution)/shard_map/all_to_all | solution.py:115
  9.8 1.2 %dynamic_slice.70 = s32[1]{0:T(128)} dynamic-slice(s32[4]{0:T(128)} %param.13, s32[]{:T(128)S(6)} %select_n.265), dynamic_slice_sizes={1} | dynamic-slice | bytes 12 | tf_op jit(solution)/shard_map/dynamic_slice | solution.py:117
  11.1 0.6 iota_compare_fusion
  11.7 0.9 %convert_reduce_fusion.1 = s32[128]{0:T(128)S(1)} fusion(s32[1024]{0:T(1024)} %bitcast.27, s32[128]{0:T(128)S(1)} %fusion.56, pred[1024]{0:T(1024)(128)(4,1)S(1)} %iota_compare_fusion), kind=kLoop, calls=%fused_computation.29 | loop fusion | flops 524160 | bytes 6144 | tf_op jit(solution)/shard_map/reduce_max | solution.py:178
  12.6 0.6 broadcast_compare_fusion.1
  13.2 1.5 %convert_reduce_fusion = s32[1024]{0:T(1024)S(1)} fusion(s32[1024]{0:T(1024)} %bitcast.28, s32[1024]{0:T(1024)S(1)} %fusion.44, pred[1024]{0:T(1024)(128)(4,1)S(1)} %iota_compare_fusion), kind=kLoop, calls=%fused_computation.11 | loop fusion | flops 4193280 | bytes 13312 | tf_op jit(solution)/shard_map/reduce_max | solution.py:124
  14.7 0.1 broadcast.255.clone.1
  14.9 1.1 %add_compare_fusion = pred[128]{0:T(512)(128)(4,1)} fusion(s32[]{:T(128)} %bitcast.1, s32[]{:T(128)S(6)} %mul.216), kind=kLoop, calls=%fused_computation.118 | loop fusion | flops 256 | bytes 136 | tf_op jit(solution)/shard_map/lt | solution.py:162
  16.5 0.6 dynamic_slice.71
  21.8 0.7 fusion.67
  26.9 0.7 dynamic_slice.69
  27.6 0.6 fusion.60
  28.1 1.9 %collective-permute-start.11 = (bf16[128,768]{1,0:T(8,128)(2,1)S(1)}, bf16[128,768]{1,0:T(8,128)(2,1)S(1)}, u32[]{:S(2)}, u32[]{:S(2)}) collective-permute-start(bf16[128,768]{1,0:T(8,128)(2,1)S(1)} %bitcast.24), channel_id=1, source_target_pairs={{0,1},{2,0},{4,2},{6,4},{7,6},{5,7},{3,5},{1,3},{8,10},{10,12},{12... | collective-permute-start | bytes 589832 | tf_op jit(solution)/shard_map/ppermute | solution.py:68
  30.0 0.1 collective-permute-start.7
  30.2 0.1 broadcast.255.clone
  30.3 2.0 %collective-permute-start.5 = (bf16[128,768]{1,0:T(8,128)(2,1)}, bf16[128,768]{1,0:T(8,128)(2,1)S(1)}, u32[]{:S(2)}, u32[]{:S(2)}) collective-permute-start(bf16[128,768]{1,0:T(8,128)(2,1)} %collective-permute-done.4), channel_id=1, source_target_pairs={{0,1},{2,0},{4,2},{6,4},{7,6},{5,7},{3,5},{1,3},{8,10},{10,12},{12... | collective-permute-start | bytes 589832 | tf_op jit(solution)/shard_map/ppermute | solution.py:68
  32.3 0.1 collective-permute-start.1
  32.4 1.0 %constant_dynamic-update-slice_fusion.14 = bf16[1024,768]{1,0:T(8,128)(2,1)S(1)} fusion(bf16[1024,768]{1,0:T(8,128)(2,1)S(1)} %constant_dynamic-update-slice_fusion.15, bf16[128,768]{1,0:T(8,128)(2,1)} %collective-permute-done, s32[]{:T(128)S(6)} %select_n.275), kind=kLoop, calls=%fused_computation.80 | loop fusion | bytes 393220 | tf_op jit(solution)/shard_map/dynamic_update_slice | solution.py:70
  33.4 2.0 %collective-permute-done.11 = bf16[128,768]{1,0:T(8,128)(2,1)S(1)} collective-permute-done((bf16[128,768]{1,0:T(8,128)(2,1)S(1)}, bf16[128,768]{1,0:T(8,128)(2,1)S(1)}, u32[]{:S(2)}, u32[]{:S(2)}) %collective-permute-start.11) | collective-permute-done | bytes 196640 | tf_op jit(solution)/shard_map/ppermute | solution.py:68
  35.3 2.5 %collective-permute-start.12 = (bf16[128,768]{1,0:T(8,128)(2,1)S(1)}, bf16[128,768]{1,0:T(8,128)(2,1)S(1)}, u32[]{:S(2)}, u32[]{:S(2)}) collective-permute-start(bf16[128,768]{1,0:T(8,128)(2,1)S(1)} %collective-permute-done.11), channel_id=1, source_target_pairs={{0,1},{2,0},{4,2},{6,4},{7,6},{5,7},{3,5},{1,3},{8,10},{10,12},{12... | collective-permute-start | bytes 589832 | tf_op jit(solution)/shard_map/ppermute | solution.py:68
  37.8 0.1 collective-permute-start.8
  38.0 1.7 %collective-permute-done.5 = bf16[128,768]{1,0:T(8,128)(2,1)S(1)} collective-permute-done((bf16[128,768]{1,0:T(8,128)(2,1)}, bf16[128,768]{1,0:T(8,128)(2,1)S(1)}, u32[]{:S(2)}, u32[]{:S(2)}) %collective-permute-start.5) | collective-permute-done | bytes 196640 | tf_op jit(solution)/shard_map/ppermute | solution.py:68
  39.7 2.4 %collective-permute-start.6 = (bf16[128,768]{1,0:T(8,128)(2,1)S(1)}, bf16[128,768]{1,0:T(8,128)(2,1)S(1)}, u32[]{:S(2)}, u32[]{:S(2)}) collective-permute-start(bf16[128,768]{1,0:T(8,128)(2,1)S(1)} %collective-permute-done.5), channel_id=1, source_target_pairs={{0,1},{2,0},{4,2},{6,4},{7,6},{5,7},{3,5},{1,3},{8,10},{10,12},{12... | collective-permute-start | bytes 589832 | tf_op jit(solution)/shard_map/ppermute | solution.py:68
  42.0 0.1 collective-permute-start.2
  42.2 1.6 %collective-permute-done.12 = bf16[128,768]{1,0:T(8,128)(2,1)S(1)} collective-permute-done((bf16[128,768]{1,0:T(8,128)(2,1)S(1)}, bf16[128,768]{1,0:T(8,128)(2,1)S(1)}, u32[]{:S(2)}, u32[]{:S(2)}) %collective-permute-start.12) | collective-permute-done | bytes 196640 | tf_op jit(solution)/shard_map/ppermute | solution.py:68
  43.8 2.5 %collective-permute-start.13 = (bf16[128,768]{1,0:T(8,128)(2,1)S(1)}, bf16[128,768]{1,0:T(8,128)(2,1)S(1)}, u32[]{:S(2)}, u32[]{:S(2)}) collective-permute-start(bf16[128,768]{1,0:T(8,128)(2,1)S(1)} %collective-permute-done.12), channel_id=1, source_target_pairs={{0,1},{2,0},{4,2},{6,4},{7,6},{5,7},{3,5},{1,3},{8,10},{10,12},{12... | collective-permute-start | bytes 589832 | tf_op jit(solution)/shard_map/ppermute | solution.py:68
  46.2 0.1 collective-permute-start.9
  46.4 3.9 %collective-permute-done.2 = bf16[128,768]{1,0:T(8,128)(2,1)S(1)} collective-permute-done((bf16[128,768]{1,0:T(8,128)(2,1)S(1)}, bf16[128,768]{1,0:T(8,128)(2,1)S(1)}, u32[]{:S(2)}, u32[]{:S(2)}) %collective-permute-start.2) | collective-permute-done | bytes 196640 | tf_op jit(solution)/shard_map/ppermute | solution.py:68
  50.3 0.3 collective-permute-start.3
  50.6 1.8 %collective-permute-done.9 = bf16[128,768]{1,0:T(8,128)(2,1)S(1)} collective-permute-done((bf16[128,768]{1,0:T(8,128)(2,1)S(1)}, bf16[128,768]{1,0:T(8,128)(2,1)S(1)}, u32[]{:S(2)}, u32[]{:S(2)}) %collective-permute-start.9) | collective-permute-done | bytes 196640 | tf_op jit(solution)/shard_map/ppermute | solution.py:68
  52.4 1.8 %collective-permute-start.10 = (bf16[128,768]{1,0:T(8,128)(2,1)S(1)}, bf16[128,768]{1,0:T(8,128)(2,1)S(1)}, u32[]{:S(2)}, u32[]{:S(2)}) collective-permute-start(bf16[128,768]{1,0:T(8,128)(2,1)S(1)} %collective-permute-done.9), channel_id=1, source_target_pairs={{0,2},{2,4},{4,6},{6,7},{7,5},{5,3},{3,1},{1,0},{8,9},{10,8},{12,1... | collective-permute-start | bytes 589832 | tf_op jit(solution)/shard_map/ppermute | solution.py:68
  54.3 1.7 %collective-permute-done.3 = bf16[128,768]{1,0:T(8,128)(2,1)S(1)} collective-permute-done((bf16[128,768]{1,0:T(8,128)(2,1)S(1)}, bf16[128,768]{1,0:T(8,128)(2,1)S(1)}, u32[]{:S(2)}, u32[]{:S(2)}) %collective-permute-start.3) | collective-permute-done | bytes 196640 | tf_op jit(solution)/shard_map/ppermute | solution.py:68
  56.0 0.9 %constant_dynamic-update-slice_fusion.10 = bf16[1024,768]{1,0:T(8,128)(2,1)S(1)} fusion(bf16[1024,768]{1,0:T(8,128)(2,1)S(1)} %constant_dynamic-update-slice_fusion.11, bf16[128,768]{1,0:T(8,128)(2,1)} %collective-permute-done.4, s32[]{:T(128)S(6)} %select_n.287), kind=kLoop, calls=%fused_computation.76 | loop fusion | bytes 393220 | tf_op jit(solution)/shard_map/dynamic_update_slice | solution.py:70
  57.0 1.1 %collective-permute-done.10 = bf16[128,768]{1,0:T(8,128)(2,1)S(1)} collective-permute-done((bf16[128,768]{1,0:T(8,128)(2,1)S(1)}, bf16[128,768]{1,0:T(8,128)(2,1)S(1)}, u32[]{:S(2)}, u32[]{:S(2)}) %collective-permute-start.10) | collective-permute-done | bytes 196640 | tf_op jit(solution)/shard_map/ppermute | solution.py:68
  58.2 2.4 %select_reduce_fusion.3 = (f32[1024]{0:T(1024)S(1)}, f32[1024]{0:T(1024)S(1)}, f32[1024,1024]{0,1:T(8,128)S(1)}) fusion(pred[1024]{0:T(1024)(128)(4,1)S(1)} %broadcast_compare_fusion, pred[1024]{0:T(1024)(128)(4,1)S(1)} %copy-done.6, s32[1024]{0:T(1024)S(1)} %bitcast.29, s32[1024]{0:T(1024)S(1)} %fusion.44, ...), kind=kOutput, calls=%fused_computation.10 | convolution fusion | flops 1618999296 | bytes 7358464 | tf_op jit(solution)/shard_map/dot_general | solution.py:75
  60.6 2.4 %fusion.1 = (f32[1024]{0:T(1024)S(1)}, f32[1024]{0:T(1024)S(1)}, f32[1024]{0:T(1024)S(1)}) fusion(f32[1024,1024]{0,1:T(8,128)S(1)} %get-tuple-element.25, s32[1024]{0:T(1024)S(1)} %bitcast.30, s32[1024]{0:T(1024)S(1)} %fusion.44, f32[1024]{0:T(1024)S(1)} %get-tuple-element.13, pred[1024]{0:T(1024)(128)(4,1)S(1)} %copy-done.6, f32[1024]{0:T(1024)S(1)} %get-tuple-element.12, ...), kind=kLoop, calls=%fused_computation.6 | loop fusion | flops 9434112 | bytes 4225024 | tf_op jit(solution)/shard_map/reduce_sum | solution.py:87
  63.1 1.2 %select_reduce_fusion.4 = (f32[]{:T(128)}, f32[1024]{0:T(1024)S(1)}, f32[]{:T(128)}, f32[1024]{0:T(1024)S(1)}) fusion(f32[1024]{0:T(1024)S(1)} %get-tuple-element.13, f32[1024]{0:T(1024)S(1)} %get-tuple-element.10, f32[1024]{0:T(1024)S(1)} %get-tuple-element.9, f32[1024]{0:T(1024)S(1)} %get-tuple-element.12, f32[1024]{0:T(1024)S(1)} %get-tuple-element.11, ...), kind=kLoop, calls=%fused_computation.93 | loop fusion | flops 16382 | bytes 32780 | tf_op jit(solution)/shard_map/reduce_sum | solution.py:157
  64.5 2.0 %fusion.3 = bf16[128,768]{1,0:T(8,128)(2,1)} fusion(bf16[1024,768]{1,0:T(8,128)(2,1)S(1)} %constant_dynamic-update-slice_fusion.8, f32[1024,1024]{0,1:T(8,128)S(1)} %get-tuple-element.25, s32[]{:T(128)S(6)} %select_n.270, f32[128]{0:T(128)S(1)} %dynamic_slice.91, f32[1024]{0:T(1024)S(1)} %get-tuple-element.27, s32[1024]{0:T(1024)S(1)} %bitcast.31, ...), kind=kOutput, calls=%fused_computation.15 | convolution fusion | flops 203096064 | bytes 2304520 | tf_op jit(solution)/shard_map/dot_general | solution.py:184
  66.5 3.4 %all-to-all-start.1 = ((bf16[4,32,768]{2,1,0:T(8,128)(2,1)}), bf16[4,32,768]{2,1,0:T(8,128)(2,1)S(1)}, u32[]{:S(2)}, u32[]{:S(2)}) async-start(bf16[4,32,768]{2,1,0:T(8,128)(2,1)} %bitcast.14), calls=%async_computation.1 | async-start | bytes 393216 | tf_op jit(solution)/shard_map/all_to_all | solution.py:188
  71.2 3.4 %fusion.2 = bf16[128,768]{1,0:T(8,128)(2,1)} fusion(bf16[1024,768]{1,0:T(8,128)(2,1)S(1)} %constant_dynamic-update-slice_fusion.6, f32[1024,1024]{0,1:T(8,128)} %copy-done.1, s32[]{:T(128)S(6)} %select_n.270, s32[128]{0:T(128)S(1)} %copy-done.12, f32[1024]{0:T(1024)S(1)} %get-tuple-element.15, f32[128]{0:T(128)S(1)} %dynamic_slice.88, f32[]{:T(128)} %bitcast, ...), kind=kOutput, calls=%fused_computation.14 | convolution fusion | flops 203096064 | bytes 2304644 | tf_op jit(solution)/shard_map/dot_general | solution.py:171
  74.6 0.5 all-to-all-done.1
  75.1 0.3 convolution_convert_fusion
  75.5 0.7 copy.16
  (60 shorter events, 0.6 us)
Async XLA Ops:
  0.6 4.5 %copy-start = (bf16[4,32,768]{2,1,0:T(8,128)(2,1)S(1)}, bf16[4,32,768]{2,1,0:T(8,128)(2,1)}, u32[]{:S(2)}) copy-start(bf16[4,32,768]{2,1,0:T(8,128)(2,1)} %param.11) | copy-start | bytes 589828
  0.6 15.9 %copy-start.13 = (s32[8]{0:T(128)S(1)}, s32[8]{0:T(128)}, u32[]{:S(2)}) copy-start(s32[8]{0:T(128)} %constant.221.clone) | copy-start | bytes 100
  0.7 21.1 %copy-start.3 = (s32[8]{0:T(128)S(1)}, s32[8]{0:T(128)}, u32[]{:S(2)}) copy-start(s32[8]{0:T(128)} %constant.220.clone) | copy-start | bytes 100
  0.7 14.2 %copy-start.2 = (bf16[128,768]{1,0:T(8,128)(2,1)S(1)}, bf16[128,768]{1,0:T(8,128)(2,1)}, u32[]{:S(2)}) copy-start(bf16[128,768]{1,0:T(8,128)(2,1)} %param.10) | copy-start | bytes 589828
  0.7 29.6 %collective-permute-start.4 = (bf16[128,768]{1,0:T(8,128)(2,1)}, bf16[128,768]{1,0:T(8,128)(2,1)}, u32[]{:S(2)}, u32[]{:S(2)}) collective-permute-start(bf16[128,768]{1,0:T(8,128)(2,1)} %param.10), channel_id=1, source_target_pairs={{0,1},{2,0},{4,2},{6,4},{7,6},{5,7},{3,5},{1,3},{8,10},{10,12},{12... | collective-permute-start | bytes 589832 | tf_op jit(solution)/shard_map/ppermute | solution.py:68
  3.7 28.5 %collective-permute-start = (bf16[128,768]{1,0:T(8,128)(2,1)}, bf16[128,768]{1,0:T(8,128)(2,1)}, u32[]{:S(2)}, u32[]{:S(2)}) collective-permute-start(bf16[128,768]{1,0:T(8,128)(2,1)} %param.10), channel_id=1, source_target_pairs={{0,2},{2,4},{4,6},{6,7},{7,5},{5,3},{3,1},{1,0},{8,9},{10,8},{12,1... | collective-permute-start | bytes 589832 | tf_op jit(solution)/shard_map/ppermute | solution.py:68
  5.1 21.7 %copy-start.9 = (f32[4]{0:T(128)S(1)}, f32[4]{0:T(128)}, u32[]{:S(2)}) copy-start(f32[4]{0:T(128)} %param.15) | copy-start | bytes 52
  5.2 22.4 %copy-start.4 = (s32[1,1024]{1,0:T(1,128)S(1)}, s32[1,1024]{1,0:T(1,128)}, u32[]{:S(2)}) copy-start(s32[1,1024]{1,0:T(1,128)} %param.14) | copy-start | bytes 12292
  6.4 21.7 %all-to-all-start = ((bf16[4,32,768]{2,1,0:T(8,128)(2,1)}), bf16[4,32,768]{2,1,0:T(8,128)(2,1)S(1)}, u32[]{:S(2)}, u32[]{:S(2)}) async-start(bf16[4,32,768]{2,1,0:T(8,128)(2,1)} %gather_fusion), calls=%async_computation | async-start | bytes 393216 | tf_op jit(solution)/shard_map/all_to_all | solution.py:115
  9.8 20.2 %copy-start.7 = (s32[128]{0:T(128)}, s32[128]{0:T(128)S(1)}, u32[]{:S(2)}) copy-start(s32[128]{0:T(128)S(1)} %fusion.56) | copy-start | bytes 1540
  11.7 18.4 %copy-start.5 = (pred[1024]{0:T(1024)(128)(4,1)}, pred[1024]{0:T(1024)(128)(4,1)S(1)}, u32[]{:S(2)}) copy-start(pred[1024]{0:T(1024)(128)(4,1)S(1)} %iota_compare_fusion) | copy-start | bytes 3076
  28.1 7.2 %collective-permute-start.11 = (bf16[128,768]{1,0:T(8,128)(2,1)S(1)}, bf16[128,768]{1,0:T(8,128)(2,1)S(1)}, u32[]{:S(2)}, u32[]{:S(2)}) collective-permute-start(bf16[128,768]{1,0:T(8,128)(2,1)S(1)} %bitcast.24), channel_id=1, source_target_pairs={{0,1},{2,0},{4,2},{6,4},{7,6},{5,7},{3,5},{1,3},{8,10},{10,12},{12... | collective-permute-start | bytes 589832 | tf_op jit(solution)/shard_map/ppermute | solution.py:68
  30.0 7.8 %collective-permute-start.7 = (bf16[128,768]{1,0:T(8,128)(2,1)S(1)}, bf16[128,768]{1,0:T(8,128)(2,1)S(1)}, u32[]{:S(2)}, u32[]{:S(2)}) collective-permute-start(bf16[128,768]{1,0:T(8,128)(2,1)S(1)} %bitcast.25), channel_id=1, source_target_pairs={{0,2},{2,4},{4,6},{6,7},{7,5},{5,3},{3,1},{1,0},{8,9},{10,8},{12,1... | collective-permute-start | bytes 589832 | tf_op jit(solution)/shard_map/ppermute | solution.py:68
  30.3 9.3 %collective-permute-start.5 = (bf16[128,768]{1,0:T(8,128)(2,1)}, bf16[128,768]{1,0:T(8,128)(2,1)S(1)}, u32[]{:S(2)}, u32[]{:S(2)}) collective-permute-start(bf16[128,768]{1,0:T(8,128)(2,1)} %collective-permute-done.4), channel_id=1, source_target_pairs={{0,1},{2,0},{4,2},{6,4},{7,6},{5,7},{3,5},{1,3},{8,10},{10,12},{12... | collective-permute-start | bytes 589832 | tf_op jit(solution)/shard_map/ppermute | solution.py:68
  32.3 9.8 %collective-permute-start.1 = (bf16[128,768]{1,0:T(8,128)(2,1)}, bf16[128,768]{1,0:T(8,128)(2,1)S(1)}, u32[]{:S(2)}, u32[]{:S(2)}) collective-permute-start(bf16[128,768]{1,0:T(8,128)(2,1)} %collective-permute-done), channel_id=1, source_target_pairs={{0,2},{2,4},{4,6},{6,7},{7,5},{5,3},{3,1},{1,0},{8,9},{10,8},{12,1... | collective-permute-start | bytes 589832 | tf_op jit(solution)/shard_map/ppermute | solution.py:68
  35.3 8.4 %collective-permute-start.12 = (bf16[128,768]{1,0:T(8,128)(2,1)S(1)}, bf16[128,768]{1,0:T(8,128)(2,1)S(1)}, u32[]{:S(2)}, u32[]{:S(2)}) collective-permute-start(bf16[128,768]{1,0:T(8,128)(2,1)S(1)} %collective-permute-done.11), channel_id=1, source_target_pairs={{0,1},{2,0},{4,2},{6,4},{7,6},{5,7},{3,5},{1,3},{8,10},{10,12},{12... | collective-permute-start | bytes 589832 | tf_op jit(solution)/shard_map/ppermute | solution.py:68
  37.8 8.4 %collective-permute-start.8 = (bf16[128,768]{1,0:T(8,128)(2,1)S(1)}, bf16[128,768]{1,0:T(8,128)(2,1)S(1)}, u32[]{:S(2)}, u32[]{:S(2)}) collective-permute-start(bf16[128,768]{1,0:T(8,128)(2,1)S(1)} %collective-permute-done.7), channel_id=1, source_target_pairs={{0,2},{2,4},{4,6},{6,7},{7,5},{5,3},{3,1},{1,0},{8,9},{10,8},{12,1... | collective-permute-start | bytes 589832 | tf_op jit(solution)/shard_map/ppermute | solution.py:68
  39.7 17.3 %collective-permute-start.6 = (bf16[128,768]{1,0:T(8,128)(2,1)S(1)}, bf16[128,768]{1,0:T(8,128)(2,1)S(1)}, u32[]{:S(2)}, u32[]{:S(2)}) collective-permute-start(bf16[128,768]{1,0:T(8,128)(2,1)S(1)} %collective-permute-done.5), channel_id=1, source_target_pairs={{0,1},{2,0},{4,2},{6,4},{7,6},{5,7},{3,5},{1,3},{8,10},{10,12},{12... | collective-permute-start | bytes 589832 | tf_op jit(solution)/shard_map/ppermute | solution.py:68
  42.0 8.3 %collective-permute-start.2 = (bf16[128,768]{1,0:T(8,128)(2,1)S(1)}, bf16[128,768]{1,0:T(8,128)(2,1)S(1)}, u32[]{:S(2)}, u32[]{:S(2)}) collective-permute-start(bf16[128,768]{1,0:T(8,128)(2,1)S(1)} %collective-permute-done.1), channel_id=1, source_target_pairs={{0,2},{2,4},{4,6},{6,7},{7,5},{5,3},{3,1},{1,0},{8,9},{10,8},{12,1... | collective-permute-start | bytes 589832 | tf_op jit(solution)/shard_map/ppermute | solution.py:68
  43.8 14.4 %collective-permute-start.13 = (bf16[128,768]{1,0:T(8,128)(2,1)S(1)}, bf16[128,768]{1,0:T(8,128)(2,1)S(1)}, u32[]{:S(2)}, u32[]{:S(2)}) collective-permute-start(bf16[128,768]{1,0:T(8,128)(2,1)S(1)} %collective-permute-done.12), channel_id=1, source_target_pairs={{0,1},{2,0},{4,2},{6,4},{7,6},{5,7},{3,5},{1,3},{8,10},{10,12},{12... | collective-permute-start | bytes 589832 | tf_op jit(solution)/shard_map/ppermute | solution.py:68
  46.2 6.2 %collective-permute-start.9 = (bf16[128,768]{1,0:T(8,128)(2,1)S(1)}, bf16[128,768]{1,0:T(8,128)(2,1)S(1)}, u32[]{:S(2)}, u32[]{:S(2)}) collective-permute-start(bf16[128,768]{1,0:T(8,128)(2,1)S(1)} %collective-permute-done.8), channel_id=1, source_target_pairs={{0,2},{2,4},{4,6},{6,7},{7,5},{5,3},{3,1},{1,0},{8,9},{10,8},{12,1... | collective-permute-start | bytes 589832 | tf_op jit(solution)/shard_map/ppermute | solution.py:68
  50.3 5.7 %collective-permute-start.3 = (bf16[128,768]{1,0:T(8,128)(2,1)S(1)}, bf16[128,768]{1,0:T(8,128)(2,1)S(1)}, u32[]{:S(2)}, u32[]{:S(2)}) collective-permute-start(bf16[128,768]{1,0:T(8,128)(2,1)S(1)} %collective-permute-done.2), channel_id=1, source_target_pairs={{0,2},{2,4},{4,6},{6,7},{7,5},{5,3},{3,1},{1,0},{8,9},{10,8},{12,1... | collective-permute-start | bytes 589832 | tf_op jit(solution)/shard_map/ppermute | solution.py:68
  52.4 5.7 %collective-permute-start.10 = (bf16[128,768]{1,0:T(8,128)(2,1)S(1)}, bf16[128,768]{1,0:T(8,128)(2,1)S(1)}, u32[]{:S(2)}, u32[]{:S(2)}) collective-permute-start(bf16[128,768]{1,0:T(8,128)(2,1)S(1)} %collective-permute-done.9), channel_id=1, source_target_pairs={{0,2},{2,4},{4,6},{6,7},{7,5},{5,3},{3,1},{1,0},{8,9},{10,8},{12,1... | collective-permute-start | bytes 589832 | tf_op jit(solution)/shard_map/ppermute | solution.py:68
  54.2 4.0 %copy-start.6 = (pred[1024]{0:T(1024)(128)(4,1)S(1)}, pred[1024]{0:T(1024)(128)(4,1)}, u32[]{:S(2)}) copy-start(pred[1024]{0:T(1024)(128)(4,1)} %copy-done.5) | copy-start | bytes 3076
  60.6 3.8 %copy-start.1 = (f32[1024,1024]{0,1:T(8,128)}, f32[1024,1024]{0,1:T(8,128)S(1)}, u32[]{:S(2)}) copy-start(f32[1024,1024]{0,1:T(8,128)S(1)} %get-tuple-element.25) | copy-start | bytes 12582916
  60.6 3.8 %copy-start.8 = (s32[128]{0:T(128)S(1)}, s32[128]{0:T(128)}, u32[]{:S(2)}) copy-start(s32[128]{0:T(128)} %copy-done.7) | copy-start | bytes 1540
  60.6 3.8 %copy-start.14 = (pred[128]{0:T(512)(128)(4,1)S(1)}, pred[128]{0:T(512)(128)(4,1)}, u32[]{:S(2)}) copy-start(pred[128]{0:T(512)(128)(4,1)} %broadcast_compare_fusion.1) | copy-start | bytes 388
  64.4 6.8 %copy-start.11 = (pred[128]{0:T(512)(128)(4,1)S(1)}, pred[128]{0:T(512)(128)(4,1)}, u32[]{:S(2)}) copy-start(pred[128]{0:T(512)(128)(4,1)} %add_compare_fusion) | copy-start | bytes 388
  64.4 6.8 %copy-start.12 = (s32[128]{0:T(128)S(1)}, s32[128]{0:T(128)}, u32[]{:S(2)}) copy-start(s32[128]{0:T(128)} %fusion.60) | copy-start | bytes 1540
  66.5 8.6 %all-to-all-start.1 = ((bf16[4,32,768]{2,1,0:T(8,128)(2,1)}), bf16[4,32,768]{2,1,0:T(8,128)(2,1)S(1)}, u32[]{:S(2)}, u32[]{:S(2)}) async-start(bf16[4,32,768]{2,1,0:T(8,128)(2,1)} %bitcast.14), calls=%async_computation.1 | async-start | bytes 393216 | tf_op jit(solution)/shard_map/all_to_all | solution.py:188
  71.2 3.9 %copy-start.10 = (s32[4]{0:T(128)S(1)}, s32[4]{0:T(128)}, u32[]{:S(2)}) copy-start(s32[4]{0:T(128)} %param.12) | copy-start | bytes 52

commit v18 on v17

--- a/solution.py
+++ b/solution.py
@@ -161,7 +161,10 @@
     a_my = lax.dynamic_slice_in_dim(pair_align, mine, row_count)
     r_my = (mine + jnp.arange(row_count, dtype=jnp.int32)) < live_count
     lse_my = lax.dynamic_slice_in_dim(row_lse, mine, row_count)
-    pos_rows = perm[None, :] == a_my[:, None]
+    if steps == 1:
+        pos_rows = lax.dynamic_slice_in_dim(is_pos, mine, row_count, 0)
+    else:
+        pos_rows = perm[None, :] == a_my[:, None]
     if steps == 1:
         s_rows = lax.dynamic_slice_in_dim(scores_f, mine, row_count, 0)
     else:
@@ -174,7 +177,10 @@
     q_my = jnp.arange(row_count, dtype=jnp.int32)
     p_my = (q_my // per_slot * data_size + shard_index) * per_slot + q_my % per_slot
     clse_my = lax.dynamic_slice_in_dim(col_lse, mine, row_count)
-    pos_cols = p_my[None, :] == pair_align[:, None]
+    if steps == 1:
+        pos_cols = lax.dynamic_slice_in_dim(is_pos, mine, row_count, 1)
+    else:
+        pos_cols = p_my[None, :] == pair_align[:, None]
     c_my = jnp.max((pos_cols & row_live[:, None]).astype(jnp.int32), axis=0) > 0
     if steps == 1:
         s_cols = lax.dynamic_slice_in_dim(scores_f, mine, row_count, 1)

time: 78 us -> 78.7 us (level)
    eq x0 -> x1, other arithmetic: none -> 1.35 us  [per_device(): live_pos = (perm[None, :] == pair_align[:, None]) & row_live[:, None]]
  transfers between devices with their start and end apart: 16 -> 16, of which waited for: 8 -> 8; matrix products, arithmetic and copies ran while one was open for 22% -> 21% of each run, Pallas kernels for 0% -> 0%
where the time goes in v18:
time: 78.7 us; the launch traced here: 78 us
  starting transfers between devices  23.9 us (30%)
  waiting for transfers between devices  14.4 us (18%)
  between operations  13.1 us (17%)
  other arithmetic  9.53 us (12%)
  matrix products  8.78 us (11%)
  local copies, waits for them, and re-layouts  8.27 us (11%)
    ppermute x14, starting transfers between devices, ring_gather(): cur = lax.ppermute(cur, ('lang', 'dp'), pairs)  17.1 us
    ppermute x14, waiting for transfers between devices, ring_gather(): cur = lax.ppermute(cur, ('lang', 'dp'), pairs)  13.8 us
    all_to_all x1, starting transfers between devices, per_device(): lax.all_to_all(ordered, 'lang', split_axis=0, concat_axis=1, tiled=True)  3.5 us
    all_to_all x1, starting transfers between devices, per_device(): lax.all_to_all(grad_local.reshape(lang_size, per_slot, emb_width), 'lang'...  3.37 us
    dot_general x1, matrix products, per_device(): jnp.dot(g_rows, y_all, preferred_element_type=jnp.float32) * inv_root  3.26 us
    dot_general x1, matrix products, per_device(): lax.dot_general(g_cols, x_all, (((0,), (0,)), ((), ())), preferred_elemen...  2.81 us
    reduce_sum x1, other arithmetic, block_stats(): pos_score = jnp.sum(jnp.where(is_pos, scores_f, 0.0), axis=1)  2.43 us
    dot_general x1, matrix products, scores_of(): lax.dot_general(x_rows, y_rows, (((1,), (1,)), ((), ())), preferred_eleme...  2.39 us
  transfers between devices with their start and end apart: 16, of which 8 were waited for; matrix products, arithmetic and copies ran while one was open for 21% of the time, Pallas kernels for 0%

profile of v18, /device:TPU:0, one launch (start us, length us, event | category | flops | bytes accessed | tf_op | source)
XLA Modules:
  0.0 78.0 jit_solution(15361072449950081338)
XLA Ops:
  0.7 3.0 %collective-permute-start.4 = (bf16[128,768]{1,0:T(8,128)(2,1)}, bf16[128,768]{1,0:T(8,128)(2,1)}, u32[]{:S(2)}, u32[]{:S(2)}) collective-permute-start(bf16[128,768]{1,0:T(8,128)(2,1)} %param.10), channel_id=1, source_target_pairs={{0,1},{2,0},{4,2},{6,4},{7,6},{5,7},{3,5},{1,3},{8,10},{10,12},{12... | collective-permute-start | bytes 589832 | tf_op jit(solution)/shard_map/ppermute | solution.py:68
  3.7 0.1 collective-permute-start
  3.8 0.7 compare_select_fusion.1
  4.5 0.6 scatter_custom_fusion
  5.1 1.2 %gather_fusion = bf16[4,32,768]{2,1,0:T(8,128)(2,1)} fusion(bf16[4,32,768]{2,1,0:T(8,128)(2,1)S(1)} %copy-done, s32[1024]{0:T(1024)S(1)} %pad_clamp_fusion), kind=kCustom, calls=%fused_computation | custom fusion | bytes 393232 | tf_op jit(solution)/shard_map/gather | solution.py:114
  6.4 3.5 %all-to-all-start = ((bf16[4,32,768]{2,1,0:T(8,128)(2,1)}), bf16[4,32,768]{2,1,0:T(8,128)(2,1)S(1)}, u32[]{:S(2)}, u32[]{:S(2)}) async-start(bf16[4,32,768]{2,1,0:T(8,128)(2,1)} %gather_fusion), calls=%async_computation | async-start | bytes 393216 | tf_op jit(solution)/shard_map/all_to_all | solution.py:115
  9.9 1.2 %dynamic_slice.73 = s32[1]{0:T(128)} dynamic-slice(s32[4]{0:T(128)} %param.13, s32[]{:T(128)S(6)} %select_n.239), dynamic_slice_sizes={1} | dynamic-slice | bytes 12 | tf_op jit(solution)/shard_map/dynamic_slice | solution.py:117
  11.1 0.6 iota_compare_fusion
  11.8 1.3 %broadcast_compare_fusion = pred[1024,1024]{0,1:T(32,128)(4,1)S(1)} fusion(s32[1024]{0:T(1024)} %bitcast.25, s32[1024]{0:T(1024)S(1)} %fusion.38), kind=kLoop, calls=%fused_computation.9 | loop fusion | flops 1048576 | bytes 1056768 | tf_op jit(solution)/shard_map/eq | solution.py:123
  13.1 0.8 %convert_reduce_fusion = s32[1024]{0:T(1024)S(1)} fusion(s32[1024]{0:T(1024)S(1)} %bitcast.26, s32[1024]{0:T(1024)S(1)} %fusion.38, pred[1024]{0:T(1024)(128)(4,1)S(1)} %iota_compare_fusion), kind=kLoop, calls=%fused_computation.8 | loop fusion | flops 4193280 | bytes 13312 | tf_op jit(solution)/shard_map/reduce_max | solution.py:124
  14.0 0.6 broadcast_compare_fusion.1
  14.5 0.2 convert_reduce_fusion.1
  14.7 0.6 broadcast_compare_fusion.2
  15.3 0.1 broadcast.191.clone.1
  16.0 0.6 dynamic_slice.74
  21.3 0.7 fusion.56
  26.4 0.6 dynamic_slice.72
  26.9 1.2 %add_compare_fusion = pred[128]{0:T(512)(128)(4,1)} fusion(s32[]{:T(128)} %bitcast.1, s32[]{:T(128)S(6)} %mul.194), kind=kLoop, calls=%fused_computation.101 | loop fusion | flops 256 | bytes 136 | tf_op jit(solution)/shard_map/lt | solution.py:162
  28.1 1.9 %collective-permute-start.11 = (bf16[128,768]{1,0:T(8,128)(2,1)S(1)}, bf16[128,768]{1,0:T(8,128)(2,1)S(1)}, u32[]{:S(2)}, u32[]{:S(2)}) collective-permute-start(bf16[128,768]{1,0:T(8,128)(2,1)S(1)} %bitcast.22), channel_id=1, source_target_pairs={{0,1},{2,0},{4,2},{6,4},{7,6},{5,7},{3,5},{1,3},{8,10},{10,12},{12... | collective-permute-start | bytes 589832 | tf_op jit(solution)/shard_map/ppermute | solution.py:68
  30.0 0.1 collective-permute-start.7
  30.3 2.0 %collective-permute-start.5 = (bf16[128,768]{1,0:T(8,128)(2,1)}, bf16[128,768]{1,0:T(8,128)(2,1)S(1)}, u32[]{:S(2)}, u32[]{:S(2)}) collective-permute-start(bf16[128,768]{1,0:T(8,128)(2,1)} %collective-permute-done.4), channel_id=1, source_target_pairs={{0,1},{2,0},{4,2},{6,4},{7,6},{5,7},{3,5},{1,3},{8,10},{10,12},{12... | collective-permute-start | bytes 589832 | tf_op jit(solution)/shard_map/ppermute | solution.py:68
  32.2 0.1 collective-permute-start.1
  32.4 1.0 %constant_dynamic-update-slice_fusion.14 = bf16[1024,768]{1,0:T(8,128)(2,1)S(1)} fusion(bf16[1024,768]{1,0:T(8,128)(2,1)S(1)} %constant_dynamic-update-slice_fusion.15, bf16[128,768]{1,0:T(8,128)(2,1)} %collective-permute-done, s32[]{:T(128)S(6)} %select_n.249), kind=kLoop, calls=%fused_computation.73 | loop fusion | bytes 393220 | tf_op jit(solution)/shard_map/dynamic_update_slice | solution.py:70
  33.4 2.0 %collective-permute-done.11 = bf16[128,768]{1,0:T(8,128)(2,1)S(1)} collective-permute-done((bf16[128,768]{1,0:T(8,128)(2,1)S(1)}, bf16[128,768]{1,0:T(8,128)(2,1)S(1)}, u32[]{:S(2)}, u32[]{:S(2)}) %collective-permute-start.11) | collective-permute-done | bytes 196640 | tf_op jit(solution)/shard_map/ppermute | solution.py:68
  35.3 2.5 %collective-permute-start.12 = (bf16[128,768]{1,0:T(8,128)(2,1)S(1)}, bf16[128,768]{1,0:T(8,128)(2,1)S(1)}, u32[]{:S(2)}, u32[]{:S(2)}) collective-permute-start(bf16[128,768]{1,0:T(8,128)(2,1)S(1)} %collective-permute-done.11), channel_id=1, source_target_pairs={{0,1},{2,0},{4,2},{6,4},{7,6},{5,7},{3,5},{1,3},{8,10},{10,12},{12... | collective-permute-start | bytes 589832 | tf_op jit(solution)/shard_map/ppermute | solution.py:68
  37.8 0.1 collective-permute-start.8
  37.9 1.7 %collective-permute-done.5 = bf16[128,768]{1,0:T(8,128)(2,1)S(1)} collective-permute-done((bf16[128,768]{1,0:T(8,128)(2,1)}, bf16[128,768]{1,0:T(8,128)(2,1)S(1)}, u32[]{:S(2)}, u32[]{:S(2)}) %collective-permute-start.5) | collective-permute-done | bytes 196640 | tf_op jit(solution)/shard_map/ppermute | solution.py:68
  39.6 2.4 %collective-permute-start.6 = (bf16[128,768]{1,0:T(8,128)(2,1)S(1)}, bf16[128,768]{1,0:T(8,128)(2,1)S(1)}, u32[]{:S(2)}, u32[]{:S(2)}) collective-permute-start(bf16[128,768]{1,0:T(8,128)(2,1)S(1)} %collective-permute-done.5), channel_id=1, source_target_pairs={{0,1},{2,0},{4,2},{6,4},{7,6},{5,7},{3,5},{1,3},{8,10},{10,12},{12... | collective-permute-start | bytes 589832 | tf_op jit(solution)/shard_map/ppermute | solution.py:68
  42.0 0.1 collective-permute-start.2
  42.2 1.6 %collective-permute-done.12 = bf16[128,768]{1,0:T(8,128)(2,1)S(1)} collective-permute-done((bf16[128,768]{1,0:T(8,128)(2,1)S(1)}, bf16[128,768]{1,0:T(8,128)(2,1)S(1)}, u32[]{:S(2)}, u32[]{:S(2)}) %collective-permute-start.12) | collective-permute-done | bytes 196640 | tf_op jit(solution)/shard_map/ppermute | solution.py:68
  43.7 2.5 %collective-permute-start.13 = (bf16[128,768]{1,0:T(8,128)(2,1)S(1)}, bf16[128,768]{1,0:T(8,128)(2,1)S(1)}, u32[]{:S(2)}, u32[]{:S(2)}) collective-permute-start(bf16[128,768]{1,0:T(8,128)(2,1)S(1)} %collective-permute-done.12), channel_id=1, source_target_pairs={{0,1},{2,0},{4,2},{6,4},{7,6},{5,7},{3,5},{1,3},{8,10},{10,12},{12... | collective-permute-start | bytes 589832 | tf_op jit(solution)/shard_map/ppermute | solution.py:68
  46.2 0.1 collective-permute-start.9
  46.4 3.9 %collective-permute-done.2 = bf16[128,768]{1,0:T(8,128)(2,1)S(1)} collective-permute-done((bf16[128,768]{1,0:T(8,128)(2,1)S(1)}, bf16[128,768]{1,0:T(8,128)(2,1)S(1)}, u32[]{:S(2)}, u32[]{:S(2)}) %collective-permute-start.2) | collective-permute-done | bytes 196640 | tf_op jit(solution)/shard_map/ppermute | solution.py:68
  50.3 0.3 collective-permute-start.3
  50.6 1.8 %collective-permute-done.9 = bf16[128,768]{1,0:T(8,128)(2,1)S(1)} collective-permute-done((bf16[128,768]{1,0:T(8,128)(2,1)S(1)}, bf16[128,768]{1,0:T(8,128)(2,1)S(1)}, u32[]{:S(2)}, u32[]{:S(2)}) %collective-permute-start.9) | collective-permute-done | bytes 196640 | tf_op jit(solution)/shard_map/ppermute | solution.py:68
  52.4 1.8 %collective-permute-start.10 = (bf16[128,768]{1,0:T(8,128)(2,1)S(1)}, bf16[128,768]{1,0:T(8,128)(2,1)S(1)}, u32[]{:S(2)}, u32[]{:S(2)}) collective-permute-start(bf16[128,768]{1,0:T(8,128)(2,1)S(1)} %collective-permute-done.9), channel_id=1, source_target_pairs={{0,2},{2,4},{4,6},{6,7},{7,5},{5,3},{3,1},{1,0},{8,9},{10,8},{12,1... | collective-permute-start | bytes 589832 | tf_op jit(solution)/shard_map/ppermute | solution.py:68
  54.2 1.7 %collective-permute-done.3 = bf16[128,768]{1,0:T(8,128)(2,1)S(1)} collective-permute-done((bf16[128,768]{1,0:T(8,128)(2,1)S(1)}, bf16[128,768]{1,0:T(8,128)(2,1)S(1)}, u32[]{:S(2)}, u32[]{:S(2)}) %collective-permute-start.3) | collective-permute-done | bytes 196640 | tf_op jit(solution)/shard_map/ppermute | solution.py:68
  56.0 0.9 %constant_dynamic-update-slice_fusion.10 = bf16[1024,768]{1,0:T(8,128)(2,1)S(1)} fusion(bf16[1024,768]{1,0:T(8,128)(2,1)S(1)} %constant_dynamic-update-slice_fusion.11, bf16[128,768]{1,0:T(8,128)(2,1)} %collective-permute-done.4, s32[]{:T(128)S(6)} %select_n.261), kind=kLoop, calls=%fused_computation.69 | loop fusion | bytes 393220 | tf_op jit(solution)/shard_map/dynamic_update_slice | solution.py:70
  57.0 1.1 %collective-permute-done.10 = bf16[128,768]{1,0:T(8,128)(2,1)S(1)} collective-permute-done((bf16[128,768]{1,0:T(8,128)(2,1)S(1)}, bf16[128,768]{1,0:T(8,128)(2,1)S(1)}, u32[]{:S(2)}, u32[]{:S(2)}) %collective-permute-start.10) | collective-permute-done | bytes 196640 | tf_op jit(solution)/shard_map/ppermute | solution.py:68
  58.2 2.4 %select_reduce_fusion.4 = (f32[1024]{0:T(1024)S(1)}, f32[1024]{0:T(1024)S(1)}, f32[1024,1024]{0,1:T(8,128)S(1)}) fusion(pred[1024]{0:T(1024)(128)(4,1)S(1)} %copy-done.6, pred[1024]{0:T(1024)(128)(4,1)S(1)} %iota_compare_fusion, s32[1024]{0:T(1024)S(1)} %bitcast.27, s32[1024]{0:T(1024)S(1)} %fusion.38, ...), kind=kOutput, calls=%fused_computation.6 | convolution fusion | flops 1618999296 | bytes 7358464 | tf_op jit(solution)/shard_map/dot_general | solution.py:75
  60.6 2.4 %select_reduce_fusion = (f32[1024]{0:T(1024)S(1)}, f32[1024]{0:T(1024)S(1)}, f32[1024]{0:T(1024)S(1)}) fusion(f32[1024,1024]{0,1:T(8,128)S(1)} %get-tuple-element.25, s32[1024]{0:T(1024)S(1)} %bitcast.28, s32[1024]{0:T(1024)S(1)} %fusion.38, f32[1024]{0:T(1024)S(1)} %get-tuple-element.13, pred[1024]{0:T(1024)(128)(4,1)S(1)} %iota_compare_fusion, ...), kind=kLoop, calls=%fused_computation.2 | loop fusion | flops 9434112 | bytes 4225024 | tf_op jit(solution)/shard_map/reduce_sum | solution.py:87
  63.1 1.2 %select_reduce_fusion.5 = (f32[]{:T(128)}, f32[1024]{0:T(1024)S(1)}, f32[]{:T(128)}, f32[1024]{0:T(1024)S(1)}) fusion(f32[1024]{0:T(1024)S(1)} %get-tuple-element.13, f32[1024]{0:T(1024)S(1)} %get-tuple-element.10, f32[1024]{0:T(1024)S(1)} %get-tuple-element.9, f32[1024]{0:T(1024)S(1)} %get-tuple-element.12, f32[1024]{0:T(1024)S(1)} %get-tuple-element.11, ...), kind=kLoop, calls=%fused_computation.86 | loop fusion | flops 16382 | bytes 32780 | tf_op jit(solution)/shard_map/reduce_sum | solution.py:157
  64.4 2.8 %fusion.1 = bf16[128,768]{1,0:T(8,128)(2,1)} fusion(bf16[1024,768]{1,0:T(8,128)(2,1)S(1)} %constant_dynamic-update-slice_fusion.8, f32[1024,1024]{0,1:T(8,128)S(1)} %get-tuple-element.25, s32[]{:T(128)S(6)} %select_n.244, pred[1024,1024]{0,1:T(32,128)(4,1)} %copy-done.2, f32[128]{0:T(128)S(1)} %dynamic_slice.95, f32[1024]{0:T(1024)S(1)} %get-tuple-element.27, ...), kind=kOutput, calls=%fused_computation.13 | convolution fusion | flops 202964992 | bytes 2431492 | tf_op jit(solution)/shard_map/dot_general | solution.py:190
  67.2 3.4 %all-to-all-start.1 = ((bf16[4,32,768]{2,1,0:T(8,128)(2,1)}), bf16[4,32,768]{2,1,0:T(8,128)(2,1)S(1)}, u32[]{:S(2)}, u32[]{:S(2)}) async-start(bf16[4,32,768]{2,1,0:T(8,128)(2,1)} %bitcast.13), calls=%async_computation.1 | async-start | bytes 393216 | tf_op jit(solution)/shard_map/all_to_all | solution.py:194
  71.9 3.3 %fusion = bf16[128,768]{1,0:T(8,128)(2,1)} fusion(bf16[1024,768]{1,0:T(8,128)(2,1)S(1)} %constant_dynamic-update-slice_fusion.4, f32[1024,1024]{0,1:T(8,128)} %copy-done.1, s32[]{:T(128)S(6)} %select_n.244, pred[1024,1024]{0,1:T(32,128)(4,1)} %copy-done.2, f32[1024]{0:T(1024)S(1)} %get-tuple-element.15, f32[128]{0:T(128)S(1)} %dynamic_slice.91, f32[]{:T(128)} %bitcast, ...), kind=kOutput, calls=%fused_computation.12 | convolution fusion | flops 202964992 | bytes 2431108 | tf_op jit(solution)/shard_map/dot_general | solution.py:174
  75.2 0.7 all-to-all-done.1
  75.8 0.3 convolution_convert_fusion
  76.2 0.7 copy.16
  (53 shorter events, 0.6 us)
Async XLA Ops:
  0.6 4.5 %copy-start = (bf16[4,32,768]{2,1,0:T(8,128)(2,1)S(1)}, bf16[4,32,768]{2,1,0:T(8,128)(2,1)}, u32[]{:S(2)}) copy-start(bf16[4,32,768]{2,1,0:T(8,128)(2,1)} %param.11) | copy-start | bytes 589828
  0.6 12.5 %copy-start.5 = (s32[1,1024]{1,0:T(1,128)S(1)}, s32[1,1024]{1,0:T(1,128)}, u32[]{:S(2)}) copy-start(s32[1,1024]{1,0:T(1,128)} %param.14) | copy-start | bytes 12292
  0.7 29.6 %collective-permute-start.4 = (bf16[128,768]{1,0:T(8,128)(2,1)}, bf16[128,768]{1,0:T(8,128)(2,1)}, u32[]{:S(2)}, u32[]{:S(2)}) collective-permute-start(bf16[128,768]{1,0:T(8,128)(2,1)} %param.10), channel_id=1, source_target_pairs={{0,1},{2,0},{4,2},{6,4},{7,6},{5,7},{3,5},{1,3},{8,10},{10,12},{12... | collective-permute-start | bytes 589832 | tf_op jit(solution)/shard_map/ppermute | solution.py:68
  3.7 28.5 %collective-permute-start = (bf16[128,768]{1,0:T(8,128)(2,1)}, bf16[128,768]{1,0:T(8,128)(2,1)}, u32[]{:S(2)}, u32[]{:S(2)}) collective-permute-start(bf16[128,768]{1,0:T(8,128)(2,1)} %param.10), channel_id=1, source_target_pairs={{0,2},{2,4},{4,6},{6,7},{7,5},{5,3},{3,1},{1,0},{8,9},{10,8},{12,1... | collective-permute-start | bytes 589832 | tf_op jit(solution)/shard_map/ppermute | solution.py:68
  6.4 9.0 %copy-start.3 = (bf16[128,768]{1,0:T(8,128)(2,1)S(1)}, bf16[128,768]{1,0:T(8,128)(2,1)}, u32[]{:S(2)}) copy-start(bf16[128,768]{1,0:T(8,128)(2,1)} %param.10) | copy-start | bytes 589828
  6.4 21.8 %all-to-all-start = ((bf16[4,32,768]{2,1,0:T(8,128)(2,1)}), bf16[4,32,768]{2,1,0:T(8,128)(2,1)S(1)}, u32[]{:S(2)}, u32[]{:S(2)}) async-start(bf16[4,32,768]{2,1,0:T(8,128)(2,1)} %gather_fusion), calls=%async_computation | async-start | bytes 393216 | tf_op jit(solution)/shard_map/all_to_all | solution.py:115
  11.7 4.3 %copy-start.10 = (s32[8]{0:T(128)S(1)}, s32[8]{0:T(128)}, u32[]{:S(2)}) copy-start(s32[8]{0:T(128)} %constant.198.clone) | copy-start | bytes 100
  11.7 9.6 %copy-start.4 = (s32[8]{0:T(128)S(1)}, s32[8]{0:T(128)}, u32[]{:S(2)}) copy-start(s32[8]{0:T(128)} %constant.197.clone) | copy-start | bytes 100
  11.7 14.6 %copy-start.7 = (f32[4]{0:T(128)S(1)}, f32[4]{0:T(128)}, u32[]{:S(2)}) copy-start(f32[4]{0:T(128)} %param.15) | copy-start | bytes 52
  13.1 1.6 %copy-start.2 = (pred[1024,1024]{0,1:T(32,128)(4,1)}, pred[1024,1024]{0,1:T(32,128)(4,1)S(1)}, u32[]{:S(2)}) copy-start(pred[1024,1024]{0,1:T(32,128)(4,1)S(1)} %broadcast_compare_fusion) | copy-start | bytes 3145732
  28.1 7.2 %collective-permute-start.11 = (bf16[128,768]{1,0:T(8,128)(2,1)S(1)}, bf16[128,768]{1,0:T(8,128)(2,1)S(1)}, u32[]{:S(2)}, u32[]{:S(2)}) collective-permute-start(bf16[128,768]{1,0:T(8,128)(2,1)S(1)} %bitcast.22), channel_id=1, source_target_pairs={{0,1},{2,0},{4,2},{6,4},{7,6},{5,7},{3,5},{1,3},{8,10},{10,12},{12... | collective-permute-start | bytes 589832 | tf_op jit(solution)/shard_map/ppermute | solution.py:68
  30.0 7.8 %collective-permute-start.7 = (bf16[128,768]{1,0:T(8,128)(2,1)S(1)}, bf16[128,768]{1,0:T(8,128)(2,1)S(1)}, u32[]{:S(2)}, u32[]{:S(2)}) collective-permute-start(bf16[128,768]{1,0:T(8,128)(2,1)S(1)} %bitcast.23), channel_id=1, source_target_pairs={{0,2},{2,4},{4,6},{6,7},{7,5},{5,3},{3,1},{1,0},{8,9},{10,8},{12,1... | collective-permute-start | bytes 589832 | tf_op jit(solution)/shard_map/ppermute | solution.py:68
  30.3 9.3 %collective-permute-start.5 = (bf16[128,768]{1,0:T(8,128)(2,1)}, bf16[128,768]{1,0:T(8,128)(2,1)S(1)}, u32[]{:S(2)}, u32[]{:S(2)}) collective-permute-start(bf16[128,768]{1,0:T(8,128)(2,1)} %collective-permute-done.4), channel_id=1, source_target_pairs={{0,1},{2,0},{4,2},{6,4},{7,6},{5,7},{3,5},{1,3},{8,10},{10,12},{12... | collective-permute-start | bytes 589832 | tf_op jit(solution)/shard_map/ppermute | solution.py:68
  32.2 9.8 %collective-permute-start.1 = (bf16[128,768]{1,0:T(8,128)(2,1)}, bf16[128,768]{1,0:T(8,128)(2,1)S(1)}, u32[]{:S(2)}, u32[]{:S(2)}) collective-permute-start(bf16[128,768]{1,0:T(8,128)(2,1)} %collective-permute-done), channel_id=1, source_target_pairs={{0,2},{2,4},{4,6},{6,7},{7,5},{5,3},{3,1},{1,0},{8,9},{10,8},{12,1... | collective-permute-start | bytes 589832 | tf_op jit(solution)/shard_map/ppermute | solution.py:68
  35.3 8.4 %collective-permute-start.12 = (bf16[128,768]{1,0:T(8,128)(2,1)S(1)}, bf16[128,768]{1,0:T(8,128)(2,1)S(1)}, u32[]{:S(2)}, u32[]{:S(2)}) collective-permute-start(bf16[128,768]{1,0:T(8,128)(2,1)S(1)} %collective-permute-done.11), channel_id=1, source_target_pairs={{0,1},{2,0},{4,2},{6,4},{7,6},{5,7},{3,5},{1,3},{8,10},{10,12},{12... | collective-permute-start | bytes 589832 | tf_op jit(solution)/shard_map/ppermute | solution.py:68
  37.8 8.4 %collective-permute-start.8 = (bf16[128,768]{1,0:T(8,128)(2,1)S(1)}, bf16[128,768]{1,0:T(8,128)(2,1)S(1)}, u32[]{:S(2)}, u32[]{:S(2)}) collective-permute-start(bf16[128,768]{1,0:T(8,128)(2,1)S(1)} %collective-permute-done.7), channel_id=1, source_target_pairs={{0,2},{2,4},{4,6},{6,7},{7,5},{5,3},{3,1},{1,0},{8,9},{10,8},{12,1... | collective-permute-start | bytes 589832 | tf_op jit(solution)/shard_map/ppermute | solution.py:68
  39.6 17.3 %collective-permute-start.6 = (bf16[128,768]{1,0:T(8,128)(2,1)S(1)}, bf16[128,768]{1,0:T(8,128)(2,1)S(1)}, u32[]{:S(2)}, u32[]{:S(2)}) collective-permute-start(bf16[128,768]{1,0:T(8,128)(2,1)S(1)} %collective-permute-done.5), channel_id=1, source_target_pairs={{0,1},{2,0},{4,2},{6,4},{7,6},{5,7},{3,5},{1,3},{8,10},{10,12},{12... | collective-permute-start | bytes 589832 | tf_op jit(solution)/shard_map/ppermute | solution.py:68
  42.0 8.3 %collective-permute-start.2 = (bf16[128,768]{1,0:T(8,128)(2,1)S(1)}, bf16[128,768]{1,0:T(8,128)(2,1)S(1)}, u32[]{:S(2)}, u32[]{:S(2)}) collective-permute-start(bf16[128,768]{1,0:T(8,128)(2,1)S(1)} %collective-permute-done.1), channel_id=1, source_target_pairs={{0,2},{2,4},{4,6},{6,7},{7,5},{5,3},{3,1},{1,0},{8,9},{10,8},{12,1... | collective-permute-start | bytes 589832 | tf_op jit(solution)/shard_map/ppermute | solution.py:68
  43.7 14.4 %collective-permute-start.13 = (bf16[128,768]{1,0:T(8,128)(2,1)S(1)}, bf16[128,768]{1,0:T(8,128)(2,1)S(1)}, u32[]{:S(2)}, u32[]{:S(2)}) collective-permute-start(bf16[128,768]{1,0:T(8,128)(2,1)S(1)} %collective-permute-done.12), channel_id=1, source_target_pairs={{0,1},{2,0},{4,2},{6,4},{7,6},{5,7},{3,5},{1,3},{8,10},{10,12},{12... | collective-permute-start | bytes 589832 | tf_op jit(solution)/shard_map/ppermute | solution.py:68
  46.2 6.2 %collective-permute-start.9 = (bf16[128,768]{1,0:T(8,128)(2,1)S(1)}, bf16[128,768]{1,0:T(8,128)(2,1)S(1)}, u32[]{:S(2)}, u32[]{:S(2)}) collective-permute-start(bf16[128,768]{1,0:T(8,128)(2,1)S(1)} %collective-permute-done.8), channel_id=1, source_target_pairs={{0,2},{2,4},{4,6},{6,7},{7,5},{5,3},{3,1},{1,0},{8,9},{10,8},{12,1... | collective-permute-start | bytes 589832 | tf_op jit(solution)/shard_map/ppermute | solution.py:68
  50.3 5.7 %collective-permute-start.3 = (bf16[128,768]{1,0:T(8,128)(2,1)S(1)}, bf16[128,768]{1,0:T(8,128)(2,1)S(1)}, u32[]{:S(2)}, u32[]{:S(2)}) collective-permute-start(bf16[128,768]{1,0:T(8,128)(2,1)S(1)} %collective-permute-done.2), channel_id=1, source_target_pairs={{0,2},{2,4},{4,6},{6,7},{7,5},{5,3},{3,1},{1,0},{8,9},{10,8},{12,1... | collective-permute-start | bytes 589832 | tf_op jit(solution)/shard_map/ppermute | solution.py:68
  52.4 5.7 %collective-permute-start.10 = (bf16[128,768]{1,0:T(8,128)(2,1)S(1)}, bf16[128,768]{1,0:T(8,128)(2,1)S(1)}, u32[]{:S(2)}, u32[]{:S(2)}) collective-permute-start(bf16[128,768]{1,0:T(8,128)(2,1)S(1)} %collective-permute-done.9), channel_id=1, source_target_pairs={{0,2},{2,4},{4,6},{6,7},{7,5},{5,3},{3,1},{1,0},{8,9},{10,8},{12,1... | collective-permute-start | bytes 589832 | tf_op jit(solution)/shard_map/ppermute | solution.py:68
  54.2 4.0 %copy-start.6 = (pred[1024]{0:T(1024)(128)(4,1)S(1)}, pred[1024]{0:T(1024)(128)(4,1)}, u32[]{:S(2)}) copy-start(pred[1024]{0:T(1024)(128)(4,1)} %broadcast_compare_fusion.1) | copy-start | bytes 3076
  60.6 3.8 %copy-start.1 = (f32[1024,1024]{0,1:T(8,128)}, f32[1024,1024]{0,1:T(8,128)S(1)}, u32[]{:S(2)}) copy-start(f32[1024,1024]{0,1:T(8,128)S(1)} %get-tuple-element.25) | copy-start | bytes 12582916
  60.6 3.8 %copy-start.11 = (pred[128]{0:T(512)(128)(4,1)S(1)}, pred[128]{0:T(512)(128)(4,1)}, u32[]{:S(2)}) copy-start(pred[128]{0:T(512)(128)(4,1)} %broadcast_compare_fusion.2) | copy-start | bytes 388
  64.4 7.5 %copy-start.9 = (pred[128]{0:T(512)(128)(4,1)S(1)}, pred[128]{0:T(512)(128)(4,1)}, u32[]{:S(2)}) copy-start(pred[128]{0:T(512)(128)(4,1)} %add_compare_fusion) | copy-start | bytes 388
  67.2 8.6 %all-to-all-start.1 = ((bf16[4,32,768]{2,1,0:T(8,128)(2,1)}), bf16[4,32,768]{2,1,0:T(8,128)(2,1)S(1)}, u32[]{:S(2)}, u32[]{:S(2)}) async-start(bf16[4,32,768]{2,1,0:T(8,128)(2,1)} %bitcast.13), calls=%async_computation.1 | async-start | bytes 393216 | tf_op jit(solution)/shard_map/all_to_all | solution.py:194
  71.9 3.9 %copy-start.8 = (s32[4]{0:T(128)S(1)}, s32[4]{0:T(128)}, u32[]{:S(2)}) copy-start(s32[4]{0:T(128)} %param.12) | copy-start | bytes 52
